TPU v7x, 32 devices: a whole 2x2x4 slice. The times are simulated.
32 devices in a mesh: groups: 2 (over x), tok: 16 (over z, y, core).
Axes of the slice: x: 2, y: 2, z: 4, core: 2. Of those that a mesh axis runs over, the one named last changes fastest.
Arguments:
- queries: bfloat16 [2, 8192, 1024], P(None, ('groups', 'tok')), parts along dimension 1, may hold values from -6 to 6
- keys: bfloat16 [2, 8192, 1024], P(None, ('groups', 'tok')), parts along dimension 1, may hold values from -6 to 6
- values: bfloat16 [2, 8192, 1024], P(None, ('groups', 'tok')), parts along dimension 1, may hold values from -6 to 6
- rates: float32 [2, 3, 2, 8192], P(None, None, None, ('groups', 'tok')), parts along dimension 3, may hold values from 0.0002 to 0.002
- fast_weights: float32 [2, 3, 512, 512], P(None, None, 'tok'), may hold values from -0.25 to 0.25
Outputs:
- attended: bfloat16 [2, 8192, 1024], P(None, ('groups', 'tok')), parts along dimension 1
- final_weights: float32 [4, 3, 512, 512], P('groups', None, 'tok'), parts along dimension 0
There are 2 independent parts, one for each index of `groups`. A program takes and returns all parts, laid end to end along the dimension named above; an argument that names none is the same for every part. Nothing has to cross between parts.
All inputs are finite; a program needn't handle non-finite values.
Results may differ from a plain program's by a relative error of at most 0.0098.
Values may be sent and summed in bfloat16 or wider, within the bound.
No kernel may reach another device: no remote copies, remote signals or barrier semaphores. Data moves between devices by JAX's collectives and lax.ppermute only.
A program may use at most 64 MiB of HBM per device.

v0:
```python
import jax
import jax.numpy as jnp
from jax import lax
from jax.sharding import PartitionSpec as P


def cross(left, right):
    return lax.dot_general(
        left, right, (((1,), (1,)), ((), ())), preferred_element_type=jnp.float32
    )


def inner(left, right):
    return lax.dot_general(
        left, right, (((0,), (0,)), ((), ())), preferred_element_type=jnp.float32
    )


def renorm(old, upd):
    old_norm = jnp.sqrt(jnp.mean(old * old, axis=-1))
    new_norm = jnp.sqrt(jnp.mean(upd * upd, axis=-1) + 1e-06)
    return upd * (old_norm / new_norm)[..., None]


def head_step(query, key_rows, value_rows, rate_rows, wbf):
    hidden_q = (jax.nn.silu(cross(query, wbf[0])) * cross(query, wbf[1])).astype(jnp.bfloat16)
    raw = cross(hidden_q, wbf[2])
    normed = (raw / jnp.sqrt(jnp.mean(raw * raw, axis=-1, keepdims=True) + 1e-06)).astype(
        jnp.bfloat16
    )
    h1 = cross(key_rows, wbf[0])
    h3 = cross(key_rows, wbf[1])
    sig = jax.nn.sigmoid(h1)
    act = h1 * sig
    back = jnp.dot(value_rows, wbf[2], preferred_element_type=jnp.float32)
    d1 = back * h3 * sig * (1.0 + h1 * (1.0 - sig))
    d3 = back * act
    e1 = (rate_rows[0][:, None] * d1).astype(jnp.bfloat16)
    e3 = (rate_rows[1][:, None] * d3).astype(jnp.bfloat16)
    b2 = (rate_rows[2][:, None] * (act * h3)).astype(jnp.bfloat16)
    grad = jnp.stack([inner(e1, key_rows), inner(e3, key_rows), inner(value_rows, b2)])
    return (normed, grad)


def block_step(span, gathered, queries, keys, values, rates):
    heads = gathered.shape[0]
    width = gathered.shape[3]
    pieces = []
    grads = []
    for head in range(heads):
        lo = head * width
        normed, grad = head_step(
            queries[span][:, lo : lo + width],
            keys[span][:, lo : lo + width],
            values[span][:, lo : lo + width],
            rates[span][:, head],
            gathered[head],
        )
        pieces.append(normed)
        grads.append(grad)
    return (jnp.concatenate(pieces, axis=1), jnp.stack(grads))


def fetch(own):
    return lax.all_gather(own.astype(jnp.bfloat16), "tok", axis=2, tiled=True)


def settle(partial_value, own):
    total = lax.psum_scatter(partial_value, "tok", scatter_dimension=2, tiled=True)
    return renorm(own, own + total)


def on_device(queries, keys, values, rates, fast_weights):
    nblocks = queries.shape[0]
    own = fast_weights
    blocks = []
    for span in range(nblocks):
        gathered = fetch(own)
        normed, partial_value = block_step(span, gathered, queries, keys, values, rates)
        blocks.append(normed)
        own = settle(partial_value, own)
    return (jnp.stack(blocks), own)


def solution(mesh):
    placed = (
        P(None, ("groups", "tok"), None),
        P(None, ("groups", "tok"), None),
        P(None, ("groups", "tok"), None),
        P(None, None, None, ("groups", "tok")),
        P(None, None, "tok", None),
    )
    return jax.shard_map(
        on_device,
        mesh=mesh,
        in_specs=placed,
        out_specs=(P(None, ("groups", "tok"), None), P("groups", None, "tok", None)),
        check_vma=False,
    )
```

profile of v0, /device:TPU:0, one launch (start us, length us, event | category | flops | bytes accessed | tf_op | source)
XLA Modules:
  0.0 308.0 jit_solution(13420339890189697955)
XLA Ops:
  7.2 1.9 multiply_reduce_fusion.7
  9.2 0.7 slice_bitcast_fusion.46
  9.9 0.6 fusion.122
  10.5 2.2 slice_bitcast_fusion.12
  12.8 1.1 slice_bitcast_fusion.13
  13.8 45.2 %all-gather.3.cloned.1.call-done = bf16[2,3,512,512]{3,2,1,0:T(8,128)(2,1)} async-done(((bf16[2,3,32,512]{3,2,1,0:T(8,128)(2,1)}), bf16[2,3,512,512]{3,2,1,0:T(8,128)(2,1)}) %all-gather.3.cloned.1.call-update) | async-done | bytes 3145744 | tf_op jit(solution)/shard_map/all_gather | solution.py:65
  59.0 1.6 fusion.34
  60.6 1.4 fusion.37
  62.0 1.4 convolution_bitcast_fusion.10
  63.5 0.3 fusion.36
  63.8 0.5 convolution_bitcast_fusion.11
  64.5 0.4 convolution_bitcast_fusion.9
  65.0 0.3 fusion.38
  65.6 0.4 convolution_bitcast_fusion.6
  66.4 0.5 convolution_bitcast_fusion.8
  66.9 0.5 convolution_bitcast_fusion.7
  68.0 3.4 %pad_maximum_fusion = f32[2,3,512,512]{3,2,1,0:T(8,128)} fusion(f32[1,3,512,512]{3,2,1,0:T(8,128)S(1)} %maximum_bitcast_fusion.1, f32[1,3,512,512]{3,2,1,0:T(8,128)S(1)} %maximum_bitcast_fusion), kind=kLoop, calls=%fused_computation | loop fusion | flops 1572864 | bytes 12582912 | tf_op jit(solution)/shard_map/stack | solution.py:61
  71.5 83.5 %reduce-scatter.3.cloned.1.call-done = f32[2,3,32,512]{3,2,1,0:T(8,128)} async-done(((f32[2,3,512,512]{3,2,1,0:T(8,128)}), f32[2,3,32,512]{3,2,1,0:T(8,128)}) %reduce-scatter.3.cloned.1.call-update) | async-done | bytes 393232 | tf_op jit(solution)/shard_map/reduce_scatter | solution.py:69
  155.0 1.2 multiply_reduce_fusion.6
  156.2 0.8 multiply_convert_fusion.12
  157.2 45.1 %all-gather.5.cloned.1.call-done = bf16[2,3,512,512]{3,2,1,0:T(8,128)(2,1)} async-done(((bf16[2,3,32,512]{3,2,1,0:T(8,128)(2,1)}), bf16[2,3,512,512]{3,2,1,0:T(8,128)(2,1)}) %all-gather.5.cloned.1.call-update) | async-done | bytes 3145744 | tf_op jit(solution)/shard_map/all_gather | solution.py:65
  202.4 1.6 convolution_bitcast_fusion.16
  204.0 1.4 convolution_bitcast_fusion.13
  205.4 1.4 convolution_bitcast_fusion.4
  207.2 0.5 convolution_bitcast_fusion.5
  207.9 0.4 convolution_bitcast_fusion.3
  209.0 0.4 convolution_bitcast_fusion
  209.8 0.5 convolution_bitcast_fusion.2
  210.3 0.5 convolution_bitcast_fusion.1
  211.4 3.4 %pad_maximum_fusion.1 = f32[2,3,512,512]{3,2,1,0:T(8,128)} fusion(f32[1,3,512,512]{3,2,1,0:T(8,128)S(1)} %maximum_bitcast_fusion.3, f32[1,3,512,512]{3,2,1,0:T(8,128)S(1)} %maximum_bitcast_fusion.2), kind=kLoop, calls=%fused_computation.1 | loop fusion | flops 1572864 | bytes 12582912 | tf_op jit(solution)/shard_map/stack | solution.py:61
  214.8 2.1 slice_bitcast_fusion.17
  216.9 0.8 copy-done.7
  217.6 1.2 fusion.39
  218.8 2.5 multiply_reduce_fusion.2
  221.3 2.1 fusion.35
  223.4 2.5 multiply_reduce_fusion.3
  226.0 1.6 divide_convert_fusion.2
  227.5 0.9 maximum_bitcast_fusion.4
  228.4 2.3 convolution_bitcast_fusion.19
  230.7 2.5 multiply_reduce_fusion
  233.2 2.1 convolution_bitcast_fusion.21
  235.3 2.5 multiply_reduce_fusion.1
  237.8 1.1 divide_convert_fusion
  239.0 1.1 divide_convert_fusion.1
  240.2 2.1 pad_maximum_fusion.2
  242.3 56.0 %reduce-scatter.5.cloned.1.call-done = f32[2,3,32,512]{3,2,1,0:T(8,128)} async-done(((f32[2,3,512,512]{3,2,1,0:T(8,128)}), f32[2,3,32,512]{3,2,1,0:T(8,128)}) %reduce-scatter.5.cloned.1.call-update) | async-done | bytes 393232 | tf_op jit(solution)/shard_map/reduce_scatter | solution.py:69
  298.3 1.2 multiply_reduce_fusion.5
  299.6 1.9 broadcast_multiply_fusion
  (48 shorter events, 4.0 us)
Async XLA Ops:
  7.2 5.6 %copy-start.8 = (bf16[2,256,1024]{2,1,0:T(8,128)(2,1)S(1)}, bf16[2,256,1024]{2,1,0:T(8,128)(2,1)}, u32[]{:S(2)}) copy-start(bf16[2,256,1024]{2,1,0:T(8,128)(2,1)} %param.7) | copy-start | bytes 3145732
  7.2 51.8 %all-gather.3.cloned.1.call-start = ((), (), s32[]{:S(2)}) async-start(), calls=%async_computation.2 | async-start | bytes 3342336 | tf_op jit(solution)/shard_map/all_gather | solution.py:65
  9.2 145.8 %reduce-scatter.3.cloned.1.call-start = ((), (), s32[]{:S(2)}) async-start(), calls=%async_computation.3 | async-start | bytes 6684672 | tf_op jit(solution)/shard_map/reduce_scatter | solution.py:69
  59.0 4.5 %copy-start = (bf16[2,3,512,512]{3,2,1,0:T(8,128)(2,1)S(1)}, bf16[2,3,512,512]{3,2,1,0:T(8,128)(2,1)}, u32[]{:S(2)}) copy-start(bf16[2,3,512,512]{3,2,1,0:T(8,128)(2,1)} %all-gather.3.cloned.1.call-done) | copy-start | bytes 9437188
  59.0 4.5 %copy-start.4 = (bf16[256,1024]{1,0:T(8,128)(2,1)S(1)}, bf16[256,1024]{1,0:T(8,128)(2,1)}, u32[]{:S(2)}) copy-start(bf16[256,1024]{1,0:T(8,128)(2,1)} %get-tuple-element.9) | copy-start | bytes 1572868
  63.5 1.0 copy-start.6
  71.4 131.0 %all-gather.5.cloned.1.call-start = ((), (), s32[]{:S(2)}) async-start(), calls=%async_computation.4 | async-start | bytes 3342336 | tf_op jit(solution)/shard_map/all_gather | solution.py:65
  157.0 141.3 %reduce-scatter.5.cloned.1.call-start = ((), (), s32[]{:S(2)}) async-start(), calls=%async_computation.5 | async-start | bytes 6684672 | tf_op jit(solution)/shard_map/reduce_scatter | solution.py:69
  202.4 4.5 %copy-start.1 = (bf16[2,3,512,512]{3,2,1,0:T(8,128)(2,1)S(1)}, bf16[2,3,512,512]{3,2,1,0:T(8,128)(2,1)}, u32[]{:S(2)}) copy-start(bf16[2,3,512,512]{3,2,1,0:T(8,128)(2,1)} %all-gather.5.cloned.1.call-done) | copy-start | bytes 9437188
  202.4 4.5 %copy-start.3 = (bf16[256,1024]{1,0:T(8,128)(2,1)S(1)}, bf16[256,1024]{1,0:T(8,128)(2,1)}, u32[]{:S(2)}) copy-start(bf16[256,1024]{1,0:T(8,128)(2,1)} %get-tuple-element.8) | copy-start | bytes 1572868
  204.0 3.2 %copy-start.11 = (f32[1,1,256]{2,1,0:T(1,128)S(1)}, f32[1,1,256]{2,1,0:T(1,128)}, u32[]{:S(2)}) copy-start(f32[1,1,256]{2,1,0:T(1,128)} %get-tuple-element.16) | copy-start | bytes 3076
  206.8 1.0 copy-start.5
  206.9 1.0 copy-start.10
  207.7 1.3 copy-start.9
  216.9 0.8 copy-start.7
  225.9 4.8 %copy-start.2 = (bf16[2,3,512,512]{3,2,1,0:T(8,128)(2,1)S(1)}, bf16[2,3,512,512]{3,2,1,0:T(8,128)(2,1)}, u32[]{:S(2)}) copy-start(bf16[2,3,512,512]{3,2,1,0:T(8,128)(2,1)} %all-gather.5.cloned.1.call-done) | copy-start | bytes 9437188
Sparse Core Ops, SparseCore 0:
  10.7 48.2 all-gather.2
  71.5 83.3 reduce-scatter.2
  157.7 44.6 all-gather.4
  214.9 83.3 reduce-scatter.4
where the time goes:
time: 309 us; the launch traced here: 308 us
  waiting for transfers between devices  230 us (74%)
  matrix products  33.9 us (11%)
  other arithmetic  22 us (7%)
  between operations  14.1 us (5%)
  local copies, waits for them, and re-layouts  7.79 us (3%)
    reduce_scatter x2, waiting for transfers between devices, settle(): lax.psum_scatter(partial_value, 'tok', scatter_dimension=2, tiled=True)  140 us
    all_gather x2, waiting for transfers between devices, fetch(): return lax.all_gather(own.astype(jnp.bfloat16), 'tok', axis=2, tiled=True)  90.3 us
    dot_general x16, matrix products, cross(): lax.dot_general(left, right, (((1,), (1,)), ((), ())), preferred_element_...  22.8 us
    another operation x6, other arithmetic, block_step(): return (jnp.concatenate(pieces, axis=1), jnp.stack(grads))  7.97 us
    dot_general x12, matrix products, inner(): lax.dot_general(left, right, (((0,), (0,)), ((), ())), preferred_element_...  7.62 us
  transfers between devices with their start and end apart: 4, of which 4 were waited for; matrix products, arithmetic and copies ran while one was open for 10% of the time, Pallas kernels for 0%

commit v1 on v0

--- a/solution.py
+++ b/solution.py
@@ -61,28 +61,104 @@
     return (jnp.concatenate(pieces, axis=1), jnp.stack(grads))
 
 
-def fetch(own):
-    return lax.all_gather(own.astype(jnp.bfloat16), "tok", axis=2, tiled=True)
+class Ring:
+    def __init__(self, mesh):
+        tok = mesh.shape["tok"]
+        chips = tok // 2
+        coords = [tuple(mesh.devices[0, 2 * c].coords) for c in range(chips)]
+        ys = sorted({c[1] for c in coords})
+        if len(ys) == 2:
+            ahead = sorted((c for c in range(chips) if coords[c][1] == ys[0]), key=lambda c: coords[c][2])
+            back = sorted((c for c in range(chips) if coords[c][1] == ys[1]), key=lambda c: -coords[c][2])
+            cycle = ahead + back
+        else:
+            cycle = sorted(range(chips), key=lambda c: (coords[c][1], coords[c][2]))
+        self.chips = chips
+        self.cycle = cycle
+        place = [0] * chips
+        for i, c in enumerate(cycle):
+            place[c] = i
+        self.place = place
+        self.cw = [(cycle[p] * 2 + k, cycle[(p + 1) % chips] * 2 + k) for p in range(chips) for k in range(2)]
+        self.ccw = [(cycle[p] * 2 + k, cycle[(p - 1) % chips] * 2 + k) for p in range(chips) for k in range(2)]
+        self.swap = [(t, t ^ 1) for t in range(tok)]
+        self.ncw = chips // 2
+        self.nccw = chips - 1 - self.ncw
 
+    def chip_at(self, step):
+        me = lax.axis_index("tok") // 2
+        where = jnp.array(self.place, jnp.int32)[me]
+        return jnp.array(self.cycle, jnp.int32)[(where + step) % self.chips]
 
-def settle(partial_value, own):
-    total = lax.psum_scatter(partial_value, "tok", scatter_dimension=2, tiled=True)
-    return renorm(own, own + total)
+    def gather(self, own):
+        h, g, rows, f = own.shape
+        core = lax.axis_index("tok") % 2
+        full = jnp.zeros((self.chips, 2, h, g, rows, f), own.dtype)
 
+        def put(full, piece, chip):
+            full = lax.dynamic_update_slice(full, piece[None, None], (chip, core, 0, 0, 0, 0))
+            other = lax.ppermute(piece, "tok", self.swap)
+            return lax.dynamic_update_slice(full, other[None, None], (chip, 1 - core, 0, 0, 0, 0))
 
-def on_device(queries, keys, values, rates, fast_weights):
-    nblocks = queries.shape[0]
-    own = fast_weights
-    blocks = []
-    for span in range(nblocks):
-        gathered = fetch(own)
-        normed, partial_value = block_step(span, gathered, queries, keys, values, rates)
-        blocks.append(normed)
-        own = settle(partial_value, own)
-    return (jnp.stack(blocks), own)
+        full = put(full, own, lax.axis_index("tok") // 2)
+        a = own
+        b = own
+        for k in range(1, max(self.ncw, self.nccw) + 1):
+            if k <= self.ncw:
+                a = lax.ppermute(a, "tok", self.cw)
+                full = put(full, a, self.chip_at(-k))
+            if k <= self.nccw:
+                b = lax.ppermute(b, "tok", self.ccw)
+                full = put(full, b, self.chip_at(k))
+        full = jnp.moveaxis(full, (0, 1), (2, 3))
+        return full.reshape(h, g, self.chips * 2 * rows, f)
+
+    def reduce(self, part):
+        h, g, r, f = part.shape
+        rows = r // (2 * self.chips)
+        q = part.reshape(h, g, self.chips, 2, rows, f)
+        core = lax.axis_index("tok") % 2
+
+        def chip_sum(step):
+            chip = self.chip_at(step)
+            keep = lax.dynamic_slice(q, (0, 0, chip, core, 0, 0), (h, g, 1, 1, rows, f))
+            send = lax.dynamic_slice(q, (0, 0, chip, 1 - core, 0, 0), (h, g, 1, 1, rows, f))
+            got = lax.ppermute(send, "tok", self.swap)
+            return (keep + got).reshape(h, g, rows, f)
+
+        total = chip_sum(0)
+        a = chip_sum(self.ncw) if self.ncw else None
+        b = chip_sum(-self.nccw) if self.nccw else None
+        for k in range(1, max(self.ncw, self.nccw) + 1):
+            if k <= self.ncw:
+                a = lax.ppermute(a, "tok", self.cw)
+                if k < self.ncw:
+                    a = a + chip_sum(self.ncw - k)
+            if k <= self.nccw:
+                b = lax.ppermute(b, "tok", self.ccw)
+                if k < self.nccw:
+                    b = b + chip_sum(-self.nccw + k)
+        if a is not None:
+            total = total + a
+        if b is not None:
+            total = total + b
+        return total
 
 
 def solution(mesh):
+    ring = Ring(mesh)
+
+    def on_device(queries, keys, values, rates, fast_weights):
+        nblocks = queries.shape[0]
+        own = fast_weights
+        blocks = []
+        for span in range(nblocks):
+            gathered = ring.gather(own.astype(jnp.bfloat16))
+            normed, partial_value = block_step(span, gathered, queries, keys, values, rates)
+            blocks.append(normed)
+            own = renorm(own, own + ring.reduce(partial_value))
+        return (jnp.stack(blocks), own)
+
     placed = (
         P(None, ("groups", "tok"), None),
         P(None, ("groups", "tok"), None),

time: 309 us -> 205 us (0.66)
  waiting for transfers between devices: 230 us -> 85.5 us
  starting transfers between devices: 0.34 us -> 36 us
  between operations: 14.1 us -> 26.1 us
  matrix products: 33.9 us -> 22.8 us
  local copies, waits for them, and re-layouts: 7.79 us -> 15.2 us
  other arithmetic: 22 us -> 18.8 us
    reduce_scatter x2 -> x0, waiting for transfers between devices: 140 us -> none  [settle(): lax.psum_scatter(partial_value, 'tok', scatter_dimension=2, tiled=True)]
    all_gather x2 -> x0, waiting for transfers between devices: 90.3 us -> none  [fetch(): return lax.all_gather(own.astype(jnp.bfloat16), 'tok', axis=2, tiled=True)]
    ppermute x0 -> x60, waiting for transfers between devices: none -> 85.5 us  [the longest x8 48.5 us: reduce(): a = lax.ppermute(a, 'tok', self.cw)]
    ppermute x0 -> x60, starting transfers between devices: none -> 36 us  [the longest x8 14.8 us: gather(): a = lax.ppermute(a, 'tok', self.cw)]
    add x0 -> x6, other arithmetic: none -> 9.35 us  [reduce(): a = a + chip_sum(self.ncw - k)]
    dot_general x16, matrix products: 22.8 us -> 16.4 us  [cross(): lax.dot_general(left, right, (((1,), (1,)), ((), ())), preferred_element_...]
    another operation x6 -> x2, other arithmetic: 7.97 us -> 2.11 us  [block_step(): return (jnp.concatenate(pieces, axis=1), jnp.stack(grads))]
    dynamic_slice x0 -> x4, local copies, waits for them, and re-layouts: none -> 4.21 us  [the longest x2 2.93 us: chip_sum(): lax.dynamic_slice(q, (0, 0, chip, 1 - core, 0, 0), (h, g, 1, 1, rows, f))]
  transfers between devices with their start and end apart: 4 -> 60, of which waited for: 4 -> 29; matrix products, arithmetic and copies ran while one was open for 10% -> 17% of each run, Pallas kernels for 0% -> 0%
where the time goes in v1:
time: 205 us; the launch traced here: 204 us
  waiting for transfers between devices  85.5 us (42%)
  starting transfers between devices  36 us (18%)
  between operations  26.1 us (13%)
  matrix products  22.8 us (11%)
  other arithmetic  18.8 us (9%)
  local copies, waits for them, and re-layouts  15.2 us (7%)
    ppermute x8, waiting for transfers between devices, reduce(): a = lax.ppermute(a, 'tok', self.cw)  48.5 us
    ppermute x8, waiting for transfers between devices, gather(): a = lax.ppermute(a, 'tok', self.cw)  21.9 us
    dot_general x16, matrix products, cross(): lax.dot_general(left, right, (((1,), (1,)), ((), ())), preferred_element_...  16.4 us
    ppermute x8, starting transfers between devices, gather(): a = lax.ppermute(a, 'tok', self.cw)  14.8 us
    ppermute x8, starting transfers between devices, reduce(): a = lax.ppermute(a, 'tok', self.cw)  12.5 us
    add x6, other arithmetic, reduce(): a = a + chip_sum(self.ncw - k)  9.35 us
    ppermute x6, waiting for transfers between devices, gather(): b = lax.ppermute(b, 'tok', self.ccw)  5.68 us
    ppermute x6, waiting for transfers between devices, reduce(): b = lax.ppermute(b, 'tok', self.ccw)  5.03 us
  transfers between devices with their start and end apart: 60, of which 29 were waited for; matrix products, arithmetic and copies ran while one was open for 17% of the time, Pallas kernels for 0%

profile of v1, /device:TPU:0, one launch (start us, length us, event | category | flops | bytes accessed | tf_op | source)
XLA Modules:
  0.0 204.4 jit_solution(8217441935833956892)
XLA Ops:
  2.4 3.1 %collective-permute-start.1 = (bf16[2,3,32,512]{3,2,1,0:T(8,128)(2,1)}, bf16[2,3,32,512]{3,2,1,0:T(8,128)(2,1)S(1)}, u32[]{:S(2)}, u32[]{:S(2)}) collective-permute-start(bf16[2,3,32,512]{3,2,1,0:T(8,128)(2,1)} %get-tuple-element.9), channel_id=1, source_target_pairs={{0,4},{1,5},{4,8},{5,9},{8,12},{9,13},{12,14},{13,15},{14,10},{15,... | collective-permute-start | bytes 589832 | tf_op jit(solution)/shard_map/ppermute | solution.py:108
  26.2 2.3 %slice_bitcast_fusion = (bf16[256,1024]{1,0:T(8,128)(2,1)}, bf16[256,1024]{1,0:T(8,128)(2,1)}) fusion(bf16[2,256,1024]{2,1,0:T(8,128)(2,1)} %param.66), kind=kLoop, calls=%fused_computation.47 | loop fusion | bytes 2097152 | tf_op jit(solution)/shard_map/squeeze | solution.py:54
  28.5 2.3 %slice_bitcast_fusion.1 = (bf16[256,1024]{1,0:T(8,128)(2,1)}, bf16[256,1024]{1,0:T(8,128)(2,1)}) fusion(bf16[2,256,1024]{2,1,0:T(8,128)(2,1)} %param.67), kind=kLoop, calls=%fused_computation.48 | loop fusion | bytes 2097152 | tf_op jit(solution)/shard_map/squeeze | solution.py:55
  37.2 2.0 collective-permute-start.5
  40.7 3.8 %collective-permute-done.5 = bf16[2,3,32,512]{3,2,1,0:T(8,128)(2,1)S(1)} collective-permute-done((bf16[2,3,32,512]{3,2,1,0:T(8,128)(2,1)S(1)}, bf16[2,3,32,512]{3,2,1,0:T(8,128)(2,1)S(1)}, u32[]{:S(2)}, u32[]{:S(2)}) %collective-permute-start.5) | collective-permute-done | bytes 196640 | tf_op jit(solution)/shard_map/ppermute | solution.py:108
  44.5 1.7 collective-permute-start.9
  47.0 4.0 %collective-permute-done.9 = bf16[2,3,32,512]{3,2,1,0:T(8,128)(2,1)S(1)} collective-permute-done((bf16[2,3,32,512]{3,2,1,0:T(8,128)(2,1)S(1)}, bf16[2,3,32,512]{3,2,1,0:T(8,128)(2,1)S(1)}, u32[]{:S(2)}, u32[]{:S(2)}) %collective-permute-start.9) | collective-permute-done | bytes 196640 | tf_op jit(solution)/shard_map/ppermute | solution.py:108
  51.0 1.5 collective-permute-start.13
  53.7 2.9 %collective-permute-done.13 = bf16[2,3,32,512]{3,2,1,0:T(8,128)(2,1)S(1)} collective-permute-done((bf16[2,3,32,512]{3,2,1,0:T(8,128)(2,1)S(1)}, bf16[2,3,32,512]{3,2,1,0:T(8,128)(2,1)S(1)}, u32[]{:S(2)}, u32[]{:S(2)}) %collective-permute-start.13) | collective-permute-done | bytes 196640 | tf_op jit(solution)/shard_map/ppermute | solution.py:108
  56.8 1.3 collective-permute-done.14
  64.9 1.5 constant_dynamic-slice_fusion.15
  68.8 1.5 collective-permute-start.17
  71.4 8.6 %collective-permute-done.17 = f32[2,3,32,512]{3,2,1,0:T(8,128)S(1)} collective-permute-done((f32[2,3,32,512]{3,2,1,0:T(8,128)S(1)}, f32[2,3,32,512]{3,2,1,0:T(8,128)S(1)}, u32[]{:S(2)}, u32[]{:S(2)}) %collective-permute-start.17) | collective-permute-done | bytes 393248 | tf_op jit(solution)/shard_map/ppermute | solution.py:134
  80.1 1.5 collective-permute-start.19
  83.5 7.0 %collective-permute-done.19 = f32[2,3,32,512]{3,2,1,0:T(8,128)S(1)} collective-permute-done((f32[2,3,32,512]{3,2,1,0:T(8,128)S(1)}, f32[2,3,32,512]{3,2,1,0:T(8,128)S(1)}, u32[]{:S(2)}, u32[]{:S(2)}) %collective-permute-start.19) | collective-permute-done | bytes 393248 | tf_op jit(solution)/shard_map/ppermute | solution.py:134
  91.7 1.5 collective-permute-start.21
  94.8 2.8 %multiply_reduce_fusion.2 = (f32[256]{0:T(256)S(1)}, f32[256,512]{1,0:T(8,128)}) fusion(bf16[512,512]{1,0:T(8,128)(2,1)S(1)} %bitcast.325, bf16[512,512]{1,0:T(8,128)(2,1)S(1)} %bitcast.327, f32[256,512]{0,1:T(8,128)} %convolution_bitcast_fusion.17, bf16[256,1024]{1,0:T(8,128)(2,1)S(1)} %get-tuple-element.54), kind=kOutput, calls=%fused_computation.77 | convolution fusion | flops 269483776 | bytes 2360320 | tf_op jit(solution)/shard_map/dot_general | solution.py:8
  97.7 3.7 %collective-permute-done.21 = f32[2,3,32,512]{3,2,1,0:T(8,128)} collective-permute-done((f32[2,3,32,512]{3,2,1,0:T(8,128)}, f32[2,3,32,512]{3,2,1,0:T(8,128)}, u32[]{:S(2)}, u32[]{:S(2)}) %collective-permute-start.21) | collective-permute-done | bytes 393248 | tf_op jit(solution)/shard_map/ppermute | solution.py:134
  102.6 2.8 %bitcast_add_fusion.8 = (f32[2,3,32,512]{3,2,1,0:T(8,128)}, f32[2,3,32,512]{3,2,1,0:T(8,128)}) fusion(f32[2,3,32,512]{3,2,1,0:T(8,128)} %collective-permute-done.21, f32[2,3,1,1,32,512]{5,4,1,0,3,2:T(8,128)} %collective-permute-done.22, f32[2,3,8,2,32,512]{5,4,1,0,3,2:T(8,128)} %copy-done.1, s32[]{:T(128)S(6)} %select_n.492, s32[]{:T(128)S(6)} %select_n.485, ...), kind=kLoop, calls=%fused_computation.101 | loop fusion | flops 393216 | bytes 3145740 | tf_op jit(solution)/shard_map/add | solution.py:136
  105.4 1.6 collective-permute-start.23
  107.4 1.7 multiply_reduce_fusion.3
  109.1 4.9 %collective-permute-done.23 = f32[2,3,32,512]{3,2,1,0:T(8,128)} collective-permute-done((f32[2,3,32,512]{3,2,1,0:T(8,128)}, f32[2,3,32,512]{3,2,1,0:T(8,128)}, u32[]{:S(2)}, u32[]{:S(2)}) %collective-permute-start.23) | collective-permute-done | bytes 393248 | tf_op jit(solution)/shard_map/ppermute | solution.py:134
  115.3 1.5 multiply_reduce_fusion.6
  117.4 1.8 collective-permute-start.31
  119.6 4.4 %collective-permute-done.31 = bf16[2,3,32,512]{3,2,1,0:T(8,128)(2,1)S(1)} collective-permute-done((bf16[2,3,32,512]{3,2,1,0:T(8,128)(2,1)S(1)}, bf16[2,3,32,512]{3,2,1,0:T(8,128)(2,1)S(1)}, u32[]{:S(2)}, u32[]{:S(2)}) %collective-permute-start.31) | collective-permute-done | bytes 196640 | tf_op jit(solution)/shard_map/ppermute | solution.py:108
  124.0 1.6 collective-permute-start.35
  127.0 2.7 %collective-permute-done.35 = bf16[2,3,32,512]{3,2,1,0:T(8,128)(2,1)S(1)} collective-permute-done((bf16[2,3,32,512]{3,2,1,0:T(8,128)(2,1)S(1)}, bf16[2,3,32,512]{3,2,1,0:T(8,128)(2,1)S(1)}, u32[]{:S(2)}, u32[]{:S(2)}) %collective-permute-start.35) | collective-permute-done | bytes 196640 | tf_op jit(solution)/shard_map/ppermute | solution.py:108
  129.7 1.6 collective-permute-start.39
  131.3 1.7 collective-permute-done.37
  133.5 1.8 collective-permute-done.39
  135.4 1.6 collective-permute-start.43
  136.9 1.7 collective-permute-done.41
  138.7 2.3 %collective-permute-done.43 = bf16[2,3,32,512]{3,2,1,0:T(8,128)(2,1)S(1)} collective-permute-done((bf16[2,3,32,512]{3,2,1,0:T(8,128)(2,1)S(1)}, bf16[2,3,32,512]{3,2,1,0:T(8,128)(2,1)S(1)}, u32[]{:S(2)}, u32[]{:S(2)}) %collective-permute-start.43) | collective-permute-done | bytes 196640 | tf_op jit(solution)/shard_map/ppermute | solution.py:108
  149.3 1.4 constant_dynamic-slice_fusion.8
  154.0 1.6 collective-permute-start.47
  157.3 2.7 %multiply_reduce_fusion.1 = (f32[256]{0:T(256)S(1)}, f32[256,512]{1,0:T(8,128)}) fusion(bf16[512,512]{1,0:T(8,128)(2,1)S(1)} %bitcast.333, bf16[512,512]{1,0:T(8,128)(2,1)S(1)} %bitcast.335, f32[256,512]{0,1:T(8,128)} %convolution_bitcast_fusion.9, bf16[256,1024]{1,0:T(8,128)(2,1)S(1)} %get-tuple-element.55), kind=kOutput, calls=%fused_computation.57 | convolution fusion | flops 269483776 | bytes 2360320 | tf_op jit(solution)/shard_map/dot_general | solution.py:8
  160.4 5.2 %collective-permute-done.47 = f32[2,3,32,512]{3,2,1,0:T(8,128)} collective-permute-done((f32[2,3,32,512]{3,2,1,0:T(8,128)}, f32[2,3,32,512]{3,2,1,0:T(8,128)}, u32[]{:S(2)}, u32[]{:S(2)}) %collective-permute-start.47) | collective-permute-done | bytes 393248 | tf_op jit(solution)/shard_map/ppermute | solution.py:134
  165.6 2.1 %bitcast_add_fusion.4 = f32[2,3,32,512]{3,2,1,0:T(8,128)} fusion(f32[2,3,32,512]{3,2,1,0:T(8,128)} %collective-permute-done.47, f32[2,3,1,1,32,512]{5,4,1,0,3,2:T(8,128)} %collective-permute-done.48, f32[2,3,8,2,32,512]{5,4,1,0,3,2:T(8,128)} %copy-done, s32[]{:T(128)S(6)} %select_n.504, s32[]{:T(128)S(6)} %select_n.485), kind=kLoop, calls=%fused_computation.95 | loop fusion | flops 196608 | bytes 1572872 | tf_op jit(solution)/shard_map/add | solution.py:136
  167.7 1.6 collective-permute-start.49
  169.4 2.0 multiply_reduce_fusion
  172.0 6.5 %collective-permute-done.49 = f32[2,3,32,512]{3,2,1,0:T(8,128)} collective-permute-done((f32[2,3,32,512]{3,2,1,0:T(8,128)}, f32[2,3,32,512]{3,2,1,0:T(8,128)}, u32[]{:S(2)}, u32[]{:S(2)}) %collective-permute-start.49) | collective-permute-done | bytes 393248 | tf_op jit(solution)/shard_map/ppermute | solution.py:134
  178.4 1.9 bitcast_add_fusion.3
  180.3 1.6 collective-permute-start.51
  182.5 7.4 %collective-permute-done.51 = f32[2,3,32,512]{3,2,1,0:T(8,128)S(1)} collective-permute-done((f32[2,3,32,512]{3,2,1,0:T(8,128)S(1)}, f32[2,3,32,512]{3,2,1,0:T(8,128)S(1)}, u32[]{:S(2)}, u32[]{:S(2)}) %collective-permute-start.51) | collective-permute-done | bytes 393248 | tf_op jit(solution)/shard_map/ppermute | solution.py:134
  191.2 1.4 bitcast_add_fusion.2
  192.5 1.6 collective-permute-start.53
  195.9 5.1 %collective-permute-done.53 = f32[2,3,32,512]{3,2,1,0:T(8,128)S(1)} collective-permute-done((f32[2,3,32,512]{3,2,1,0:T(8,128)S(1)}, f32[2,3,32,512]{3,2,1,0:T(8,128)S(1)}, u32[]{:S(2)}, u32[]{:S(2)}) %collective-permute-start.53) | collective-permute-done | bytes 393248 | tf_op jit(solution)/shard_map/ppermute | solution.py:134
  202.2 1.4 multiply_reduce_fusion.4
  (232 shorter events, 48.4 us)
Async XLA Ops:
  2.4 34.9 %collective-permute-start.1 = (bf16[2,3,32,512]{3,2,1,0:T(8,128)(2,1)}, bf16[2,3,32,512]{3,2,1,0:T(8,128)(2,1)S(1)}, u32[]{:S(2)}, u32[]{:S(2)}) collective-permute-start(bf16[2,3,32,512]{3,2,1,0:T(8,128)(2,1)} %get-tuple-element.9), channel_id=1, source_target_pairs={{0,4},{1,5},{4,8},{5,9},{8,12},{9,13},{12,14},{13,15},{14,10},{15,... | collective-permute-start | bytes 589832 | tf_op jit(solution)/shard_map/ppermute | solution.py:108
  5.4 34.3 %collective-permute-start = (bf16[2,3,32,512]{3,2,1,0:T(8,128)(2,1)}, bf16[2,3,32,512]{3,2,1,0:T(8,128)(2,1)}, u32[]{:S(2)}, u32[]{:S(2)}) collective-permute-start(bf16[2,3,32,512]{3,2,1,0:T(8,128)(2,1)} %get-tuple-element.9), channel_id=1, source_target_pairs={{0,1},{1,0},{2,3},{3,2},{4,5},{5,4},{6,7},{7,6},{8,9},{9,8},{10,11... | collective-permute-start | bytes 589832 | tf_op jit(solution)/shard_map/ppermute | solution.py:100
  5.4 33.8 %collective-permute-start.3 = (bf16[2,3,32,512]{3,2,1,0:T(8,128)(2,1)}, bf16[2,3,32,512]{3,2,1,0:T(8,128)(2,1)S(1)}, u32[]{:S(2)}, u32[]{:S(2)}) collective-permute-start(bf16[2,3,32,512]{3,2,1,0:T(8,128)(2,1)} %get-tuple-element.9), channel_id=1, source_target_pairs={{0,2},{1,3},{4,0},{5,1},{8,4},{9,5},{12,8},{13,9},{14,12},{15,13},... | collective-permute-start | bytes 589832 | tf_op jit(solution)/shard_map/ppermute | solution.py:111
  37.2 7.3 %collective-permute-start.5 = (bf16[2,3,32,512]{3,2,1,0:T(8,128)(2,1)S(1)}, bf16[2,3,32,512]{3,2,1,0:T(8,128)(2,1)S(1)}, u32[]{:S(2)}, u32[]{:S(2)}) collective-permute-start(bf16[2,3,32,512]{3,2,1,0:T(8,128)(2,1)S(1)} %collective-permute-done.1), channel_id=1, source_target_pairs={{0,4},{1,5},{4,8},{5,9},{8,12},{9,13},{12,14},{13,15},{14,10},{15,... | collective-permute-start | bytes 589832 | tf_op jit(solution)/shard_map/ppermute | solution.py:108
  39.2 7.6 %collective-permute-start.2 = (bf16[2,3,32,512]{3,2,1,0:T(8,128)(2,1)S(1)}, bf16[2,3,32,512]{3,2,1,0:T(8,128)(2,1)S(1)}, u32[]{:S(2)}, u32[]{:S(2)}) collective-permute-start(bf16[2,3,32,512]{3,2,1,0:T(8,128)(2,1)S(1)} %collective-permute-done.1), channel_id=1, source_target_pairs={{0,1},{1,0},{2,3},{3,2},{4,5},{5,4},{6,7},{7,6},{8,9},{9,8},{10,11... | collective-permute-start | bytes 589832 | tf_op jit(solution)/shard_map/ppermute | solution.py:100
  39.3 7.3 %collective-permute-start.7 = (bf16[2,3,32,512]{3,2,1,0:T(8,128)(2,1)S(1)}, bf16[2,3,32,512]{3,2,1,0:T(8,128)(2,1)S(1)}, u32[]{:S(2)}, u32[]{:S(2)}) collective-permute-start(bf16[2,3,32,512]{3,2,1,0:T(8,128)(2,1)S(1)} %collective-permute-done.3), channel_id=1, source_target_pairs={{0,2},{1,3},{4,0},{5,1},{8,4},{9,5},{12,8},{13,9},{14,12},{15,13},... | collective-permute-start | bytes 589832 | tf_op jit(solution)/shard_map/ppermute | solution.py:111
  39.5 7.4 %collective-permute-start.4 = (bf16[2,3,32,512]{3,2,1,0:T(8,128)(2,1)S(1)}, bf16[2,3,32,512]{3,2,1,0:T(8,128)(2,1)S(1)}, u32[]{:S(2)}, u32[]{:S(2)}) collective-permute-start(bf16[2,3,32,512]{3,2,1,0:T(8,128)(2,1)S(1)} %collective-permute-done.3), channel_id=1, source_target_pairs={{0,1},{1,0},{2,3},{3,2},{4,5},{5,4},{6,7},{7,6},{8,9},{9,8},{10,11... | collective-permute-start | bytes 589832 | tf_op jit(solution)/shard_map/ppermute | solution.py:100
  44.5 6.5 %collective-permute-start.9 = (bf16[2,3,32,512]{3,2,1,0:T(8,128)(2,1)S(1)}, bf16[2,3,32,512]{3,2,1,0:T(8,128)(2,1)S(1)}, u32[]{:S(2)}, u32[]{:S(2)}) collective-permute-start(bf16[2,3,32,512]{3,2,1,0:T(8,128)(2,1)S(1)} %collective-permute-done.5), channel_id=1, source_target_pairs={{0,4},{1,5},{4,8},{5,9},{8,12},{9,13},{12,14},{13,15},{14,10},{15,... | collective-permute-start | bytes 589832 | tf_op jit(solution)/shard_map/ppermute | solution.py:108
  46.3 7.3 %collective-permute-start.6 = (bf16[2,3,32,512]{3,2,1,0:T(8,128)(2,1)S(1)}, bf16[2,3,32,512]{3,2,1,0:T(8,128)(2,1)S(1)}, u32[]{:S(2)}, u32[]{:S(2)}) collective-permute-start(bf16[2,3,32,512]{3,2,1,0:T(8,128)(2,1)S(1)} %collective-permute-done.5), channel_id=1, source_target_pairs={{0,1},{1,0},{2,3},{3,2},{4,5},{5,4},{6,7},{7,6},{8,9},{9,8},{10,11... | collective-permute-start | bytes 589832 | tf_op jit(solution)/shard_map/ppermute | solution.py:100
  46.6 7.0 %collective-permute-start.11 = (bf16[2,3,32,512]{3,2,1,0:T(8,128)(2,1)S(1)}, bf16[2,3,32,512]{3,2,1,0:T(8,128)(2,1)S(1)}, u32[]{:S(2)}, u32[]{:S(2)}) collective-permute-start(bf16[2,3,32,512]{3,2,1,0:T(8,128)(2,1)S(1)} %collective-permute-done.7), channel_id=1, source_target_pairs={{0,2},{1,3},{4,0},{5,1},{8,4},{9,5},{12,8},{13,9},{14,12},{15,13},... | collective-permute-start | bytes 589832 | tf_op jit(solution)/shard_map/ppermute | solution.py:111
  46.9 6.8 %collective-permute-start.8 = (bf16[2,3,32,512]{3,2,1,0:T(8,128)(2,1)S(1)}, bf16[2,3,32,512]{3,2,1,0:T(8,128)(2,1)S(1)}, u32[]{:S(2)}, u32[]{:S(2)}) collective-permute-start(bf16[2,3,32,512]{3,2,1,0:T(8,128)(2,1)S(1)} %collective-permute-done.7), channel_id=1, source_target_pairs={{0,1},{1,0},{2,3},{3,2},{4,5},{5,4},{6,7},{7,6},{8,9},{9,8},{10,11... | collective-permute-start | bytes 589832 | tf_op jit(solution)/shard_map/ppermute | solution.py:100
  51.0 5.7 %collective-permute-start.13 = (bf16[2,3,32,512]{3,2,1,0:T(8,128)(2,1)S(1)}, bf16[2,3,32,512]{3,2,1,0:T(8,128)(2,1)S(1)}, u32[]{:S(2)}, u32[]{:S(2)}) collective-permute-start(bf16[2,3,32,512]{3,2,1,0:T(8,128)(2,1)S(1)} %collective-permute-done.9), channel_id=1, source_target_pairs={{0,4},{1,5},{4,8},{5,9},{8,12},{9,13},{12,14},{13,15},{14,10},{15,... | collective-permute-start | bytes 589832 | tf_op jit(solution)/shard_map/ppermute | solution.py:108
  68.8 11.2 %collective-permute-start.17 = (f32[2,3,32,512]{3,2,1,0:T(8,128)S(1)}, f32[2,3,32,512]{3,2,1,0:T(8,128)S(1)}, u32[]{:S(2)}, u32[]{:S(2)}) collective-permute-start(f32[2,3,32,512]{3,2,1,0:T(8,128)S(1)} %get-tuple-element.36), channel_id=1, source_target_pairs={{0,4},{1,5},{4,8},{5,9},{8,12},{9,13},{12,14},{13,15},{14,10},{15,... | collective-permute-start | bytes 1179656 | tf_op jit(solution)/shard_map/ppermute | solution.py:134
  70.3 12.6 %collective-permute-start.26 = (f32[2,3,1,1,32,512]{5,4,1,0,3,2:T(8,128)S(1)}, f32[2,3,1,1,32,512]{5,4,1,0,3,2:T(8,128)S(1)}, u32[]{:S(2)}, u32[]{:S(2)}) collective-permute-start(f32[2,3,1,1,32,512]{5,4,1,0,3,2:T(8,128)S(1)} %get-tuple-element.26), channel_id=1, source_target_pairs={{0,1},{1,0},{2,3},{3,2},{4,5},{5,4},{6,7},{7,6},{8,9},{9,8},{10,11... | collective-permute-start | bytes 1179656 | tf_op jit(solution)/shard_map/ppermute | solution.py:126
  70.3 13.1 %collective-permute-start.20 = (f32[2,3,1,1,32,512]{5,4,1,0,3,2:T(8,128)S(1)}, f32[2,3,1,1,32,512]{5,4,1,0,3,2:T(8,128)S(1)}, u32[]{:S(2)}, u32[]{:S(2)}) collective-permute-start(f32[2,3,1,1,32,512]{5,4,1,0,3,2:T(8,128)S(1)} %get-tuple-element.29), channel_id=1, source_target_pairs={{0,1},{1,0},{2,3},{3,2},{4,5},{5,4},{6,7},{7,6},{8,9},{9,8},{10,11... | collective-permute-start | bytes 1179656 | tf_op jit(solution)/shard_map/ppermute | solution.py:126
  70.9 12.6 %collective-permute-start.25 = (f32[2,3,32,512]{3,2,1,0:T(8,128)S(1)}, f32[2,3,32,512]{3,2,1,0:T(8,128)S(1)}, u32[]{:S(2)}, u32[]{:S(2)}) collective-permute-start(f32[2,3,32,512]{3,2,1,0:T(8,128)S(1)} %get-tuple-element.37), channel_id=1, source_target_pairs={{0,2},{1,3},{4,0},{5,1},{8,4},{9,5},{12,8},{13,9},{14,12},{15,13},... | collective-permute-start | bytes 1179656 | tf_op jit(solution)/shard_map/ppermute | solution.py:138
  80.1 10.4 %collective-permute-start.19 = (f32[2,3,32,512]{3,2,1,0:T(8,128)S(1)}, f32[2,3,32,512]{3,2,1,0:T(8,128)S(1)}, u32[]{:S(2)}, u32[]{:S(2)}) collective-permute-start(f32[2,3,32,512]{3,2,1,0:T(8,128)S(1)} %bitcast_add_fusion.10), channel_id=1, source_target_pairs={{0,4},{1,5},{4,8},{5,9},{8,12},{9,13},{12,14},{13,15},{14,10},{15,... | collective-permute-start | bytes 1179656 | tf_op jit(solution)/shard_map/ppermute | solution.py:134
  81.8 15.9 %collective-permute-start.28 = (f32[2,3,1,1,32,512]{5,4,1,0,3,2:T(8,128)}, f32[2,3,1,1,32,512]{5,4,1,0,3,2:T(8,128)}, u32[]{:S(2)}, u32[]{:S(2)}) collective-permute-start(f32[2,3,1,1,32,512]{5,4,1,0,3,2:T(8,128)} %get-tuple-element.25), channel_id=1, source_target_pairs={{0,1},{1,0},{2,3},{3,2},{4,5},{5,4},{6,7},{7,6},{8,9},{9,8},{10,11... | collective-permute-start | bytes 1179656 | tf_op jit(solution)/shard_map/ppermute | solution.py:126
  83.0 14.7 %collective-permute-start.22 = (f32[2,3,1,1,32,512]{5,4,1,0,3,2:T(8,128)}, f32[2,3,1,1,32,512]{5,4,1,0,3,2:T(8,128)}, u32[]{:S(2)}, u32[]{:S(2)}) collective-permute-start(f32[2,3,1,1,32,512]{5,4,1,0,3,2:T(8,128)} %get-tuple-element.28), channel_id=1, source_target_pairs={{0,1},{1,0},{2,3},{3,2},{4,5},{5,4},{6,7},{7,6},{8,9},{9,8},{10,11... | collective-permute-start | bytes 1179656 | tf_op jit(solution)/shard_map/ppermute | solution.py:126
  91.7 9.8 %collective-permute-start.21 = (f32[2,3,32,512]{3,2,1,0:T(8,128)}, f32[2,3,32,512]{3,2,1,0:T(8,128)}, u32[]{:S(2)}, u32[]{:S(2)}) collective-permute-start(f32[2,3,32,512]{3,2,1,0:T(8,128)} %get-tuple-element.34), channel_id=1, source_target_pairs={{0,4},{1,5},{4,8},{5,9},{8,12},{9,13},{12,14},{13,15},{14,10},{15,... | collective-permute-start | bytes 1179656 | tf_op jit(solution)/shard_map/ppermute | solution.py:134
  93.1 9.5 %collective-permute-start.27 = (f32[2,3,32,512]{3,2,1,0:T(8,128)}, f32[2,3,32,512]{3,2,1,0:T(8,128)}, u32[]{:S(2)}, u32[]{:S(2)}) collective-permute-start(f32[2,3,32,512]{3,2,1,0:T(8,128)} %get-tuple-element.35), channel_id=1, source_target_pairs={{0,2},{1,3},{4,0},{5,1},{8,4},{9,5},{12,8},{13,9},{14,12},{15,13},... | collective-permute-start | bytes 1179656 | tf_op jit(solution)/shard_map/ppermute | solution.py:138
  94.8 14.3 %collective-permute-start.15 = (f32[2,3,1,1,32,512]{5,4,1,0,3,2:T(8,128)S(1)}, f32[2,3,1,1,32,512]{5,4,1,0,3,2:T(8,128)}, u32[]{:S(2)}, u32[]{:S(2)}) collective-permute-start(f32[2,3,1,1,32,512]{5,4,1,0,3,2:T(8,128)S(1)} %get-tuple-element.24), channel_id=1, source_target_pairs={{0,1},{1,0},{2,3},{3,2},{4,5},{5,4},{6,7},{7,6},{8,9},{9,8},{10,11... | collective-permute-start | bytes 1179656 | tf_op jit(solution)/shard_map/ppermute | solution.py:126
  105.4 8.6 %collective-permute-start.23 = (f32[2,3,32,512]{3,2,1,0:T(8,128)}, f32[2,3,32,512]{3,2,1,0:T(8,128)}, u32[]{:S(2)}, u32[]{:S(2)}) collective-permute-start(f32[2,3,32,512]{3,2,1,0:T(8,128)} %get-tuple-element.32), channel_id=1, source_target_pairs={{0,4},{1,5},{4,8},{5,9},{8,12},{9,13},{12,14},{13,15},{14,10},{15,... | collective-permute-start | bytes 1179656 | tf_op jit(solution)/shard_map/ppermute | solution.py:134
  107.0 8.3 %collective-permute-start.29 = (f32[2,3,32,512]{3,2,1,0:T(8,128)}, f32[2,3,32,512]{3,2,1,0:T(8,128)}, u32[]{:S(2)}, u32[]{:S(2)}) collective-permute-start(f32[2,3,32,512]{3,2,1,0:T(8,128)} %get-tuple-element.33), channel_id=1, source_target_pairs={{0,2},{1,3},{4,0},{5,1},{8,4},{9,5},{12,8},{13,9},{14,12},{15,13},... | collective-permute-start | bytes 1179656 | tf_op jit(solution)/shard_map/ppermute | solution.py:138
  117.4 6.7 %collective-permute-start.31 = (bf16[2,3,32,512]{3,2,1,0:T(8,128)(2,1)S(1)}, bf16[2,3,32,512]{3,2,1,0:T(8,128)(2,1)S(1)}, u32[]{:S(2)}, u32[]{:S(2)}) collective-permute-start(bf16[2,3,32,512]{3,2,1,0:T(8,128)(2,1)S(1)} %get-tuple-element.5), channel_id=1, source_target_pairs={{0,4},{1,5},{4,8},{5,9},{8,12},{9,13},{12,14},{13,15},{14,10},{15,... | collective-permute-start | bytes 589832 | tf_op jit(solution)/shard_map/ppermute | solution.py:108
  119.2 7.8 %collective-permute-start.30 = (bf16[2,3,32,512]{3,2,1,0:T(8,128)(2,1)S(1)}, bf16[2,3,32,512]{3,2,1,0:T(8,128)(2,1)S(1)}, u32[]{:S(2)}, u32[]{:S(2)}) collective-permute-start(bf16[2,3,32,512]{3,2,1,0:T(8,128)(2,1)S(1)} %get-tuple-element.5), channel_id=1, source_target_pairs={{0,1},{1,0},{2,3},{3,2},{4,5},{5,4},{6,7},{7,6},{8,9},{9,8},{10,11... | collective-permute-start | bytes 589832 | tf_op jit(solution)/shard_map/ppermute | solution.py:100
  119.2 7.3 %collective-permute-start.33 = (bf16[2,3,32,512]{3,2,1,0:T(8,128)(2,1)S(1)}, bf16[2,3,32,512]{3,2,1,0:T(8,128)(2,1)S(1)}, u32[]{:S(2)}, u32[]{:S(2)}) collective-permute-start(bf16[2,3,32,512]{3,2,1,0:T(8,128)(2,1)S(1)} %get-tuple-element.5), channel_id=1, source_target_pairs={{0,2},{1,3},{4,0},{5,1},{8,4},{9,5},{12,8},{13,9},{14,12},{15,13},... | collective-permute-start | bytes 589832 | tf_op jit(solution)/shard_map/ppermute | solution.py:111
  124.0 5.7 %collective-permute-start.35 = (bf16[2,3,32,512]{3,2,1,0:T(8,128)(2,1)S(1)}, bf16[2,3,32,512]{3,2,1,0:T(8,128)(2,1)S(1)}, u32[]{:S(2)}, u32[]{:S(2)}) collective-permute-start(bf16[2,3,32,512]{3,2,1,0:T(8,128)(2,1)S(1)} %collective-permute-done.31), channel_id=1, source_target_pairs={{0,4},{1,5},{4,8},{5,9},{8,12},{9,13},{12,14},{13,15},{14,10},{15,... | collective-permute-start | bytes 589832 | tf_op jit(solution)/shard_map/ppermute | solution.py:108
  125.6 7.8 %collective-permute-start.32 = (bf16[2,3,32,512]{3,2,1,0:T(8,128)(2,1)S(1)}, bf16[2,3,32,512]{3,2,1,0:T(8,128)(2,1)S(1)}, u32[]{:S(2)}, u32[]{:S(2)}) collective-permute-start(bf16[2,3,32,512]{3,2,1,0:T(8,128)(2,1)S(1)} %collective-permute-done.31), channel_id=1, source_target_pairs={{0,1},{1,0},{2,3},{3,2},{4,5},{5,4},{6,7},{7,6},{8,9},{9,8},{10,11... | collective-permute-start | bytes 589832 | tf_op jit(solution)/shard_map/ppermute | solution.py:100
  126.5 6.5 %collective-permute-start.37 = (bf16[2,3,32,512]{3,2,1,0:T(8,128)(2,1)S(1)}, bf16[2,3,32,512]{3,2,1,0:T(8,128)(2,1)S(1)}, u32[]{:S(2)}, u32[]{:S(2)}) collective-permute-start(bf16[2,3,32,512]{3,2,1,0:T(8,128)(2,1)S(1)} %collective-permute-done.33), channel_id=1, source_target_pairs={{0,2},{1,3},{4,0},{5,1},{8,4},{9,5},{12,8},{13,9},{14,12},{15,13},... | collective-permute-start | bytes 589832 | tf_op jit(solution)/shard_map/ppermute | solution.py:111
  126.9 6.5 %collective-permute-start.34 = (bf16[2,3,32,512]{3,2,1,0:T(8,128)(2,1)S(1)}, bf16[2,3,32,512]{3,2,1,0:T(8,128)(2,1)S(1)}, u32[]{:S(2)}, u32[]{:S(2)}) collective-permute-start(bf16[2,3,32,512]{3,2,1,0:T(8,128)(2,1)S(1)} %collective-permute-done.33), channel_id=1, source_target_pairs={{0,1},{1,0},{2,3},{3,2},{4,5},{5,4},{6,7},{7,6},{8,9},{9,8},{10,11... | collective-permute-start | bytes 589832 | tf_op jit(solution)/shard_map/ppermute | solution.py:100
  129.7 5.7 %collective-permute-start.39 = (bf16[2,3,32,512]{3,2,1,0:T(8,128)(2,1)S(1)}, bf16[2,3,32,512]{3,2,1,0:T(8,128)(2,1)S(1)}, u32[]{:S(2)}, u32[]{:S(2)}) collective-permute-start(bf16[2,3,32,512]{3,2,1,0:T(8,128)(2,1)S(1)} %collective-permute-done.35), channel_id=1, source_target_pairs={{0,4},{1,5},{4,8},{5,9},{8,12},{9,13},{12,14},{13,15},{14,10},{15,... | collective-permute-start | bytes 589832 | tf_op jit(solution)/shard_map/ppermute | solution.py:108
  131.3 7.4 %collective-permute-start.36 = (bf16[2,3,32,512]{3,2,1,0:T(8,128)(2,1)S(1)}, bf16[2,3,32,512]{3,2,1,0:T(8,128)(2,1)S(1)}, u32[]{:S(2)}, u32[]{:S(2)}) collective-permute-start(bf16[2,3,32,512]{3,2,1,0:T(8,128)(2,1)S(1)} %collective-permute-done.35), channel_id=1, source_target_pairs={{0,1},{1,0},{2,3},{3,2},{4,5},{5,4},{6,7},{7,6},{8,9},{9,8},{10,11... | collective-permute-start | bytes 589832 | tf_op jit(solution)/shard_map/ppermute | solution.py:100
  132.9 5.7 %collective-permute-start.41 = (bf16[2,3,32,512]{3,2,1,0:T(8,128)(2,1)S(1)}, bf16[2,3,32,512]{3,2,1,0:T(8,128)(2,1)S(1)}, u32[]{:S(2)}, u32[]{:S(2)}) collective-permute-start(bf16[2,3,32,512]{3,2,1,0:T(8,128)(2,1)S(1)} %collective-permute-done.37), channel_id=1, source_target_pairs={{0,2},{1,3},{4,0},{5,1},{8,4},{9,5},{12,8},{13,9},{14,12},{15,13},... | collective-permute-start | bytes 589832 | tf_op jit(solution)/shard_map/ppermute | solution.py:111
  135.4 5.7 %collective-permute-start.43 = (bf16[2,3,32,512]{3,2,1,0:T(8,128)(2,1)S(1)}, bf16[2,3,32,512]{3,2,1,0:T(8,128)(2,1)S(1)}, u32[]{:S(2)}, u32[]{:S(2)}) collective-permute-start(bf16[2,3,32,512]{3,2,1,0:T(8,128)(2,1)S(1)} %collective-permute-done.39), channel_id=1, source_target_pairs={{0,4},{1,5},{4,8},{5,9},{8,12},{9,13},{12,14},{13,15},{14,10},{15,... | collective-permute-start | bytes 589832 | tf_op jit(solution)/shard_map/ppermute | solution.py:108
  151.4 8.9 %collective-permute-start.48 = (f32[2,3,1,1,32,512]{5,4,1,0,3,2:T(8,128)}, f32[2,3,1,1,32,512]{5,4,1,0,3,2:T(8,128)}, u32[]{:S(2)}, u32[]{:S(2)}) collective-permute-start(f32[2,3,1,1,32,512]{5,4,1,0,3,2:T(8,128)} %get-tuple-element.16), channel_id=1, source_target_pairs={{0,1},{1,0},{2,3},{3,2},{4,5},{5,4},{6,7},{7,6},{8,9},{9,8},{10,11... | collective-permute-start | bytes 1179656 | tf_op jit(solution)/shard_map/ppermute | solution.py:126
  154.0 11.6 %collective-permute-start.47 = (f32[2,3,32,512]{3,2,1,0:T(8,128)}, f32[2,3,32,512]{3,2,1,0:T(8,128)}, u32[]{:S(2)}, u32[]{:S(2)}) collective-permute-start(f32[2,3,32,512]{3,2,1,0:T(8,128)} %get-tuple-element.22), channel_id=1, source_target_pairs={{0,4},{1,5},{4,8},{5,9},{8,12},{9,13},{12,14},{13,15},{14,10},{15,... | collective-permute-start | bytes 1179656 | tf_op jit(solution)/shard_map/ppermute | solution.py:134
  156.7 14.6 %collective-permute-start.56 = (f32[2,3,1,1,32,512]{5,4,1,0,3,2:T(8,128)}, f32[2,3,1,1,32,512]{5,4,1,0,3,2:T(8,128)}, u32[]{:S(2)}, u32[]{:S(2)}) collective-permute-start(f32[2,3,1,1,32,512]{5,4,1,0,3,2:T(8,128)} %get-tuple-element.12), channel_id=1, source_target_pairs={{0,1},{1,0},{2,3},{3,2},{4,5},{5,4},{6,7},{7,6},{8,9},{9,8},{10,11... | collective-permute-start | bytes 1179656 | tf_op jit(solution)/shard_map/ppermute | solution.py:126
  156.7 15.1 %collective-permute-start.50 = (f32[2,3,1,1,32,512]{5,4,1,0,3,2:T(8,128)}, f32[2,3,1,1,32,512]{5,4,1,0,3,2:T(8,128)}, u32[]{:S(2)}, u32[]{:S(2)}) collective-permute-start(f32[2,3,1,1,32,512]{5,4,1,0,3,2:T(8,128)} %get-tuple-element.15), channel_id=1, source_target_pairs={{0,1},{1,0},{2,3},{3,2},{4,5},{5,4},{6,7},{7,6},{8,9},{9,8},{10,11... | collective-permute-start | bytes 1179656 | tf_op jit(solution)/shard_map/ppermute | solution.py:126
  159.9 12.0 %collective-permute-start.55 = (f32[2,3,32,512]{3,2,1,0:T(8,128)}, f32[2,3,32,512]{3,2,1,0:T(8,128)}, u32[]{:S(2)}, u32[]{:S(2)}) collective-permute-start(f32[2,3,32,512]{3,2,1,0:T(8,128)} %get-tuple-element.23), channel_id=1, source_target_pairs={{0,2},{1,3},{4,0},{5,1},{8,4},{9,5},{12,8},{13,9},{14,12},{15,13},... | collective-permute-start | bytes 1179656 | tf_op jit(solution)/shard_map/ppermute | solution.py:138
  167.7 10.7 %collective-permute-start.49 = (f32[2,3,32,512]{3,2,1,0:T(8,128)}, f32[2,3,32,512]{3,2,1,0:T(8,128)}, u32[]{:S(2)}, u32[]{:S(2)}) collective-permute-start(f32[2,3,32,512]{3,2,1,0:T(8,128)} %bitcast_add_fusion.4), channel_id=1, source_target_pairs={{0,4},{1,5},{4,8},{5,9},{8,12},{9,13},{12,14},{13,15},{14,10},{15,... | collective-permute-start | bytes 1179656 | tf_op jit(solution)/shard_map/ppermute | solution.py:134
  169.3 26.6 %collective-permute-start.45 = (f32[2,3,1,1,32,512]{5,4,1,0,3,2:T(8,128)}, f32[2,3,1,1,32,512]{5,4,1,0,3,2:T(8,128)}, u32[]{:S(2)}, u32[]{:S(2)}) collective-permute-start(f32[2,3,1,1,32,512]{5,4,1,0,3,2:T(8,128)} %get-tuple-element.10), channel_id=1, source_target_pairs={{0,1},{1,0},{2,3},{3,2},{4,5},{5,4},{6,7},{7,6},{8,9},{9,8},{10,11... | collective-permute-start | bytes 1179656 | tf_op jit(solution)/shard_map/ppermute | solution.py:126
  171.3 11.1 %collective-permute-start.58 = (f32[2,3,1,1,32,512]{5,4,1,0,3,2:T(8,128)}, f32[2,3,1,1,32,512]{5,4,1,0,3,2:T(8,128)S(1)}, u32[]{:S(2)}, u32[]{:S(2)}) collective-permute-start(f32[2,3,1,1,32,512]{5,4,1,0,3,2:T(8,128)} %get-tuple-element.11), channel_id=1, source_target_pairs={{0,1},{1,0},{2,3},{3,2},{4,5},{5,4},{6,7},{7,6},{8,9},{9,8},{10,11... | collective-permute-start | bytes 1179656 | tf_op jit(solution)/shard_map/ppermute | solution.py:126
  171.9 10.6 %collective-permute-start.52 = (f32[2,3,1,1,32,512]{5,4,1,0,3,2:T(8,128)}, f32[2,3,1,1,32,512]{5,4,1,0,3,2:T(8,128)S(1)}, u32[]{:S(2)}, u32[]{:S(2)}) collective-permute-start(f32[2,3,1,1,32,512]{5,4,1,0,3,2:T(8,128)} %get-tuple-element.14), channel_id=1, source_target_pairs={{0,1},{1,0},{2,3},{3,2},{4,5},{5,4},{6,7},{7,6},{8,9},{9,8},{10,11... | collective-permute-start | bytes 1179656 | tf_op jit(solution)/shard_map/ppermute | solution.py:126
  180.3 9.6 %collective-permute-start.51 = (f32[2,3,32,512]{3,2,1,0:T(8,128)S(1)}, f32[2,3,32,512]{3,2,1,0:T(8,128)S(1)}, u32[]{:S(2)}, u32[]{:S(2)}) collective-permute-start(f32[2,3,32,512]{3,2,1,0:T(8,128)S(1)} %get-tuple-element.20), channel_id=1, source_target_pairs={{0,4},{1,5},{4,8},{5,9},{8,12},{9,13},{12,14},{13,15},{14,10},{15,... | collective-permute-start | bytes 1179656 | tf_op jit(solution)/shard_map/ppermute | solution.py:134
  181.9 9.3 %collective-permute-start.57 = (f32[2,3,32,512]{3,2,1,0:T(8,128)S(1)}, f32[2,3,32,512]{3,2,1,0:T(8,128)S(1)}, u32[]{:S(2)}, u32[]{:S(2)}) collective-permute-start(f32[2,3,32,512]{3,2,1,0:T(8,128)S(1)} %get-tuple-element.21), channel_id=1, source_target_pairs={{0,2},{1,3},{4,0},{5,1},{8,4},{9,5},{12,8},{13,9},{14,12},{15,13},... | collective-permute-start | bytes 1179656 | tf_op jit(solution)/shard_map/ppermute | solution.py:138
  192.5 8.5 %collective-permute-start.53 = (f32[2,3,32,512]{3,2,1,0:T(8,128)S(1)}, f32[2,3,32,512]{3,2,1,0:T(8,128)S(1)}, u32[]{:S(2)}, u32[]{:S(2)}) collective-permute-start(f32[2,3,32,512]{3,2,1,0:T(8,128)S(1)} %get-tuple-element.18), channel_id=1, source_target_pairs={{0,4},{1,5},{4,8},{5,9},{8,12},{9,13},{12,14},{13,15},{14,10},{15,... | collective-permute-start | bytes 1179656 | tf_op jit(solution)/shard_map/ppermute | solution.py:134
  194.1 8.1 %collective-permute-start.59 = (f32[2,3,32,512]{3,2,1,0:T(8,128)S(1)}, f32[2,3,32,512]{3,2,1,0:T(8,128)S(1)}, u32[]{:S(2)}, u32[]{:S(2)}) collective-permute-start(f32[2,3,32,512]{3,2,1,0:T(8,128)S(1)} %get-tuple-element.19), channel_id=1, source_target_pairs={{0,2},{1,3},{4,0},{5,1},{8,4},{9,5},{12,8},{13,9},{14,12},{15,13},... | collective-permute-start | bytes 1179656 | tf_op jit(solution)/shard_map/ppermute | solution.py:138
  (41 other events, 216.6 us)

commit v2 on v1

--- a/solution.py
+++ b/solution.py
@@ -131,11 +131,11 @@
         b = chip_sum(-self.nccw) if self.nccw else None
         for k in range(1, max(self.ncw, self.nccw) + 1):
             if k <= self.ncw:
-                a = lax.ppermute(a, "tok", self.cw)
+                a = lax.ppermute(a.astype(jnp.bfloat16), "tok", self.cw).astype(jnp.float32)
                 if k < self.ncw:
                     a = a + chip_sum(self.ncw - k)
             if k <= self.nccw:
-                b = lax.ppermute(b, "tok", self.ccw)
+                b = lax.ppermute(b.astype(jnp.bfloat16), "tok", self.ccw).astype(jnp.float32)
                 if k < self.nccw:
                     b = b + chip_sum(-self.nccw + k)
         if a is not None:

time: 205 us -> 193 us (0.941)
  waiting for transfers between devices: 85.5 us -> 61.8 us
  local copies, waits for them, and re-layouts: 15.2 us -> 22.7 us
  other arithmetic: 18.8 us -> 21.1 us
    ppermute x14, waiting for transfers between devices: 53.5 us -> 34.2 us  [the longest x8 28.1 us: reduce(): a = lax.ppermute(a.astype(jnp.bfloat16), 'tok', self.cw).astype(jnp.float32)]
    convert_element_type x0 -> x8, other arithmetic: none -> 12.2 us  [reduce(): a = lax.ppermute(a.astype(jnp.bfloat16), 'tok', self.cw).astype(jnp.float32)]
    add x6 -> x0, other arithmetic: 9.35 us -> none  [reduce(): a = a + chip_sum(self.ncw - k)]
    ppermute x8, waiting for transfers between devices: 21.9 us -> 16.9 us  [gather(): a = lax.ppermute(a, 'tok', self.cw)]
    unnamed x58 -> x72, local copies, waits for them, and re-layouts: 2.2 us -> 6.41 us
    ppermute x6, waiting for transfers between devices: 5.68 us -> 7.93 us  [gather(): b = lax.ppermute(b, 'tok', self.ccw)]
    squeeze x1, local copies, waits for them, and re-layouts: 0.07 us -> 2.29 us  [block_step(): queries[span][:, lo:lo + width]]
  transfers between devices with their start and end apart: 60 -> 60, of which waited for: 29 -> 27; matrix products, arithmetic and copies ran while one was open for 17% -> 16% of each run, Pallas kernels for 0% -> 0%
where the time goes in v2:
time: 193 us; the launch traced here: 192 us
  waiting for transfers between devices  61.8 us (32%)
  starting transfers between devices  36.9 us (19%)
  between operations  26.4 us (14%)
  matrix products  23.4 us (12%)
  local copies, waits for them, and re-layouts  22.7 us (12%)
  other arithmetic  21.1 us (11%)
    ppermute x8, waiting for transfers between devices, reduce(): a = lax.ppermute(a.astype(jnp.bfloat16), 'tok', self.cw).astype(jnp.float32)  28.1 us
    ppermute x8, waiting for transfers between devices, gather(): a = lax.ppermute(a, 'tok', self.cw)  16.9 us
    dot_general x16, matrix products, cross(): lax.dot_general(left, right, (((1,), (1,)), ((), ())), preferred_element_...  15.1 us
    ppermute x8, starting transfers between devices, gather(): a = lax.ppermute(a, 'tok', self.cw)  14.7 us
    ppermute x8, starting transfers between devices, reduce(): a = lax.ppermute(a.astype(jnp.bfloat16), 'tok', self.cw).astype(jnp.float32)  12.5 us
    convert_element_type x8, other arithmetic, reduce(): a = lax.ppermute(a.astype(jnp.bfloat16), 'tok', self.cw).astype(jnp.float32)  12.2 us
    ppermute x6, waiting for transfers between devices, gather(): b = lax.ppermute(b, 'tok', self.ccw)  7.93 us
    unnamed x72, local copies, waits for them, and re-layouts  6.41 us
  transfers between devices with their start and end apart: 60, of which 27 were waited for; matrix products, arithmetic and copies ran while one was open for 16% of the time, Pallas kernels for 0%

profile of v2, /device:TPU:0, one launch (start us, length us, event | category | flops | bytes accessed | tf_op | source)
XLA Modules:
  0.0 192.2 jit_solution(18088291722066755437)
XLA Ops:
  2.4 3.1 %collective-permute-start.1 = (bf16[2,3,32,512]{3,2,1,0:T(8,128)(2,1)}, bf16[2,3,32,512]{3,2,1,0:T(8,128)(2,1)}, u32[]{:S(2)}, u32[]{:S(2)}) collective-permute-start(bf16[2,3,32,512]{3,2,1,0:T(8,128)(2,1)} %get-tuple-element.9), channel_id=1, source_target_pairs={{0,4},{1,5},{4,8},{5,9},{8,12},{9,13},{12,14},{13,15},{14,10},{15,... | collective-permute-start | bytes 589832 | tf_op jit(solution)/shard_map/ppermute | solution.py:108
  26.5 2.3 %slice_bitcast_fusion.5 = (bf16[256,1024]{1,0:T(8,128)(2,1)}, bf16[256,1024]{1,0:T(8,128)(2,1)}) fusion(bf16[2,256,1024]{2,1,0:T(8,128)(2,1)} %param.65), kind=kLoop, calls=%fused_computation.90 | loop fusion | bytes 2097152 | tf_op jit(solution)/shard_map/squeeze | solution.py:53
  28.7 2.2 %slice_bitcast_fusion = (bf16[256,1024]{1,0:T(8,128)(2,1)}, bf16[256,1024]{1,0:T(8,128)(2,1)}) fusion(bf16[2,256,1024]{2,1,0:T(8,128)(2,1)} %param.66), kind=kLoop, calls=%fused_computation.47 | loop fusion | bytes 2097152 | tf_op jit(solution)/shard_map/squeeze | solution.py:54
  38.5 2.1 %collective-permute-start.5 = (bf16[2,3,32,512]{3,2,1,0:T(8,128)(2,1)}, bf16[2,3,32,512]{3,2,1,0:T(8,128)(2,1)S(1)}, u32[]{:S(2)}, u32[]{:S(2)}) collective-permute-start(bf16[2,3,32,512]{3,2,1,0:T(8,128)(2,1)} %collective-permute-done.1), channel_id=1, source_target_pairs={{0,4},{1,5},{4,8},{5,9},{8,12},{9,13},{12,14},{13,15},{14,10},{15,... | collective-permute-start | bytes 589832 | tf_op jit(solution)/shard_map/ppermute | solution.py:108
  43.0 3.1 %collective-permute-done.5 = bf16[2,3,32,512]{3,2,1,0:T(8,128)(2,1)S(1)} collective-permute-done((bf16[2,3,32,512]{3,2,1,0:T(8,128)(2,1)}, bf16[2,3,32,512]{3,2,1,0:T(8,128)(2,1)S(1)}, u32[]{:S(2)}, u32[]{:S(2)}) %collective-permute-start.5) | collective-permute-done | bytes 196640 | tf_op jit(solution)/shard_map/ppermute | solution.py:108
  46.0 1.7 collective-permute-start.9
  49.4 3.1 %collective-permute-done.9 = bf16[2,3,32,512]{3,2,1,0:T(8,128)(2,1)S(1)} collective-permute-done((bf16[2,3,32,512]{3,2,1,0:T(8,128)(2,1)S(1)}, bf16[2,3,32,512]{3,2,1,0:T(8,128)(2,1)S(1)}, u32[]{:S(2)}, u32[]{:S(2)}) %collective-permute-start.9) | collective-permute-done | bytes 196640 | tf_op jit(solution)/shard_map/ppermute | solution.py:108
  52.5 1.5 collective-permute-start.13
  55.2 2.9 %collective-permute-done.13 = bf16[2,3,32,512]{3,2,1,0:T(8,128)(2,1)S(1)} collective-permute-done((bf16[2,3,32,512]{3,2,1,0:T(8,128)(2,1)S(1)}, bf16[2,3,32,512]{3,2,1,0:T(8,128)(2,1)S(1)}, u32[]{:S(2)}, u32[]{:S(2)}) %collective-permute-start.13) | collective-permute-done | bytes 196640 | tf_op jit(solution)/shard_map/ppermute | solution.py:108
  66.4 1.6 constant_dynamic-slice_fusion.15
  68.1 1.9 %copy-done.1 = f32[2,3,8,2,32,512]{5,4,1,0,3,2:T(8,128)} copy-done((f32[2,3,8,2,32,512]{5,4,1,0,3,2:T(8,128)}, f32[2,3,8,2,32,512]{5,4,1,0,3,2:T(8,128)S(1)}, u32[]{:S(2)}) %copy-start.1) | copy-done | bytes 6291480
  72.9 2.1 %fusion.94 = (bf16[2,3,32,512]{3,2,1,0:T(8,128)(2,1)S(1)}, bf16[2,3,32,512]{3,2,1,0:T(8,128)(2,1)}) fusion(f32[2,3,1,1,32,512]{5,4,1,0,3,2:T(8,128)} %collective-permute-done.16, f32[2,3,8,2,32,512]{5,4,1,0,3,2:T(8,128)} %copy-done.1, s32[]{:T(128)S(6)} %select_n.513, s32[]{:T(128)S(6)} %select_n.485, f32[2,3,1,1,32,512]{5,4,1,0,3,2:T(8,128)} %collective-permute-done.24, ...), kind=kLoop, calls=%fused_computation.166 | loop fusion | flops 393216 | bytes 1966092 | tf_op jit(solution)/shard_map/convert_element_type | solution.py:134
  75.1 1.5 collective-permute-start.17
  78.2 3.9 %collective-permute-done.17 = bf16[2,3,32,512]{3,2,1,0:T(8,128)(2,1)S(1)} collective-permute-done((bf16[2,3,32,512]{3,2,1,0:T(8,128)(2,1)S(1)}, bf16[2,3,32,512]{3,2,1,0:T(8,128)(2,1)S(1)}, u32[]{:S(2)}, u32[]{:S(2)}) %collective-permute-start.17) | collective-permute-done | bytes 196640 | tf_op jit(solution)/shard_map/ppermute | solution.py:134
  82.1 1.8 fusion.47
  85.4 1.9 %multiply_reduce_fusion.3 = (f32[256]{0:T(256)S(1)}, f32[256,512]{1,0:T(8,128)S(1)}) fusion(bf16[512,512]{1,0:T(8,128)(2,1)S(1)} %bitcast.341, bf16[512,512]{1,0:T(8,128)(2,1)S(1)} %bitcast.343, f32[256,512]{0,1:T(8,128)} %convolution_bitcast_fusion.19, bf16[256,1024]{1,0:T(8,128)(2,1)S(1)} %copy-done.16), kind=kOutput, calls=%fused_computation.84 | convolution fusion | flops 269483776 | bytes 2360320 | tf_op jit(solution)/shard_map/dot_general | solution.py:8
  87.9 2.4 %collective-permute-done.19 = bf16[2,3,32,512]{3,2,1,0:T(8,128)(2,1)S(1)} collective-permute-done((bf16[2,3,32,512]{3,2,1,0:T(8,128)(2,1)}, bf16[2,3,32,512]{3,2,1,0:T(8,128)(2,1)S(1)}, u32[]{:S(2)}, u32[]{:S(2)}) %collective-permute-start.19) | collective-permute-done | bytes 196640 | tf_op jit(solution)/shard_map/ppermute | solution.py:134
  90.3 1.6 fusion.46
  91.8 1.5 collective-permute-start.21
  93.9 3.6 %collective-permute-done.21 = bf16[2,3,32,512]{3,2,1,0:T(8,128)(2,1)S(1)} collective-permute-done((bf16[2,3,32,512]{3,2,1,0:T(8,128)(2,1)S(1)}, bf16[2,3,32,512]{3,2,1,0:T(8,128)(2,1)S(1)}, u32[]{:S(2)}, u32[]{:S(2)}) %collective-permute-start.21) | collective-permute-done | bytes 196640 | tf_op jit(solution)/shard_map/ppermute | solution.py:134
  97.5 1.5 collective-permute-done.27
  100.3 1.6 collective-permute-start.23
  102.4 3.6 %collective-permute-done.23 = bf16[2,3,32,512]{3,2,1,0:T(8,128)(2,1)S(1)} collective-permute-done((bf16[2,3,32,512]{3,2,1,0:T(8,128)(2,1)S(1)}, bf16[2,3,32,512]{3,2,1,0:T(8,128)(2,1)S(1)}, u32[]{:S(2)}, u32[]{:S(2)}) %collective-permute-start.23) | collective-permute-done | bytes 196640 | tf_op jit(solution)/shard_map/ppermute | solution.py:134
  106.1 1.6 collective-permute-done.29
  109.5 1.6 collective-permute-start.31
  112.6 2.6 %collective-permute-done.31 = bf16[2,3,32,512]{3,2,1,0:T(8,128)(2,1)S(1)} collective-permute-done((bf16[2,3,32,512]{3,2,1,0:T(8,128)(2,1)S(1)}, bf16[2,3,32,512]{3,2,1,0:T(8,128)(2,1)S(1)}, u32[]{:S(2)}, u32[]{:S(2)}) %collective-permute-start.31) | collective-permute-done | bytes 196640 | tf_op jit(solution)/shard_map/ppermute | solution.py:108
  115.2 1.6 collective-permute-start.35
  116.8 1.6 collective-permute-done.33
  118.9 1.9 %collective-permute-done.35 = bf16[2,3,32,512]{3,2,1,0:T(8,128)(2,1)S(1)} collective-permute-done((bf16[2,3,32,512]{3,2,1,0:T(8,128)(2,1)S(1)}, bf16[2,3,32,512]{3,2,1,0:T(8,128)(2,1)S(1)}, u32[]{:S(2)}, u32[]{:S(2)}) %collective-permute-start.35) | collective-permute-done | bytes 196640 | tf_op jit(solution)/shard_map/ppermute | solution.py:108
  120.9 1.6 collective-permute-start.39
  122.4 2.4 %collective-permute-done.37 = bf16[2,3,32,512]{3,2,1,0:T(8,128)(2,1)S(1)} collective-permute-done((bf16[2,3,32,512]{3,2,1,0:T(8,128)(2,1)S(1)}, bf16[2,3,32,512]{3,2,1,0:T(8,128)(2,1)S(1)}, u32[]{:S(2)}, u32[]{:S(2)}) %collective-permute-start.37) | collective-permute-done | bytes 196640 | tf_op jit(solution)/shard_map/ppermute | solution.py:111
  126.5 1.6 collective-permute-start.43
  128.1 2.4 %collective-permute-done.41 = bf16[2,3,32,512]{3,2,1,0:T(8,128)(2,1)S(1)} collective-permute-done((bf16[2,3,32,512]{3,2,1,0:T(8,128)(2,1)S(1)}, bf16[2,3,32,512]{3,2,1,0:T(8,128)(2,1)S(1)}, u32[]{:S(2)}, u32[]{:S(2)}) %collective-permute-start.41) | collective-permute-done | bytes 196640 | tf_op jit(solution)/shard_map/ppermute | solution.py:111
  130.7 2.2 %collective-permute-done.43 = bf16[2,3,32,512]{3,2,1,0:T(8,128)(2,1)S(1)} collective-permute-done((bf16[2,3,32,512]{3,2,1,0:T(8,128)(2,1)S(1)}, bf16[2,3,32,512]{3,2,1,0:T(8,128)(2,1)S(1)}, u32[]{:S(2)}, u32[]{:S(2)}) %collective-permute-start.43) | collective-permute-done | bytes 196640 | tf_op jit(solution)/shard_map/ppermute | solution.py:108
  141.0 2.6 %multiply_reduce_fusion.1 = (f32[256]{0:T(256)S(1)}, f32[256,512]{1,0:T(8,128)}) fusion(bf16[512,512]{1,0:T(8,128)(2,1)S(1)} %bitcast.352, bf16[512,512]{1,0:T(8,128)(2,1)S(1)} %bitcast.355, f32[256,512]{0,1:T(8,128)} %convolution_bitcast_fusion.9, bf16[256,1024]{1,0:T(8,128)(2,1)S(1)} %copy-done.14), kind=kOutput, calls=%fused_computation.57 | convolution fusion | flops 269483776 | bytes 2360320 | tf_op jit(solution)/shard_map/dot_general | solution.py:8
  150.7 1.6 constant_dynamic-slice_fusion.8
  152.3 2.0 %copy-done = f32[2,3,8,2,32,512]{5,4,1,0,3,2:T(8,128)} copy-done((f32[2,3,8,2,32,512]{5,4,1,0,3,2:T(8,128)}, f32[2,3,8,2,32,512]{5,4,1,0,3,2:T(8,128)S(1)}, u32[]{:S(2)}) %copy-start) | copy-done | bytes 6291480
  158.3 1.6 collective-permute-start.47
  160.6 4.7 %collective-permute-done.47 = bf16[2,3,32,512]{3,2,1,0:T(8,128)(2,1)S(1)} collective-permute-done((bf16[2,3,32,512]{3,2,1,0:T(8,128)(2,1)S(1)}, bf16[2,3,32,512]{3,2,1,0:T(8,128)(2,1)S(1)}, u32[]{:S(2)}, u32[]{:S(2)}) %collective-permute-start.47) | collective-permute-done | bytes 196640 | tf_op jit(solution)/shard_map/ppermute | solution.py:134
  166.4 1.6 collective-permute-start.49
  168.7 3.8 %collective-permute-done.49 = bf16[2,3,32,512]{3,2,1,0:T(8,128)(2,1)S(1)} collective-permute-done((bf16[2,3,32,512]{3,2,1,0:T(8,128)(2,1)S(1)}, bf16[2,3,32,512]{3,2,1,0:T(8,128)(2,1)S(1)}, u32[]{:S(2)}, u32[]{:S(2)}) %collective-permute-start.49) | collective-permute-done | bytes 196640 | tf_op jit(solution)/shard_map/ppermute | solution.py:134
  172.6 1.6 fusion.39
  174.1 1.6 collective-permute-start.51
  176.4 3.5 %collective-permute-done.51 = bf16[2,3,32,512]{3,2,1,0:T(8,128)(2,1)S(1)} collective-permute-done((bf16[2,3,32,512]{3,2,1,0:T(8,128)(2,1)S(1)}, bf16[2,3,32,512]{3,2,1,0:T(8,128)(2,1)S(1)}, u32[]{:S(2)}, u32[]{:S(2)}) %collective-permute-start.51) | collective-permute-done | bytes 196640 | tf_op jit(solution)/shard_map/ppermute | solution.py:134
  179.9 1.6 collective-permute-done.57
  182.8 1.6 collective-permute-start.53
  186.0 2.5 %collective-permute-done.53 = bf16[2,3,32,512]{3,2,1,0:T(8,128)(2,1)S(1)} collective-permute-done((bf16[2,3,32,512]{3,2,1,0:T(8,128)(2,1)S(1)}, bf16[2,3,32,512]{3,2,1,0:T(8,128)(2,1)S(1)}, u32[]{:S(2)}, u32[]{:S(2)}) %collective-permute-start.53) | collective-permute-done | bytes 196640 | tf_op jit(solution)/shard_map/ppermute | solution.py:134
  188.5 1.5 collective-permute-done.59
  (246 shorter events, 60.3 us)
Async XLA Ops:
  2.4 36.1 %collective-permute-start.1 = (bf16[2,3,32,512]{3,2,1,0:T(8,128)(2,1)}, bf16[2,3,32,512]{3,2,1,0:T(8,128)(2,1)}, u32[]{:S(2)}, u32[]{:S(2)}) collective-permute-start(bf16[2,3,32,512]{3,2,1,0:T(8,128)(2,1)} %get-tuple-element.9), channel_id=1, source_target_pairs={{0,4},{1,5},{4,8},{5,9},{8,12},{9,13},{12,14},{13,15},{14,10},{15,... | collective-permute-start | bytes 589832 | tf_op jit(solution)/shard_map/ppermute | solution.py:108
  5.4 35.6 %collective-permute-start = (bf16[2,3,32,512]{3,2,1,0:T(8,128)(2,1)}, bf16[2,3,32,512]{3,2,1,0:T(8,128)(2,1)}, u32[]{:S(2)}, u32[]{:S(2)}) collective-permute-start(bf16[2,3,32,512]{3,2,1,0:T(8,128)(2,1)} %get-tuple-element.9), channel_id=1, source_target_pairs={{0,1},{1,0},{2,3},{3,2},{4,5},{5,4},{6,7},{7,6},{8,9},{9,8},{10,11... | collective-permute-start | bytes 589832 | tf_op jit(solution)/shard_map/ppermute | solution.py:100
  5.4 35.1 %collective-permute-start.3 = (bf16[2,3,32,512]{3,2,1,0:T(8,128)(2,1)}, bf16[2,3,32,512]{3,2,1,0:T(8,128)(2,1)}, u32[]{:S(2)}, u32[]{:S(2)}) collective-permute-start(bf16[2,3,32,512]{3,2,1,0:T(8,128)(2,1)} %get-tuple-element.9), channel_id=1, source_target_pairs={{0,2},{1,3},{4,0},{5,1},{8,4},{9,5},{12,8},{13,9},{14,12},{15,13},... | collective-permute-start | bytes 589832 | tf_op jit(solution)/shard_map/ppermute | solution.py:111
  38.5 7.6 %collective-permute-start.5 = (bf16[2,3,32,512]{3,2,1,0:T(8,128)(2,1)}, bf16[2,3,32,512]{3,2,1,0:T(8,128)(2,1)S(1)}, u32[]{:S(2)}, u32[]{:S(2)}) collective-permute-start(bf16[2,3,32,512]{3,2,1,0:T(8,128)(2,1)} %collective-permute-done.1), channel_id=1, source_target_pairs={{0,4},{1,5},{4,8},{5,9},{8,12},{9,13},{12,14},{13,15},{14,10},{15,... | collective-permute-start | bytes 589832 | tf_op jit(solution)/shard_map/ppermute | solution.py:108
  40.5 7.8 %collective-permute-start.2 = (bf16[2,3,32,512]{3,2,1,0:T(8,128)(2,1)}, bf16[2,3,32,512]{3,2,1,0:T(8,128)(2,1)S(1)}, u32[]{:S(2)}, u32[]{:S(2)}) collective-permute-start(bf16[2,3,32,512]{3,2,1,0:T(8,128)(2,1)} %collective-permute-done.1), channel_id=1, source_target_pairs={{0,1},{1,0},{2,3},{3,2},{4,5},{5,4},{6,7},{7,6},{8,9},{9,8},{10,11... | collective-permute-start | bytes 589832 | tf_op jit(solution)/shard_map/ppermute | solution.py:100
  40.6 7.5 %collective-permute-start.7 = (bf16[2,3,32,512]{3,2,1,0:T(8,128)(2,1)}, bf16[2,3,32,512]{3,2,1,0:T(8,128)(2,1)S(1)}, u32[]{:S(2)}, u32[]{:S(2)}) collective-permute-start(bf16[2,3,32,512]{3,2,1,0:T(8,128)(2,1)} %collective-permute-done.3), channel_id=1, source_target_pairs={{0,2},{1,3},{4,0},{5,1},{8,4},{9,5},{12,8},{13,9},{14,12},{15,13},... | collective-permute-start | bytes 589832 | tf_op jit(solution)/shard_map/ppermute | solution.py:111
  40.8 8.6 %collective-permute-start.4 = (bf16[2,3,32,512]{3,2,1,0:T(8,128)(2,1)}, bf16[2,3,32,512]{3,2,1,0:T(8,128)(2,1)S(1)}, u32[]{:S(2)}, u32[]{:S(2)}) collective-permute-start(bf16[2,3,32,512]{3,2,1,0:T(8,128)(2,1)} %collective-permute-done.3), channel_id=1, source_target_pairs={{0,1},{1,0},{2,3},{3,2},{4,5},{5,4},{6,7},{7,6},{8,9},{9,8},{10,11... | collective-permute-start | bytes 589832 | tf_op jit(solution)/shard_map/ppermute | solution.py:100
  46.0 6.5 %collective-permute-start.9 = (bf16[2,3,32,512]{3,2,1,0:T(8,128)(2,1)S(1)}, bf16[2,3,32,512]{3,2,1,0:T(8,128)(2,1)S(1)}, u32[]{:S(2)}, u32[]{:S(2)}) collective-permute-start(bf16[2,3,32,512]{3,2,1,0:T(8,128)(2,1)S(1)} %collective-permute-done.5), channel_id=1, source_target_pairs={{0,4},{1,5},{4,8},{5,9},{8,12},{9,13},{12,14},{13,15},{14,10},{15,... | collective-permute-start | bytes 589832 | tf_op jit(solution)/shard_map/ppermute | solution.py:108
  47.8 7.3 %collective-permute-start.6 = (bf16[2,3,32,512]{3,2,1,0:T(8,128)(2,1)S(1)}, bf16[2,3,32,512]{3,2,1,0:T(8,128)(2,1)S(1)}, u32[]{:S(2)}, u32[]{:S(2)}) collective-permute-start(bf16[2,3,32,512]{3,2,1,0:T(8,128)(2,1)S(1)} %collective-permute-done.5), channel_id=1, source_target_pairs={{0,1},{1,0},{2,3},{3,2},{4,5},{5,4},{6,7},{7,6},{8,9},{9,8},{10,11... | collective-permute-start | bytes 589832 | tf_op jit(solution)/shard_map/ppermute | solution.py:100
  48.1 7.0 %collective-permute-start.11 = (bf16[2,3,32,512]{3,2,1,0:T(8,128)(2,1)S(1)}, bf16[2,3,32,512]{3,2,1,0:T(8,128)(2,1)S(1)}, u32[]{:S(2)}, u32[]{:S(2)}) collective-permute-start(bf16[2,3,32,512]{3,2,1,0:T(8,128)(2,1)S(1)} %collective-permute-done.7), channel_id=1, source_target_pairs={{0,2},{1,3},{4,0},{5,1},{8,4},{9,5},{12,8},{13,9},{14,12},{15,13},... | collective-permute-start | bytes 589832 | tf_op jit(solution)/shard_map/ppermute | solution.py:111
  48.4 6.8 %collective-permute-start.8 = (bf16[2,3,32,512]{3,2,1,0:T(8,128)(2,1)S(1)}, bf16[2,3,32,512]{3,2,1,0:T(8,128)(2,1)S(1)}, u32[]{:S(2)}, u32[]{:S(2)}) collective-permute-start(bf16[2,3,32,512]{3,2,1,0:T(8,128)(2,1)S(1)} %collective-permute-done.7), channel_id=1, source_target_pairs={{0,1},{1,0},{2,3},{3,2},{4,5},{5,4},{6,7},{7,6},{8,9},{9,8},{10,11... | collective-permute-start | bytes 589832 | tf_op jit(solution)/shard_map/ppermute | solution.py:100
  52.5 5.7 %collective-permute-start.13 = (bf16[2,3,32,512]{3,2,1,0:T(8,128)(2,1)S(1)}, bf16[2,3,32,512]{3,2,1,0:T(8,128)(2,1)S(1)}, u32[]{:S(2)}, u32[]{:S(2)}) collective-permute-start(bf16[2,3,32,512]{3,2,1,0:T(8,128)(2,1)S(1)} %collective-permute-done.9), channel_id=1, source_target_pairs={{0,4},{1,5},{4,8},{5,9},{8,12},{9,13},{12,14},{13,15},{14,10},{15,... | collective-permute-start | bytes 589832 | tf_op jit(solution)/shard_map/ppermute | solution.py:108
  70.8 31.6 %collective-permute-start.15 = (f32[2,3,1,1,32,512]{5,4,1,0,3,2:T(8,128)}, f32[2,3,1,1,32,512]{5,4,1,0,3,2:T(8,128)}, u32[]{:S(2)}, u32[]{:S(2)}) collective-permute-start(f32[2,3,1,1,32,512]{5,4,1,0,3,2:T(8,128)} %get-tuple-element.24), channel_id=1, source_target_pairs={{0,1},{1,0},{2,3},{3,2},{4,5},{5,4},{6,7},{7,6},{8,9},{9,8},{10,11... | collective-permute-start | bytes 1179656 | tf_op jit(solution)/shard_map/ppermute | solution.py:126
  71.0 16.2 %collective-permute-start.26 = (f32[2,3,1,1,32,512]{5,4,1,0,3,2:T(8,128)}, f32[2,3,1,1,32,512]{5,4,1,0,3,2:T(8,128)}, u32[]{:S(2)}, u32[]{:S(2)}) collective-permute-start(f32[2,3,1,1,32,512]{5,4,1,0,3,2:T(8,128)} %get-tuple-element.26), channel_id=1, source_target_pairs={{0,1},{1,0},{2,3},{3,2},{4,5},{5,4},{6,7},{7,6},{8,9},{9,8},{10,11... | collective-permute-start | bytes 1179656 | tf_op jit(solution)/shard_map/ppermute | solution.py:126
  71.4 16.0 %collective-permute-start.20 = (f32[2,3,1,1,32,512]{5,4,1,0,3,2:T(8,128)}, f32[2,3,1,1,32,512]{5,4,1,0,3,2:T(8,128)}, u32[]{:S(2)}, u32[]{:S(2)}) collective-permute-start(f32[2,3,1,1,32,512]{5,4,1,0,3,2:T(8,128)} %get-tuple-element.29), channel_id=1, source_target_pairs={{0,1},{1,0},{2,3},{3,2},{4,5},{5,4},{6,7},{7,6},{8,9},{9,8},{10,11... | collective-permute-start | bytes 1179656 | tf_op jit(solution)/shard_map/ppermute | solution.py:126
  75.1 7.0 %collective-permute-start.17 = (bf16[2,3,32,512]{3,2,1,0:T(8,128)(2,1)S(1)}, bf16[2,3,32,512]{3,2,1,0:T(8,128)(2,1)S(1)}, u32[]{:S(2)}, u32[]{:S(2)}) collective-permute-start(bf16[2,3,32,512]{3,2,1,0:T(8,128)(2,1)S(1)} %get-tuple-element.36), channel_id=1, source_target_pairs={{0,4},{1,5},{4,8},{5,9},{8,12},{9,13},{12,14},{13,15},{14,10},{15,... | collective-permute-start | bytes 589832 | tf_op jit(solution)/shard_map/ppermute | solution.py:134
  77.7 10.2 %collective-permute-start.25 = (bf16[2,3,32,512]{3,2,1,0:T(8,128)(2,1)}, bf16[2,3,32,512]{3,2,1,0:T(8,128)(2,1)S(1)}, u32[]{:S(2)}, u32[]{:S(2)}) collective-permute-start(bf16[2,3,32,512]{3,2,1,0:T(8,128)(2,1)} %get-tuple-element.37), channel_id=1, source_target_pairs={{0,2},{1,3},{4,0},{5,1},{8,4},{9,5},{12,8},{13,9},{14,12},{15,13},... | collective-permute-start | bytes 589832 | tf_op jit(solution)/shard_map/ppermute | solution.py:138
  83.9 6.4 %collective-permute-start.19 = (bf16[2,3,32,512]{3,2,1,0:T(8,128)(2,1)}, bf16[2,3,32,512]{3,2,1,0:T(8,128)(2,1)S(1)}, u32[]{:S(2)}, u32[]{:S(2)}) collective-permute-start(bf16[2,3,32,512]{3,2,1,0:T(8,128)(2,1)} %fusion.47), channel_id=1, source_target_pairs={{0,4},{1,5},{4,8},{5,9},{8,12},{9,13},{12,14},{13,15},{14,10},{15,... | collective-permute-start | bytes 589832 | tf_op jit(solution)/shard_map/ppermute | solution.py:134
  87.3 6.6 %collective-permute-start.28 = (f32[2,3,1,1,32,512]{5,4,1,0,3,2:T(8,128)}, f32[2,3,1,1,32,512]{5,4,1,0,3,2:T(8,128)S(1)}, u32[]{:S(2)}, u32[]{:S(2)}) collective-permute-start(f32[2,3,1,1,32,512]{5,4,1,0,3,2:T(8,128)} %get-tuple-element.25), channel_id=1, source_target_pairs={{0,1},{1,0},{2,3},{3,2},{4,5},{5,4},{6,7},{7,6},{8,9},{9,8},{10,11... | collective-permute-start | bytes 1179656 | tf_op jit(solution)/shard_map/ppermute | solution.py:126
  87.4 6.5 %collective-permute-start.22 = (f32[2,3,1,1,32,512]{5,4,1,0,3,2:T(8,128)}, f32[2,3,1,1,32,512]{5,4,1,0,3,2:T(8,128)S(1)}, u32[]{:S(2)}, u32[]{:S(2)}) collective-permute-start(f32[2,3,1,1,32,512]{5,4,1,0,3,2:T(8,128)} %get-tuple-element.28), channel_id=1, source_target_pairs={{0,1},{1,0},{2,3},{3,2},{4,5},{5,4},{6,7},{7,6},{8,9},{9,8},{10,11... | collective-permute-start | bytes 1179656 | tf_op jit(solution)/shard_map/ppermute | solution.py:126
  91.8 5.7 %collective-permute-start.21 = (bf16[2,3,32,512]{3,2,1,0:T(8,128)(2,1)S(1)}, bf16[2,3,32,512]{3,2,1,0:T(8,128)(2,1)S(1)}, u32[]{:S(2)}, u32[]{:S(2)}) collective-permute-start(bf16[2,3,32,512]{3,2,1,0:T(8,128)(2,1)S(1)} %get-tuple-element.34), channel_id=1, source_target_pairs={{0,4},{1,5},{4,8},{5,9},{8,12},{9,13},{12,14},{13,15},{14,10},{15,... | collective-permute-start | bytes 589832 | tf_op jit(solution)/shard_map/ppermute | solution.py:134
  93.3 5.7 %collective-permute-start.27 = (bf16[2,3,32,512]{3,2,1,0:T(8,128)(2,1)S(1)}, bf16[2,3,32,512]{3,2,1,0:T(8,128)(2,1)S(1)}, u32[]{:S(2)}, u32[]{:S(2)}) collective-permute-start(bf16[2,3,32,512]{3,2,1,0:T(8,128)(2,1)S(1)} %get-tuple-element.35), channel_id=1, source_target_pairs={{0,2},{1,3},{4,0},{5,1},{8,4},{9,5},{12,8},{13,9},{14,12},{15,13},... | collective-permute-start | bytes 589832 | tf_op jit(solution)/shard_map/ppermute | solution.py:138
  100.3 5.7 %collective-permute-start.23 = (bf16[2,3,32,512]{3,2,1,0:T(8,128)(2,1)S(1)}, bf16[2,3,32,512]{3,2,1,0:T(8,128)(2,1)S(1)}, u32[]{:S(2)}, u32[]{:S(2)}) collective-permute-start(bf16[2,3,32,512]{3,2,1,0:T(8,128)(2,1)S(1)} %get-tuple-element.32), channel_id=1, source_target_pairs={{0,4},{1,5},{4,8},{5,9},{8,12},{9,13},{12,14},{13,15},{14,10},{15,... | collective-permute-start | bytes 589832 | tf_op jit(solution)/shard_map/ppermute | solution.py:134
  102.0 5.7 %collective-permute-start.29 = (bf16[2,3,32,512]{3,2,1,0:T(8,128)(2,1)S(1)}, bf16[2,3,32,512]{3,2,1,0:T(8,128)(2,1)S(1)}, u32[]{:S(2)}, u32[]{:S(2)}) collective-permute-start(bf16[2,3,32,512]{3,2,1,0:T(8,128)(2,1)S(1)} %get-tuple-element.33), channel_id=1, source_target_pairs={{0,2},{1,3},{4,0},{5,1},{8,4},{9,5},{12,8},{13,9},{14,12},{15,13},... | collective-permute-start | bytes 589832 | tf_op jit(solution)/shard_map/ppermute | solution.py:138
  109.5 5.7 %collective-permute-start.31 = (bf16[2,3,32,512]{3,2,1,0:T(8,128)(2,1)S(1)}, bf16[2,3,32,512]{3,2,1,0:T(8,128)(2,1)S(1)}, u32[]{:S(2)}, u32[]{:S(2)}) collective-permute-start(bf16[2,3,32,512]{3,2,1,0:T(8,128)(2,1)S(1)} %get-tuple-element.5), channel_id=1, source_target_pairs={{0,4},{1,5},{4,8},{5,9},{8,12},{9,13},{12,14},{13,15},{14,10},{15,... | collective-permute-start | bytes 589832 | tf_op jit(solution)/shard_map/ppermute | solution.py:108
  111.1 7.8 %collective-permute-start.30 = (bf16[2,3,32,512]{3,2,1,0:T(8,128)(2,1)S(1)}, bf16[2,3,32,512]{3,2,1,0:T(8,128)(2,1)S(1)}, u32[]{:S(2)}, u32[]{:S(2)}) collective-permute-start(bf16[2,3,32,512]{3,2,1,0:T(8,128)(2,1)S(1)} %get-tuple-element.5), channel_id=1, source_target_pairs={{0,1},{1,0},{2,3},{3,2},{4,5},{5,4},{6,7},{7,6},{8,9},{9,8},{10,11... | collective-permute-start | bytes 589832 | tf_op jit(solution)/shard_map/ppermute | solution.py:100
  111.1 7.3 %collective-permute-start.33 = (bf16[2,3,32,512]{3,2,1,0:T(8,128)(2,1)S(1)}, bf16[2,3,32,512]{3,2,1,0:T(8,128)(2,1)S(1)}, u32[]{:S(2)}, u32[]{:S(2)}) collective-permute-start(bf16[2,3,32,512]{3,2,1,0:T(8,128)(2,1)S(1)} %get-tuple-element.5), channel_id=1, source_target_pairs={{0,2},{1,3},{4,0},{5,1},{8,4},{9,5},{12,8},{13,9},{14,12},{15,13},... | collective-permute-start | bytes 589832 | tf_op jit(solution)/shard_map/ppermute | solution.py:111
  115.2 5.7 %collective-permute-start.35 = (bf16[2,3,32,512]{3,2,1,0:T(8,128)(2,1)S(1)}, bf16[2,3,32,512]{3,2,1,0:T(8,128)(2,1)S(1)}, u32[]{:S(2)}, u32[]{:S(2)}) collective-permute-start(bf16[2,3,32,512]{3,2,1,0:T(8,128)(2,1)S(1)} %collective-permute-done.31), channel_id=1, source_target_pairs={{0,4},{1,5},{4,8},{5,9},{8,12},{9,13},{12,14},{13,15},{14,10},{15,... | collective-permute-start | bytes 589832 | tf_op jit(solution)/shard_map/ppermute | solution.py:108
  116.8 8.6 %collective-permute-start.32 = (bf16[2,3,32,512]{3,2,1,0:T(8,128)(2,1)S(1)}, bf16[2,3,32,512]{3,2,1,0:T(8,128)(2,1)S(1)}, u32[]{:S(2)}, u32[]{:S(2)}) collective-permute-start(bf16[2,3,32,512]{3,2,1,0:T(8,128)(2,1)S(1)} %collective-permute-done.31), channel_id=1, source_target_pairs={{0,1},{1,0},{2,3},{3,2},{4,5},{5,4},{6,7},{7,6},{8,9},{9,8},{10,11... | collective-permute-start | bytes 589832 | tf_op jit(solution)/shard_map/ppermute | solution.py:100
  118.4 6.5 %collective-permute-start.37 = (bf16[2,3,32,512]{3,2,1,0:T(8,128)(2,1)S(1)}, bf16[2,3,32,512]{3,2,1,0:T(8,128)(2,1)S(1)}, u32[]{:S(2)}, u32[]{:S(2)}) collective-permute-start(bf16[2,3,32,512]{3,2,1,0:T(8,128)(2,1)S(1)} %collective-permute-done.33), channel_id=1, source_target_pairs={{0,2},{1,3},{4,0},{5,1},{8,4},{9,5},{12,8},{13,9},{14,12},{15,13},... | collective-permute-start | bytes 589832 | tf_op jit(solution)/shard_map/ppermute | solution.py:111
  118.9 6.5 %collective-permute-start.34 = (bf16[2,3,32,512]{3,2,1,0:T(8,128)(2,1)S(1)}, bf16[2,3,32,512]{3,2,1,0:T(8,128)(2,1)S(1)}, u32[]{:S(2)}, u32[]{:S(2)}) collective-permute-start(bf16[2,3,32,512]{3,2,1,0:T(8,128)(2,1)S(1)} %collective-permute-done.33), channel_id=1, source_target_pairs={{0,1},{1,0},{2,3},{3,2},{4,5},{5,4},{6,7},{7,6},{8,9},{9,8},{10,11... | collective-permute-start | bytes 589832 | tf_op jit(solution)/shard_map/ppermute | solution.py:100
  120.9 5.7 %collective-permute-start.39 = (bf16[2,3,32,512]{3,2,1,0:T(8,128)(2,1)S(1)}, bf16[2,3,32,512]{3,2,1,0:T(8,128)(2,1)S(1)}, u32[]{:S(2)}, u32[]{:S(2)}) collective-permute-start(bf16[2,3,32,512]{3,2,1,0:T(8,128)(2,1)S(1)} %collective-permute-done.35), channel_id=1, source_target_pairs={{0,4},{1,5},{4,8},{5,9},{8,12},{9,13},{12,14},{13,15},{14,10},{15,... | collective-permute-start | bytes 589832 | tf_op jit(solution)/shard_map/ppermute | solution.py:108
  122.4 8.1 %collective-permute-start.36 = (bf16[2,3,32,512]{3,2,1,0:T(8,128)(2,1)S(1)}, bf16[2,3,32,512]{3,2,1,0:T(8,128)(2,1)S(1)}, u32[]{:S(2)}, u32[]{:S(2)}) collective-permute-start(bf16[2,3,32,512]{3,2,1,0:T(8,128)(2,1)S(1)} %collective-permute-done.35), channel_id=1, source_target_pairs={{0,1},{1,0},{2,3},{3,2},{4,5},{5,4},{6,7},{7,6},{8,9},{9,8},{10,11... | collective-permute-start | bytes 589832 | tf_op jit(solution)/shard_map/ppermute | solution.py:100
  124.9 5.7 %collective-permute-start.41 = (bf16[2,3,32,512]{3,2,1,0:T(8,128)(2,1)S(1)}, bf16[2,3,32,512]{3,2,1,0:T(8,128)(2,1)S(1)}, u32[]{:S(2)}, u32[]{:S(2)}) collective-permute-start(bf16[2,3,32,512]{3,2,1,0:T(8,128)(2,1)S(1)} %collective-permute-done.37), channel_id=1, source_target_pairs={{0,2},{1,3},{4,0},{5,1},{8,4},{9,5},{12,8},{13,9},{14,12},{15,13},... | collective-permute-start | bytes 589832 | tf_op jit(solution)/shard_map/ppermute | solution.py:111
  125.3 5.3 %collective-permute-start.38 = (bf16[2,3,32,512]{3,2,1,0:T(8,128)(2,1)S(1)}, bf16[2,3,32,512]{3,2,1,0:T(8,128)(2,1)S(1)}, u32[]{:S(2)}, u32[]{:S(2)}) collective-permute-start(bf16[2,3,32,512]{3,2,1,0:T(8,128)(2,1)S(1)} %collective-permute-done.37), channel_id=1, source_target_pairs={{0,1},{1,0},{2,3},{3,2},{4,5},{5,4},{6,7},{7,6},{8,9},{9,8},{10,11... | collective-permute-start | bytes 589832 | tf_op jit(solution)/shard_map/ppermute | solution.py:100
  126.5 6.3 %collective-permute-start.43 = (bf16[2,3,32,512]{3,2,1,0:T(8,128)(2,1)S(1)}, bf16[2,3,32,512]{3,2,1,0:T(8,128)(2,1)S(1)}, u32[]{:S(2)}, u32[]{:S(2)}) collective-permute-start(bf16[2,3,32,512]{3,2,1,0:T(8,128)(2,1)S(1)} %collective-permute-done.39), channel_id=1, source_target_pairs={{0,4},{1,5},{4,8},{5,9},{8,12},{9,13},{12,14},{13,15},{14,10},{15,... | collective-permute-start | bytes 589832 | tf_op jit(solution)/shard_map/ppermute | solution.py:108
  154.8 31.2 %collective-permute-start.45 = (f32[2,3,1,1,32,512]{5,4,1,0,3,2:T(8,128)}, f32[2,3,1,1,32,512]{5,4,1,0,3,2:T(8,128)}, u32[]{:S(2)}, u32[]{:S(2)}) collective-permute-start(f32[2,3,1,1,32,512]{5,4,1,0,3,2:T(8,128)} %get-tuple-element.10), channel_id=1, source_target_pairs={{0,1},{1,0},{2,3},{3,2},{4,5},{5,4},{6,7},{7,6},{8,9},{9,8},{10,11... | collective-permute-start | bytes 1179656 | tf_op jit(solution)/shard_map/ppermute | solution.py:126
  154.9 13.2 %collective-permute-start.56 = (f32[2,3,1,1,32,512]{5,4,1,0,3,2:T(8,128)}, f32[2,3,1,1,32,512]{5,4,1,0,3,2:T(8,128)}, u32[]{:S(2)}, u32[]{:S(2)}) collective-permute-start(f32[2,3,1,1,32,512]{5,4,1,0,3,2:T(8,128)} %get-tuple-element.12), channel_id=1, source_target_pairs={{0,1},{1,0},{2,3},{3,2},{4,5},{5,4},{6,7},{7,6},{8,9},{9,8},{10,11... | collective-permute-start | bytes 1179656 | tf_op jit(solution)/shard_map/ppermute | solution.py:126
  155.3 12.9 %collective-permute-start.50 = (f32[2,3,1,1,32,512]{5,4,1,0,3,2:T(8,128)}, f32[2,3,1,1,32,512]{5,4,1,0,3,2:T(8,128)}, u32[]{:S(2)}, u32[]{:S(2)}) collective-permute-start(f32[2,3,1,1,32,512]{5,4,1,0,3,2:T(8,128)} %get-tuple-element.15), channel_id=1, source_target_pairs={{0,1},{1,0},{2,3},{3,2},{4,5},{5,4},{6,7},{7,6},{8,9},{9,8},{10,11... | collective-permute-start | bytes 1179656 | tf_op jit(solution)/shard_map/ppermute | solution.py:126
  158.3 7.0 %collective-permute-start.47 = (bf16[2,3,32,512]{3,2,1,0:T(8,128)(2,1)S(1)}, bf16[2,3,32,512]{3,2,1,0:T(8,128)(2,1)S(1)}, u32[]{:S(2)}, u32[]{:S(2)}) collective-permute-start(bf16[2,3,32,512]{3,2,1,0:T(8,128)(2,1)S(1)} %get-tuple-element.22), channel_id=1, source_target_pairs={{0,4},{1,5},{4,8},{5,9},{8,12},{9,13},{12,14},{13,15},{14,10},{15,... | collective-permute-start | bytes 589832 | tf_op jit(solution)/shard_map/ppermute | solution.py:134
  160.1 8.6 %collective-permute-start.55 = (bf16[2,3,32,512]{3,2,1,0:T(8,128)(2,1)S(1)}, bf16[2,3,32,512]{3,2,1,0:T(8,128)(2,1)S(1)}, u32[]{:S(2)}, u32[]{:S(2)}) collective-permute-start(bf16[2,3,32,512]{3,2,1,0:T(8,128)(2,1)S(1)} %get-tuple-element.23), channel_id=1, source_target_pairs={{0,2},{1,3},{4,0},{5,1},{8,4},{9,5},{12,8},{13,9},{14,12},{15,13},... | collective-permute-start | bytes 589832 | tf_op jit(solution)/shard_map/ppermute | solution.py:138
  166.4 6.1 %collective-permute-start.49 = (bf16[2,3,32,512]{3,2,1,0:T(8,128)(2,1)S(1)}, bf16[2,3,32,512]{3,2,1,0:T(8,128)(2,1)S(1)}, u32[]{:S(2)}, u32[]{:S(2)}) collective-permute-start(bf16[2,3,32,512]{3,2,1,0:T(8,128)(2,1)S(1)} %fusion.40), channel_id=1, source_target_pairs={{0,4},{1,5},{4,8},{5,9},{8,12},{9,13},{12,14},{13,15},{14,10},{15,... | collective-permute-start | bytes 589832 | tf_op jit(solution)/shard_map/ppermute | solution.py:134
  168.1 8.2 %collective-permute-start.58 = (f32[2,3,1,1,32,512]{5,4,1,0,3,2:T(8,128)S(1)}, f32[2,3,1,1,32,512]{5,4,1,0,3,2:T(8,128)S(1)}, u32[]{:S(2)}, u32[]{:S(2)}) collective-permute-start(f32[2,3,1,1,32,512]{5,4,1,0,3,2:T(8,128)S(1)} %copy-done.27), channel_id=1, source_target_pairs={{0,1},{1,0},{2,3},{3,2},{4,5},{5,4},{6,7},{7,6},{8,9},{9,8},{10,11... | collective-permute-start | bytes 1179656 | tf_op jit(solution)/shard_map/ppermute | solution.py:126
  168.2 8.2 %collective-permute-start.52 = (f32[2,3,1,1,32,512]{5,4,1,0,3,2:T(8,128)S(1)}, f32[2,3,1,1,32,512]{5,4,1,0,3,2:T(8,128)S(1)}, u32[]{:S(2)}, u32[]{:S(2)}) collective-permute-start(f32[2,3,1,1,32,512]{5,4,1,0,3,2:T(8,128)S(1)} %copy-done.26), channel_id=1, source_target_pairs={{0,1},{1,0},{2,3},{3,2},{4,5},{5,4},{6,7},{7,6},{8,9},{9,8},{10,11... | collective-permute-start | bytes 1179656 | tf_op jit(solution)/shard_map/ppermute | solution.py:126
  174.1 5.7 %collective-permute-start.51 = (bf16[2,3,32,512]{3,2,1,0:T(8,128)(2,1)S(1)}, bf16[2,3,32,512]{3,2,1,0:T(8,128)(2,1)S(1)}, u32[]{:S(2)}, u32[]{:S(2)}) collective-permute-start(bf16[2,3,32,512]{3,2,1,0:T(8,128)(2,1)S(1)} %get-tuple-element.20), channel_id=1, source_target_pairs={{0,4},{1,5},{4,8},{5,9},{8,12},{9,13},{12,14},{13,15},{14,10},{15,... | collective-permute-start | bytes 589832 | tf_op jit(solution)/shard_map/ppermute | solution.py:134
  175.8 5.7 %collective-permute-start.57 = (bf16[2,3,32,512]{3,2,1,0:T(8,128)(2,1)S(1)}, bf16[2,3,32,512]{3,2,1,0:T(8,128)(2,1)S(1)}, u32[]{:S(2)}, u32[]{:S(2)}) collective-permute-start(bf16[2,3,32,512]{3,2,1,0:T(8,128)(2,1)S(1)} %get-tuple-element.21), channel_id=1, source_target_pairs={{0,2},{1,3},{4,0},{5,1},{8,4},{9,5},{12,8},{13,9},{14,12},{15,13},... | collective-permute-start | bytes 589832 | tf_op jit(solution)/shard_map/ppermute | solution.py:138
  182.8 5.7 %collective-permute-start.53 = (bf16[2,3,32,512]{3,2,1,0:T(8,128)(2,1)S(1)}, bf16[2,3,32,512]{3,2,1,0:T(8,128)(2,1)S(1)}, u32[]{:S(2)}, u32[]{:S(2)}) collective-permute-start(bf16[2,3,32,512]{3,2,1,0:T(8,128)(2,1)S(1)} %get-tuple-element.18), channel_id=1, source_target_pairs={{0,4},{1,5},{4,8},{5,9},{8,12},{9,13},{12,14},{13,15},{14,10},{15,... | collective-permute-start | bytes 589832 | tf_op jit(solution)/shard_map/ppermute | solution.py:134
  184.3 5.7 %collective-permute-start.59 = (bf16[2,3,32,512]{3,2,1,0:T(8,128)(2,1)S(1)}, bf16[2,3,32,512]{3,2,1,0:T(8,128)(2,1)S(1)}, u32[]{:S(2)}, u32[]{:S(2)}) collective-permute-start(bf16[2,3,32,512]{3,2,1,0:T(8,128)(2,1)S(1)} %get-tuple-element.19), channel_id=1, source_target_pairs={{0,2},{1,3},{4,0},{5,1},{8,4},{9,5},{12,8},{13,9},{14,12},{15,13},... | collective-permute-start | bytes 589832 | tf_op jit(solution)/shard_map/ppermute | solution.py:138
  (48 other events, 201.4 us)

commit v3 on v2

--- a/solution.py
+++ b/solution.py
@@ -152,12 +152,32 @@
         nblocks = queries.shape[0]
         own = fast_weights
         blocks = []
+        heads = own.shape[0]
+        width = queries.shape[2] // heads
+        if ring.chips > 8:
+            for span in range(nblocks):
+                gathered = ring.gather(own.astype(jnp.bfloat16))
+                normed, partial_value = block_step(span, gathered, queries, keys, values, rates)
+                blocks.append(normed)
+                own = renorm(own, own + ring.reduce(partial_value))
+            return (jnp.stack(blocks), own)
+        own = [own[head] for head in range(heads)]
         for span in range(nblocks):
-            gathered = ring.gather(own.astype(jnp.bfloat16))
-            normed, partial_value = block_step(span, gathered, queries, keys, values, rates)
-            blocks.append(normed)
-            own = renorm(own, own + ring.reduce(partial_value))
-        return (jnp.stack(blocks), own)
+            pieces = []
+            for head in range(heads):
+                wbf = ring.gather(own[head][None].astype(jnp.bfloat16))[0]
+                lo = head * width
+                normed, grad = head_step(
+                    queries[span][:, lo : lo + width],
+                    keys[span][:, lo : lo + width],
+                    values[span][:, lo : lo + width],
+                    rates[span][:, head],
+                    wbf,
+                )
+                pieces.append(normed)
+                own[head] = renorm(own[head], own[head] + ring.reduce(grad[None])[0])
+            blocks.append(jnp.concatenate(pieces, axis=1))
+        return (jnp.stack(blocks), jnp.stack(own))
 
     placed = (
         P(None, ("groups", "tok"), None),

time: 193 us -> 222 us (1.15)
  starting transfers between devices: 36.9 us -> 81.4 us
  waiting for transfers between devices: 61.8 us -> 41.2 us
  matrix products: 23.4 us -> 41.9 us
  other arithmetic: 21.1 us -> 8.76 us
    ppermute x8 -> x16, starting transfers between devices: 14.7 us -> 28 us  [gather(): a = lax.ppermute(a, 'tok', self.cw)]
    convert_element_type x8 -> x16, other arithmetic: 12.2 us -> 1.15 us  [reduce(): a = lax.ppermute(a.astype(jnp.bfloat16), 'tok', self.cw).astype(jnp.float32)]
    dot_general x16, matrix products: 15.1 us -> 25.9 us  [cross(): lax.dot_general(left, right, (((1,), (1,)), ((), ())), preferred_element_...]
    ppermute x6 -> x12, starting transfers between devices: 3.02 us -> 13.4 us  [reduce(): lax.ppermute(b.astype(jnp.bfloat16), 'tok', self.ccw).astype(jnp.float32)]
    ppermute x8 -> x16, waiting for transfers between devices: 16.9 us -> 7.09 us  [gather(): a = lax.ppermute(a, 'tok', self.cw)]
    ppermute x8 -> x16, starting transfers between devices: 12.5 us -> 22 us  [reduce(): a = lax.ppermute(a.astype(jnp.bfloat16), 'tok', self.cw).astype(jnp.float32)]
    ppermute x6 -> x12, waiting for transfers between devices: 7.93 us -> 0.75 us  [gather(): b = lax.ppermute(b, 'tok', self.ccw)]
    dot_general x12, matrix products: 4.92 us -> 11.1 us  [inner(): lax.dot_general(left, right, (((0,), (0,)), ((), ())), preferred_element_...]
  transfers between devices with their start and end apart: 60 -> 120, of which waited for: 27 -> 43; matrix products, arithmetic and copies ran while one was open for 16% -> 10% of each run, Pallas kernels for 0% -> 0%
where the time goes in v3:
time: 222 us; the launch traced here: 221 us
  starting transfers between devices  81.4 us (37%)
  matrix products  41.9 us (19%)
  waiting for transfers between devices  41.2 us (19%)
  between operations  26.8 us (12%)
  local copies, waits for them, and re-layouts  20.7 us (9%)
  other arithmetic  8.76 us (4%)
    ppermute x16, starting transfers between devices, gather(): a = lax.ppermute(a, 'tok', self.cw)  28 us
    dot_general x16, matrix products, cross(): lax.dot_general(left, right, (((1,), (1,)), ((), ())), preferred_element_...  25.9 us
    ppermute x16, waiting for transfers between devices, reduce(): a = lax.ppermute(a.astype(jnp.bfloat16), 'tok', self.cw).astype(jnp.float32)  22.5 us
    ppermute x16, starting transfers between devices, reduce(): a = lax.ppermute(a.astype(jnp.bfloat16), 'tok', self.cw).astype(jnp.float32)  22 us
    ppermute x12, starting transfers between devices, reduce(): lax.ppermute(b.astype(jnp.bfloat16), 'tok', self.ccw).astype(jnp.float32)  13.4 us
    dot_general x12, matrix products, inner(): lax.dot_general(left, right, (((0,), (0,)), ((), ())), preferred_element_...  11.1 us
    ppermute x32, starting transfers between devices, chip_sum(): got = lax.ppermute(send, 'tok', self.swap)  8.45 us
    ppermute x16, waiting for transfers between devices, gather(): a = lax.ppermute(a, 'tok', self.cw)  7.09 us
  transfers between devices with their start and end apart: 120, of which 43 were waited for; matrix products, arithmetic and copies ran while one was open for 10% of the time, Pallas kernels for 0%

profile of v3, /device:TPU:0, one launch (start us, length us, event | category | flops | bytes accessed | tf_op | source)
XLA Modules:
  0.0 220.8 jit_solution(17752144775721168522)
XLA Ops:
  2.3 3.1 %collective-permute-start.16 = (bf16[1,3,32,512]{3,2,1,0:T(8,128)(2,1)}, bf16[1,3,32,512]{3,2,1,0:T(8,128)(2,1)}, u32[]{:S(2)}, u32[]{:S(2)}) collective-permute-start(bf16[1,3,32,512]{3,2,1,0:T(8,128)(2,1)} %get-tuple-element.21), channel_id=1, source_target_pairs={{0,4},{1,5},{4,8},{5,9},{8,12},{9,13},{12,14},{13,15},{14,10},{15,... | collective-permute-start | bytes 294920 | tf_op jit(solution)/shard_map/ppermute | solution.py:108
  6.2 2.0 collective-permute-start.1
  29.1 2.4 %slice_bitcast_fusion.5 = (bf16[256,1024]{1,0:T(8,128)(2,1)}, bf16[256,1024]{1,0:T(8,128)(2,1)}) fusion(bf16[2,256,1024]{2,1,0:T(8,128)(2,1)} %param.125), kind=kLoop, calls=%fused_computation.92 | loop fusion | bytes 2097152 | tf_op jit(solution)/shard_map/squeeze | solution.py:171
  40.4 1.8 collective-permute-start.20
  47.8 1.9 collective-permute-start.5
  50.0 1.9 collective-permute-start.24
  54.3 1.6 collective-permute-start.9
  56.4 1.6 collective-permute-start.28
  58.9 1.6 collective-permute-start.13
  62.1 2.0 collective-permute-done.13
  71.6 3.5 %multiply_reduce_fusion.2 = (f32[256]{0:T(256)}, f32[256,512]{1,0:T(8,128)}) fusion(bf16[512,512]{1,0:T(8,128)(2,1)S(1)} %bitcast.504, bf16[512,512]{1,0:T(8,128)(2,1)} %bitcast.507, f32[256,512]{0,1:T(8,128)} %convolution_bitcast_fusion.17, bf16[256,1024]{1,0:T(8,128)(2,1)S(1)} %copy-done.8), kind=kOutput, calls=%fused_computation.79 | convolution fusion | flops 269483776 | bytes 2360320 | tf_op jit(solution)/shard_map/dot_general | solution.py:8
  82.7 3.2 %multiply_reduce_fusion.3 = (f32[256]{0:T(256)}, f32[256,512]{1,0:T(8,128)}) fusion(bf16[512,512]{1,0:T(8,128)(2,1)S(1)} %bitcast.501, bf16[512,512]{1,0:T(8,128)(2,1)S(1)} %bitcast.503, f32[256,512]{0,1:T(8,128)} %convolution_bitcast_fusion.19, bf16[256,1024]{1,0:T(8,128)(2,1)S(1)} %copy-done.8), kind=kOutput, calls=%fused_computation.86 | convolution fusion | flops 269483776 | bytes 2360320 | tf_op jit(solution)/shard_map/dot_general | solution.py:8
  95.6 1.6 collective-permute-start.32
  97.3 3.2 %collective-permute-done.32 = bf16[1,3,32,512]{3,2,1,0:T(8,128)(2,1)S(1)} collective-permute-done((bf16[1,3,32,512]{3,2,1,0:T(8,128)(2,1)S(1)}, bf16[1,3,32,512]{3,2,1,0:T(8,128)(2,1)S(1)}, u32[]{:S(2)}, u32[]{:S(2)}) %collective-permute-start.32) | collective-permute-done | bytes 98336 | tf_op jit(solution)/shard_map/ppermute | solution.py:134
  100.5 1.6 collective-permute-start.62
  102.7 2.5 %collective-permute-done.62 = bf16[1,3,32,512]{3,2,1,0:T(8,128)(2,1)S(1)} collective-permute-done((bf16[1,3,32,512]{3,2,1,0:T(8,128)(2,1)S(1)}, bf16[1,3,32,512]{3,2,1,0:T(8,128)(2,1)S(1)}, u32[]{:S(2)}, u32[]{:S(2)}) %collective-permute-start.62) | collective-permute-done | bytes 98336 | tf_op jit(solution)/shard_map/ppermute | solution.py:134
  105.2 1.6 collective-permute-start.34
  107.8 2.0 collective-permute-done.34
  109.8 1.6 collective-permute-start.64
  112.2 1.6 collective-permute-start.36
  114.4 1.7 collective-permute-start.42
  116.8 1.6 collective-permute-start.66
  119.0 1.7 collective-permute-start.72
  121.7 1.7 collective-permute-start.44
  123.7 1.6 collective-permute-start.68
  126.8 1.6 collective-permute-done.68
  128.4 1.6 collective-permute-done.74
  130.5 1.6 collective-permute-start.46
  132.8 1.6 collective-permute-start.76
  135.6 1.6 collective-permute-start.50
  138.6 1.8 collective-permute-start.80
  141.8 1.7 collective-permute-start.54
  149.8 1.6 collective-permute-start.88
  153.4 1.6 collective-permute-done.88
  163.1 3.0 %multiply_reduce_fusion = (f32[256]{0:T(256)S(1)}, f32[256,512]{1,0:T(8,128)}) fusion(bf16[512,512]{1,0:T(8,128)(2,1)} %bitcast.508, bf16[512,512]{1,0:T(8,128)(2,1)} %bitcast.511, f32[256,512]{0,1:T(8,128)} %convolution_bitcast_fusion.7, bf16[256,1024]{1,0:T(8,128)(2,1)S(1)} %copy-done.5), kind=kOutput, calls=%fused_computation.52 | convolution fusion | flops 269483776 | bytes 2360320 | tf_op jit(solution)/shard_map/dot_general | solution.py:8
  166.2 2.2 convolution_bitcast_fusion.2
  170.6 3.2 %multiply_reduce_fusion.1 = (f32[256]{0:T(256)}, f32[256,512]{1,0:T(8,128)}) fusion(bf16[512,512]{1,0:T(8,128)(2,1)S(1)} %bitcast.497, bf16[512,512]{1,0:T(8,128)(2,1)S(1)} %bitcast.499, f32[256,512]{0,1:T(8,128)} %convolution_bitcast_fusion.12, bf16[256,1024]{1,0:T(8,128)(2,1)S(1)} %copy-done.5), kind=kOutput, calls=%fused_computation.64 | convolution fusion | flops 269483776 | bytes 2360320 | tf_op jit(solution)/shard_map/dot_general | solution.py:8
  185.3 1.6 collective-permute-start.107
  187.0 3.3 %collective-permute-done.107 = bf16[1,3,32,512]{3,2,1,0:T(8,128)(2,1)S(1)} collective-permute-done((bf16[1,3,32,512]{3,2,1,0:T(8,128)(2,1)S(1)}, bf16[1,3,32,512]{3,2,1,0:T(8,128)(2,1)S(1)}, u32[]{:S(2)}, u32[]{:S(2)}) %collective-permute-start.107) | collective-permute-done | bytes 98336 | tf_op jit(solution)/shard_map/ppermute | solution.py:134
  190.3 1.6 collective-permute-start.92
  192.4 2.5 %collective-permute-done.92 = bf16[1,3,32,512]{3,2,1,0:T(8,128)(2,1)S(1)} collective-permute-done((bf16[1,3,32,512]{3,2,1,0:T(8,128)(2,1)S(1)}, bf16[1,3,32,512]{3,2,1,0:T(8,128)(2,1)S(1)}, u32[]{:S(2)}, u32[]{:S(2)}) %collective-permute-start.92) | collective-permute-done | bytes 98336 | tf_op jit(solution)/shard_map/ppermute | solution.py:134
  197.6 2.0 collective-permute-done.109
  199.5 1.6 collective-permute-start.94
  204.1 1.9 collective-permute-start.117
  208.7 1.9 collective-permute-start.102
  211.5 1.7 collective-permute-start.119
  213.5 1.6 collective-permute-start.98
  218.1 1.6 collective-permute-done.104
  (448 shorter events, 99.5 us)
Async XLA Ops:
  2.3 37.8 %collective-permute-start.16 = (bf16[1,3,32,512]{3,2,1,0:T(8,128)(2,1)}, bf16[1,3,32,512]{3,2,1,0:T(8,128)(2,1)}, u32[]{:S(2)}, u32[]{:S(2)}) collective-permute-start(bf16[1,3,32,512]{3,2,1,0:T(8,128)(2,1)} %get-tuple-element.21), channel_id=1, source_target_pairs={{0,4},{1,5},{4,8},{5,9},{8,12},{9,13},{12,14},{13,15},{14,10},{15,... | collective-permute-start | bytes 294920 | tf_op jit(solution)/shard_map/ppermute | solution.py:108
  5.3 35.1 %collective-permute-start.15 = (bf16[1,3,32,512]{3,2,1,0:T(8,128)(2,1)}, bf16[1,3,32,512]{3,2,1,0:T(8,128)(2,1)}, u32[]{:S(2)}, u32[]{:S(2)}) collective-permute-start(bf16[1,3,32,512]{3,2,1,0:T(8,128)(2,1)} %get-tuple-element.21), channel_id=1, source_target_pairs={{0,1},{1,0},{2,3},{3,2},{4,5},{5,4},{6,7},{7,6},{8,9},{9,8},{10,11... | collective-permute-start | bytes 294920 | tf_op jit(solution)/shard_map/ppermute | solution.py:100
  5.3 38.7 %collective-permute-start.18 = (bf16[1,3,32,512]{3,2,1,0:T(8,128)(2,1)}, bf16[1,3,32,512]{3,2,1,0:T(8,128)(2,1)}, u32[]{:S(2)}, u32[]{:S(2)}) collective-permute-start(bf16[1,3,32,512]{3,2,1,0:T(8,128)(2,1)} %get-tuple-element.21), channel_id=1, source_target_pairs={{0,2},{1,3},{4,0},{5,1},{8,4},{9,5},{12,8},{13,9},{14,12},{15,13},... | collective-permute-start | bytes 294920 | tf_op jit(solution)/shard_map/ppermute | solution.py:111
  6.2 39.1 %collective-permute-start.1 = (bf16[1,3,32,512]{3,2,1,0:T(8,128)(2,1)}, bf16[1,3,32,512]{3,2,1,0:T(8,128)(2,1)}, u32[]{:S(2)}, u32[]{:S(2)}) collective-permute-start(bf16[1,3,32,512]{3,2,1,0:T(8,128)(2,1)} %get-tuple-element.15), channel_id=1, source_target_pairs={{0,4},{1,5},{4,8},{5,9},{8,12},{9,13},{12,14},{13,15},{14,10},{15,... | collective-permute-start | bytes 294920 | tf_op jit(solution)/shard_map/ppermute | solution.py:108
  8.2 35.9 %collective-permute-start = (bf16[1,3,32,512]{3,2,1,0:T(8,128)(2,1)}, bf16[1,3,32,512]{3,2,1,0:T(8,128)(2,1)}, u32[]{:S(2)}, u32[]{:S(2)}) collective-permute-start(bf16[1,3,32,512]{3,2,1,0:T(8,128)(2,1)} %get-tuple-element.15), channel_id=1, source_target_pairs={{0,1},{1,0},{2,3},{3,2},{4,5},{5,4},{6,7},{7,6},{8,9},{9,8},{10,11... | collective-permute-start | bytes 294920 | tf_op jit(solution)/shard_map/ppermute | solution.py:100
  40.1 7.7 %collective-permute-start.3 = (bf16[1,3,32,512]{3,2,1,0:T(8,128)(2,1)}, bf16[1,3,32,512]{3,2,1,0:T(8,128)(2,1)S(1)}, u32[]{:S(2)}, u32[]{:S(2)}) collective-permute-start(bf16[1,3,32,512]{3,2,1,0:T(8,128)(2,1)} %get-tuple-element.15), channel_id=1, source_target_pairs={{0,2},{1,3},{4,0},{5,1},{8,4},{9,5},{12,8},{13,9},{14,12},{15,13},... | collective-permute-start | bytes 294920 | tf_op jit(solution)/shard_map/ppermute | solution.py:111
  40.4 9.5 %collective-permute-start.20 = (bf16[1,3,32,512]{3,2,1,0:T(8,128)(2,1)}, bf16[1,3,32,512]{3,2,1,0:T(8,128)(2,1)S(1)}, u32[]{:S(2)}, u32[]{:S(2)}) collective-permute-start(bf16[1,3,32,512]{3,2,1,0:T(8,128)(2,1)} %collective-permute-done.16), channel_id=1, source_target_pairs={{0,4},{1,5},{4,8},{5,9},{8,12},{9,13},{12,14},{13,15},{14,10},{15,... | collective-permute-start | bytes 294920 | tf_op jit(solution)/shard_map/ppermute | solution.py:108
  44.1 7.8 %collective-permute-start.22 = (bf16[1,3,32,512]{3,2,1,0:T(8,128)(2,1)}, bf16[1,3,32,512]{3,2,1,0:T(8,128)(2,1)S(1)}, u32[]{:S(2)}, u32[]{:S(2)}) collective-permute-start(bf16[1,3,32,512]{3,2,1,0:T(8,128)(2,1)} %collective-permute-done.18), channel_id=1, source_target_pairs={{0,2},{1,3},{4,0},{5,1},{8,4},{9,5},{12,8},{13,9},{14,12},{15,13},... | collective-permute-start | bytes 294920 | tf_op jit(solution)/shard_map/ppermute | solution.py:111
  47.8 5.3 %collective-permute-start.5 = (bf16[1,3,32,512]{3,2,1,0:T(8,128)(2,1)}, bf16[1,3,32,512]{3,2,1,0:T(8,128)(2,1)S(1)}, u32[]{:S(2)}, u32[]{:S(2)}) collective-permute-start(bf16[1,3,32,512]{3,2,1,0:T(8,128)(2,1)} %collective-permute-done.1), channel_id=1, source_target_pairs={{0,4},{1,5},{4,8},{5,9},{8,12},{9,13},{12,14},{13,15},{14,10},{15,... | collective-permute-start | bytes 294920 | tf_op jit(solution)/shard_map/ppermute | solution.py:108
  50.0 6.3 %collective-permute-start.24 = (bf16[1,3,32,512]{3,2,1,0:T(8,128)(2,1)S(1)}, bf16[1,3,32,512]{3,2,1,0:T(8,128)(2,1)S(1)}, u32[]{:S(2)}, u32[]{:S(2)}) collective-permute-start(bf16[1,3,32,512]{3,2,1,0:T(8,128)(2,1)S(1)} %collective-permute-done.20), channel_id=1, source_target_pairs={{0,4},{1,5},{4,8},{5,9},{8,12},{9,13},{12,14},{13,15},{14,10},{15,... | collective-permute-start | bytes 294920 | tf_op jit(solution)/shard_map/ppermute | solution.py:108
  52.1 8.4 %collective-permute-start.26 = (bf16[1,3,32,512]{3,2,1,0:T(8,128)(2,1)S(1)}, bf16[1,3,32,512]{3,2,1,0:T(8,128)(2,1)S(1)}, u32[]{:S(2)}, u32[]{:S(2)}) collective-permute-start(bf16[1,3,32,512]{3,2,1,0:T(8,128)(2,1)S(1)} %collective-permute-done.22), channel_id=1, source_target_pairs={{0,2},{1,3},{4,0},{5,1},{8,4},{9,5},{12,8},{13,9},{14,12},{15,13},... | collective-permute-start | bytes 294920 | tf_op jit(solution)/shard_map/ppermute | solution.py:111
  55.8 5.0 %collective-permute-start.11 = (bf16[1,3,32,512]{3,2,1,0:T(8,128)(2,1)S(1)}, bf16[1,3,32,512]{3,2,1,0:T(8,128)(2,1)S(1)}, u32[]{:S(2)}, u32[]{:S(2)}) collective-permute-start(bf16[1,3,32,512]{3,2,1,0:T(8,128)(2,1)S(1)} %collective-permute-done.7), channel_id=1, source_target_pairs={{0,2},{1,3},{4,0},{5,1},{8,4},{9,5},{12,8},{13,9},{14,12},{15,13},... | collective-permute-start | bytes 294920 | tf_op jit(solution)/shard_map/ppermute | solution.py:111
  56.4 5.2 %collective-permute-start.28 = (bf16[1,3,32,512]{3,2,1,0:T(8,128)(2,1)S(1)}, bf16[1,3,32,512]{3,2,1,0:T(8,128)(2,1)S(1)}, u32[]{:S(2)}, u32[]{:S(2)}) collective-permute-start(bf16[1,3,32,512]{3,2,1,0:T(8,128)(2,1)S(1)} %collective-permute-done.24), channel_id=1, source_target_pairs={{0,4},{1,5},{4,8},{5,9},{8,12},{9,13},{12,14},{13,15},{14,10},{15,... | collective-permute-start | bytes 294920 | tf_op jit(solution)/shard_map/ppermute | solution.py:108
  58.9 5.2 %collective-permute-start.13 = (bf16[1,3,32,512]{3,2,1,0:T(8,128)(2,1)S(1)}, bf16[1,3,32,512]{3,2,1,0:T(8,128)(2,1)S(1)}, u32[]{:S(2)}, u32[]{:S(2)}) collective-permute-start(bf16[1,3,32,512]{3,2,1,0:T(8,128)(2,1)S(1)} %collective-permute-done.9), channel_id=1, source_target_pairs={{0,4},{1,5},{4,8},{5,9},{8,12},{9,13},{12,14},{13,15},{14,10},{15,... | collective-permute-start | bytes 294920 | tf_op jit(solution)/shard_map/ppermute | solution.py:108
  90.8 34.6 %collective-permute-start.30 = (f32[1,3,1,1,32,512]{5,4,1,3,2,0:T(8,128)S(1)}, f32[1,3,1,1,32,512]{5,4,1,3,2,0:T(8,128)S(1)}, u32[]{:S(2)}, u32[]{:S(2)}) collective-permute-start(f32[1,3,1,1,32,512]{5,4,1,3,2,0:T(8,128)S(1)} %get-tuple-element.50), channel_id=1, source_target_pairs={{0,1},{1,0},{2,3},{3,2},{4,5},{5,4},{6,7},{7,6},{8,9},{9,8},{10,11... | collective-permute-start | bytes 589832 | tf_op jit(solution)/shard_map/ppermute | solution.py:126
  91.4 15.4 %collective-permute-start.41 = (f32[1,3,1,1,32,512]{5,4,1,3,2,0:T(8,128)S(1)}, f32[1,3,1,1,32,512]{5,4,1,3,2,0:T(8,128)S(1)}, u32[]{:S(2)}, u32[]{:S(2)}) collective-permute-start(f32[1,3,1,1,32,512]{5,4,1,3,2,0:T(8,128)S(1)} %get-tuple-element.52), channel_id=1, source_target_pairs={{0,1},{1,0},{2,3},{3,2},{4,5},{5,4},{6,7},{7,6},{8,9},{9,8},{10,11... | collective-permute-start | bytes 589832 | tf_op jit(solution)/shard_map/ppermute | solution.py:126
  91.9 15.0 %collective-permute-start.35 = (f32[1,3,1,1,32,512]{5,4,1,3,2,0:T(8,128)S(1)}, f32[1,3,1,1,32,512]{5,4,1,3,2,0:T(8,128)S(1)}, u32[]{:S(2)}, u32[]{:S(2)}) collective-permute-start(f32[1,3,1,1,32,512]{5,4,1,3,2,0:T(8,128)S(1)} %get-tuple-element.55), channel_id=1, source_target_pairs={{0,1},{1,0},{2,3},{3,2},{4,5},{5,4},{6,7},{7,6},{8,9},{9,8},{10,11... | collective-permute-start | bytes 589832 | tf_op jit(solution)/shard_map/ppermute | solution.py:126
  95.6 5.0 %collective-permute-start.32 = (bf16[1,3,32,512]{3,2,1,0:T(8,128)(2,1)S(1)}, bf16[1,3,32,512]{3,2,1,0:T(8,128)(2,1)S(1)}, u32[]{:S(2)}, u32[]{:S(2)}) collective-permute-start(bf16[1,3,32,512]{3,2,1,0:T(8,128)(2,1)S(1)} %get-tuple-element.62), channel_id=1, source_target_pairs={{0,4},{1,5},{4,8},{5,9},{8,12},{9,13},{12,14},{13,15},{14,10},{15,... | collective-permute-start | bytes 294920 | tf_op jit(solution)/shard_map/ppermute | solution.py:134
  97.2 4.9 %collective-permute-start.63 = (f32[1,3,1,1,32,512]{5,4,1,3,2,0:T(8,128)S(1)}, f32[1,3,1,1,32,512]{5,4,1,3,2,0:T(8,128)S(1)}, u32[]{:S(2)}, u32[]{:S(2)}) collective-permute-start(f32[1,3,1,1,32,512]{5,4,1,3,2,0:T(8,128)S(1)} %get-tuple-element.70), channel_id=1, source_target_pairs={{0,1},{1,0},{2,3},{3,2},{4,5},{5,4},{6,7},{7,6},{8,9},{9,8},{10,11... | collective-permute-start | bytes 589832 | tf_op jit(solution)/shard_map/ppermute | solution.py:126
  102.2 5.2 %collective-permute-start.40 = (bf16[1,3,32,512]{3,2,1,0:T(8,128)(2,1)S(1)}, bf16[1,3,32,512]{3,2,1,0:T(8,128)(2,1)S(1)}, u32[]{:S(2)}, u32[]{:S(2)}) collective-permute-start(bf16[1,3,32,512]{3,2,1,0:T(8,128)(2,1)S(1)} %get-tuple-element.63), channel_id=1, source_target_pairs={{0,2},{1,3},{4,0},{5,1},{8,4},{9,5},{12,8},{13,9},{14,12},{15,13},... | collective-permute-start | bytes 294920 | tf_op jit(solution)/shard_map/ppermute | solution.py:138
  116.8 4.9 %collective-permute-start.66 = (bf16[1,3,32,512]{3,2,1,0:T(8,128)(2,1)S(1)}, bf16[1,3,32,512]{3,2,1,0:T(8,128)(2,1)S(1)}, u32[]{:S(2)}, u32[]{:S(2)}) collective-permute-start(bf16[1,3,32,512]{3,2,1,0:T(8,128)(2,1)S(1)} %get-tuple-element.74), channel_id=1, source_target_pairs={{0,4},{1,5},{4,8},{5,9},{8,12},{9,13},{12,14},{13,15},{14,10},{15,... | collective-permute-start | bytes 294920 | tf_op jit(solution)/shard_map/ppermute | solution.py:134
  120.8 5.1 %collective-permute-start.60 = (f32[1,3,1,1,32,512]{5,4,1,3,2,0:T(8,128)S(1)}, f32[1,3,1,1,32,512]{5,4,1,3,2,0:T(8,128)S(1)}, u32[]{:S(2)}, u32[]{:S(2)}) collective-permute-start(f32[1,3,1,1,32,512]{5,4,1,3,2,0:T(8,128)S(1)} %get-tuple-element.64), channel_id=1, source_target_pairs={{0,1},{1,0},{2,3},{3,2},{4,5},{5,4},{6,7},{7,6},{8,9},{9,8},{10,11... | collective-permute-start | bytes 589832 | tf_op jit(solution)/shard_map/ppermute | solution.py:126
  120.9 5.7 %collective-permute-start.38 = (bf16[1,3,32,512]{3,2,1,0:T(8,128)(2,1)S(1)}, bf16[1,3,32,512]{3,2,1,0:T(8,128)(2,1)S(1)}, u32[]{:S(2)}, u32[]{:S(2)}) collective-permute-start(bf16[1,3,32,512]{3,2,1,0:T(8,128)(2,1)S(1)} %get-tuple-element.58), channel_id=1, source_target_pairs={{0,4},{1,5},{4,8},{5,9},{8,12},{9,13},{12,14},{13,15},{14,10},{15,... | collective-permute-start | bytes 294920 | tf_op jit(solution)/shard_map/ppermute | solution.py:134
  121.7 5.1 %collective-permute-start.44 = (bf16[1,3,32,512]{3,2,1,0:T(8,128)(2,1)S(1)}, bf16[1,3,32,512]{3,2,1,0:T(8,128)(2,1)S(1)}, u32[]{:S(2)}, u32[]{:S(2)}) collective-permute-start(bf16[1,3,32,512]{3,2,1,0:T(8,128)(2,1)S(1)} %get-tuple-element.59), channel_id=1, source_target_pairs={{0,2},{1,3},{4,0},{5,1},{8,4},{9,5},{12,8},{13,9},{14,12},{15,13},... | collective-permute-start | bytes 294920 | tf_op jit(solution)/shard_map/ppermute | solution.py:138
  132.1 5.2 %collective-permute-start.48 = (bf16[1,3,32,512]{3,2,1,0:T(8,128)(2,1)S(1)}, bf16[1,3,32,512]{3,2,1,0:T(8,128)(2,1)S(1)}, u32[]{:S(2)}, u32[]{:S(2)}) collective-permute-start(bf16[1,3,32,512]{3,2,1,0:T(8,128)(2,1)S(1)} %get-tuple-element.11), channel_id=1, source_target_pairs={{0,2},{1,3},{4,0},{5,1},{8,4},{9,5},{12,8},{13,9},{14,12},{15,13},... | collective-permute-start | bytes 294920 | tf_op jit(solution)/shard_map/ppermute | solution.py:111
  132.8 5.0 %collective-permute-start.76 = (bf16[1,3,32,512]{3,2,1,0:T(8,128)(2,1)S(1)}, bf16[1,3,32,512]{3,2,1,0:T(8,128)(2,1)S(1)}, u32[]{:S(2)}, u32[]{:S(2)}) collective-permute-start(bf16[1,3,32,512]{3,2,1,0:T(8,128)(2,1)S(1)} %get-tuple-element.17), channel_id=1, source_target_pairs={{0,4},{1,5},{4,8},{5,9},{8,12},{9,13},{12,14},{13,15},{14,10},{15,... | collective-permute-start | bytes 294920 | tf_op jit(solution)/shard_map/ppermute | solution.py:108
  135.1 5.3 %collective-permute-start.78 = (bf16[1,3,32,512]{3,2,1,0:T(8,128)(2,1)S(1)}, bf16[1,3,32,512]{3,2,1,0:T(8,128)(2,1)S(1)}, u32[]{:S(2)}, u32[]{:S(2)}) collective-permute-start(bf16[1,3,32,512]{3,2,1,0:T(8,128)(2,1)S(1)} %get-tuple-element.17), channel_id=1, source_target_pairs={{0,2},{1,3},{4,0},{5,1},{8,4},{9,5},{12,8},{13,9},{14,12},{15,13},... | collective-permute-start | bytes 294920 | tf_op jit(solution)/shard_map/ppermute | solution.py:111
  135.6 5.3 %collective-permute-start.50 = (bf16[1,3,32,512]{3,2,1,0:T(8,128)(2,1)S(1)}, bf16[1,3,32,512]{3,2,1,0:T(8,128)(2,1)S(1)}, u32[]{:S(2)}, u32[]{:S(2)}) collective-permute-start(bf16[1,3,32,512]{3,2,1,0:T(8,128)(2,1)S(1)} %collective-permute-done.46), channel_id=1, source_target_pairs={{0,4},{1,5},{4,8},{5,9},{8,12},{9,13},{12,14},{13,15},{14,10},{15,... | collective-permute-start | bytes 294920 | tf_op jit(solution)/shard_map/ppermute | solution.py:108
  137.3 6.3 %collective-permute-start.52 = (bf16[1,3,32,512]{3,2,1,0:T(8,128)(2,1)S(1)}, bf16[1,3,32,512]{3,2,1,0:T(8,128)(2,1)S(1)}, u32[]{:S(2)}, u32[]{:S(2)}) collective-permute-start(bf16[1,3,32,512]{3,2,1,0:T(8,128)(2,1)S(1)} %collective-permute-done.48), channel_id=1, source_target_pairs={{0,2},{1,3},{4,0},{5,1},{8,4},{9,5},{12,8},{13,9},{14,12},{15,13},... | collective-permute-start | bytes 294920 | tf_op jit(solution)/shard_map/ppermute | solution.py:111
  138.6 5.6 %collective-permute-start.80 = (bf16[1,3,32,512]{3,2,1,0:T(8,128)(2,1)S(1)}, bf16[1,3,32,512]{3,2,1,0:T(8,128)(2,1)S(1)}, u32[]{:S(2)}, u32[]{:S(2)}) collective-permute-start(bf16[1,3,32,512]{3,2,1,0:T(8,128)(2,1)S(1)} %collective-permute-done.76), channel_id=1, source_target_pairs={{0,4},{1,5},{4,8},{5,9},{8,12},{9,13},{12,14},{13,15},{14,10},{15,... | collective-permute-start | bytes 294920 | tf_op jit(solution)/shard_map/ppermute | solution.py:108
  140.5 6.0 %collective-permute-start.82 = (bf16[1,3,32,512]{3,2,1,0:T(8,128)(2,1)S(1)}, bf16[1,3,32,512]{3,2,1,0:T(8,128)(2,1)S(1)}, u32[]{:S(2)}, u32[]{:S(2)}) collective-permute-start(bf16[1,3,32,512]{3,2,1,0:T(8,128)(2,1)S(1)} %collective-permute-done.78), channel_id=1, source_target_pairs={{0,2},{1,3},{4,0},{5,1},{8,4},{9,5},{12,8},{13,9},{14,12},{15,13},... | collective-permute-start | bytes 294920 | tf_op jit(solution)/shard_map/ppermute | solution.py:111
  141.8 5.4 %collective-permute-start.54 = (bf16[1,3,32,512]{3,2,1,0:T(8,128)(2,1)S(1)}, bf16[1,3,32,512]{3,2,1,0:T(8,128)(2,1)S(1)}, u32[]{:S(2)}, u32[]{:S(2)}) collective-permute-start(bf16[1,3,32,512]{3,2,1,0:T(8,128)(2,1)S(1)} %collective-permute-done.50), channel_id=1, source_target_pairs={{0,4},{1,5},{4,8},{5,9},{8,12},{9,13},{12,14},{13,15},{14,10},{15,... | collective-permute-start | bytes 294920 | tf_op jit(solution)/shard_map/ppermute | solution.py:108
  143.7 7.7 %collective-permute-start.56 = (bf16[1,3,32,512]{3,2,1,0:T(8,128)(2,1)S(1)}, bf16[1,3,32,512]{3,2,1,0:T(8,128)(2,1)S(1)}, u32[]{:S(2)}, u32[]{:S(2)}) collective-permute-start(bf16[1,3,32,512]{3,2,1,0:T(8,128)(2,1)S(1)} %collective-permute-done.52), channel_id=1, source_target_pairs={{0,2},{1,3},{4,0},{5,1},{8,4},{9,5},{12,8},{13,9},{14,12},{15,13},... | collective-permute-start | bytes 294920 | tf_op jit(solution)/shard_map/ppermute | solution.py:111
  145.0 4.9 %collective-permute-start.84 = (bf16[1,3,32,512]{3,2,1,0:T(8,128)(2,1)S(1)}, bf16[1,3,32,512]{3,2,1,0:T(8,128)(2,1)S(1)}, u32[]{:S(2)}, u32[]{:S(2)}) collective-permute-start(bf16[1,3,32,512]{3,2,1,0:T(8,128)(2,1)S(1)} %collective-permute-done.80), channel_id=1, source_target_pairs={{0,4},{1,5},{4,8},{5,9},{8,12},{9,13},{12,14},{13,15},{14,10},{15,... | collective-permute-start | bytes 294920 | tf_op jit(solution)/shard_map/ppermute | solution.py:108
  146.7 5.2 %collective-permute-start.86 = (bf16[1,3,32,512]{3,2,1,0:T(8,128)(2,1)S(1)}, bf16[1,3,32,512]{3,2,1,0:T(8,128)(2,1)S(1)}, u32[]{:S(2)}, u32[]{:S(2)}) collective-permute-start(bf16[1,3,32,512]{3,2,1,0:T(8,128)(2,1)S(1)} %collective-permute-done.82), channel_id=1, source_target_pairs={{0,2},{1,3},{4,0},{5,1},{8,4},{9,5},{12,8},{13,9},{14,12},{15,13},... | collective-permute-start | bytes 294920 | tf_op jit(solution)/shard_map/ppermute | solution.py:111
  147.9 4.9 %collective-permute-start.58 = (bf16[1,3,32,512]{3,2,1,0:T(8,128)(2,1)S(1)}, bf16[1,3,32,512]{3,2,1,0:T(8,128)(2,1)S(1)}, u32[]{:S(2)}, u32[]{:S(2)}) collective-permute-start(bf16[1,3,32,512]{3,2,1,0:T(8,128)(2,1)S(1)} %collective-permute-done.54), channel_id=1, source_target_pairs={{0,4},{1,5},{4,8},{5,9},{8,12},{9,13},{12,14},{13,15},{14,10},{15,... | collective-permute-start | bytes 294920 | tf_op jit(solution)/shard_map/ppermute | solution.py:108
  149.8 5.2 %collective-permute-start.88 = (bf16[1,3,32,512]{3,2,1,0:T(8,128)(2,1)S(1)}, bf16[1,3,32,512]{3,2,1,0:T(8,128)(2,1)S(1)}, u32[]{:S(2)}, u32[]{:S(2)}) collective-permute-start(bf16[1,3,32,512]{3,2,1,0:T(8,128)(2,1)S(1)} %collective-permute-done.84), channel_id=1, source_target_pairs={{0,4},{1,5},{4,8},{5,9},{8,12},{9,13},{12,14},{13,15},{14,10},{15,... | collective-permute-start | bytes 294920 | tf_op jit(solution)/shard_map/ppermute | solution.py:108
  180.1 35.0 %collective-permute-start.105 = (f32[1,3,1,1,32,512]{5,4,1,3,2,0:T(8,128)S(1)}, f32[1,3,1,1,32,512]{5,4,1,3,2,0:T(8,128)S(1)}, u32[]{:S(2)}, u32[]{:S(2)}) collective-permute-start(f32[1,3,1,1,32,512]{5,4,1,3,2,0:T(8,128)S(1)} %get-tuple-element.36), channel_id=1, source_target_pairs={{0,1},{1,0},{2,3},{3,2},{4,5},{5,4},{6,7},{7,6},{8,9},{9,8},{10,11... | collective-permute-start | bytes 589832 | tf_op jit(solution)/shard_map/ppermute | solution.py:126
  180.3 16.2 %collective-permute-start.116 = (f32[1,3,1,1,32,512]{5,4,1,3,2,0:T(8,128)S(1)}, f32[1,3,1,1,32,512]{5,4,1,3,2,0:T(8,128)S(1)}, u32[]{:S(2)}, u32[]{:S(2)}) collective-permute-start(f32[1,3,1,1,32,512]{5,4,1,3,2,0:T(8,128)S(1)} %get-tuple-element.38), channel_id=1, source_target_pairs={{0,1},{1,0},{2,3},{3,2},{4,5},{5,4},{6,7},{7,6},{8,9},{9,8},{10,11... | collective-permute-start | bytes 589832 | tf_op jit(solution)/shard_map/ppermute | solution.py:126
  180.8 15.8 %collective-permute-start.110 = (f32[1,3,1,1,32,512]{5,4,1,3,2,0:T(8,128)S(1)}, f32[1,3,1,1,32,512]{5,4,1,3,2,0:T(8,128)S(1)}, u32[]{:S(2)}, u32[]{:S(2)}) collective-permute-start(f32[1,3,1,1,32,512]{5,4,1,3,2,0:T(8,128)S(1)} %get-tuple-element.41), channel_id=1, source_target_pairs={{0,1},{1,0},{2,3},{3,2},{4,5},{5,4},{6,7},{7,6},{8,9},{9,8},{10,11... | collective-permute-start | bytes 589832 | tf_op jit(solution)/shard_map/ppermute | solution.py:126
  185.3 5.0 %collective-permute-start.107 = (bf16[1,3,32,512]{3,2,1,0:T(8,128)(2,1)S(1)}, bf16[1,3,32,512]{3,2,1,0:T(8,128)(2,1)S(1)}, u32[]{:S(2)}, u32[]{:S(2)}) collective-permute-start(bf16[1,3,32,512]{3,2,1,0:T(8,128)(2,1)S(1)} %get-tuple-element.48), channel_id=1, source_target_pairs={{0,4},{1,5},{4,8},{5,9},{8,12},{9,13},{12,14},{13,15},{14,10},{15,... | collective-permute-start | bytes 294920 | tf_op jit(solution)/shard_map/ppermute | solution.py:134
  186.9 4.9 %collective-permute-start.93 = (f32[1,3,1,1,32,512]{5,4,1,3,2,0:T(8,128)S(1)}, f32[1,3,1,1,32,512]{5,4,1,3,2,0:T(8,128)S(1)}, u32[]{:S(2)}, u32[]{:S(2)}) collective-permute-start(f32[1,3,1,1,32,512]{5,4,1,3,2,0:T(8,128)S(1)} %get-tuple-element.28), channel_id=1, source_target_pairs={{0,1},{1,0},{2,3},{3,2},{4,5},{5,4},{6,7},{7,6},{8,9},{9,8},{10,11... | collective-permute-start | bytes 589832 | tf_op jit(solution)/shard_map/ppermute | solution.py:126
  191.9 5.2 %collective-permute-start.115 = (bf16[1,3,32,512]{3,2,1,0:T(8,128)(2,1)S(1)}, bf16[1,3,32,512]{3,2,1,0:T(8,128)(2,1)S(1)}, u32[]{:S(2)}, u32[]{:S(2)}) collective-permute-start(bf16[1,3,32,512]{3,2,1,0:T(8,128)(2,1)S(1)} %get-tuple-element.49), channel_id=1, source_target_pairs={{0,2},{1,3},{4,0},{5,1},{8,4},{9,5},{12,8},{13,9},{14,12},{15,13},... | collective-permute-start | bytes 294920 | tf_op jit(solution)/shard_map/ppermute | solution.py:138
  201.2 4.9 %collective-permute-start.118 = (f32[1,3,1,1,32,512]{5,4,1,3,2,0:T(8,128)S(1)}, f32[1,3,1,1,32,512]{5,4,1,3,2,0:T(8,128)S(1)}, u32[]{:S(2)}, u32[]{:S(2)}) collective-permute-start(f32[1,3,1,1,32,512]{5,4,1,3,2,0:T(8,128)S(1)} %get-tuple-element.37), channel_id=1, source_target_pairs={{0,1},{1,0},{2,3},{3,2},{4,5},{5,4},{6,7},{7,6},{8,9},{9,8},{10,11... | collective-permute-start | bytes 589832 | tf_op jit(solution)/shard_map/ppermute | solution.py:126
  201.3 4.9 %collective-permute-start.112 = (f32[1,3,1,1,32,512]{5,4,1,3,2,0:T(8,128)S(1)}, f32[1,3,1,1,32,512]{5,4,1,3,2,0:T(8,128)S(1)}, u32[]{:S(2)}, u32[]{:S(2)}) collective-permute-start(f32[1,3,1,1,32,512]{5,4,1,3,2,0:T(8,128)S(1)} %get-tuple-element.40), channel_id=1, source_target_pairs={{0,1},{1,0},{2,3},{3,2},{4,5},{5,4},{6,7},{7,6},{8,9},{9,8},{10,11... | collective-permute-start | bytes 589832 | tf_op jit(solution)/shard_map/ppermute | solution.py:126
  210.7 6.2 %collective-permute-start.90 = (f32[1,3,1,1,32,512]{5,4,1,3,2,0:T(8,128)S(1)}, f32[1,3,1,1,32,512]{5,4,1,3,2,0:T(8,128)S(1)}, u32[]{:S(2)}, u32[]{:S(2)}) collective-permute-start(f32[1,3,1,1,32,512]{5,4,1,3,2,0:T(8,128)S(1)} %get-tuple-element.22), channel_id=1, source_target_pairs={{0,1},{1,0},{2,3},{3,2},{4,5},{5,4},{6,7},{7,6},{8,9},{9,8},{10,11... | collective-permute-start | bytes 589832 | tf_op jit(solution)/shard_map/ppermute | solution.py:126
  210.8 5.7 %collective-permute-start.113 = (bf16[1,3,32,512]{3,2,1,0:T(8,128)(2,1)S(1)}, bf16[1,3,32,512]{3,2,1,0:T(8,128)(2,1)S(1)}, u32[]{:S(2)}, u32[]{:S(2)}) collective-permute-start(bf16[1,3,32,512]{3,2,1,0:T(8,128)(2,1)S(1)} %get-tuple-element.44), channel_id=1, source_target_pairs={{0,4},{1,5},{4,8},{5,9},{8,12},{9,13},{12,14},{13,15},{14,10},{15,... | collective-permute-start | bytes 294920 | tf_op jit(solution)/shard_map/ppermute | solution.py:134
  211.5 5.1 %collective-permute-start.119 = (bf16[1,3,32,512]{3,2,1,0:T(8,128)(2,1)S(1)}, bf16[1,3,32,512]{3,2,1,0:T(8,128)(2,1)S(1)}, u32[]{:S(2)}, u32[]{:S(2)}) collective-permute-start(bf16[1,3,32,512]{3,2,1,0:T(8,128)(2,1)S(1)} %get-tuple-element.45), channel_id=1, source_target_pairs={{0,2},{1,3},{4,0},{5,1},{8,4},{9,5},{12,8},{13,9},{14,12},{15,13},... | collective-permute-start | bytes 294920 | tf_op jit(solution)/shard_map/ppermute | solution.py:138
  (122 other events, 395.1 us)

commit v4 on v2

--- a/solution.py
+++ b/solution.py
@@ -93,23 +93,21 @@
     def gather(self, own):
         h, g, rows, f = own.shape
         core = lax.axis_index("tok") % 2
-        full = jnp.zeros((self.chips, 2, h, g, rows, f), own.dtype)
-
-        def put(full, piece, chip):
-            full = lax.dynamic_update_slice(full, piece[None, None], (chip, core, 0, 0, 0, 0))
-            other = lax.ppermute(piece, "tok", self.swap)
-            return lax.dynamic_update_slice(full, other[None, None], (chip, 1 - core, 0, 0, 0, 0))
-
-        full = put(full, own, lax.axis_index("tok") // 2)
+        ring = jnp.zeros((self.chips, h, g, rows, f), own.dtype)
+        ring = lax.dynamic_update_index_in_dim(ring, own, lax.axis_index("tok") // 2, 0)
         a = own
         b = own
         for k in range(1, max(self.ncw, self.nccw) + 1):
             if k <= self.ncw:
                 a = lax.ppermute(a, "tok", self.cw)
-                full = put(full, a, self.chip_at(-k))
+                ring = lax.dynamic_update_index_in_dim(ring, a, self.chip_at(-k), 0)
             if k <= self.nccw:
                 b = lax.ppermute(b, "tok", self.ccw)
-                full = put(full, b, self.chip_at(k))
+                ring = lax.dynamic_update_index_in_dim(ring, b, self.chip_at(k), 0)
+        other = lax.ppermute(ring, "tok", self.swap)
+        full = jnp.zeros((self.chips, 2, h, g, rows, f), own.dtype)
+        full = lax.dynamic_update_slice(full, ring[:, None], (0, core, 0, 0, 0, 0))
+        full = lax.dynamic_update_slice(full, other[:, None], (0, 1 - core, 0, 0, 0, 0))
         full = jnp.moveaxis(full, (0, 1), (2, 3))
         return full.reshape(h, g, self.chips * 2 * rows, f)
 

time: 193 us -> 185 us (0.959)
  local copies, waits for them, and re-layouts: 22.7 us -> 16.5 us
  other arithmetic: 21.1 us -> 15.1 us
  matrix products: 23.4 us -> 26.7 us
    convert_element_type x8, other arithmetic: 12.2 us -> 6.19 us  [reduce(): a = lax.ppermute(a.astype(jnp.bfloat16), 'tok', self.cw).astype(jnp.float32)]
    dot_general x16, matrix products: 15.1 us -> 20.4 us  [cross(): lax.dot_general(left, right, (((1,), (1,)), ((), ())), preferred_element_...]
    ppermute x16 -> x2, waiting for transfers between devices: 2.66 us -> 0.01 us  [gather(): other = lax.ppermute(ring, 'tok', self.swap)]
    squeeze x1, local copies, waits for them, and re-layouts: 2.24 us -> 0.07 us  [block_step(): keys[span][:, lo:lo + width]]
    dot_general x4, matrix products: 3.35 us -> 1.37 us  [head_step(): back = jnp.dot(value_rows, wbf[2], preferred_element_type=jnp.float32)]
    unnamed x72 -> x62, local copies, waits for them, and re-layouts: 6.41 us -> 4.44 us
    dynamic_update_slice x30 -> x18, local copies, waits for them, and re-layouts: 3.41 us -> 4.66 us  [the longest x2 3.14 us: gather(): lax.dynamic_update_slice(full, other[:, None], (0, 1 - core, 0, 0, 0, 0))]
  transfers between devices with their start and end apart: 60 -> 46, of which waited for: 27 -> 25; matrix products, arithmetic and copies ran while one was open for 16% -> 14% of each run, Pallas kernels for 0% -> 0%
where the time goes in v4:
time: 185 us; the launch traced here: 184 us
  waiting for transfers between devices  62.7 us (34%)
  starting transfers between devices  37.2 us (20%)
  matrix products  26.7 us (14%)
  between operations  26.1 us (14%)
  local copies, waits for them, and re-layouts  16.5 us (9%)
  other arithmetic  15.1 us (8%)
    ppermute x8, waiting for transfers between devices, reduce(): a = lax.ppermute(a.astype(jnp.bfloat16), 'tok', self.cw).astype(jnp.float32)  28.9 us
    dot_general x16, matrix products, cross(): lax.dot_general(left, right, (((1,), (1,)), ((), ())), preferred_element_...  20.4 us
    ppermute x8, waiting for transfers between devices, gather(): a = lax.ppermute(a, 'tok', self.cw)  16.8 us
    ppermute x8, starting transfers between devices, gather(): a = lax.ppermute(a, 'tok', self.cw)  15.1 us
    ppermute x8, starting transfers between devices, reduce(): a = lax.ppermute(a.astype(jnp.bfloat16), 'tok', self.cw).astype(jnp.float32)  13.8 us
    ppermute x6, waiting for transfers between devices, gather(): b = lax.ppermute(b, 'tok', self.ccw)  8.77 us
    ppermute x6, waiting for transfers between devices, reduce(): lax.ppermute(b.astype(jnp.bfloat16), 'tok', self.ccw).astype(jnp.float32)  6.62 us
    convert_element_type x8, other arithmetic, reduce(): a = lax.ppermute(a.astype(jnp.bfloat16), 'tok', self.cw).astype(jnp.float32)  6.19 us
  transfers between devices with their start and end apart: 46, of which 25 were waited for; matrix products, arithmetic and copies ran while one was open for 14% of the time, Pallas kernels for 0%

profile of v4, /device:TPU:0, one launch (start us, length us, event | category | flops | bytes accessed | tf_op | source)
XLA Modules:
  0.0 184.2 jit_solution(2107840584698388000)
XLA Ops:
  1.7 3.1 %collective-permute-start = (bf16[2,3,32,512]{3,2,1,0:T(8,128)(2,1)S(1)}, bf16[2,3,32,512]{3,2,1,0:T(8,128)(2,1)S(1)}, u32[]{:S(2)}, u32[]{:S(2)}) collective-permute-start(bf16[2,3,32,512]{3,2,1,0:T(8,128)(2,1)S(1)} %get-tuple-element.9), channel_id=1, source_target_pairs={{0,4},{1,5},{4,8},{5,9},{8,12},{9,13},{12,14},{13,15},{14,10},{15,... | collective-permute-start | bytes 589832 | tf_op jit(solution)/shard_map/ppermute | solution.py:102
  26.9 2.1 %collective-permute-start.2 = (bf16[2,3,32,512]{3,2,1,0:T(8,128)(2,1)S(1)}, bf16[2,3,32,512]{3,2,1,0:T(8,128)(2,1)S(1)}, u32[]{:S(2)}, u32[]{:S(2)}) collective-permute-start(bf16[2,3,32,512]{3,2,1,0:T(8,128)(2,1)S(1)} %collective-permute-done), channel_id=1, source_target_pairs={{0,4},{1,5},{4,8},{5,9},{8,12},{9,13},{12,14},{13,15},{14,10},{15,... | collective-permute-start | bytes 589832 | tf_op jit(solution)/shard_map/ppermute | solution.py:102
  29.1 4.3 %collective-permute-done.2 = bf16[2,3,32,512]{3,2,1,0:T(8,128)(2,1)S(1)} collective-permute-done((bf16[2,3,32,512]{3,2,1,0:T(8,128)(2,1)S(1)}, bf16[2,3,32,512]{3,2,1,0:T(8,128)(2,1)S(1)}, u32[]{:S(2)}, u32[]{:S(2)}) %collective-permute-start.2) | collective-permute-done | bytes 196640 | tf_op jit(solution)/shard_map/ppermute | solution.py:102
  33.4 1.7 collective-permute-start.4
  35.4 3.6 %collective-permute-done.4 = bf16[2,3,32,512]{3,2,1,0:T(8,128)(2,1)S(1)} collective-permute-done((bf16[2,3,32,512]{3,2,1,0:T(8,128)(2,1)S(1)}, bf16[2,3,32,512]{3,2,1,0:T(8,128)(2,1)S(1)}, u32[]{:S(2)}, u32[]{:S(2)}) %collective-permute-start.4) | collective-permute-done | bytes 196640 | tf_op jit(solution)/shard_map/ppermute | solution.py:102
  39.0 1.9 %collective-permute-start.6 = (bf16[2,3,32,512]{3,2,1,0:T(8,128)(2,1)S(1)}, bf16[2,3,32,512]{3,2,1,0:T(8,128)(2,1)S(1)}, u32[]{:S(2)}, u32[]{:S(2)}) collective-permute-start(bf16[2,3,32,512]{3,2,1,0:T(8,128)(2,1)S(1)} %collective-permute-done.4), channel_id=1, source_target_pairs={{0,4},{1,5},{4,8},{5,9},{8,12},{9,13},{12,14},{13,15},{14,10},{15,... | collective-permute-start | bytes 589832 | tf_op jit(solution)/shard_map/ppermute | solution.py:102
  41.0 3.7 %collective-permute-done.6 = bf16[2,3,32,512]{3,2,1,0:T(8,128)(2,1)S(1)} collective-permute-done((bf16[2,3,32,512]{3,2,1,0:T(8,128)(2,1)S(1)}, bf16[2,3,32,512]{3,2,1,0:T(8,128)(2,1)S(1)}, u32[]{:S(2)}, u32[]{:S(2)}) %collective-permute-start.6) | collective-permute-done | bytes 196640 | tf_op jit(solution)/shard_map/ppermute | solution.py:102
  51.3 1.6 bitcast_dynamic-update-slice_fusion.3
  61.9 1.9 %collective-permute-start.10 = (bf16[2,3,32,512]{3,2,1,0:T(8,128)(2,1)S(1)}, bf16[2,3,32,512]{3,2,1,0:T(8,128)(2,1)S(1)}, u32[]{:S(2)}, u32[]{:S(2)}) collective-permute-start(bf16[2,3,32,512]{3,2,1,0:T(8,128)(2,1)S(1)} %get-tuple-element.36), channel_id=1, source_target_pairs={{0,4},{1,5},{4,8},{5,9},{8,12},{9,13},{12,14},{13,15},{14,10},{15,... | collective-permute-start | bytes 589832 | tf_op jit(solution)/shard_map/ppermute | solution.py:132
  64.5 4.7 %collective-permute-done.10 = bf16[2,3,32,512]{3,2,1,0:T(8,128)(2,1)S(1)} collective-permute-done((bf16[2,3,32,512]{3,2,1,0:T(8,128)(2,1)S(1)}, bf16[2,3,32,512]{3,2,1,0:T(8,128)(2,1)S(1)}, u32[]{:S(2)}, u32[]{:S(2)}) %collective-permute-start.10) | collective-permute-done | bytes 196640 | tf_op jit(solution)/shard_map/ppermute | solution.py:132
  69.3 1.9 %collective-permute-start.12 = (bf16[2,3,32,512]{3,2,1,0:T(8,128)(2,1)S(1)}, bf16[2,3,32,512]{3,2,1,0:T(8,128)(2,1)S(1)}, u32[]{:S(2)}, u32[]{:S(2)}) collective-permute-start(bf16[2,3,32,512]{3,2,1,0:T(8,128)(2,1)S(1)} %fusion.47), channel_id=1, source_target_pairs={{0,4},{1,5},{4,8},{5,9},{8,12},{9,13},{12,14},{13,15},{14,10},{15,... | collective-permute-start | bytes 589832 | tf_op jit(solution)/shard_map/ppermute | solution.py:132
  71.7 4.1 %collective-permute-done.12 = bf16[2,3,32,512]{3,2,1,0:T(8,128)(2,1)S(1)} collective-permute-done((bf16[2,3,32,512]{3,2,1,0:T(8,128)(2,1)S(1)}, bf16[2,3,32,512]{3,2,1,0:T(8,128)(2,1)S(1)}, u32[]{:S(2)}, u32[]{:S(2)}) %collective-permute-start.12) | collective-permute-done | bytes 196640 | tf_op jit(solution)/shard_map/ppermute | solution.py:132
  76.0 1.8 collective-permute-start.14
  78.9 2.7 %collective-permute-done.14 = bf16[2,3,32,512]{3,2,1,0:T(8,128)(2,1)S(1)} collective-permute-done((bf16[2,3,32,512]{3,2,1,0:T(8,128)(2,1)S(1)}, bf16[2,3,32,512]{3,2,1,0:T(8,128)(2,1)S(1)}, u32[]{:S(2)}, u32[]{:S(2)}) %collective-permute-start.14) | collective-permute-done | bytes 196640 | tf_op jit(solution)/shard_map/ppermute | solution.py:132
  81.7 1.7 collective-permute-done.20
  83.6 1.6 collective-permute-start.16
  86.9 2.5 %collective-permute-done.16 = bf16[2,3,32,512]{3,2,1,0:T(8,128)(2,1)S(1)} collective-permute-done((bf16[2,3,32,512]{3,2,1,0:T(8,128)(2,1)S(1)}, bf16[2,3,32,512]{3,2,1,0:T(8,128)(2,1)S(1)}, u32[]{:S(2)}, u32[]{:S(2)}) %collective-permute-start.16) | collective-permute-done | bytes 196640 | tf_op jit(solution)/shard_map/ppermute | solution.py:132
  89.4 1.6 collective-permute-done.22
  92.2 1.6 collective-permute-start.23
  93.7 3.6 %multiply_reduce_fusion.2 = (f32[256]{0:T(256)}, f32[256,512]{1,0:T(8,128)}) fusion(bf16[512,512]{1,0:T(8,128)(2,1)} %bitcast.355, bf16[512,512]{1,0:T(8,128)(2,1)} %bitcast.357, f32[256,512]{0,1:T(8,128)} %convolution_bitcast_fusion.17, bf16[256,1024]{1,0:T(8,128)(2,1)} %copy-done.7), kind=kOutput, calls=%fused_computation.81 | convolution fusion | flops 269483776 | bytes 2360320 | tf_op jit(solution)/shard_map/dot_general | solution.py:8
  97.8 2.3 %collective-permute-done.23 = bf16[2,3,32,512]{3,2,1,0:T(8,128)(2,1)} collective-permute-done((bf16[2,3,32,512]{3,2,1,0:T(8,128)(2,1)}, bf16[2,3,32,512]{3,2,1,0:T(8,128)(2,1)}, u32[]{:S(2)}, u32[]{:S(2)}) %collective-permute-start.23) | collective-permute-done | bytes 196640 | tf_op jit(solution)/shard_map/ppermute | solution.py:102
  100.0 1.6 collective-permute-start.25
  102.6 2.5 %collective-permute-done.24 = bf16[2,3,32,512]{3,2,1,0:T(8,128)(2,1)S(1)} collective-permute-done((bf16[2,3,32,512]{3,2,1,0:T(8,128)(2,1)}, bf16[2,3,32,512]{3,2,1,0:T(8,128)(2,1)S(1)}, u32[]{:S(2)}, u32[]{:S(2)}) %collective-permute-start.24) | collective-permute-done | bytes 196640 | tf_op jit(solution)/shard_map/ppermute | solution.py:105
  105.6 1.4 collective-permute-done.25
  107.0 1.6 collective-permute-start.27
  108.6 3.2 %collective-permute-done.26 = bf16[2,3,32,512]{3,2,1,0:T(8,128)(2,1)S(1)} collective-permute-done((bf16[2,3,32,512]{3,2,1,0:T(8,128)(2,1)S(1)}, bf16[2,3,32,512]{3,2,1,0:T(8,128)(2,1)S(1)}, u32[]{:S(2)}, u32[]{:S(2)}) %collective-permute-start.26) | collective-permute-done | bytes 196640 | tf_op jit(solution)/shard_map/ppermute | solution.py:105
  112.8 1.6 collective-permute-start.29
  114.4 3.0 %collective-permute-done.28 = bf16[2,3,32,512]{3,2,1,0:T(8,128)(2,1)S(1)} collective-permute-done((bf16[2,3,32,512]{3,2,1,0:T(8,128)(2,1)S(1)}, bf16[2,3,32,512]{3,2,1,0:T(8,128)(2,1)S(1)}, u32[]{:S(2)}, u32[]{:S(2)}) %collective-permute-start.28) | collective-permute-done | bytes 196640 | tf_op jit(solution)/shard_map/ppermute | solution.py:105
  119.8 2.9 %multiply_reduce_fusion.3 = (f32[256]{0:T(256)S(1)}, f32[256,512]{1,0:T(8,128)}) fusion(bf16[512,512]{1,0:T(8,128)(2,1)S(1)} %bitcast.351, bf16[512,512]{1,0:T(8,128)(2,1)} %bitcast.353, f32[256,512]{0,1:T(8,128)} %convolution_bitcast_fusion.19, bf16[256,1024]{1,0:T(8,128)(2,1)} %copy-done.7), kind=kOutput, calls=%fused_computation.88 | convolution fusion | flops 269483776 | bytes 2360320 | tf_op jit(solution)/shard_map/dot_general | solution.py:8
  122.7 1.3 divide_convert_fusion.2
  125.5 1.6 bitcast_dynamic-update-slice_fusion
  133.1 3.4 %multiply_reduce_fusion.1 = (f32[256]{0:T(256)}, f32[256,512]{1,0:T(8,128)}) fusion(bf16[512,512]{1,0:T(8,128)(2,1)S(1)} %bitcast.362, bf16[512,512]{1,0:T(8,128)(2,1)S(1)} %bitcast.365, f32[256,512]{0,1:T(8,128)} %convolution_bitcast_fusion.9, bf16[256,1024]{1,0:T(8,128)(2,1)} %get-tuple-element.55), kind=kOutput, calls=%fused_computation.61 | convolution fusion | flops 269483776 | bytes 2360320 | tf_op jit(solution)/shard_map/dot_general | solution.py:8
  142.2 1.6 constant_dynamic-slice_fusion.2
  143.8 1.9 %copy-done = f32[2,3,8,2,32,512]{5,4,1,0,3,2:T(8,128)} copy-done((f32[2,3,8,2,32,512]{5,4,1,0,3,2:T(8,128)}, f32[2,3,8,2,32,512]{5,4,1,0,3,2:T(8,128)S(1)}, u32[]{:S(2)}) %copy-start) | copy-done | bytes 6291480
  148.5 1.6 fusion.96
  150.0 1.6 collective-permute-start.33
  152.3 4.9 %collective-permute-done.33 = bf16[2,3,32,512]{3,2,1,0:T(8,128)(2,1)S(1)} collective-permute-done((bf16[2,3,32,512]{3,2,1,0:T(8,128)(2,1)S(1)}, bf16[2,3,32,512]{3,2,1,0:T(8,128)(2,1)S(1)}, u32[]{:S(2)}, u32[]{:S(2)}) %collective-permute-start.33) | collective-permute-done | bytes 196640 | tf_op jit(solution)/shard_map/ppermute | solution.py:132
  158.3 1.6 collective-permute-start.35
  160.5 4.0 %collective-permute-done.35 = bf16[2,3,32,512]{3,2,1,0:T(8,128)(2,1)S(1)} collective-permute-done((bf16[2,3,32,512]{3,2,1,0:T(8,128)(2,1)S(1)}, bf16[2,3,32,512]{3,2,1,0:T(8,128)(2,1)S(1)}, u32[]{:S(2)}, u32[]{:S(2)}) %collective-permute-start.35) | collective-permute-done | bytes 196640 | tf_op jit(solution)/shard_map/ppermute | solution.py:132
  164.5 1.6 fusion.39
  166.1 1.6 collective-permute-start.37
  168.3 3.5 %collective-permute-done.37 = bf16[2,3,32,512]{3,2,1,0:T(8,128)(2,1)S(1)} collective-permute-done((bf16[2,3,32,512]{3,2,1,0:T(8,128)(2,1)S(1)}, bf16[2,3,32,512]{3,2,1,0:T(8,128)(2,1)S(1)}, u32[]{:S(2)}, u32[]{:S(2)}) %collective-permute-start.37) | collective-permute-done | bytes 196640 | tf_op jit(solution)/shard_map/ppermute | solution.py:132
  171.8 1.6 collective-permute-done.43
  173.4 1.3 fusion.38
  174.7 1.8 collective-permute-start.39
  177.9 2.5 %collective-permute-done.39 = bf16[2,3,32,512]{3,2,1,0:T(8,128)(2,1)S(1)} collective-permute-done((bf16[2,3,32,512]{3,2,1,0:T(8,128)(2,1)S(1)}, bf16[2,3,32,512]{3,2,1,0:T(8,128)(2,1)S(1)}, u32[]{:S(2)}, u32[]{:S(2)}) %collective-permute-start.39) | collective-permute-done | bytes 196640 | tf_op jit(solution)/shard_map/ppermute | solution.py:132
  180.4 1.7 collective-permute-done.45
  182.1 1.2 multiply_reduce_fusion.4
  (198 shorter events, 46.1 us)
Async XLA Ops:
  1.7 25.2 %collective-permute-start = (bf16[2,3,32,512]{3,2,1,0:T(8,128)(2,1)S(1)}, bf16[2,3,32,512]{3,2,1,0:T(8,128)(2,1)S(1)}, u32[]{:S(2)}, u32[]{:S(2)}) collective-permute-start(bf16[2,3,32,512]{3,2,1,0:T(8,128)(2,1)S(1)} %get-tuple-element.9), channel_id=1, source_target_pairs={{0,4},{1,5},{4,8},{5,9},{8,12},{9,13},{12,14},{13,15},{14,10},{15,... | collective-permute-start | bytes 589832 | tf_op jit(solution)/shard_map/ppermute | solution.py:102
  4.8 24.2 %collective-permute-start.1 = (bf16[2,3,32,512]{3,2,1,0:T(8,128)(2,1)S(1)}, bf16[2,3,32,512]{3,2,1,0:T(8,128)(2,1)S(1)}, u32[]{:S(2)}, u32[]{:S(2)}) collective-permute-start(bf16[2,3,32,512]{3,2,1,0:T(8,128)(2,1)S(1)} %get-tuple-element.9), channel_id=1, source_target_pairs={{0,2},{1,3},{4,0},{5,1},{8,4},{9,5},{12,8},{13,9},{14,12},{15,13},... | collective-permute-start | bytes 589832 | tf_op jit(solution)/shard_map/ppermute | solution.py:105
  6.1 42.5 %copy-start.23 = (f32[2,3,2,256]{3,2,1,0:T(2,128)S(1)}, f32[2,3,2,256]{3,2,1,0:T(2,128)}, u32[]{:S(2)}) copy-start(f32[2,3,2,256]{3,2,1,0:T(2,128)} %param.68) | copy-start | bytes 36868
  8.7 40.6 %copy-start.12 = (bf16[2,256,1024]{2,1,0:T(8,128)(2,1)S(1)}, bf16[2,256,1024]{2,1,0:T(8,128)(2,1)}, u32[]{:S(2)}) copy-start(bf16[2,256,1024]{2,1,0:T(8,128)(2,1)} %param.66) | copy-start | bytes 3145732
  26.9 6.4 %collective-permute-start.2 = (bf16[2,3,32,512]{3,2,1,0:T(8,128)(2,1)S(1)}, bf16[2,3,32,512]{3,2,1,0:T(8,128)(2,1)S(1)}, u32[]{:S(2)}, u32[]{:S(2)}) collective-permute-start(bf16[2,3,32,512]{3,2,1,0:T(8,128)(2,1)S(1)} %collective-permute-done), channel_id=1, source_target_pairs={{0,4},{1,5},{4,8},{5,9},{8,12},{9,13},{12,14},{13,15},{14,10},{15,... | collective-permute-start | bytes 589832 | tf_op jit(solution)/shard_map/ppermute | solution.py:102
  29.0 6.1 %collective-permute-start.3 = (bf16[2,3,32,512]{3,2,1,0:T(8,128)(2,1)S(1)}, bf16[2,3,32,512]{3,2,1,0:T(8,128)(2,1)S(1)}, u32[]{:S(2)}, u32[]{:S(2)}) collective-permute-start(bf16[2,3,32,512]{3,2,1,0:T(8,128)(2,1)S(1)} %collective-permute-done.1), channel_id=1, source_target_pairs={{0,2},{1,3},{4,0},{5,1},{8,4},{9,5},{12,8},{13,9},{14,12},{15,13},... | collective-permute-start | bytes 589832 | tf_op jit(solution)/shard_map/ppermute | solution.py:105
  33.4 5.7 %collective-permute-start.4 = (bf16[2,3,32,512]{3,2,1,0:T(8,128)(2,1)S(1)}, bf16[2,3,32,512]{3,2,1,0:T(8,128)(2,1)S(1)}, u32[]{:S(2)}, u32[]{:S(2)}) collective-permute-start(bf16[2,3,32,512]{3,2,1,0:T(8,128)(2,1)S(1)} %collective-permute-done.2), channel_id=1, source_target_pairs={{0,4},{1,5},{4,8},{5,9},{8,12},{9,13},{12,14},{13,15},{14,10},{15,... | collective-permute-start | bytes 589832 | tf_op jit(solution)/shard_map/ppermute | solution.py:102
  35.1 5.8 %collective-permute-start.5 = (bf16[2,3,32,512]{3,2,1,0:T(8,128)(2,1)S(1)}, bf16[2,3,32,512]{3,2,1,0:T(8,128)(2,1)S(1)}, u32[]{:S(2)}, u32[]{:S(2)}) collective-permute-start(bf16[2,3,32,512]{3,2,1,0:T(8,128)(2,1)S(1)} %collective-permute-done.3), channel_id=1, source_target_pairs={{0,2},{1,3},{4,0},{5,1},{8,4},{9,5},{12,8},{13,9},{14,12},{15,13},... | collective-permute-start | bytes 589832 | tf_op jit(solution)/shard_map/ppermute | solution.py:105
  39.0 5.7 %collective-permute-start.6 = (bf16[2,3,32,512]{3,2,1,0:T(8,128)(2,1)S(1)}, bf16[2,3,32,512]{3,2,1,0:T(8,128)(2,1)S(1)}, u32[]{:S(2)}, u32[]{:S(2)}) collective-permute-start(bf16[2,3,32,512]{3,2,1,0:T(8,128)(2,1)S(1)} %collective-permute-done.4), channel_id=1, source_target_pairs={{0,4},{1,5},{4,8},{5,9},{8,12},{9,13},{12,14},{13,15},{14,10},{15,... | collective-permute-start | bytes 589832 | tf_op jit(solution)/shard_map/ppermute | solution.py:102
  44.7 6.6 %collective-permute-start.7 = (bf16[8,2,3,32,512]{4,3,0,2,1:T(8,128)(2,1)S(1)}, bf16[8,2,3,32,512]{4,3,0,2,1:T(8,128)(2,1)}, u32[]{:S(2)}, u32[]{:S(2)}) collective-permute-start(bf16[8,2,3,32,512]{4,3,0,2,1:T(8,128)(2,1)S(1)} %bitcast_dynamic-update-slice_fusion.19), channel_id=1, source_target_pairs={{0,1},{1,0},{2,3},{3,2},{4,5},{5,4},{6,7},{7,6},{8,9},{9,8},{10,11... | collective-permute-start | bytes 4718600 | tf_op jit(solution)/shard_map/ppermute | solution.py:107
  59.3 1.9 %collective-permute-start.17 = (f32[2,3,1,1,32,512]{5,4,1,0,3,2:T(8,128)S(1)}, f32[2,3,1,1,32,512]{5,4,1,0,3,2:T(8,128)S(1)}, u32[]{:S(2)}, u32[]{:S(2)}) collective-permute-start(f32[2,3,1,1,32,512]{5,4,1,0,3,2:T(8,128)S(1)} %get-tuple-element.27), channel_id=1, source_target_pairs={{0,1},{1,0},{2,3},{3,2},{4,5},{5,4},{6,7},{7,6},{8,9},{9,8},{10,11... | collective-permute-start | bytes 1179656 | tf_op jit(solution)/shard_map/ppermute | solution.py:124
  59.9 1.9 %collective-permute-start.9 = (f32[2,3,1,1,32,512]{5,4,1,0,3,2:T(8,128)S(1)}, f32[2,3,1,1,32,512]{5,4,1,0,3,2:T(8,128)S(1)}, u32[]{:S(2)}, u32[]{:S(2)}) collective-permute-start(f32[2,3,1,1,32,512]{5,4,1,0,3,2:T(8,128)S(1)} %get-tuple-element.31), channel_id=1, source_target_pairs={{0,1},{1,0},{2,3},{3,2},{4,5},{5,4},{6,7},{7,6},{8,9},{9,8},{10,11... | collective-permute-start | bytes 1179656 | tf_op jit(solution)/shard_map/ppermute | solution.py:124
  60.0 4.5 %collective-permute-start.11 = (f32[2,3,1,1,32,512]{5,4,1,0,3,2:T(8,128)S(1)}, f32[2,3,1,1,32,512]{5,4,1,0,3,2:T(8,128)S(1)}, u32[]{:S(2)}, u32[]{:S(2)}) collective-permute-start(f32[2,3,1,1,32,512]{5,4,1,0,3,2:T(8,128)S(1)} %get-tuple-element.30), channel_id=1, source_target_pairs={{0,1},{1,0},{2,3},{3,2},{4,5},{5,4},{6,7},{7,6},{8,9},{9,8},{10,11... | collective-permute-start | bytes 1179656 | tf_op jit(solution)/shard_map/ppermute | solution.py:124
  61.9 7.3 %collective-permute-start.10 = (bf16[2,3,32,512]{3,2,1,0:T(8,128)(2,1)S(1)}, bf16[2,3,32,512]{3,2,1,0:T(8,128)(2,1)S(1)}, u32[]{:S(2)}, u32[]{:S(2)}) collective-permute-start(bf16[2,3,32,512]{3,2,1,0:T(8,128)(2,1)S(1)} %get-tuple-element.36), channel_id=1, source_target_pairs={{0,4},{1,5},{4,8},{5,9},{8,12},{9,13},{12,14},{13,15},{14,10},{15,... | collective-permute-start | bytes 589832 | tf_op jit(solution)/shard_map/ppermute | solution.py:132
  63.8 7.3 %collective-permute-start.19 = (f32[2,3,1,1,32,512]{5,4,1,0,3,2:T(8,128)S(1)}, f32[2,3,1,1,32,512]{5,4,1,0,3,2:T(8,128)S(1)}, u32[]{:S(2)}, u32[]{:S(2)}) collective-permute-start(f32[2,3,1,1,32,512]{5,4,1,0,3,2:T(8,128)S(1)} %get-tuple-element.26), channel_id=1, source_target_pairs={{0,1},{1,0},{2,3},{3,2},{4,5},{5,4},{6,7},{7,6},{8,9},{9,8},{10,11... | collective-permute-start | bytes 1179656 | tf_op jit(solution)/shard_map/ppermute | solution.py:124
  63.9 7.8 %collective-permute-start.13 = (f32[2,3,1,1,32,512]{5,4,1,0,3,2:T(8,128)S(1)}, f32[2,3,1,1,32,512]{5,4,1,0,3,2:T(8,128)S(1)}, u32[]{:S(2)}, u32[]{:S(2)}) collective-permute-start(f32[2,3,1,1,32,512]{5,4,1,0,3,2:T(8,128)S(1)} %get-tuple-element.29), channel_id=1, source_target_pairs={{0,1},{1,0},{2,3},{3,2},{4,5},{5,4},{6,7},{7,6},{8,9},{9,8},{10,11... | collective-permute-start | bytes 1179656 | tf_op jit(solution)/shard_map/ppermute | solution.py:124
  64.4 7.3 %collective-permute-start.18 = (bf16[2,3,32,512]{3,2,1,0:T(8,128)(2,1)S(1)}, bf16[2,3,32,512]{3,2,1,0:T(8,128)(2,1)S(1)}, u32[]{:S(2)}, u32[]{:S(2)}) collective-permute-start(bf16[2,3,32,512]{3,2,1,0:T(8,128)(2,1)S(1)} %get-tuple-element.37), channel_id=1, source_target_pairs={{0,2},{1,3},{4,0},{5,1},{8,4},{9,5},{12,8},{13,9},{14,12},{15,13},... | collective-permute-start | bytes 589832 | tf_op jit(solution)/shard_map/ppermute | solution.py:136
  69.3 6.4 %collective-permute-start.12 = (bf16[2,3,32,512]{3,2,1,0:T(8,128)(2,1)S(1)}, bf16[2,3,32,512]{3,2,1,0:T(8,128)(2,1)S(1)}, u32[]{:S(2)}, u32[]{:S(2)}) collective-permute-start(bf16[2,3,32,512]{3,2,1,0:T(8,128)(2,1)S(1)} %fusion.47), channel_id=1, source_target_pairs={{0,4},{1,5},{4,8},{5,9},{8,12},{9,13},{12,14},{13,15},{14,10},{15,... | collective-permute-start | bytes 589832 | tf_op jit(solution)/shard_map/ppermute | solution.py:132
  71.2 7.8 %collective-permute-start.21 = (f32[2,3,1,1,32,512]{5,4,1,0,3,2:T(8,128)S(1)}, f32[2,3,1,1,32,512]{5,4,1,0,3,2:T(8,128)S(1)}, u32[]{:S(2)}, u32[]{:S(2)}) collective-permute-start(f32[2,3,1,1,32,512]{5,4,1,0,3,2:T(8,128)S(1)} %get-tuple-element.25), channel_id=1, source_target_pairs={{0,1},{1,0},{2,3},{3,2},{4,5},{5,4},{6,7},{7,6},{8,9},{9,8},{10,11... | collective-permute-start | bytes 1179656 | tf_op jit(solution)/shard_map/ppermute | solution.py:124
  71.2 7.8 %collective-permute-start.15 = (f32[2,3,1,1,32,512]{5,4,1,0,3,2:T(8,128)S(1)}, f32[2,3,1,1,32,512]{5,4,1,0,3,2:T(8,128)S(1)}, u32[]{:S(2)}, u32[]{:S(2)}) collective-permute-start(f32[2,3,1,1,32,512]{5,4,1,0,3,2:T(8,128)S(1)} %get-tuple-element.28), channel_id=1, source_target_pairs={{0,1},{1,0},{2,3},{3,2},{4,5},{5,4},{6,7},{7,6},{8,9},{9,8},{10,11... | collective-permute-start | bytes 1179656 | tf_op jit(solution)/shard_map/ppermute | solution.py:124
  76.0 5.7 %collective-permute-start.14 = (bf16[2,3,32,512]{3,2,1,0:T(8,128)(2,1)S(1)}, bf16[2,3,32,512]{3,2,1,0:T(8,128)(2,1)S(1)}, u32[]{:S(2)}, u32[]{:S(2)}) collective-permute-start(bf16[2,3,32,512]{3,2,1,0:T(8,128)(2,1)S(1)} %get-tuple-element.34), channel_id=1, source_target_pairs={{0,4},{1,5},{4,8},{5,9},{8,12},{9,13},{12,14},{13,15},{14,10},{15,... | collective-permute-start | bytes 589832 | tf_op jit(solution)/shard_map/ppermute | solution.py:132
  77.8 5.7 %collective-permute-start.20 = (bf16[2,3,32,512]{3,2,1,0:T(8,128)(2,1)S(1)}, bf16[2,3,32,512]{3,2,1,0:T(8,128)(2,1)S(1)}, u32[]{:S(2)}, u32[]{:S(2)}) collective-permute-start(bf16[2,3,32,512]{3,2,1,0:T(8,128)(2,1)S(1)} %get-tuple-element.35), channel_id=1, source_target_pairs={{0,2},{1,3},{4,0},{5,1},{8,4},{9,5},{12,8},{13,9},{14,12},{15,13},... | collective-permute-start | bytes 589832 | tf_op jit(solution)/shard_map/ppermute | solution.py:136
  78.9 7.9 %collective-permute-start.8 = (f32[2,3,1,1,32,512]{5,4,1,0,3,2:T(8,128)S(1)}, f32[2,3,1,1,32,512]{5,4,1,0,3,2:T(8,128)S(1)}, u32[]{:S(2)}, u32[]{:S(2)}) collective-permute-start(f32[2,3,1,1,32,512]{5,4,1,0,3,2:T(8,128)S(1)} %get-tuple-element.24), channel_id=1, source_target_pairs={{0,1},{1,0},{2,3},{3,2},{4,5},{5,4},{6,7},{7,6},{8,9},{9,8},{10,11... | collective-permute-start | bytes 1179656 | tf_op jit(solution)/shard_map/ppermute | solution.py:124
  83.6 5.7 %collective-permute-start.16 = (bf16[2,3,32,512]{3,2,1,0:T(8,128)(2,1)S(1)}, bf16[2,3,32,512]{3,2,1,0:T(8,128)(2,1)S(1)}, u32[]{:S(2)}, u32[]{:S(2)}) collective-permute-start(bf16[2,3,32,512]{3,2,1,0:T(8,128)(2,1)S(1)} %get-tuple-element.32), channel_id=1, source_target_pairs={{0,4},{1,5},{4,8},{5,9},{8,12},{9,13},{12,14},{13,15},{14,10},{15,... | collective-permute-start | bytes 589832 | tf_op jit(solution)/shard_map/ppermute | solution.py:132
  85.3 5.7 %collective-permute-start.22 = (bf16[2,3,32,512]{3,2,1,0:T(8,128)(2,1)S(1)}, bf16[2,3,32,512]{3,2,1,0:T(8,128)(2,1)S(1)}, u32[]{:S(2)}, u32[]{:S(2)}) collective-permute-start(bf16[2,3,32,512]{3,2,1,0:T(8,128)(2,1)S(1)} %get-tuple-element.33), channel_id=1, source_target_pairs={{0,2},{1,3},{4,0},{5,1},{8,4},{9,5},{12,8},{13,9},{14,12},{15,13},... | collective-permute-start | bytes 589832 | tf_op jit(solution)/shard_map/ppermute | solution.py:136
  92.2 7.9 %collective-permute-start.23 = (bf16[2,3,32,512]{3,2,1,0:T(8,128)(2,1)}, bf16[2,3,32,512]{3,2,1,0:T(8,128)(2,1)}, u32[]{:S(2)}, u32[]{:S(2)}) collective-permute-start(bf16[2,3,32,512]{3,2,1,0:T(8,128)(2,1)} %get-tuple-element.5), channel_id=1, source_target_pairs={{0,4},{1,5},{4,8},{5,9},{8,12},{9,13},{12,14},{13,15},{14,10},{15,... | collective-permute-start | bytes 589832 | tf_op jit(solution)/shard_map/ppermute | solution.py:102
  97.3 7.8 %collective-permute-start.24 = (bf16[2,3,32,512]{3,2,1,0:T(8,128)(2,1)}, bf16[2,3,32,512]{3,2,1,0:T(8,128)(2,1)S(1)}, u32[]{:S(2)}, u32[]{:S(2)}) collective-permute-start(bf16[2,3,32,512]{3,2,1,0:T(8,128)(2,1)} %get-tuple-element.5), channel_id=1, source_target_pairs={{0,2},{1,3},{4,0},{5,1},{8,4},{9,5},{12,8},{13,9},{14,12},{15,13},... | collective-permute-start | bytes 589832 | tf_op jit(solution)/shard_map/ppermute | solution.py:105
  100.0 6.9 %collective-permute-start.25 = (bf16[2,3,32,512]{3,2,1,0:T(8,128)(2,1)}, bf16[2,3,32,512]{3,2,1,0:T(8,128)(2,1)S(1)}, u32[]{:S(2)}, u32[]{:S(2)}) collective-permute-start(bf16[2,3,32,512]{3,2,1,0:T(8,128)(2,1)} %collective-permute-done.23), channel_id=1, source_target_pairs={{0,4},{1,5},{4,8},{5,9},{8,12},{9,13},{12,14},{13,15},{14,10},{15,... | collective-permute-start | bytes 589832 | tf_op jit(solution)/shard_map/ppermute | solution.py:102
  105.1 6.7 %collective-permute-start.26 = (bf16[2,3,32,512]{3,2,1,0:T(8,128)(2,1)S(1)}, bf16[2,3,32,512]{3,2,1,0:T(8,128)(2,1)S(1)}, u32[]{:S(2)}, u32[]{:S(2)}) collective-permute-start(bf16[2,3,32,512]{3,2,1,0:T(8,128)(2,1)S(1)} %collective-permute-done.24), channel_id=1, source_target_pairs={{0,2},{1,3},{4,0},{5,1},{8,4},{9,5},{12,8},{13,9},{14,12},{15,13},... | collective-permute-start | bytes 589832 | tf_op jit(solution)/shard_map/ppermute | solution.py:105
  107.0 5.9 %collective-permute-start.27 = (bf16[2,3,32,512]{3,2,1,0:T(8,128)(2,1)S(1)}, bf16[2,3,32,512]{3,2,1,0:T(8,128)(2,1)S(1)}, u32[]{:S(2)}, u32[]{:S(2)}) collective-permute-start(bf16[2,3,32,512]{3,2,1,0:T(8,128)(2,1)S(1)} %collective-permute-done.25), channel_id=1, source_target_pairs={{0,4},{1,5},{4,8},{5,9},{8,12},{9,13},{12,14},{13,15},{14,10},{15,... | collective-permute-start | bytes 589832 | tf_op jit(solution)/shard_map/ppermute | solution.py:102
  111.8 5.7 %collective-permute-start.28 = (bf16[2,3,32,512]{3,2,1,0:T(8,128)(2,1)S(1)}, bf16[2,3,32,512]{3,2,1,0:T(8,128)(2,1)S(1)}, u32[]{:S(2)}, u32[]{:S(2)}) collective-permute-start(bf16[2,3,32,512]{3,2,1,0:T(8,128)(2,1)S(1)} %collective-permute-done.26), channel_id=1, source_target_pairs={{0,2},{1,3},{4,0},{5,1},{8,4},{9,5},{12,8},{13,9},{14,12},{15,13},... | collective-permute-start | bytes 589832 | tf_op jit(solution)/shard_map/ppermute | solution.py:105
  112.8 5.7 %collective-permute-start.29 = (bf16[2,3,32,512]{3,2,1,0:T(8,128)(2,1)S(1)}, bf16[2,3,32,512]{3,2,1,0:T(8,128)(2,1)S(1)}, u32[]{:S(2)}, u32[]{:S(2)}) collective-permute-start(bf16[2,3,32,512]{3,2,1,0:T(8,128)(2,1)S(1)} %collective-permute-done.27), channel_id=1, source_target_pairs={{0,4},{1,5},{4,8},{5,9},{8,12},{9,13},{12,14},{13,15},{14,10},{15,... | collective-permute-start | bytes 589832 | tf_op jit(solution)/shard_map/ppermute | solution.py:102
  118.5 7.0 %collective-permute-start.30 = (bf16[8,2,3,32,512]{4,3,0,2,1:T(8,128)(2,1)S(1)}, bf16[8,2,3,32,512]{4,3,0,2,1:T(8,128)(2,1)}, u32[]{:S(2)}, u32[]{:S(2)}) collective-permute-start(bf16[8,2,3,32,512]{4,3,0,2,1:T(8,128)(2,1)S(1)} %bitcast_dynamic-update-slice_fusion.18), channel_id=1, source_target_pairs={{0,1},{1,0},{2,3},{3,2},{4,5},{5,4},{6,7},{7,6},{8,9},{9,8},{10,11... | collective-permute-start | bytes 4718600 | tf_op jit(solution)/shard_map/ppermute | solution.py:107
  145.7 2.5 %collective-permute-start.40 = (f32[2,3,1,1,32,512]{5,4,1,0,3,2:T(8,128)}, f32[2,3,1,1,32,512]{5,4,1,0,3,2:T(8,128)}, u32[]{:S(2)}, u32[]{:S(2)}) collective-permute-start(f32[2,3,1,1,32,512]{5,4,1,0,3,2:T(8,128)} %get-tuple-element.13), channel_id=1, source_target_pairs={{0,1},{1,0},{2,3},{3,2},{4,5},{5,4},{6,7},{7,6},{8,9},{9,8},{10,11... | collective-permute-start | bytes 1179656 | tf_op jit(solution)/shard_map/ppermute | solution.py:124
  146.2 2.3 %collective-permute-start.32 = (f32[2,3,1,1,32,512]{5,4,1,0,3,2:T(8,128)}, f32[2,3,1,1,32,512]{5,4,1,0,3,2:T(8,128)}, u32[]{:S(2)}, u32[]{:S(2)}) collective-permute-start(f32[2,3,1,1,32,512]{5,4,1,0,3,2:T(8,128)} %get-tuple-element.17), channel_id=1, source_target_pairs={{0,1},{1,0},{2,3},{3,2},{4,5},{5,4},{6,7},{7,6},{8,9},{9,8},{10,11... | collective-permute-start | bytes 1179656 | tf_op jit(solution)/shard_map/ppermute | solution.py:124
  146.2 31.7 %collective-permute-start.31 = (f32[2,3,1,1,32,512]{5,4,1,0,3,2:T(8,128)}, f32[2,3,1,1,32,512]{5,4,1,0,3,2:T(8,128)S(1)}, u32[]{:S(2)}, u32[]{:S(2)}) collective-permute-start(f32[2,3,1,1,32,512]{5,4,1,0,3,2:T(8,128)} %get-tuple-element.10), channel_id=1, source_target_pairs={{0,1},{1,0},{2,3},{3,2},{4,5},{5,4},{6,7},{7,6},{8,9},{9,8},{10,11... | collective-permute-start | bytes 1179656 | tf_op jit(solution)/shard_map/ppermute | solution.py:124
  146.8 13.1 %collective-permute-start.42 = (f32[2,3,1,1,32,512]{5,4,1,0,3,2:T(8,128)}, f32[2,3,1,1,32,512]{5,4,1,0,3,2:T(8,128)}, u32[]{:S(2)}, u32[]{:S(2)}) collective-permute-start(f32[2,3,1,1,32,512]{5,4,1,0,3,2:T(8,128)} %get-tuple-element.12), channel_id=1, source_target_pairs={{0,1},{1,0},{2,3},{3,2},{4,5},{5,4},{6,7},{7,6},{8,9},{9,8},{10,11... | collective-permute-start | bytes 1179656 | tf_op jit(solution)/shard_map/ppermute | solution.py:124
  146.9 13.1 %collective-permute-start.36 = (f32[2,3,1,1,32,512]{5,4,1,0,3,2:T(8,128)}, f32[2,3,1,1,32,512]{5,4,1,0,3,2:T(8,128)}, u32[]{:S(2)}, u32[]{:S(2)}) collective-permute-start(f32[2,3,1,1,32,512]{5,4,1,0,3,2:T(8,128)} %get-tuple-element.15), channel_id=1, source_target_pairs={{0,1},{1,0},{2,3},{3,2},{4,5},{5,4},{6,7},{7,6},{8,9},{9,8},{10,11... | collective-permute-start | bytes 1179656 | tf_op jit(solution)/shard_map/ppermute | solution.py:124
  148.2 3.5 %collective-permute-start.34 = (f32[2,3,1,1,32,512]{5,4,1,0,3,2:T(8,128)}, f32[2,3,1,1,32,512]{5,4,1,0,3,2:T(8,128)S(1)}, u32[]{:S(2)}, u32[]{:S(2)}) collective-permute-start(f32[2,3,1,1,32,512]{5,4,1,0,3,2:T(8,128)} %get-tuple-element.16), channel_id=1, source_target_pairs={{0,1},{1,0},{2,3},{3,2},{4,5},{5,4},{6,7},{7,6},{8,9},{9,8},{10,11... | collective-permute-start | bytes 1179656 | tf_op jit(solution)/shard_map/ppermute | solution.py:124
  150.0 7.1 %collective-permute-start.33 = (bf16[2,3,32,512]{3,2,1,0:T(8,128)(2,1)S(1)}, bf16[2,3,32,512]{3,2,1,0:T(8,128)(2,1)S(1)}, u32[]{:S(2)}, u32[]{:S(2)}) collective-permute-start(bf16[2,3,32,512]{3,2,1,0:T(8,128)(2,1)S(1)} %get-tuple-element.22), channel_id=1, source_target_pairs={{0,4},{1,5},{4,8},{5,9},{8,12},{9,13},{12,14},{13,15},{14,10},{15,... | collective-permute-start | bytes 589832 | tf_op jit(solution)/shard_map/ppermute | solution.py:132
  151.8 8.7 %collective-permute-start.41 = (bf16[2,3,32,512]{3,2,1,0:T(8,128)(2,1)S(1)}, bf16[2,3,32,512]{3,2,1,0:T(8,128)(2,1)S(1)}, u32[]{:S(2)}, u32[]{:S(2)}) collective-permute-start(bf16[2,3,32,512]{3,2,1,0:T(8,128)(2,1)S(1)} %get-tuple-element.23), channel_id=1, source_target_pairs={{0,2},{1,3},{4,0},{5,1},{8,4},{9,5},{12,8},{13,9},{14,12},{15,13},... | collective-permute-start | bytes 589832 | tf_op jit(solution)/shard_map/ppermute | solution.py:136
  158.3 6.3 %collective-permute-start.35 = (bf16[2,3,32,512]{3,2,1,0:T(8,128)(2,1)S(1)}, bf16[2,3,32,512]{3,2,1,0:T(8,128)(2,1)S(1)}, u32[]{:S(2)}, u32[]{:S(2)}) collective-permute-start(bf16[2,3,32,512]{3,2,1,0:T(8,128)(2,1)S(1)} %fusion.40), channel_id=1, source_target_pairs={{0,4},{1,5},{4,8},{5,9},{8,12},{9,13},{12,14},{13,15},{14,10},{15,... | collective-permute-start | bytes 589832 | tf_op jit(solution)/shard_map/ppermute | solution.py:132
  159.9 8.4 %collective-permute-start.44 = (f32[2,3,1,1,32,512]{5,4,1,0,3,2:T(8,128)S(1)}, f32[2,3,1,1,32,512]{5,4,1,0,3,2:T(8,128)S(1)}, u32[]{:S(2)}, u32[]{:S(2)}) collective-permute-start(f32[2,3,1,1,32,512]{5,4,1,0,3,2:T(8,128)S(1)} %copy-done.21), channel_id=1, source_target_pairs={{0,1},{1,0},{2,3},{3,2},{4,5},{5,4},{6,7},{7,6},{8,9},{9,8},{10,11... | collective-permute-start | bytes 1179656 | tf_op jit(solution)/shard_map/ppermute | solution.py:124
  160.0 8.3 %collective-permute-start.38 = (f32[2,3,1,1,32,512]{5,4,1,0,3,2:T(8,128)S(1)}, f32[2,3,1,1,32,512]{5,4,1,0,3,2:T(8,128)S(1)}, u32[]{:S(2)}, u32[]{:S(2)}) collective-permute-start(f32[2,3,1,1,32,512]{5,4,1,0,3,2:T(8,128)S(1)} %copy-done.20), channel_id=1, source_target_pairs={{0,1},{1,0},{2,3},{3,2},{4,5},{5,4},{6,7},{7,6},{8,9},{9,8},{10,11... | collective-permute-start | bytes 1179656 | tf_op jit(solution)/shard_map/ppermute | solution.py:124
  166.1 5.7 %collective-permute-start.37 = (bf16[2,3,32,512]{3,2,1,0:T(8,128)(2,1)S(1)}, bf16[2,3,32,512]{3,2,1,0:T(8,128)(2,1)S(1)}, u32[]{:S(2)}, u32[]{:S(2)}) collective-permute-start(bf16[2,3,32,512]{3,2,1,0:T(8,128)(2,1)S(1)} %get-tuple-element.20), channel_id=1, source_target_pairs={{0,4},{1,5},{4,8},{5,9},{8,12},{9,13},{12,14},{13,15},{14,10},{15,... | collective-permute-start | bytes 589832 | tf_op jit(solution)/shard_map/ppermute | solution.py:132
  167.7 5.7 %collective-permute-start.43 = (bf16[2,3,32,512]{3,2,1,0:T(8,128)(2,1)S(1)}, bf16[2,3,32,512]{3,2,1,0:T(8,128)(2,1)S(1)}, u32[]{:S(2)}, u32[]{:S(2)}) collective-permute-start(bf16[2,3,32,512]{3,2,1,0:T(8,128)(2,1)S(1)} %get-tuple-element.21), channel_id=1, source_target_pairs={{0,2},{1,3},{4,0},{5,1},{8,4},{9,5},{12,8},{13,9},{14,12},{15,13},... | collective-permute-start | bytes 589832 | tf_op jit(solution)/shard_map/ppermute | solution.py:136
  174.7 5.7 %collective-permute-start.39 = (bf16[2,3,32,512]{3,2,1,0:T(8,128)(2,1)S(1)}, bf16[2,3,32,512]{3,2,1,0:T(8,128)(2,1)S(1)}, u32[]{:S(2)}, u32[]{:S(2)}) collective-permute-start(bf16[2,3,32,512]{3,2,1,0:T(8,128)(2,1)S(1)} %get-tuple-element.18), channel_id=1, source_target_pairs={{0,4},{1,5},{4,8},{5,9},{8,12},{9,13},{12,14},{13,15},{14,10},{15,... | collective-permute-start | bytes 589832 | tf_op jit(solution)/shard_map/ppermute | solution.py:132
  176.5 5.7 %collective-permute-start.45 = (bf16[2,3,32,512]{3,2,1,0:T(8,128)(2,1)S(1)}, bf16[2,3,32,512]{3,2,1,0:T(8,128)(2,1)S(1)}, u32[]{:S(2)}, u32[]{:S(2)}) collective-permute-start(bf16[2,3,32,512]{3,2,1,0:T(8,128)(2,1)S(1)} %get-tuple-element.19), channel_id=1, source_target_pairs={{0,2},{1,3},{4,0},{5,1},{8,4},{9,5},{12,8},{13,9},{14,12},{15,13},... | collective-permute-start | bytes 589832 | tf_op jit(solution)/shard_map/ppermute | solution.py:136
  (29 other events, 167.2 us)

commit v5 on v4

--- a/solution.py
+++ b/solution.py
@@ -1,6 +1,8 @@
 import jax
 import jax.numpy as jnp
 from jax import lax
+from jax.experimental import pallas as pl
+from jax.experimental.pallas import tpu as pltpu
 from jax.sharding import PartitionSpec as P
 
 
@@ -59,6 +61,59 @@
         pieces.append(normed)
         grads.append(grad)
     return (jnp.concatenate(pieces, axis=1), jnp.stack(grads))
+
+
+def _nt(left, right):
+    return lax.dot_general(left, right, (((1,), (1,)), ((), ())), preferred_element_type=jnp.float32)
+
+
+def _tn(left, right):
+    return lax.dot_general(left, right, (((0,), (0,)), ((), ())), preferred_element_type=jnp.float32)
+
+
+def _block_kernel(q_ref, k_ref, v_ref, r_ref, w_ref, o_ref, g_ref):
+    heads = w_ref.shape[0]
+    width = w_ref.shape[3]
+    for head in range(heads):
+        lo = head * width
+        query = q_ref[:, lo : lo + width]
+        key_rows = k_ref[:, lo : lo + width]
+        value_rows = v_ref[:, lo : lo + width]
+        gate = w_ref[head, 0]
+        up = w_ref[head, 1]
+        down = w_ref[head, 2]
+        a1 = _nt(query, gate)
+        a3 = _nt(query, up)
+        hidden_q = (a1 / (1.0 + jnp.exp(-a1)) * a3).astype(jnp.bfloat16)
+        raw = _nt(hidden_q, down)
+        scale = jnp.sqrt(jnp.mean(raw * raw, axis=-1, keepdims=True) + 1e-06)
+        o_ref[:, lo : lo + width] = (raw / scale).astype(jnp.bfloat16)
+        h1 = _nt(key_rows, gate)
+        h3 = _nt(key_rows, up)
+        sig = 1.0 / (1.0 + jnp.exp(-h1))
+        act = h1 * sig
+        back = jnp.dot(value_rows, down, preferred_element_type=jnp.float32)
+        d1 = back * h3 * sig * (1.0 + h1 * (1.0 - sig))
+        d3 = back * act
+        e1 = (r_ref[:, head : head + 1] * d1).astype(jnp.bfloat16)
+        e3 = (r_ref[:, heads + head : heads + head + 1] * d3).astype(jnp.bfloat16)
+        b2 = (r_ref[:, 2 * heads + head : 2 * heads + head + 1] * (act * h3)).astype(jnp.bfloat16)
+        g_ref[head, 0] = _tn(e1, key_rows)
+        g_ref[head, 1] = _tn(e3, key_rows)
+        g_ref[head, 2] = _tn(value_rows, b2)
+
+
+def fused_block(query, key_rows, value_rows, rate_rows, wbf):
+    tokens = query.shape[0]
+    rates_t = rate_rows.reshape(-1, tokens).T
+    return pl.pallas_call(
+        _block_kernel,
+        out_shape=(
+            jax.ShapeDtypeStruct(query.shape, jnp.bfloat16),
+            jax.ShapeDtypeStruct(wbf.shape, jnp.float32),
+        ),
+        compiler_params=pltpu.CompilerParams(vmem_limit_bytes=48 * 1024 * 1024),
+    )(query, key_rows, value_rows, rates_t, wbf)
 
 
 class Ring:
@@ -152,7 +207,7 @@
         blocks = []
         for span in range(nblocks):
             gathered = ring.gather(own.astype(jnp.bfloat16))
-            normed, partial_value = block_step(span, gathered, queries, keys, values, rates)
+            normed, partial_value = fused_block(queries[span], keys[span], values[span], rates[span], gathered)
             blocks.append(normed)
             own = renorm(own, own + ring.reduce(partial_value))
         return (jnp.stack(blocks), own)

time: 185 us -> 168 us (0.908)
  matrix products: 26.7 us -> 0 us
  Pallas kernels: 0 us -> 12.6 us
  other arithmetic: 15.1 us -> 4.51 us
  local copies, waits for them, and re-layouts: 16.5 us -> 21.5 us
  waiting for transfers between devices: 62.7 us -> 66.9 us
    dot_general x32 -> x0, matrix products: 26.7 us -> none  [the longest x16 20.4 us: cross(): lax.dot_general(left, right, (((1,), (1,)), ((), ())), preferred_element_...]
    pallas_call x0 -> x2, Pallas kernels: none -> 12.6 us  [fused_block(): pl.pallas_call(_block_kernel, out_shape=(jax.ShapeDtypeStruct(query.shape...]
    ppermute x6, waiting for transfers between devices: 8.77 us -> 0.02 us  [gather(): b = lax.ppermute(b, 'tok', self.ccw)]
    ppermute x8, waiting for transfers between devices: 16.8 us -> 25.1 us  [gather(): a = lax.ppermute(a, 'tok', self.cw)]
    convert_element_type x8, other arithmetic: 6.19 us -> 1.26 us  [reduce(): a = lax.ppermute(a.astype(jnp.bfloat16), 'tok', self.cw).astype(jnp.float32)]
    unnamed x62 -> x22, local copies, waits for them, and re-layouts: 4.44 us -> 7.1 us
    another operation x2 -> x0, other arithmetic: 2.15 us -> none  [block_step(): return (jnp.concatenate(pieces, axis=1), jnp.stack(grads))]
    dynamic_slice x2 -> x0, local copies, waits for them, and re-layouts: 2.11 us -> none  [chip_sum(): lax.dynamic_slice(q, (0, 0, chip, 1 - core, 0, 0), (h, g, 1, 1, rows, f))]
  transfers between devices with their start and end apart: 46 -> 46, of which waited for: 25 -> 24; matrix products, arithmetic and copies ran while one was open for 14% -> 7% of each run, Pallas kernels for 0% -> 0%
where the time goes in v5:
time: 168 us
  waiting for transfers between devices  66.9 us (40%)
  starting transfers between devices  36.5 us (22%)
  between operations  25.7 us (15%)
  local copies, waits for them, and re-layouts  21.5 us (13%)
  Pallas kernels  12.6 us (8%)
  other arithmetic  4.51 us (3%)
    ppermute x8, waiting for transfers between devices, reduce(): a = lax.ppermute(a.astype(jnp.bfloat16), 'tok', self.cw).astype(jnp.float32)  30.7 us
    ppermute x8, waiting for transfers between devices, gather(): a = lax.ppermute(a, 'tok', self.cw)  25.1 us
    ppermute x8, starting transfers between devices, gather(): a = lax.ppermute(a, 'tok', self.cw)  14.9 us
    ppermute x8, starting transfers between devices, reduce(): a = lax.ppermute(a.astype(jnp.bfloat16), 'tok', self.cw).astype(jnp.float32)  13.5 us
    pallas_call x2, Pallas kernels, fused_block(): pl.pallas_call(_block_kernel, out_shape=(jax.ShapeDtypeStruct(query.shape...  12.6 us
    unnamed x22, local copies, waits for them, and re-layouts  7.1 us
    ppermute x6, waiting for transfers between devices, reduce(): lax.ppermute(b.astype(jnp.bfloat16), 'tok', self.ccw).astype(jnp.float32)  6.4 us
    ppermute x16, starting transfers between devices, chip_sum(): got = lax.ppermute(send, 'tok', self.swap)  3.84 us
  transfers between devices with their start and end apart: 46, of which 24 were waited for; matrix products, arithmetic and copies ran while one was open for 7% of the time, Pallas kernels for 0%

profile of v5, /device:TPU:0, one launch (start us, length us, event | category | flops | bytes accessed | tf_op | source)
XLA Modules:
  0.0 167.6 jit_solution(12414122394786207224)
XLA Ops:
  1.7 3.1 %collective-permute-start = (bf16[2,3,32,512]{3,2,1,0:T(8,128)(2,1)S(1)}, bf16[2,3,32,512]{3,2,1,0:T(8,128)(2,1)S(1)}, u32[]{:S(2)}, u32[]{:S(2)}) collective-permute-start(bf16[2,3,32,512]{3,2,1,0:T(8,128)(2,1)S(1)} %get-tuple-element.17), channel_id=1, source_target_pairs={{0,4},{1,5},{4,8},{5,9},{8,12},{9,13},{12,14},{13,15},{14,10},{15,... | collective-permute-start | bytes 589832 | tf_op jit(solution)/shard_map/ppermute | solution.py:157
  26.8 2.1 %collective-permute-start.2 = (bf16[2,3,32,512]{3,2,1,0:T(8,128)(2,1)S(1)}, bf16[2,3,32,512]{3,2,1,0:T(8,128)(2,1)S(1)}, u32[]{:S(2)}, u32[]{:S(2)}) collective-permute-start(bf16[2,3,32,512]{3,2,1,0:T(8,128)(2,1)S(1)} %collective-permute-done), channel_id=1, source_target_pairs={{0,4},{1,5},{4,8},{5,9},{8,12},{9,13},{12,14},{13,15},{14,10},{15,... | collective-permute-start | bytes 589832 | tf_op jit(solution)/shard_map/ppermute | solution.py:157
  28.9 4.3 %collective-permute-done.2 = bf16[2,3,32,512]{3,2,1,0:T(8,128)(2,1)S(1)} collective-permute-done((bf16[2,3,32,512]{3,2,1,0:T(8,128)(2,1)S(1)}, bf16[2,3,32,512]{3,2,1,0:T(8,128)(2,1)S(1)}, u32[]{:S(2)}, u32[]{:S(2)}) %collective-permute-start.2) | collective-permute-done | bytes 196640 | tf_op jit(solution)/shard_map/ppermute | solution.py:157
  33.2 1.7 %collective-permute-start.4 = (bf16[2,3,32,512]{3,2,1,0:T(8,128)(2,1)S(1)}, bf16[2,3,32,512]{3,2,1,0:T(8,128)(2,1)S(1)}, u32[]{:S(2)}, u32[]{:S(2)}) collective-permute-start(bf16[2,3,32,512]{3,2,1,0:T(8,128)(2,1)S(1)} %collective-permute-done.2), channel_id=1, source_target_pairs={{0,4},{1,5},{4,8},{5,9},{8,12},{9,13},{12,14},{13,15},{14,10},{15,... | collective-permute-start | bytes 589832 | tf_op jit(solution)/shard_map/ppermute | solution.py:157
  35.3 3.6 %collective-permute-done.4 = bf16[2,3,32,512]{3,2,1,0:T(8,128)(2,1)S(1)} collective-permute-done((bf16[2,3,32,512]{3,2,1,0:T(8,128)(2,1)S(1)}, bf16[2,3,32,512]{3,2,1,0:T(8,128)(2,1)S(1)}, u32[]{:S(2)}, u32[]{:S(2)}) %collective-permute-start.4) | collective-permute-done | bytes 196640 | tf_op jit(solution)/shard_map/ppermute | solution.py:157
  38.9 1.9 %collective-permute-start.6 = (bf16[2,3,32,512]{3,2,1,0:T(8,128)(2,1)S(1)}, bf16[2,3,32,512]{3,2,1,0:T(8,128)(2,1)S(1)}, u32[]{:S(2)}, u32[]{:S(2)}) collective-permute-start(bf16[2,3,32,512]{3,2,1,0:T(8,128)(2,1)S(1)} %collective-permute-done.4), channel_id=1, source_target_pairs={{0,4},{1,5},{4,8},{5,9},{8,12},{9,13},{12,14},{13,15},{14,10},{15,... | collective-permute-start | bytes 589832 | tf_op jit(solution)/shard_map/ppermute | solution.py:157
  40.8 3.7 %collective-permute-done.6 = bf16[2,3,32,512]{3,2,1,0:T(8,128)(2,1)S(1)} collective-permute-done((bf16[2,3,32,512]{3,2,1,0:T(8,128)(2,1)S(1)}, bf16[2,3,32,512]{3,2,1,0:T(8,128)(2,1)S(1)}, u32[]{:S(2)}, u32[]{:S(2)}) %collective-permute-start.6) | collective-permute-done | bytes 196640 | tf_op jit(solution)/shard_map/ppermute | solution.py:157
  49.0 1.1 copy-done.5
  51.2 1.6 bitcast_dynamic-update-slice_fusion.1
  52.9 6.3 %shard_map.608 = (bf16[256,1024]{1,0:T(8,128)(2,1)S(1)}, f32[2,3,512,512]{3,2,1,0:T(8,128)}) custom-call(bf16[256,1024]{1,0:T(8,128)(2,1)S(1)} %get-tuple-element.50.q_ref, bf16[256,1024]{1,0:T(8,128)(2,1)S(1)} %get-tuple-element.66.k_ref, bf16[256,1024]{1,0:T(8,128)(2,1)S(1)} %get-tuple-element.46.v_ref, f32[256,6]{1,0:T(8,128)S(1)} %bitcast.366, ...), custom_call_target="tpu_custom_call" | custom-call | tf_op jit(solution)/shard_map/pallas_call | solution.py:109
  59.2 2.3 %dynamic-slice_bitcast_fusion.15 = (f32[2,3,1,1,32,512]{5,4,1,0,3,2:T(8,128)S(1)}, f32[2,3,1,1,32,512]{5,4,1,0,3,2:T(8,128)S(1)}, f32[2,3,1,1,32,512]{5,4,1,0,3,...) fusion(f32[2,3,8,2,32,512]{5,4,3,2,1,0:T(8,128)} %bitcast.376, ...), kind=kLoop, calls=%fused_computation.88 | loop fusion | bytes 6291492
  64.1 1.9 %collective-permute-start.10 = (bf16[2,3,32,512]{3,2,1,0:T(8,128)(2,1)S(1)}, bf16[2,3,32,512]{3,2,1,0:T(8,128)(2,1)S(1)}, u32[]{:S(2)}, u32[]{:S(2)}) collective-permute-start(bf16[2,3,32,512]{3,2,1,0:T(8,128)(2,1)S(1)} %get-tuple-element.44), channel_id=1, source_target_pairs={{0,4},{1,5},{4,8},{5,9},{8,12},{9,13},{12,14},{13,15},{14,10},{15,... | collective-permute-start | bytes 589832 | tf_op jit(solution)/shard_map/ppermute | solution.py:187
  66.7 4.7 %collective-permute-done.10 = bf16[2,3,32,512]{3,2,1,0:T(8,128)(2,1)S(1)} collective-permute-done((bf16[2,3,32,512]{3,2,1,0:T(8,128)(2,1)S(1)}, bf16[2,3,32,512]{3,2,1,0:T(8,128)(2,1)S(1)}, u32[]{:S(2)}, u32[]{:S(2)}) %collective-permute-start.10) | collective-permute-done | bytes 196640 | tf_op jit(solution)/shard_map/ppermute | solution.py:187
  71.5 1.9 %collective-permute-start.12 = (bf16[2,3,32,512]{3,2,1,0:T(8,128)(2,1)S(1)}, bf16[2,3,32,512]{3,2,1,0:T(8,128)(2,1)S(1)}, u32[]{:S(2)}, u32[]{:S(2)}) collective-permute-start(bf16[2,3,32,512]{3,2,1,0:T(8,128)(2,1)S(1)} %fusion.36), channel_id=1, source_target_pairs={{0,4},{1,5},{4,8},{5,9},{8,12},{9,13},{12,14},{13,15},{14,10},{15,... | collective-permute-start | bytes 589832 | tf_op jit(solution)/shard_map/ppermute | solution.py:187
  73.8 4.1 %collective-permute-done.12 = bf16[2,3,32,512]{3,2,1,0:T(8,128)(2,1)S(1)} collective-permute-done((bf16[2,3,32,512]{3,2,1,0:T(8,128)(2,1)S(1)}, bf16[2,3,32,512]{3,2,1,0:T(8,128)(2,1)S(1)}, u32[]{:S(2)}, u32[]{:S(2)}) %collective-permute-start.12) | collective-permute-done | bytes 196640 | tf_op jit(solution)/shard_map/ppermute | solution.py:187
  78.1 1.8 %collective-permute-start.14 = (bf16[2,3,32,512]{3,2,1,0:T(8,128)(2,1)S(1)}, bf16[2,3,32,512]{3,2,1,0:T(8,128)(2,1)S(1)}, u32[]{:S(2)}, u32[]{:S(2)}) collective-permute-start(bf16[2,3,32,512]{3,2,1,0:T(8,128)(2,1)S(1)} %get-tuple-element.42), channel_id=1, source_target_pairs={{0,4},{1,5},{4,8},{5,9},{8,12},{9,13},{12,14},{13,15},{14,10},{15,... | collective-permute-start | bytes 589832 | tf_op jit(solution)/shard_map/ppermute | solution.py:187
  80.2 3.6 %collective-permute-done.14 = bf16[2,3,32,512]{3,2,1,0:T(8,128)(2,1)S(1)} collective-permute-done((bf16[2,3,32,512]{3,2,1,0:T(8,128)(2,1)S(1)}, bf16[2,3,32,512]{3,2,1,0:T(8,128)(2,1)S(1)}, u32[]{:S(2)}, u32[]{:S(2)}) %collective-permute-start.14) | collective-permute-done | bytes 196640 | tf_op jit(solution)/shard_map/ppermute | solution.py:187
  83.9 1.7 %collective-permute-done.20 = bf16[2,3,32,512]{3,2,1,0:T(8,128)(2,1)S(1)} collective-permute-done((bf16[2,3,32,512]{3,2,1,0:T(8,128)(2,1)S(1)}, bf16[2,3,32,512]{3,2,1,0:T(8,128)(2,1)S(1)}, u32[]{:S(2)}, u32[]{:S(2)}) %collective-permute-start.20) | collective-permute-done | bytes 196640 | tf_op jit(solution)/shard_map/ppermute | solution.py:191
  85.8 1.6 collective-permute-start.16
  87.9 3.6 %collective-permute-done.16 = bf16[2,3,32,512]{3,2,1,0:T(8,128)(2,1)S(1)} collective-permute-done((bf16[2,3,32,512]{3,2,1,0:T(8,128)(2,1)S(1)}, bf16[2,3,32,512]{3,2,1,0:T(8,128)(2,1)S(1)}, u32[]{:S(2)}, u32[]{:S(2)}) %collective-permute-start.16) | collective-permute-done | bytes 196640 | tf_op jit(solution)/shard_map/ppermute | solution.py:187
  91.5 1.6 collective-permute-done.22
  93.4 1.4 broadcast.73
  95.5 1.5 collective-permute-start.23
  97.6 5.4 %collective-permute-done.23 = bf16[2,3,32,512]{3,2,1,0:T(8,128)(2,1)S(1)} collective-permute-done((bf16[2,3,32,512]{3,2,1,0:T(8,128)(2,1)S(1)}, bf16[2,3,32,512]{3,2,1,0:T(8,128)(2,1)S(1)}, u32[]{:S(2)}, u32[]{:S(2)}) %collective-permute-start.23) | collective-permute-done | bytes 196640 | tf_op jit(solution)/shard_map/ppermute | solution.py:157
  103.0 1.5 collective-permute-start.25
  106.4 3.1 %collective-permute-done.25 = bf16[2,3,32,512]{3,2,1,0:T(8,128)(2,1)S(1)} collective-permute-done((bf16[2,3,32,512]{3,2,1,0:T(8,128)(2,1)S(1)}, bf16[2,3,32,512]{3,2,1,0:T(8,128)(2,1)S(1)}, u32[]{:S(2)}, u32[]{:S(2)}) %collective-permute-start.25) | collective-permute-done | bytes 196640 | tf_op jit(solution)/shard_map/ppermute | solution.py:157
  109.5 1.5 collective-permute-start.27
  113.0 2.3 %collective-permute-done.27 = bf16[2,3,32,512]{3,2,1,0:T(8,128)(2,1)S(1)} collective-permute-done((bf16[2,3,32,512]{3,2,1,0:T(8,128)(2,1)S(1)}, bf16[2,3,32,512]{3,2,1,0:T(8,128)(2,1)S(1)}, u32[]{:S(2)}, u32[]{:S(2)}) %collective-permute-start.27) | collective-permute-done | bytes 196640 | tf_op jit(solution)/shard_map/ppermute | solution.py:157
  115.2 1.5 collective-permute-start.29
  118.2 2.7 %collective-permute-done.29 = bf16[2,3,32,512]{3,2,1,0:T(8,128)(2,1)S(1)} collective-permute-done((bf16[2,3,32,512]{3,2,1,0:T(8,128)(2,1)S(1)}, bf16[2,3,32,512]{3,2,1,0:T(8,128)(2,1)S(1)}, u32[]{:S(2)}, u32[]{:S(2)}) %collective-permute-start.29) | collective-permute-done | bytes 196640 | tf_op jit(solution)/shard_map/ppermute | solution.py:157
  122.2 1.6 bitcast_dynamic-update-slice_fusion
  123.8 1.6 collective-permute-done.30
  125.4 1.6 bitcast_dynamic-update-slice_fusion.3
  127.0 6.3 %shard_map.609 = (bf16[256,1024]{1,0:T(8,128)(2,1)S(1)}, f32[2,3,512,512]{3,2,1,0:T(8,128)}) custom-call(bf16[256,1024]{1,0:T(8,128)(2,1)S(1)} %get-tuple-element.51.q_ref, bf16[256,1024]{1,0:T(8,128)(2,1)S(1)} %get-tuple-element.65.k_ref, bf16[256,1024]{1,0:T(8,128)(2,1)S(1)} %get-tuple-element.47.v_ref, f32[256,6]{1,0:T(8,128)S(1)} %bitcast.367, ...), custom_call_target="tpu_custom_call" | custom-call | tf_op jit(solution)/shard_map/pallas_call | solution.py:109
  133.3 2.5 %dynamic-slice_bitcast_fusion.7 = (f32[2,3,1,1,32,512]{5,4,1,0,3,2:T(8,128)S(1)}, f32[2,3,1,1,32,512]{5,4,1,0,3,2:T(8,128)S(1)}, f32[2,3,1,1,32,512]{5,4,1,0,3,2...) fusion(f32[2,3,8,2,32,512]{5,4,3,2,1,0:T(8,128)} %bitcast.370, ...), kind=kLoop, calls=%fused_computation.78 | loop fusion | bytes 6291492
  136.6 1.1 collective-permute-done.32
  138.3 1.6 collective-permute-start.33
  140.9 4.4 %collective-permute-done.33 = bf16[2,3,32,512]{3,2,1,0:T(8,128)(2,1)S(1)} collective-permute-done((bf16[2,3,32,512]{3,2,1,0:T(8,128)(2,1)S(1)}, bf16[2,3,32,512]{3,2,1,0:T(8,128)(2,1)S(1)}, u32[]{:S(2)}, u32[]{:S(2)}) %collective-permute-start.33) | collective-permute-done | bytes 196640 | tf_op jit(solution)/shard_map/ppermute | solution.py:187
  145.4 1.6 collective-permute-start.35
  147.5 4.1 %collective-permute-done.35 = bf16[2,3,32,512]{3,2,1,0:T(8,128)(2,1)S(1)} collective-permute-done((bf16[2,3,32,512]{3,2,1,0:T(8,128)(2,1)S(1)}, bf16[2,3,32,512]{3,2,1,0:T(8,128)(2,1)S(1)}, u32[]{:S(2)}, u32[]{:S(2)}) %collective-permute-start.35) | collective-permute-done | bytes 196640 | tf_op jit(solution)/shard_map/ppermute | solution.py:187
  151.8 1.6 collective-permute-start.37
  153.9 3.6 %collective-permute-done.37 = bf16[2,3,32,512]{3,2,1,0:T(8,128)(2,1)S(1)} collective-permute-done((bf16[2,3,32,512]{3,2,1,0:T(8,128)(2,1)S(1)}, bf16[2,3,32,512]{3,2,1,0:T(8,128)(2,1)S(1)}, u32[]{:S(2)}, u32[]{:S(2)}) %collective-permute-start.37) | collective-permute-done | bytes 196640 | tf_op jit(solution)/shard_map/ppermute | solution.py:187
  157.5 1.5 collective-permute-done.43
  159.2 1.6 collective-permute-start.39
  161.3 1.1 pad_maximum_fusion
  162.4 2.6 %collective-permute-done.39 = bf16[2,3,32,512]{3,2,1,0:T(8,128)(2,1)S(1)} collective-permute-done((bf16[2,3,32,512]{3,2,1,0:T(8,128)(2,1)S(1)}, bf16[2,3,32,512]{3,2,1,0:T(8,128)(2,1)S(1)}, u32[]{:S(2)}, u32[]{:S(2)}) %collective-permute-start.39) | collective-permute-done | bytes 196640 | tf_op jit(solution)/shard_map/ppermute | solution.py:187
  164.9 1.6 collective-permute-done.45
  166.8 0.8 broadcast_multiply_fusion
  (115 shorter events, 22.0 us)
Async XLA Ops:
  1.7 25.1 %collective-permute-start = (bf16[2,3,32,512]{3,2,1,0:T(8,128)(2,1)S(1)}, bf16[2,3,32,512]{3,2,1,0:T(8,128)(2,1)S(1)}, u32[]{:S(2)}, u32[]{:S(2)}) collective-permute-start(bf16[2,3,32,512]{3,2,1,0:T(8,128)(2,1)S(1)} %get-tuple-element.17), channel_id=1, source_target_pairs={{0,4},{1,5},{4,8},{5,9},{8,12},{9,13},{12,14},{13,15},{14,10},{15,... | collective-permute-start | bytes 589832 | tf_op jit(solution)/shard_map/ppermute | solution.py:157
  4.8 24.0 %collective-permute-start.1 = (bf16[2,3,32,512]{3,2,1,0:T(8,128)(2,1)S(1)}, bf16[2,3,32,512]{3,2,1,0:T(8,128)(2,1)S(1)}, u32[]{:S(2)}, u32[]{:S(2)}) collective-permute-start(bf16[2,3,32,512]{3,2,1,0:T(8,128)(2,1)S(1)} %get-tuple-element.17), channel_id=1, source_target_pairs={{0,2},{1,3},{4,0},{5,1},{8,4},{9,5},{12,8},{13,9},{14,12},{15,13},... | collective-permute-start | bytes 589832 | tf_op jit(solution)/shard_map/ppermute | solution.py:160
  6.1 41.3 %copy-start.8 = (f32[2,3,2,256]{3,2,1,0:T(2,128)S(1)}, f32[2,3,2,256]{3,2,1,0:T(2,128)}, u32[]{:S(2)}) copy-start(f32[2,3,2,256]{3,2,1,0:T(2,128)} %param.68) | copy-start | bytes 36868
  10.0 38.8 %copy-start.4 = (bf16[2,256,1024]{2,1,0:T(8,128)(2,1)S(1)}, bf16[2,256,1024]{2,1,0:T(8,128)(2,1)}, u32[]{:S(2)}) copy-start(bf16[2,256,1024]{2,1,0:T(8,128)(2,1)} %param.65) | copy-start | bytes 3145732
  26.8 6.4 %collective-permute-start.2 = (bf16[2,3,32,512]{3,2,1,0:T(8,128)(2,1)S(1)}, bf16[2,3,32,512]{3,2,1,0:T(8,128)(2,1)S(1)}, u32[]{:S(2)}, u32[]{:S(2)}) collective-permute-start(bf16[2,3,32,512]{3,2,1,0:T(8,128)(2,1)S(1)} %collective-permute-done), channel_id=1, source_target_pairs={{0,4},{1,5},{4,8},{5,9},{8,12},{9,13},{12,14},{13,15},{14,10},{15,... | collective-permute-start | bytes 589832 | tf_op jit(solution)/shard_map/ppermute | solution.py:157
  28.8 6.1 %collective-permute-start.3 = (bf16[2,3,32,512]{3,2,1,0:T(8,128)(2,1)S(1)}, bf16[2,3,32,512]{3,2,1,0:T(8,128)(2,1)S(1)}, u32[]{:S(2)}, u32[]{:S(2)}) collective-permute-start(bf16[2,3,32,512]{3,2,1,0:T(8,128)(2,1)S(1)} %collective-permute-done.1), channel_id=1, source_target_pairs={{0,2},{1,3},{4,0},{5,1},{8,4},{9,5},{12,8},{13,9},{14,12},{15,13},... | collective-permute-start | bytes 589832 | tf_op jit(solution)/shard_map/ppermute | solution.py:160
  33.2 5.7 %collective-permute-start.4 = (bf16[2,3,32,512]{3,2,1,0:T(8,128)(2,1)S(1)}, bf16[2,3,32,512]{3,2,1,0:T(8,128)(2,1)S(1)}, u32[]{:S(2)}, u32[]{:S(2)}) collective-permute-start(bf16[2,3,32,512]{3,2,1,0:T(8,128)(2,1)S(1)} %collective-permute-done.2), channel_id=1, source_target_pairs={{0,4},{1,5},{4,8},{5,9},{8,12},{9,13},{12,14},{13,15},{14,10},{15,... | collective-permute-start | bytes 589832 | tf_op jit(solution)/shard_map/ppermute | solution.py:157
  34.9 5.8 %collective-permute-start.5 = (bf16[2,3,32,512]{3,2,1,0:T(8,128)(2,1)S(1)}, bf16[2,3,32,512]{3,2,1,0:T(8,128)(2,1)S(1)}, u32[]{:S(2)}, u32[]{:S(2)}) collective-permute-start(bf16[2,3,32,512]{3,2,1,0:T(8,128)(2,1)S(1)} %collective-permute-done.3), channel_id=1, source_target_pairs={{0,2},{1,3},{4,0},{5,1},{8,4},{9,5},{12,8},{13,9},{14,12},{15,13},... | collective-permute-start | bytes 589832 | tf_op jit(solution)/shard_map/ppermute | solution.py:160
  38.9 5.7 %collective-permute-start.6 = (bf16[2,3,32,512]{3,2,1,0:T(8,128)(2,1)S(1)}, bf16[2,3,32,512]{3,2,1,0:T(8,128)(2,1)S(1)}, u32[]{:S(2)}, u32[]{:S(2)}) collective-permute-start(bf16[2,3,32,512]{3,2,1,0:T(8,128)(2,1)S(1)} %collective-permute-done.4), channel_id=1, source_target_pairs={{0,4},{1,5},{4,8},{5,9},{8,12},{9,13},{12,14},{13,15},{14,10},{15,... | collective-permute-start | bytes 589832 | tf_op jit(solution)/shard_map/ppermute | solution.py:157
  44.5 6.7 %collective-permute-start.7 = (bf16[8,2,3,32,512]{4,3,0,2,1:T(8,128)(2,1)S(1)}, bf16[8,2,3,32,512]{4,3,0,2,1:T(8,128)(2,1)}, u32[]{:S(2)}, u32[]{:S(2)}) collective-permute-start(bf16[8,2,3,32,512]{4,3,0,2,1:T(8,128)(2,1)S(1)} %bitcast_dynamic-update-slice_fusion.12), channel_id=1, source_target_pairs={{0,1},{1,0},{2,3},{3,2},{4,5},{5,4},{6,7},{7,6},{8,9},{9,8},{10,11... | collective-permute-start | bytes 4718600 | tf_op jit(solution)/shard_map/ppermute | solution.py:162
  61.5 1.9 %collective-permute-start.17 = (f32[2,3,1,1,32,512]{5,4,1,0,3,2:T(8,128)S(1)}, f32[2,3,1,1,32,512]{5,4,1,0,3,2:T(8,128)S(1)}, u32[]{:S(2)}, u32[]{:S(2)}) collective-permute-start(f32[2,3,1,1,32,512]{5,4,1,0,3,2:T(8,128)S(1)} %get-tuple-element.34), channel_id=1, source_target_pairs={{0,1},{1,0},{2,3},{3,2},{4,5},{5,4},{6,7},{7,6},{8,9},{9,8},{10,11... | collective-permute-start | bytes 1179656 | tf_op jit(solution)/shard_map/ppermute | solution.py:179
  62.0 1.9 %collective-permute-start.9 = (f32[2,3,1,1,32,512]{5,4,1,0,3,2:T(8,128)S(1)}, f32[2,3,1,1,32,512]{5,4,1,0,3,2:T(8,128)S(1)}, u32[]{:S(2)}, u32[]{:S(2)}) collective-permute-start(f32[2,3,1,1,32,512]{5,4,1,0,3,2:T(8,128)S(1)} %get-tuple-element.38), channel_id=1, source_target_pairs={{0,1},{1,0},{2,3},{3,2},{4,5},{5,4},{6,7},{7,6},{8,9},{9,8},{10,11... | collective-permute-start | bytes 1179656 | tf_op jit(solution)/shard_map/ppermute | solution.py:179
  62.1 4.5 %collective-permute-start.11 = (f32[2,3,1,1,32,512]{5,4,1,0,3,2:T(8,128)S(1)}, f32[2,3,1,1,32,512]{5,4,1,0,3,2:T(8,128)S(1)}, u32[]{:S(2)}, u32[]{:S(2)}) collective-permute-start(f32[2,3,1,1,32,512]{5,4,1,0,3,2:T(8,128)S(1)} %get-tuple-element.37), channel_id=1, source_target_pairs={{0,1},{1,0},{2,3},{3,2},{4,5},{5,4},{6,7},{7,6},{8,9},{9,8},{10,11... | collective-permute-start | bytes 1179656 | tf_op jit(solution)/shard_map/ppermute | solution.py:179
  64.1 7.3 %collective-permute-start.10 = (bf16[2,3,32,512]{3,2,1,0:T(8,128)(2,1)S(1)}, bf16[2,3,32,512]{3,2,1,0:T(8,128)(2,1)S(1)}, u32[]{:S(2)}, u32[]{:S(2)}) collective-permute-start(bf16[2,3,32,512]{3,2,1,0:T(8,128)(2,1)S(1)} %get-tuple-element.44), channel_id=1, source_target_pairs={{0,4},{1,5},{4,8},{5,9},{8,12},{9,13},{12,14},{13,15},{14,10},{15,... | collective-permute-start | bytes 589832 | tf_op jit(solution)/shard_map/ppermute | solution.py:187
  66.0 7.3 %collective-permute-start.13 = (f32[2,3,1,1,32,512]{5,4,1,0,3,2:T(8,128)S(1)}, f32[2,3,1,1,32,512]{5,4,1,0,3,2:T(8,128)S(1)}, u32[]{:S(2)}, u32[]{:S(2)}) collective-permute-start(f32[2,3,1,1,32,512]{5,4,1,0,3,2:T(8,128)S(1)} %get-tuple-element.36), channel_id=1, source_target_pairs={{0,1},{1,0},{2,3},{3,2},{4,5},{5,4},{6,7},{7,6},{8,9},{9,8},{10,11... | collective-permute-start | bytes 1179656 | tf_op jit(solution)/shard_map/ppermute | solution.py:179
  66.1 7.8 %collective-permute-start.19 = (f32[2,3,1,1,32,512]{5,4,1,0,3,2:T(8,128)S(1)}, f32[2,3,1,1,32,512]{5,4,1,0,3,2:T(8,128)S(1)}, u32[]{:S(2)}, u32[]{:S(2)}) collective-permute-start(f32[2,3,1,1,32,512]{5,4,1,0,3,2:T(8,128)S(1)} %get-tuple-element.33), channel_id=1, source_target_pairs={{0,1},{1,0},{2,3},{3,2},{4,5},{5,4},{6,7},{7,6},{8,9},{9,8},{10,11... | collective-permute-start | bytes 1179656 | tf_op jit(solution)/shard_map/ppermute | solution.py:179
  66.5 7.3 %collective-permute-start.18 = (bf16[2,3,32,512]{3,2,1,0:T(8,128)(2,1)S(1)}, bf16[2,3,32,512]{3,2,1,0:T(8,128)(2,1)S(1)}, u32[]{:S(2)}, u32[]{:S(2)}) collective-permute-start(bf16[2,3,32,512]{3,2,1,0:T(8,128)(2,1)S(1)} %get-tuple-element.45), channel_id=1, source_target_pairs={{0,2},{1,3},{4,0},{5,1},{8,4},{9,5},{12,8},{13,9},{14,12},{15,13},... | collective-permute-start | bytes 589832 | tf_op jit(solution)/shard_map/ppermute | solution.py:191
  71.5 6.4 %collective-permute-start.12 = (bf16[2,3,32,512]{3,2,1,0:T(8,128)(2,1)S(1)}, bf16[2,3,32,512]{3,2,1,0:T(8,128)(2,1)S(1)}, u32[]{:S(2)}, u32[]{:S(2)}) collective-permute-start(bf16[2,3,32,512]{3,2,1,0:T(8,128)(2,1)S(1)} %fusion.36), channel_id=1, source_target_pairs={{0,4},{1,5},{4,8},{5,9},{8,12},{9,13},{12,14},{13,15},{14,10},{15,... | collective-permute-start | bytes 589832 | tf_op jit(solution)/shard_map/ppermute | solution.py:187
  73.3 6.9 %collective-permute-start.15 = (f32[2,3,1,1,32,512]{5,4,1,0,3,2:T(8,128)S(1)}, f32[2,3,1,1,32,512]{5,4,1,0,3,2:T(8,128)S(1)}, u32[]{:S(2)}, u32[]{:S(2)}) collective-permute-start(f32[2,3,1,1,32,512]{5,4,1,0,3,2:T(8,128)S(1)} %get-tuple-element.35), channel_id=1, source_target_pairs={{0,1},{1,0},{2,3},{3,2},{4,5},{5,4},{6,7},{7,6},{8,9},{9,8},{10,11... | collective-permute-start | bytes 1179656 | tf_op jit(solution)/shard_map/ppermute | solution.py:179
  73.3 6.9 %collective-permute-start.21 = (f32[2,3,1,1,32,512]{5,4,1,0,3,2:T(8,128)S(1)}, f32[2,3,1,1,32,512]{5,4,1,0,3,2:T(8,128)S(1)}, u32[]{:S(2)}, u32[]{:S(2)}) collective-permute-start(f32[2,3,1,1,32,512]{5,4,1,0,3,2:T(8,128)S(1)} %get-tuple-element.39), channel_id=1, source_target_pairs={{0,1},{1,0},{2,3},{3,2},{4,5},{5,4},{6,7},{7,6},{8,9},{9,8},{10,11... | collective-permute-start | bytes 1179656 | tf_op jit(solution)/shard_map/ppermute | solution.py:179
  78.1 5.7 %collective-permute-start.14 = (bf16[2,3,32,512]{3,2,1,0:T(8,128)(2,1)S(1)}, bf16[2,3,32,512]{3,2,1,0:T(8,128)(2,1)S(1)}, u32[]{:S(2)}, u32[]{:S(2)}) collective-permute-start(bf16[2,3,32,512]{3,2,1,0:T(8,128)(2,1)S(1)} %get-tuple-element.42), channel_id=1, source_target_pairs={{0,4},{1,5},{4,8},{5,9},{8,12},{9,13},{12,14},{13,15},{14,10},{15,... | collective-permute-start | bytes 589832 | tf_op jit(solution)/shard_map/ppermute | solution.py:187
  79.9 5.7 %collective-permute-start.20 = (bf16[2,3,32,512]{3,2,1,0:T(8,128)(2,1)S(1)}, bf16[2,3,32,512]{3,2,1,0:T(8,128)(2,1)S(1)}, u32[]{:S(2)}, u32[]{:S(2)}) collective-permute-start(bf16[2,3,32,512]{3,2,1,0:T(8,128)(2,1)S(1)} %get-tuple-element.43), channel_id=1, source_target_pairs={{0,2},{1,3},{4,0},{5,1},{8,4},{9,5},{12,8},{13,9},{14,12},{15,13},... | collective-permute-start | bytes 589832 | tf_op jit(solution)/shard_map/ppermute | solution.py:191
  80.2 7.7 %collective-permute-start.8 = (f32[2,3,1,1,32,512]{5,4,1,0,3,2:T(8,128)S(1)}, f32[2,3,1,1,32,512]{5,4,1,0,3,2:T(8,128)S(1)}, u32[]{:S(2)}, u32[]{:S(2)}) collective-permute-start(f32[2,3,1,1,32,512]{5,4,1,0,3,2:T(8,128)S(1)} %get-tuple-element.32), channel_id=1, source_target_pairs={{0,1},{1,0},{2,3},{3,2},{4,5},{5,4},{6,7},{7,6},{8,9},{9,8},{10,11... | collective-permute-start | bytes 1179656 | tf_op jit(solution)/shard_map/ppermute | solution.py:179
  85.8 5.7 %collective-permute-start.16 = (bf16[2,3,32,512]{3,2,1,0:T(8,128)(2,1)S(1)}, bf16[2,3,32,512]{3,2,1,0:T(8,128)(2,1)S(1)}, u32[]{:S(2)}, u32[]{:S(2)}) collective-permute-start(bf16[2,3,32,512]{3,2,1,0:T(8,128)(2,1)S(1)} %get-tuple-element.40), channel_id=1, source_target_pairs={{0,4},{1,5},{4,8},{5,9},{8,12},{9,13},{12,14},{13,15},{14,10},{15,... | collective-permute-start | bytes 589832 | tf_op jit(solution)/shard_map/ppermute | solution.py:187
  87.4 5.7 %collective-permute-start.22 = (bf16[2,3,32,512]{3,2,1,0:T(8,128)(2,1)S(1)}, bf16[2,3,32,512]{3,2,1,0:T(8,128)(2,1)S(1)}, u32[]{:S(2)}, u32[]{:S(2)}) collective-permute-start(bf16[2,3,32,512]{3,2,1,0:T(8,128)(2,1)S(1)} %get-tuple-element.41), channel_id=1, source_target_pairs={{0,2},{1,3},{4,0},{5,1},{8,4},{9,5},{12,8},{13,9},{14,12},{15,13},... | collective-permute-start | bytes 589832 | tf_op jit(solution)/shard_map/ppermute | solution.py:191
  95.5 7.4 %collective-permute-start.23 = (bf16[2,3,32,512]{3,2,1,0:T(8,128)(2,1)S(1)}, bf16[2,3,32,512]{3,2,1,0:T(8,128)(2,1)S(1)}, u32[]{:S(2)}, u32[]{:S(2)}) collective-permute-start(bf16[2,3,32,512]{3,2,1,0:T(8,128)(2,1)S(1)} %get-tuple-element.13), channel_id=1, source_target_pairs={{0,4},{1,5},{4,8},{5,9},{8,12},{9,13},{12,14},{13,15},{14,10},{15,... | collective-permute-start | bytes 589832 | tf_op jit(solution)/shard_map/ppermute | solution.py:157
  97.1 8.2 %collective-permute-start.24 = (bf16[2,3,32,512]{3,2,1,0:T(8,128)(2,1)S(1)}, bf16[2,3,32,512]{3,2,1,0:T(8,128)(2,1)S(1)}, u32[]{:S(2)}, u32[]{:S(2)}) collective-permute-start(bf16[2,3,32,512]{3,2,1,0:T(8,128)(2,1)S(1)} %get-tuple-element.13), channel_id=1, source_target_pairs={{0,2},{1,3},{4,0},{5,1},{8,4},{9,5},{12,8},{13,9},{14,12},{15,13},... | collective-permute-start | bytes 589832 | tf_op jit(solution)/shard_map/ppermute | solution.py:160
  103.0 6.6 %collective-permute-start.25 = (bf16[2,3,32,512]{3,2,1,0:T(8,128)(2,1)S(1)}, bf16[2,3,32,512]{3,2,1,0:T(8,128)(2,1)S(1)}, u32[]{:S(2)}, u32[]{:S(2)}) collective-permute-start(bf16[2,3,32,512]{3,2,1,0:T(8,128)(2,1)S(1)} %collective-permute-done.23), channel_id=1, source_target_pairs={{0,4},{1,5},{4,8},{5,9},{8,12},{9,13},{12,14},{13,15},{14,10},{15,... | collective-permute-start | bytes 589832 | tf_op jit(solution)/shard_map/ppermute | solution.py:157
  105.2 6.6 %collective-permute-start.26 = (bf16[2,3,32,512]{3,2,1,0:T(8,128)(2,1)S(1)}, bf16[2,3,32,512]{3,2,1,0:T(8,128)(2,1)S(1)}, u32[]{:S(2)}, u32[]{:S(2)}) collective-permute-start(bf16[2,3,32,512]{3,2,1,0:T(8,128)(2,1)S(1)} %collective-permute-done.24), channel_id=1, source_target_pairs={{0,2},{1,3},{4,0},{5,1},{8,4},{9,5},{12,8},{13,9},{14,12},{15,13},... | collective-permute-start | bytes 589832 | tf_op jit(solution)/shard_map/ppermute | solution.py:160
  109.5 5.7 %collective-permute-start.27 = (bf16[2,3,32,512]{3,2,1,0:T(8,128)(2,1)S(1)}, bf16[2,3,32,512]{3,2,1,0:T(8,128)(2,1)S(1)}, u32[]{:S(2)}, u32[]{:S(2)}) collective-permute-start(bf16[2,3,32,512]{3,2,1,0:T(8,128)(2,1)S(1)} %collective-permute-done.25), channel_id=1, source_target_pairs={{0,4},{1,5},{4,8},{5,9},{8,12},{9,13},{12,14},{13,15},{14,10},{15,... | collective-permute-start | bytes 589832 | tf_op jit(solution)/shard_map/ppermute | solution.py:157
  111.8 5.7 %collective-permute-start.28 = (bf16[2,3,32,512]{3,2,1,0:T(8,128)(2,1)S(1)}, bf16[2,3,32,512]{3,2,1,0:T(8,128)(2,1)S(1)}, u32[]{:S(2)}, u32[]{:S(2)}) collective-permute-start(bf16[2,3,32,512]{3,2,1,0:T(8,128)(2,1)S(1)} %collective-permute-done.26), channel_id=1, source_target_pairs={{0,2},{1,3},{4,0},{5,1},{8,4},{9,5},{12,8},{13,9},{14,12},{15,13},... | collective-permute-start | bytes 589832 | tf_op jit(solution)/shard_map/ppermute | solution.py:160
  115.2 5.7 %collective-permute-start.29 = (bf16[2,3,32,512]{3,2,1,0:T(8,128)(2,1)S(1)}, bf16[2,3,32,512]{3,2,1,0:T(8,128)(2,1)S(1)}, u32[]{:S(2)}, u32[]{:S(2)}) collective-permute-start(bf16[2,3,32,512]{3,2,1,0:T(8,128)(2,1)S(1)} %collective-permute-done.27), channel_id=1, source_target_pairs={{0,4},{1,5},{4,8},{5,9},{8,12},{9,13},{12,14},{13,15},{14,10},{15,... | collective-permute-start | bytes 589832 | tf_op jit(solution)/shard_map/ppermute | solution.py:157
  121.6 3.8 %collective-permute-start.30 = (bf16[8,2,3,32,512]{4,3,0,2,1:T(8,128)(2,1)}, bf16[8,2,3,32,512]{4,3,0,2,1:T(8,128)(2,1)}, u32[]{:S(2)}, u32[]{:S(2)}) collective-permute-start(bf16[8,2,3,32,512]{4,3,0,2,1:T(8,128)(2,1)} %bitcast_dynamic-update-slice_fusion.4), channel_id=1, source_target_pairs={{0,1},{1,0},{2,3},{3,2},{4,5},{5,4},{6,7},{7,6},{8,9},{9,8},{10,11... | collective-permute-start | bytes 4718600 | tf_op jit(solution)/shard_map/ppermute | solution.py:162
  135.8 1.8 %collective-permute-start.32 = (f32[2,3,1,1,32,512]{5,4,1,0,3,2:T(8,128)S(1)}, f32[2,3,1,1,32,512]{5,4,1,0,3,2:T(8,128)S(1)}, u32[]{:S(2)}, u32[]{:S(2)}) collective-permute-start(f32[2,3,1,1,32,512]{5,4,1,0,3,2:T(8,128)S(1)} %get-tuple-element.24), channel_id=1, source_target_pairs={{0,1},{1,0},{2,3},{3,2},{4,5},{5,4},{6,7},{7,6},{8,9},{9,8},{10,11... | collective-permute-start | bytes 1179656 | tf_op jit(solution)/shard_map/ppermute | solution.py:179
  136.0 2.1 %collective-permute-start.40 = (f32[2,3,1,1,32,512]{5,4,1,0,3,2:T(8,128)S(1)}, f32[2,3,1,1,32,512]{5,4,1,0,3,2:T(8,128)S(1)}, u32[]{:S(2)}, u32[]{:S(2)}) collective-permute-start(f32[2,3,1,1,32,512]{5,4,1,0,3,2:T(8,128)S(1)} %get-tuple-element.20), channel_id=1, source_target_pairs={{0,1},{1,0},{2,3},{3,2},{4,5},{5,4},{6,7},{7,6},{8,9},{9,8},{10,11... | collective-permute-start | bytes 1179656 | tf_op jit(solution)/shard_map/ppermute | solution.py:179
  136.4 4.5 %collective-permute-start.34 = (f32[2,3,1,1,32,512]{5,4,1,0,3,2:T(8,128)S(1)}, f32[2,3,1,1,32,512]{5,4,1,0,3,2:T(8,128)S(1)}, u32[]{:S(2)}, u32[]{:S(2)}) collective-permute-start(f32[2,3,1,1,32,512]{5,4,1,0,3,2:T(8,128)S(1)} %get-tuple-element.23), channel_id=1, source_target_pairs={{0,1},{1,0},{2,3},{3,2},{4,5},{5,4},{6,7},{7,6},{8,9},{9,8},{10,11... | collective-permute-start | bytes 1179656 | tf_op jit(solution)/shard_map/ppermute | solution.py:179
  138.3 7.0 %collective-permute-start.33 = (bf16[2,3,32,512]{3,2,1,0:T(8,128)(2,1)S(1)}, bf16[2,3,32,512]{3,2,1,0:T(8,128)(2,1)S(1)}, u32[]{:S(2)}, u32[]{:S(2)}) collective-permute-start(bf16[2,3,32,512]{3,2,1,0:T(8,128)(2,1)S(1)} %get-tuple-element.30), channel_id=1, source_target_pairs={{0,4},{1,5},{4,8},{5,9},{8,12},{9,13},{12,14},{13,15},{14,10},{15,... | collective-permute-start | bytes 589832 | tf_op jit(solution)/shard_map/ppermute | solution.py:187
  139.9 7.1 %collective-permute-start.36 = (f32[2,3,1,1,32,512]{5,4,1,0,3,2:T(8,128)S(1)}, f32[2,3,1,1,32,512]{5,4,1,0,3,2:T(8,128)S(1)}, u32[]{:S(2)}, u32[]{:S(2)}) collective-permute-start(f32[2,3,1,1,32,512]{5,4,1,0,3,2:T(8,128)S(1)} %get-tuple-element.22), channel_id=1, source_target_pairs={{0,1},{1,0},{2,3},{3,2},{4,5},{5,4},{6,7},{7,6},{8,9},{9,8},{10,11... | collective-permute-start | bytes 1179656 | tf_op jit(solution)/shard_map/ppermute | solution.py:179
  139.9 7.6 %collective-permute-start.42 = (f32[2,3,1,1,32,512]{5,4,1,0,3,2:T(8,128)S(1)}, f32[2,3,1,1,32,512]{5,4,1,0,3,2:T(8,128)S(1)}, u32[]{:S(2)}, u32[]{:S(2)}) collective-permute-start(f32[2,3,1,1,32,512]{5,4,1,0,3,2:T(8,128)S(1)} %get-tuple-element.19), channel_id=1, source_target_pairs={{0,1},{1,0},{2,3},{3,2},{4,5},{5,4},{6,7},{7,6},{8,9},{9,8},{10,11... | collective-permute-start | bytes 1179656 | tf_op jit(solution)/shard_map/ppermute | solution.py:179
  140.4 7.1 %collective-permute-start.41 = (bf16[2,3,32,512]{3,2,1,0:T(8,128)(2,1)S(1)}, bf16[2,3,32,512]{3,2,1,0:T(8,128)(2,1)S(1)}, u32[]{:S(2)}, u32[]{:S(2)}) collective-permute-start(bf16[2,3,32,512]{3,2,1,0:T(8,128)(2,1)S(1)} %get-tuple-element.31), channel_id=1, source_target_pairs={{0,2},{1,3},{4,0},{5,1},{8,4},{9,5},{12,8},{13,9},{14,12},{15,13},... | collective-permute-start | bytes 589832 | tf_op jit(solution)/shard_map/ppermute | solution.py:191
  145.4 6.1 %collective-permute-start.35 = (bf16[2,3,32,512]{3,2,1,0:T(8,128)(2,1)S(1)}, bf16[2,3,32,512]{3,2,1,0:T(8,128)(2,1)S(1)}, u32[]{:S(2)}, u32[]{:S(2)}) collective-permute-start(bf16[2,3,32,512]{3,2,1,0:T(8,128)(2,1)S(1)} %fusion.15), channel_id=1, source_target_pairs={{0,4},{1,5},{4,8},{5,9},{8,12},{9,13},{12,14},{13,15},{14,10},{15,... | collective-permute-start | bytes 589832 | tf_op jit(solution)/shard_map/ppermute | solution.py:187
  147.0 6.9 %collective-permute-start.38 = (f32[2,3,1,1,32,512]{5,4,1,0,3,2:T(8,128)S(1)}, f32[2,3,1,1,32,512]{5,4,1,0,3,2:T(8,128)S(1)}, u32[]{:S(2)}, u32[]{:S(2)}) collective-permute-start(f32[2,3,1,1,32,512]{5,4,1,0,3,2:T(8,128)S(1)} %get-tuple-element.21), channel_id=1, source_target_pairs={{0,1},{1,0},{2,3},{3,2},{4,5},{5,4},{6,7},{7,6},{8,9},{9,8},{10,11... | collective-permute-start | bytes 1179656 | tf_op jit(solution)/shard_map/ppermute | solution.py:179
  147.0 6.9 %collective-permute-start.44 = (f32[2,3,1,1,32,512]{5,4,1,0,3,2:T(8,128)S(1)}, f32[2,3,1,1,32,512]{5,4,1,0,3,2:T(8,128)S(1)}, u32[]{:S(2)}, u32[]{:S(2)}) collective-permute-start(f32[2,3,1,1,32,512]{5,4,1,0,3,2:T(8,128)S(1)} %get-tuple-element.25), channel_id=1, source_target_pairs={{0,1},{1,0},{2,3},{3,2},{4,5},{5,4},{6,7},{7,6},{8,9},{9,8},{10,11... | collective-permute-start | bytes 1179656 | tf_op jit(solution)/shard_map/ppermute | solution.py:179
  151.8 5.7 %collective-permute-start.37 = (bf16[2,3,32,512]{3,2,1,0:T(8,128)(2,1)S(1)}, bf16[2,3,32,512]{3,2,1,0:T(8,128)(2,1)S(1)}, u32[]{:S(2)}, u32[]{:S(2)}) collective-permute-start(bf16[2,3,32,512]{3,2,1,0:T(8,128)(2,1)S(1)} %get-tuple-element.28), channel_id=1, source_target_pairs={{0,4},{1,5},{4,8},{5,9},{8,12},{9,13},{12,14},{13,15},{14,10},{15,... | collective-permute-start | bytes 589832 | tf_op jit(solution)/shard_map/ppermute | solution.py:187
  153.3 5.7 %collective-permute-start.43 = (bf16[2,3,32,512]{3,2,1,0:T(8,128)(2,1)S(1)}, bf16[2,3,32,512]{3,2,1,0:T(8,128)(2,1)S(1)}, u32[]{:S(2)}, u32[]{:S(2)}) collective-permute-start(bf16[2,3,32,512]{3,2,1,0:T(8,128)(2,1)S(1)} %get-tuple-element.29), channel_id=1, source_target_pairs={{0,2},{1,3},{4,0},{5,1},{8,4},{9,5},{12,8},{13,9},{14,12},{15,13},... | collective-permute-start | bytes 589832 | tf_op jit(solution)/shard_map/ppermute | solution.py:191
  153.8 8.5 %collective-permute-start.31 = (f32[2,3,1,1,32,512]{5,4,1,0,3,2:T(8,128)S(1)}, f32[2,3,1,1,32,512]{5,4,1,0,3,2:T(8,128)S(1)}, u32[]{:S(2)}, u32[]{:S(2)}) collective-permute-start(f32[2,3,1,1,32,512]{5,4,1,0,3,2:T(8,128)S(1)} %get-tuple-element.18), channel_id=1, source_target_pairs={{0,1},{1,0},{2,3},{3,2},{4,5},{5,4},{6,7},{7,6},{8,9},{9,8},{10,11... | collective-permute-start | bytes 1179656 | tf_op jit(solution)/shard_map/ppermute | solution.py:179
  159.2 5.7 %collective-permute-start.39 = (bf16[2,3,32,512]{3,2,1,0:T(8,128)(2,1)S(1)}, bf16[2,3,32,512]{3,2,1,0:T(8,128)(2,1)S(1)}, u32[]{:S(2)}, u32[]{:S(2)}) collective-permute-start(bf16[2,3,32,512]{3,2,1,0:T(8,128)(2,1)S(1)} %get-tuple-element.26), channel_id=1, source_target_pairs={{0,4},{1,5},{4,8},{5,9},{8,12},{9,13},{12,14},{13,15},{14,10},{15,... | collective-permute-start | bytes 589832 | tf_op jit(solution)/shard_map/ppermute | solution.py:187
  160.8 5.7 %collective-permute-start.45 = (bf16[2,3,32,512]{3,2,1,0:T(8,128)(2,1)S(1)}, bf16[2,3,32,512]{3,2,1,0:T(8,128)(2,1)S(1)}, u32[]{:S(2)}, u32[]{:S(2)}) collective-permute-start(bf16[2,3,32,512]{3,2,1,0:T(8,128)(2,1)S(1)} %get-tuple-element.27), channel_id=1, source_target_pairs={{0,2},{1,3},{4,0},{5,1},{8,4},{9,5},{12,8},{13,9},{14,12},{15,13},... | collective-permute-start | bytes 589832 | tf_op jit(solution)/shard_map/ppermute | solution.py:191
  (8 other events, 44.7 us)

commit v6 on v5

--- a/solution.py
+++ b/solution.py
@@ -145,57 +145,74 @@
         where = jnp.array(self.place, jnp.int32)[me]
         return jnp.array(self.cycle, jnp.int32)[(where + step) % self.chips]
 
+    def offset_table(self):
+        return [[(self.place[c] - self.place[t // 2]) % self.chips for c in range(self.chips)] for t in range(2 * self.chips)]
+
     def gather(self, own):
         h, g, rows, f = own.shape
-        core = lax.axis_index("tok") % 2
-        ring = jnp.zeros((self.chips, h, g, rows, f), own.dtype)
-        ring = lax.dynamic_update_index_in_dim(ring, own, lax.axis_index("tok") // 2, 0)
+        chips = self.chips
+        me = lax.axis_index("tok")
+        core = me % 2
+        by_offset = [own] + [None] * (chips - 1)
         a = own
         b = own
         for k in range(1, max(self.ncw, self.nccw) + 1):
             if k <= self.ncw:
                 a = lax.ppermute(a, "tok", self.cw)
-                ring = lax.dynamic_update_index_in_dim(ring, a, self.chip_at(-k), 0)
+                by_offset[chips - k] = a
             if k <= self.nccw:
                 b = lax.ppermute(b, "tok", self.ccw)
-                ring = lax.dynamic_update_index_in_dim(ring, b, self.chip_at(k), 0)
-        other = lax.ppermute(ring, "tok", self.swap)
-        full = jnp.zeros((self.chips, 2, h, g, rows, f), own.dtype)
-        full = lax.dynamic_update_slice(full, ring[:, None], (0, core, 0, 0, 0, 0))
-        full = lax.dynamic_update_slice(full, other[:, None], (0, 1 - core, 0, 0, 0, 0))
+                by_offset[k] = b
+        mine = jnp.stack(by_offset)
+        other = lax.ppermute(mine, "tok", self.swap)
+        both = jnp.concatenate([mine, other], axis=0)
+        offsets = jnp.array(self.offset_table(), jnp.int32)[me]
+        pick = jnp.stack([offsets + chips * core, offsets + chips * (1 - core)], axis=1).reshape(-1)
+        full = jnp.take(both, pick, axis=0)
+        full = full.reshape(chips, 2, h, g, rows, f)
         full = jnp.moveaxis(full, (0, 1), (2, 3))
-        return full.reshape(h, g, self.chips * 2 * rows, f)
+        return full.reshape(h, g, chips * 2 * rows, f)
 
     def reduce(self, part):
         h, g, r, f = part.shape
         rows = r // (2 * self.chips)
         q = part.reshape(h, g, self.chips, 2, rows, f)
         core = lax.axis_index("tok") % 2
-
-        def chip_sum(step):
-            chip = self.chip_at(step)
-            keep = lax.dynamic_slice(q, (0, 0, chip, core, 0, 0), (h, g, 1, 1, rows, f))
-            send = lax.dynamic_slice(q, (0, 0, chip, 1 - core, 0, 0), (h, g, 1, 1, rows, f))
-            got = lax.ppermute(send, "tok", self.swap)
-            return (keep + got).reshape(h, g, rows, f)
-
-        total = chip_sum(0)
-        a = chip_sum(self.ncw) if self.ncw else None
-        b = chip_sum(-self.nccw) if self.nccw else None
+        need = []
+        for k in range(max(self.ncw, self.nccw)):
+            if k < self.ncw:
+                need.append(self.ncw - k)
+            if k < self.nccw:
+                need.append(k - self.nccw)
+        need.append(0)
+        batches = [need[:2], need[2:4], need[4:]]
+        sums = {}
+        for batch in batches:
+            if not batch:
+                continue
+            chips = [self.chip_at(j) for j in batch]
+            keep = jnp.stack([lax.dynamic_slice(q, (0, 0, c, core, 0, 0), (h, g, 1, 1, rows, f)) for c in chips])
+            send = jnp.stack([lax.dynamic_slice(q, (0, 0, c, 1 - core, 0, 0), (h, g, 1, 1, rows, f)) for c in chips])
+            total = keep + lax.ppermute(send, "tok", self.swap)
+            for i, j in enumerate(batch):
+                sums[j] = total[i].reshape(h, g, rows, f)
+        out = sums[0]
+        a = sums[self.ncw] if self.ncw else None
+        b = sums[-self.nccw] if self.nccw else None
         for k in range(1, max(self.ncw, self.nccw) + 1):
             if k <= self.ncw:
                 a = lax.ppermute(a.astype(jnp.bfloat16), "tok", self.cw).astype(jnp.float32)
                 if k < self.ncw:
-                    a = a + chip_sum(self.ncw - k)
+                    a = a + sums[self.ncw - k]
             if k <= self.nccw:
                 b = lax.ppermute(b.astype(jnp.bfloat16), "tok", self.ccw).astype(jnp.float32)
                 if k < self.nccw:
-                    b = b + chip_sum(-self.nccw + k)
+                    b = b + sums[-self.nccw + k]
         if a is not None:
-            total = total + a
+            out = out + a
         if b is not None:
-            total = total + b
-        return total
+            out = out + b
+        return out
 
 
 def solution(mesh):

time: 168 us -> 192 us (1.14)
  local copies, waits for them, and re-layouts: 21.5 us -> 40.5 us
  other arithmetic: 4.51 us -> 12.6 us
  starting transfers between devices: 36.5 us -> 32.4 us
  waiting for transfers between devices: 66.9 us -> 70.4 us
  between operations: 25.7 us -> 22.7 us
    ppermute x6, waiting for transfers between devices: 0.02 us -> 11.3 us  [gather(): b = lax.ppermute(b, 'tok', self.ccw)]
    dynamic_update_slice x18 -> x0, local copies, waits for them, and re-layouts: 10.2 us -> none  [the longest x2 3.22 us: gather(): lax.dynamic_update_slice(full, other[:, None], (0, 1 - core, 0, 0, 0, 0))]
    gather x0 -> x2, local copies, waits for them, and re-layouts: none -> 8.63 us  [gather(): full = jnp.take(both, pick, axis=0)]
    ppermute x8, waiting for transfers between devices: 25.1 us -> 16.5 us  [gather(): a = lax.ppermute(a, 'tok', self.cw)]
    ppermute x8, starting transfers between devices: 14.9 us -> 6.43 us  [gather(): a = lax.ppermute(a, 'tok', self.cw)]
    another operation x4 -> x5, local copies, waits for them, and re-layouts: 2.31 us -> 9.5 us  [the longest x2 7.81 us: reduce(): jnp.stack([lax.dynamic_slice(q, (0, 0, c, core, 0, 0), (h, g, 1, 1, rows,...]
    ppermute x6, starting transfers between devices: 1.8 us -> 8.34 us  [gather(): b = lax.ppermute(b, 'tok', self.ccw)]
    concatenate x0 -> x2, local copies, waits for them, and re-layouts: none -> 5.44 us  [gather(): both = jnp.concatenate([mine, other], axis=0)]
  transfers between devices with their start and end apart: 46 -> 36, of which waited for: 24 -> 24; matrix products, arithmetic and copies ran while one was open for 7% -> 8% of each run, Pallas kernels for 0% -> 0%
where the time goes in v6:
time: 192 us; the launch traced here: 191 us
  waiting for transfers between devices  70.4 us (37%)
  local copies, waits for them, and re-layouts  40.5 us (21%)
  starting transfers between devices  32.4 us (17%)
  between operations  22.7 us (12%)
  other arithmetic  12.6 us (7%)
  Pallas kernels  12.6 us (7%)
    ppermute x8, waiting for transfers between devices, reduce(): a = lax.ppermute(a.astype(jnp.bfloat16), 'tok', self.cw).astype(jnp.float32)  29.6 us
    ppermute x8, waiting for transfers between devices, gather(): a = lax.ppermute(a, 'tok', self.cw)  16.5 us
    pallas_call x2, Pallas kernels, fused_block(): pl.pallas_call(_block_kernel, out_shape=(jax.ShapeDtypeStruct(query.shape...  12.6 us
    ppermute x8, starting transfers between devices, reduce(): a = lax.ppermute(a.astype(jnp.bfloat16), 'tok', self.cw).astype(jnp.float32)  11.4 us
    ppermute x6, waiting for transfers between devices, gather(): b = lax.ppermute(b, 'tok', self.ccw)  11.3 us
    unnamed x24, local copies, waits for them, and re-layouts  11 us
    gather x2, local copies, waits for them, and re-layouts, gather(): full = jnp.take(both, pick, axis=0)  8.63 us
    ppermute x6, starting transfers between devices, gather(): b = lax.ppermute(b, 'tok', self.ccw)  8.34 us
  transfers between devices with their start and end apart: 36, of which 24 were waited for; matrix products, arithmetic and copies ran while one was open for 8% of the time, Pallas kernels for 0%

profile of v6, /device:TPU:0, one launch (start us, length us, event | category | flops | bytes accessed | tf_op | source)
XLA Modules:
  0.0 191.3 jit_solution(16266267695228493374)
XLA Ops:
  0.6 1.7 bitcast_dynamic-update-slice_fusion.31
  2.3 3.0 %collective-permute-start = (bf16[2,3,32,512]{3,2,1,0:T(8,128)(2,1)S(1)}, bf16[2,3,32,512]{3,2,1,0:T(8,128)(2,1)S(1)}, u32[]{:S(2)}, u32[]{:S(2)}) collective-permute-start(bf16[2,3,32,512]{3,2,1,0:T(8,128)(2,1)S(1)} %get-tuple-element.18), channel_id=1, source_target_pairs={{0,2},{1,3},{4,0},{5,1},{8,4},{9,5},{12,8},{13,9},{14,12},{15,13},... | collective-permute-start | bytes 589832 | tf_op jit(solution)/shard_map/ppermute | solution.py:164
  5.4 1.2 dynamic_slice.199
  13.3 1.6 fusion.31
  25.7 2.0 %collective-permute-start.1 = (bf16[2,3,32,512]{3,2,1,0:T(8,128)(2,1)S(1)}, bf16[2,3,32,512]{3,2,1,0:T(8,128)(2,1)S(1)}, u32[]{:S(2)}, u32[]{:S(2)}) collective-permute-start(bf16[2,3,32,512]{3,2,1,0:T(8,128)(2,1)S(1)} %collective-permute-done), channel_id=1, source_target_pairs={{0,2},{1,3},{4,0},{5,1},{8,4},{9,5},{12,8},{13,9},{14,12},{15,13},... | collective-permute-start | bytes 589832 | tf_op jit(solution)/shard_map/ppermute | solution.py:164
  28.6 3.5 %collective-permute-done.1 = bf16[2,3,32,512]{3,2,1,0:T(8,128)(2,1)S(1)} collective-permute-done((bf16[2,3,32,512]{3,2,1,0:T(8,128)(2,1)S(1)}, bf16[2,3,32,512]{3,2,1,0:T(8,128)(2,1)S(1)}, u32[]{:S(2)}, u32[]{:S(2)}) %collective-permute-start.1) | collective-permute-done | bytes 196640 | tf_op jit(solution)/shard_map/ppermute | solution.py:164
  32.0 1.7 collective-permute-start.2
  34.9 4.7 %collective-permute-done.5 = bf16[2,3,32,512]{3,2,1,0:T(8,128)(2,1)S(1)} collective-permute-done((bf16[2,3,32,512]{3,2,1,0:T(8,128)(2,1)S(1)}, bf16[2,3,32,512]{3,2,1,0:T(8,128)(2,1)S(1)}, u32[]{:S(2)}, u32[]{:S(2)}) %collective-permute-start.5) | collective-permute-done | bytes 196640 | tf_op jit(solution)/shard_map/ppermute | solution.py:161
  40.7 4.5 %collective-permute-done.6 = bf16[2,3,32,512]{3,2,1,0:T(8,128)(2,1)S(1)} collective-permute-done((bf16[2,3,32,512]{3,2,1,0:T(8,128)(2,1)S(1)}, bf16[2,3,32,512]{3,2,1,0:T(8,128)(2,1)S(1)}, u32[]{:S(2)}, u32[]{:S(2)}) %collective-permute-start.6) | collective-permute-done | bytes 196640 | tf_op jit(solution)/shard_map/ppermute | solution.py:161
  54.6 1.7 slice_bitcast_fusion.3
  56.3 2.7 %constant_dynamic-update-slice_fusion = bf16[16,2,3,32,512]{4,3,2,1,0:T(8,128)(2,1)} fusion(bf16[16,2,3,32,512]{4,3,2,1,0:T(8,128)(2,1)} %get-tuple-element.86, bf16[8,2,3,32,512]{4,3,2,1,0:T(8,128)(2,1)} %collective-permute-done.7), kind=kLoop, calls=%fused_computation.137 | loop fusion | bytes 3145728 | tf_op jit(solution)/shard_map/concatenate | solution.py:168
  59.0 4.3 %gather_fusion = bf16[16,2,3,32,512]{4,3,2,1,0:T(8,128)(2,1)} fusion(bf16[16,2,3,32,512]{4,3,2,1,0:T(8,128)(2,1)} %constant_dynamic-update-slice_fusion, s32[1024]{0:T(1024)S(1)} %pad_clamp_fusion), kind=kCustom, calls=%fused_computation.clone | custom fusion | bytes 6291520 | tf_op jit(solution)/shard_map/jit(_take)/gather | solution.py:171
  63.3 2.2 %broadcast_select_fusion.1 = bf16[16,2,3,32,512]{4,3,2,1,0:T(8,128)(2,1)S(1)} fusion(bf16[16,2,3,32,512]{4,3,2,1,0:T(8,128)(2,1)} %gather_fusion, pred[16]{0:T(512)(128)(4,1)S(1)} %compare_and_fusion), kind=kLoop, calls=%fused_computation.3 | loop fusion | flops 1572864 | bytes 6291472 | tf_op jit(solution)/shard_map/jit(_take)/select_n | solution.py:171
  66.0 6.3 %shard_map.374 = (bf16[256,1024]{1,0:T(8,128)(2,1)S(1)}, f32[2,3,512,512]{3,2,1,0:T(8,128)}) custom-call(bf16[256,1024]{1,0:T(8,128)(2,1)S(1)} %get-tuple-element.59.q_ref, bf16[256,1024]{1,0:T(8,128)(2,1)S(1)} %get-tuple-element.112.k_ref, bf16[256,1024]{1,0:T(8,128)(2,1)S(1)} %get-tuple-element.55.v_ref, f32[256,6]{1,0:T(8,128)S(1)} %bitcast.246, ...), custom_call_target="tpu_custom_call" | custom-call | tf_op jit(solution)/shard_map/pallas_call | solution.py:109
  72.3 3.7 %dynamic-slice_bitcast_fusion.23 = (f32[1,2,3,1,1,32,512]{6,5,2,1,4,3,0:T(8,128)S(1)}, f32[1,2,3,1,1,32,512]{6,5,2,1,4,3,0:T(8,128)S(1)}, f32[1,2,3,1,1,32,512]{...) fusion(f32[2,3,8,2,32,512]{5,4,3,2,1,0:T(8,128)} %bitcast.253, ...), kind=kLoop, calls=%fused_computation.90 | loop fusion | bytes 12582952 | tf_op jit(solution)/shard_map/stack | solution.py:194
  79.2 1.7 collective-permute-start.15
  82.1 3.9 %collective-permute-done.10 = bf16[2,3,32,512]{3,2,1,0:T(8,128)(2,1)S(1)} collective-permute-done((bf16[2,3,32,512]{3,2,1,0:T(8,128)(2,1)S(1)}, bf16[2,3,32,512]{3,2,1,0:T(8,128)(2,1)S(1)}, u32[]{:S(2)}, u32[]{:S(2)}) %collective-permute-start.10) | collective-permute-done | bytes 196640 | tf_op jit(solution)/shard_map/ppermute | solution.py:204
  86.5 1.8 collective-permute-start.12
  89.0 3.9 %collective-permute-done.12 = bf16[2,3,32,512]{3,2,1,0:T(8,128)(2,1)S(1)} collective-permute-done((bf16[2,3,32,512]{3,2,1,0:T(8,128)(2,1)S(1)}, bf16[2,3,32,512]{3,2,1,0:T(8,128)(2,1)S(1)}, u32[]{:S(2)}, u32[]{:S(2)}) %collective-permute-start.12) | collective-permute-done | bytes 196640 | tf_op jit(solution)/shard_map/ppermute | solution.py:204
  92.9 1.5 collective-permute-start.13
  94.5 4.2 %collective-permute-done.13 = bf16[2,3,32,512]{3,2,1,0:T(8,128)(2,1)S(1)} collective-permute-done((bf16[2,3,32,512]{3,2,1,0:T(8,128)(2,1)S(1)}, bf16[2,3,32,512]{3,2,1,0:T(8,128)(2,1)S(1)}, u32[]{:S(2)}, u32[]{:S(2)}) %collective-permute-start.13) | collective-permute-done | bytes 196640 | tf_op jit(solution)/shard_map/ppermute | solution.py:204
  98.8 1.5 collective-permute-start.14
  100.9 3.6 %collective-permute-done.14 = bf16[2,3,32,512]{3,2,1,0:T(8,128)(2,1)S(1)} collective-permute-done((bf16[2,3,32,512]{3,2,1,0:T(8,128)(2,1)S(1)}, bf16[2,3,32,512]{3,2,1,0:T(8,128)(2,1)S(1)}, u32[]{:S(2)}, u32[]{:S(2)}) %collective-permute-start.14) | collective-permute-done | bytes 196640 | tf_op jit(solution)/shard_map/ppermute | solution.py:204
  104.5 2.1 %collective-permute-done.17 = bf16[2,3,32,512]{3,2,1,0:T(8,128)(2,1)S(1)} collective-permute-done((bf16[2,3,32,512]{3,2,1,0:T(8,128)(2,1)S(1)}, bf16[2,3,32,512]{3,2,1,0:T(8,128)(2,1)S(1)}, u32[]{:S(2)}, u32[]{:S(2)}) %collective-permute-start.17) | collective-permute-done | bytes 196640 | tf_op jit(solution)/shard_map/ppermute | solution.py:208
  107.9 1.7 collective-permute-start.21
  110.3 4.4 %collective-permute-done.18 = bf16[2,3,32,512]{3,2,1,0:T(8,128)(2,1)S(1)} collective-permute-done((bf16[2,3,32,512]{3,2,1,0:T(8,128)(2,1)S(1)}, bf16[2,3,32,512]{3,2,1,0:T(8,128)(2,1)S(1)}, u32[]{:S(2)}, u32[]{:S(2)}) %collective-permute-start.18) | collective-permute-done | bytes 196640 | tf_op jit(solution)/shard_map/ppermute | solution.py:164
  115.3 1.5 collective-permute-start.22
  117.6 3.4 %collective-permute-done.19 = bf16[2,3,32,512]{3,2,1,0:T(8,128)(2,1)S(1)} collective-permute-done((bf16[2,3,32,512]{3,2,1,0:T(8,128)(2,1)S(1)}, bf16[2,3,32,512]{3,2,1,0:T(8,128)(2,1)S(1)}, u32[]{:S(2)}, u32[]{:S(2)}) %collective-permute-start.19) | collective-permute-done | bytes 196640 | tf_op jit(solution)/shard_map/ppermute | solution.py:164
  121.8 1.2 collective-permute-start.23
  123.8 3.7 %collective-permute-done.23 = bf16[2,3,32,512]{3,2,1,0:T(8,128)(2,1)S(1)} collective-permute-done((bf16[2,3,32,512]{3,2,1,0:T(8,128)(2,1)S(1)}, bf16[2,3,32,512]{3,2,1,0:T(8,128)(2,1)S(1)}, u32[]{:S(2)}, u32[]{:S(2)}) %collective-permute-start.23) | collective-permute-done | bytes 196640 | tf_op jit(solution)/shard_map/ppermute | solution.py:161
  127.5 1.2 collective-permute-start.24
  129.5 3.7 %collective-permute-done.24 = bf16[2,3,32,512]{3,2,1,0:T(8,128)(2,1)S(1)} collective-permute-done((bf16[2,3,32,512]{3,2,1,0:T(8,128)(2,1)S(1)}, bf16[2,3,32,512]{3,2,1,0:T(8,128)(2,1)S(1)}, u32[]{:S(2)}, u32[]{:S(2)}) %collective-permute-start.24) | collective-permute-done | bytes 196640 | tf_op jit(solution)/shard_map/ppermute | solution.py:161
  136.5 3.6 %collective-permute-done.25 = bf16[8,2,3,32,512]{4,3,2,1,0:T(8,128)(2,1)} collective-permute-done((bf16[8,2,3,32,512]{4,3,2,1,0:T(8,128)(2,1)}, bf16[8,2,3,32,512]{4,3,2,1,0:T(8,128)(2,1)}, u32[]{:S(2)}, u32[]{:S(2)}) %collective-permute-start.25) | collective-permute-done | bytes 1572896 | tf_op jit(solution)/shard_map/ppermute | solution.py:167
  140.1 2.7 %constant_dynamic-update-slice_fusion.1 = bf16[16,2,3,32,512]{4,3,2,1,0:T(8,128)(2,1)} fusion(bf16[16,2,3,32,512]{4,3,2,1,0:T(8,128)(2,1)} %get-tuple-element.72, bf16[8,2,3,32,512]{4,3,2,1,0:T(8,128)(2,1)} %collective-permute-done.25), kind=kLoop, calls=%fused_computation.138 | loop fusion | bytes 3145728 | tf_op jit(solution)/shard_map/concatenate | solution.py:168
  142.8 4.3 %gather_fusion.1 = bf16[16,2,3,32,512]{4,3,2,1,0:T(8,128)(2,1)} fusion(bf16[16,2,3,32,512]{4,3,2,1,0:T(8,128)(2,1)} %constant_dynamic-update-slice_fusion.1, s32[1024]{0:T(1024)S(1)} %pad_clamp_fusion), kind=kCustom, calls=%fused_computation.1.clone | custom fusion | bytes 6291520 | tf_op jit(solution)/shard_map/jit(_take)/gather | solution.py:171
  147.1 2.2 %broadcast_select_fusion = bf16[16,2,3,32,512]{4,3,2,1,0:T(8,128)(2,1)S(1)} fusion(bf16[16,2,3,32,512]{4,3,2,1,0:T(8,128)(2,1)} %gather_fusion.1, pred[16]{0:T(512)(128)(4,1)S(1)} %compare_and_fusion), kind=kLoop, calls=%fused_computation.2 | loop fusion | flops 1572864 | bytes 6291472 | tf_op jit(solution)/shard_map/jit(_take)/select_n | solution.py:171
  149.8 6.3 %shard_map.375 = (bf16[256,1024]{1,0:T(8,128)(2,1)S(1)}, f32[2,3,512,512]{3,2,1,0:T(8,128)}) custom-call(bf16[256,1024]{1,0:T(8,128)(2,1)S(1)} %get-tuple-element.60.q_ref, bf16[256,1024]{1,0:T(8,128)(2,1)S(1)} %get-tuple-element.111.k_ref, bf16[256,1024]{1,0:T(8,128)(2,1)S(1)} %get-tuple-element.56.v_ref, f32[256,6]{1,0:T(8,128)S(1)} %bitcast.247, ...), custom_call_target="tpu_custom_call" | custom-call | tf_op jit(solution)/shard_map/pallas_call | solution.py:109
  156.1 4.1 %dynamic-slice_bitcast_fusion.7 = (f32[1,2,3,1,1,32,512]{6,5,2,1,4,3,0:T(8,128)S(1)}, f32[1,2,3,1,1,32,512]{6,5,2,1,4,3,0:T(8,128)S(1)}, f32[1,2,3,1,1,32,512]{6...) fusion(f32[2,3,8,2,32,512]{5,4,3,2,1,0:T(8,128)} %bitcast.252, ...), kind=kLoop, calls=%fused_computation.72 | loop fusion | bytes 12582952 | tf_op jit(solution)/shard_map/stack | solution.py:194
  161.4 1.3 collective-permute-done.27
  162.9 1.2 collective-permute-start.28
  166.2 3.7 %collective-permute-done.28 = bf16[2,3,32,512]{3,2,1,0:T(8,128)(2,1)S(1)} collective-permute-done((bf16[2,3,32,512]{3,2,1,0:T(8,128)(2,1)S(1)}, bf16[2,3,32,512]{3,2,1,0:T(8,128)(2,1)S(1)}, u32[]{:S(2)}, u32[]{:S(2)}) %collective-permute-start.28) | collective-permute-done | bytes 196640 | tf_op jit(solution)/shard_map/ppermute | solution.py:204
  170.9 1.6 collective-permute-start.30
  173.4 3.3 %collective-permute-done.30 = bf16[2,3,32,512]{3,2,1,0:T(8,128)(2,1)S(1)} collective-permute-done((bf16[2,3,32,512]{3,2,1,0:T(8,128)(2,1)S(1)}, bf16[2,3,32,512]{3,2,1,0:T(8,128)(2,1)S(1)}, u32[]{:S(2)}, u32[]{:S(2)}) %collective-permute-start.30) | collective-permute-done | bytes 196640 | tf_op jit(solution)/shard_map/ppermute | solution.py:204
  176.8 1.6 collective-permute-start.31
  178.4 4.3 %collective-permute-done.31 = bf16[2,3,32,512]{3,2,1,0:T(8,128)(2,1)S(1)} collective-permute-done((bf16[2,3,32,512]{3,2,1,0:T(8,128)(2,1)S(1)}, bf16[2,3,32,512]{3,2,1,0:T(8,128)(2,1)S(1)}, u32[]{:S(2)}, u32[]{:S(2)}) %collective-permute-start.31) | collective-permute-done | bytes 196640 | tf_op jit(solution)/shard_map/ppermute | solution.py:204
  182.9 1.6 collective-permute-start.32
  186.0 2.6 %collective-permute-done.32 = bf16[2,3,32,512]{3,2,1,0:T(8,128)(2,1)S(1)} collective-permute-done((bf16[2,3,32,512]{3,2,1,0:T(8,128)(2,1)S(1)}, bf16[2,3,32,512]{3,2,1,0:T(8,128)(2,1)S(1)}, u32[]{:S(2)}, u32[]{:S(2)}) %collective-permute-start.32) | collective-permute-done | bytes 196640 | tf_op jit(solution)/shard_map/ppermute | solution.py:204
  188.6 1.6 collective-permute-done.35
  (106 shorter events, 32.5 us)
Async XLA Ops:
  2.3 23.3 %collective-permute-start = (bf16[2,3,32,512]{3,2,1,0:T(8,128)(2,1)S(1)}, bf16[2,3,32,512]{3,2,1,0:T(8,128)(2,1)S(1)}, u32[]{:S(2)}, u32[]{:S(2)}) collective-permute-start(bf16[2,3,32,512]{3,2,1,0:T(8,128)(2,1)S(1)} %get-tuple-element.18), channel_id=1, source_target_pairs={{0,2},{1,3},{4,0},{5,1},{8,4},{9,5},{12,8},{13,9},{14,12},{15,13},... | collective-permute-start | bytes 589832 | tf_op jit(solution)/shard_map/ppermute | solution.py:164
  5.3 22.3 %collective-permute-start.3 = (bf16[2,3,32,512]{3,2,1,0:T(8,128)(2,1)S(1)}, bf16[2,3,32,512]{3,2,1,0:T(8,128)(2,1)S(1)}, u32[]{:S(2)}, u32[]{:S(2)}) collective-permute-start(bf16[2,3,32,512]{3,2,1,0:T(8,128)(2,1)S(1)} %get-tuple-element.18), channel_id=1, source_target_pairs={{0,4},{1,5},{4,8},{5,9},{8,12},{9,13},{12,14},{13,15},{14,10},{15,... | collective-permute-start | bytes 589832 | tf_op jit(solution)/shard_map/ppermute | solution.py:161
  25.7 6.4 %collective-permute-start.1 = (bf16[2,3,32,512]{3,2,1,0:T(8,128)(2,1)S(1)}, bf16[2,3,32,512]{3,2,1,0:T(8,128)(2,1)S(1)}, u32[]{:S(2)}, u32[]{:S(2)}) collective-permute-start(bf16[2,3,32,512]{3,2,1,0:T(8,128)(2,1)S(1)} %collective-permute-done), channel_id=1, source_target_pairs={{0,2},{1,3},{4,0},{5,1},{8,4},{9,5},{12,8},{13,9},{14,12},{15,13},... | collective-permute-start | bytes 589832 | tf_op jit(solution)/shard_map/ppermute | solution.py:164
  27.6 6.1 %collective-permute-start.4 = (bf16[2,3,32,512]{3,2,1,0:T(8,128)(2,1)S(1)}, bf16[2,3,32,512]{3,2,1,0:T(8,128)(2,1)S(1)}, u32[]{:S(2)}, u32[]{:S(2)}) collective-permute-start(bf16[2,3,32,512]{3,2,1,0:T(8,128)(2,1)S(1)} %collective-permute-done.3), channel_id=1, source_target_pairs={{0,4},{1,5},{4,8},{5,9},{8,12},{9,13},{12,14},{13,15},{14,10},{15,... | collective-permute-start | bytes 589832 | tf_op jit(solution)/shard_map/ppermute | solution.py:161
  32.0 7.8 %collective-permute-start.2 = (bf16[2,3,32,512]{3,2,1,0:T(8,128)(2,1)S(1)}, bf16[2,3,32,512]{3,2,1,0:T(8,128)(2,1)S(1)}, u32[]{:S(2)}, u32[]{:S(2)}) collective-permute-start(bf16[2,3,32,512]{3,2,1,0:T(8,128)(2,1)S(1)} %collective-permute-done.1), channel_id=1, source_target_pairs={{0,2},{1,3},{4,0},{5,1},{8,4},{9,5},{12,8},{13,9},{14,12},{15,13},... | collective-permute-start | bytes 589832 | tf_op jit(solution)/shard_map/ppermute | solution.py:164
  33.7 5.8 %collective-permute-start.5 = (bf16[2,3,32,512]{3,2,1,0:T(8,128)(2,1)S(1)}, bf16[2,3,32,512]{3,2,1,0:T(8,128)(2,1)S(1)}, u32[]{:S(2)}, u32[]{:S(2)}) collective-permute-start(bf16[2,3,32,512]{3,2,1,0:T(8,128)(2,1)S(1)} %collective-permute-done.4), channel_id=1, source_target_pairs={{0,4},{1,5},{4,8},{5,9},{8,12},{9,13},{12,14},{13,15},{14,10},{15,... | collective-permute-start | bytes 589832 | tf_op jit(solution)/shard_map/ppermute | solution.py:161
  34.9 14.4 %copy-start.4 = (f32[2,3,2,256]{3,2,1,0:T(2,128)S(1)}, f32[2,3,2,256]{3,2,1,0:T(2,128)}, u32[]{:S(2)}) copy-start(f32[2,3,2,256]{3,2,1,0:T(2,128)} %param.44) | copy-start | bytes 36868
  39.5 5.7 %collective-permute-start.6 = (bf16[2,3,32,512]{3,2,1,0:T(8,128)(2,1)S(1)}, bf16[2,3,32,512]{3,2,1,0:T(8,128)(2,1)S(1)}, u32[]{:S(2)}, u32[]{:S(2)}) collective-permute-start(bf16[2,3,32,512]{3,2,1,0:T(8,128)(2,1)S(1)} %collective-permute-done.5), channel_id=1, source_target_pairs={{0,4},{1,5},{4,8},{5,9},{8,12},{9,13},{12,14},{13,15},{14,10},{15,... | collective-permute-start | bytes 589832 | tf_op jit(solution)/shard_map/ppermute | solution.py:161
  39.9 14.6 %copy-start.3 = (bf16[2,256,1024]{2,1,0:T(8,128)(2,1)S(1)}, bf16[2,256,1024]{2,1,0:T(8,128)(2,1)}, u32[]{:S(2)}) copy-start(bf16[2,256,1024]{2,1,0:T(8,128)(2,1)} %param.41) | copy-start | bytes 3145732
  48.4 7.9 %collective-permute-start.7 = (bf16[8,2,3,32,512]{4,3,2,1,0:T(8,128)(2,1)}, bf16[8,2,3,32,512]{4,3,2,1,0:T(8,128)(2,1)}, u32[]{:S(2)}, u32[]{:S(2)}) collective-permute-start(bf16[8,2,3,32,512]{4,3,2,1,0:T(8,128)(2,1)} %get-tuple-element.85), channel_id=1, source_target_pairs={{0,1},{1,0},{2,3},{3,2},{4,5},{5,4},{6,7},{7,6},{8,9},{9,8},{10,11... | collective-permute-start | bytes 4718600 | tf_op jit(solution)/shard_map/ppermute | solution.py:167
  72.3 3.7 %copy-start = (bf16[256,1024]{1,0:T(8,128)(2,1)}, bf16[256,1024]{1,0:T(8,128)(2,1)S(1)}, u32[]{:S(2)}) copy-start(bf16[256,1024]{1,0:T(8,128)(2,1)S(1)} %get-tuple-element.7) | copy-start | bytes 1572868
  76.1 2.5 %collective-permute-start.9 = (f32[2,2,3,1,1,32,512]{6,5,2,1,4,3,0:T(8,128)S(1)}, f32[2,2,3,1,1,32,512]{6,5,2,1,4,3,0:T(8,128)S(1)}, u32[]{:S(2)}, u32[]{:S(2)}) collective-permute-start(f32[2,2,3,1,1,32,512]{6,5,2,1,4,3,0:T(8,128)S(1)} %pad_maximum_fusion.3), channel_id=1, source_target_pairs={{0,1},{1,0},{2,3},{3,2},{4,5},{5,4},{6,7},{7,6},{8,9},{9,8},{10,11... | collective-permute-start | bytes 2359304 | tf_op jit(solution)/shard_map/ppermute | solution.py:196
  76.8 11.8 %collective-permute-start.8 = (f32[4,2,3,1,1,32,512]{6,5,2,1,4,3,0:T(8,128)S(1)}, f32[4,2,3,1,1,32,512]{6,5,2,1,4,3,0:T(8,128)S(1)}, u32[]{:S(2)}, u32[]{:S(2)}) collective-permute-start(f32[4,2,3,1,1,32,512]{6,5,2,1,4,3,0:T(8,128)S(1)} %pad_maximum_fusion), channel_id=1, source_target_pairs={{0,1},{1,0},{2,3},{3,2},{4,5},{5,4},{6,7},{7,6},{8,9},{9,8},{10,11... | collective-permute-start | bytes 4718600 | tf_op jit(solution)/shard_map/ppermute | solution.py:196
  76.9 5.0 %collective-permute-start.11 = (f32[2,2,3,1,1,32,512]{6,5,2,1,4,3,0:T(8,128)S(1)}, f32[2,2,3,1,1,32,512]{6,5,2,1,4,3,0:T(8,128)S(1)}, u32[]{:S(2)}, u32[]{:S(2)}) collective-permute-start(f32[2,2,3,1,1,32,512]{6,5,2,1,4,3,0:T(8,128)S(1)} %pad_maximum_fusion.4), channel_id=1, source_target_pairs={{0,1},{1,0},{2,3},{3,2},{4,5},{5,4},{6,7},{7,6},{8,9},{9,8},{10,11... | collective-permute-start | bytes 2359304 | tf_op jit(solution)/shard_map/ppermute | solution.py:196
  78.8 7.2 %collective-permute-start.10 = (bf16[2,3,32,512]{3,2,1,0:T(8,128)(2,1)S(1)}, bf16[2,3,32,512]{3,2,1,0:T(8,128)(2,1)S(1)}, u32[]{:S(2)}, u32[]{:S(2)}) collective-permute-start(bf16[2,3,32,512]{3,2,1,0:T(8,128)(2,1)S(1)} %get-tuple-element.69), channel_id=1, source_target_pairs={{0,4},{1,5},{4,8},{5,9},{8,12},{9,13},{12,14},{13,15},{14,10},{15,... | collective-permute-start | bytes 589832 | tf_op jit(solution)/shard_map/ppermute | solution.py:204
  79.2 7.2 %collective-permute-start.15 = (bf16[2,3,32,512]{3,2,1,0:T(8,128)(2,1)S(1)}, bf16[2,3,32,512]{3,2,1,0:T(8,128)(2,1)S(1)}, u32[]{:S(2)}, u32[]{:S(2)}) collective-permute-start(bf16[2,3,32,512]{3,2,1,0:T(8,128)(2,1)S(1)} %get-tuple-element.70), channel_id=1, source_target_pairs={{0,2},{1,3},{4,0},{5,1},{8,4},{9,5},{12,8},{13,9},{14,12},{15,13},... | collective-permute-start | bytes 589832 | tf_op jit(solution)/shard_map/ppermute | solution.py:208
  86.5 6.4 %collective-permute-start.12 = (bf16[2,3,32,512]{3,2,1,0:T(8,128)(2,1)S(1)}, bf16[2,3,32,512]{3,2,1,0:T(8,128)(2,1)S(1)}, u32[]{:S(2)}, u32[]{:S(2)}) collective-permute-start(bf16[2,3,32,512]{3,2,1,0:T(8,128)(2,1)S(1)} %get-tuple-element.63), channel_id=1, source_target_pairs={{0,4},{1,5},{4,8},{5,9},{8,12},{9,13},{12,14},{13,15},{14,10},{15,... | collective-permute-start | bytes 589832 | tf_op jit(solution)/shard_map/ppermute | solution.py:204
  88.3 6.1 %collective-permute-start.16 = (bf16[2,3,32,512]{3,2,1,0:T(8,128)(2,1)S(1)}, bf16[2,3,32,512]{3,2,1,0:T(8,128)(2,1)S(1)}, u32[]{:S(2)}, u32[]{:S(2)}) collective-permute-start(bf16[2,3,32,512]{3,2,1,0:T(8,128)(2,1)S(1)} %get-tuple-element.64), channel_id=1, source_target_pairs={{0,2},{1,3},{4,0},{5,1},{8,4},{9,5},{12,8},{13,9},{14,12},{15,13},... | collective-permute-start | bytes 589832 | tf_op jit(solution)/shard_map/ppermute | solution.py:208
  89.0 17.6 %copy-start.2 = (f32[2,3,32,512]{3,2,1,0:T(8,128)S(1)}, f32[2,3,32,512]{3,2,1,0:T(8,128)}, u32[]{:S(2)}) copy-start(f32[2,3,32,512]{3,2,1,0:T(8,128)} %param.45) | copy-start | bytes 1179652
  92.9 5.7 %collective-permute-start.13 = (bf16[2,3,32,512]{3,2,1,0:T(8,128)(2,1)S(1)}, bf16[2,3,32,512]{3,2,1,0:T(8,128)(2,1)S(1)}, u32[]{:S(2)}, u32[]{:S(2)}) collective-permute-start(bf16[2,3,32,512]{3,2,1,0:T(8,128)(2,1)S(1)} %fusion.22), channel_id=1, source_target_pairs={{0,4},{1,5},{4,8},{5,9},{8,12},{9,13},{12,14},{13,15},{14,10},{15,... | collective-permute-start | bytes 589832 | tf_op jit(solution)/shard_map/ppermute | solution.py:204
  98.8 5.7 %collective-permute-start.14 = (bf16[2,3,32,512]{3,2,1,0:T(8,128)(2,1)S(1)}, bf16[2,3,32,512]{3,2,1,0:T(8,128)(2,1)S(1)}, u32[]{:S(2)}, u32[]{:S(2)}) collective-permute-start(bf16[2,3,32,512]{3,2,1,0:T(8,128)(2,1)S(1)} %get-tuple-element.53), channel_id=1, source_target_pairs={{0,4},{1,5},{4,8},{5,9},{8,12},{9,13},{12,14},{13,15},{14,10},{15,... | collective-permute-start | bytes 589832 | tf_op jit(solution)/shard_map/ppermute | solution.py:204
  100.3 6.3 %collective-permute-start.17 = (bf16[2,3,32,512]{3,2,1,0:T(8,128)(2,1)S(1)}, bf16[2,3,32,512]{3,2,1,0:T(8,128)(2,1)S(1)}, u32[]{:S(2)}, u32[]{:S(2)}) collective-permute-start(bf16[2,3,32,512]{3,2,1,0:T(8,128)(2,1)S(1)} %get-tuple-element.54), channel_id=1, source_target_pairs={{0,2},{1,3},{4,0},{5,1},{8,4},{9,5},{12,8},{13,9},{14,12},{15,13},... | collective-permute-start | bytes 589832 | tf_op jit(solution)/shard_map/ppermute | solution.py:208
  107.6 7.1 %collective-permute-start.18 = (bf16[2,3,32,512]{3,2,1,0:T(8,128)(2,1)S(1)}, bf16[2,3,32,512]{3,2,1,0:T(8,128)(2,1)S(1)}, u32[]{:S(2)}, u32[]{:S(2)}) collective-permute-start(bf16[2,3,32,512]{3,2,1,0:T(8,128)(2,1)S(1)} %get-tuple-element.14), channel_id=1, source_target_pairs={{0,2},{1,3},{4,0},{5,1},{8,4},{9,5},{12,8},{13,9},{14,12},{15,13},... | collective-permute-start | bytes 589832 | tf_op jit(solution)/shard_map/ppermute | solution.py:164
  107.9 7.4 %collective-permute-start.21 = (bf16[2,3,32,512]{3,2,1,0:T(8,128)(2,1)S(1)}, bf16[2,3,32,512]{3,2,1,0:T(8,128)(2,1)S(1)}, u32[]{:S(2)}, u32[]{:S(2)}) collective-permute-start(bf16[2,3,32,512]{3,2,1,0:T(8,128)(2,1)S(1)} %get-tuple-element.14), channel_id=1, source_target_pairs={{0,4},{1,5},{4,8},{5,9},{8,12},{9,13},{12,14},{13,15},{14,10},{15,... | collective-permute-start | bytes 589832 | tf_op jit(solution)/shard_map/ppermute | solution.py:161
  114.7 6.3 %collective-permute-start.19 = (bf16[2,3,32,512]{3,2,1,0:T(8,128)(2,1)S(1)}, bf16[2,3,32,512]{3,2,1,0:T(8,128)(2,1)S(1)}, u32[]{:S(2)}, u32[]{:S(2)}) collective-permute-start(bf16[2,3,32,512]{3,2,1,0:T(8,128)(2,1)S(1)} %collective-permute-done.18), channel_id=1, source_target_pairs={{0,2},{1,3},{4,0},{5,1},{8,4},{9,5},{12,8},{13,9},{14,12},{15,13},... | collective-permute-start | bytes 589832 | tf_op jit(solution)/shard_map/ppermute | solution.py:164
  115.3 6.6 %collective-permute-start.22 = (bf16[2,3,32,512]{3,2,1,0:T(8,128)(2,1)S(1)}, bf16[2,3,32,512]{3,2,1,0:T(8,128)(2,1)S(1)}, u32[]{:S(2)}, u32[]{:S(2)}) collective-permute-start(bf16[2,3,32,512]{3,2,1,0:T(8,128)(2,1)S(1)} %collective-permute-done.21), channel_id=1, source_target_pairs={{0,4},{1,5},{4,8},{5,9},{8,12},{9,13},{12,14},{13,15},{14,10},{15,... | collective-permute-start | bytes 589832 | tf_op jit(solution)/shard_map/ppermute | solution.py:161
  121.0 7.7 %collective-permute-start.20 = (bf16[2,3,32,512]{3,2,1,0:T(8,128)(2,1)S(1)}, bf16[2,3,32,512]{3,2,1,0:T(8,128)(2,1)S(1)}, u32[]{:S(2)}, u32[]{:S(2)}) collective-permute-start(bf16[2,3,32,512]{3,2,1,0:T(8,128)(2,1)S(1)} %collective-permute-done.19), channel_id=1, source_target_pairs={{0,2},{1,3},{4,0},{5,1},{8,4},{9,5},{12,8},{13,9},{14,12},{15,13},... | collective-permute-start | bytes 589832 | tf_op jit(solution)/shard_map/ppermute | solution.py:164
  121.8 5.7 %collective-permute-start.23 = (bf16[2,3,32,512]{3,2,1,0:T(8,128)(2,1)S(1)}, bf16[2,3,32,512]{3,2,1,0:T(8,128)(2,1)S(1)}, u32[]{:S(2)}, u32[]{:S(2)}) collective-permute-start(bf16[2,3,32,512]{3,2,1,0:T(8,128)(2,1)S(1)} %collective-permute-done.22), channel_id=1, source_target_pairs={{0,4},{1,5},{4,8},{5,9},{8,12},{9,13},{12,14},{13,15},{14,10},{15,... | collective-permute-start | bytes 589832 | tf_op jit(solution)/shard_map/ppermute | solution.py:161
  127.5 5.7 %collective-permute-start.24 = (bf16[2,3,32,512]{3,2,1,0:T(8,128)(2,1)S(1)}, bf16[2,3,32,512]{3,2,1,0:T(8,128)(2,1)S(1)}, u32[]{:S(2)}, u32[]{:S(2)}) collective-permute-start(bf16[2,3,32,512]{3,2,1,0:T(8,128)(2,1)S(1)} %collective-permute-done.23), channel_id=1, source_target_pairs={{0,4},{1,5},{4,8},{5,9},{8,12},{9,13},{12,14},{13,15},{14,10},{15,... | collective-permute-start | bytes 589832 | tf_op jit(solution)/shard_map/ppermute | solution.py:161
  136.4 3.8 %collective-permute-start.25 = (bf16[8,2,3,32,512]{4,3,2,1,0:T(8,128)(2,1)}, bf16[8,2,3,32,512]{4,3,2,1,0:T(8,128)(2,1)}, u32[]{:S(2)}, u32[]{:S(2)}) collective-permute-start(bf16[8,2,3,32,512]{4,3,2,1,0:T(8,128)(2,1)} %get-tuple-element.71), channel_id=1, source_target_pairs={{0,1},{1,0},{2,3},{3,2},{4,5},{5,4},{6,7},{7,6},{8,9},{9,8},{10,11... | collective-permute-start | bytes 4718600 | tf_op jit(solution)/shard_map/ppermute | solution.py:167
  160.3 2.4 %collective-permute-start.27 = (f32[2,2,3,1,1,32,512]{6,5,2,1,4,3,0:T(8,128)S(1)}, f32[2,2,3,1,1,32,512]{6,5,2,1,4,3,0:T(8,128)S(1)}, u32[]{:S(2)}, u32[]{:S(2)}) collective-permute-start(f32[2,2,3,1,1,32,512]{6,5,2,1,4,3,0:T(8,128)S(1)} %pad_maximum_fusion.5), channel_id=1, source_target_pairs={{0,1},{1,0},{2,3},{3,2},{4,5},{5,4},{6,7},{7,6},{8,9},{9,8},{10,11... | collective-permute-start | bytes 2359304 | tf_op jit(solution)/shard_map/ppermute | solution.py:196
  160.7 12.3 %collective-permute-start.26 = (f32[4,2,3,1,1,32,512]{6,5,2,1,4,3,0:T(8,128)S(1)}, f32[4,2,3,1,1,32,512]{6,5,2,1,4,3,0:T(8,128)S(1)}, u32[]{:S(2)}, u32[]{:S(2)}) collective-permute-start(f32[4,2,3,1,1,32,512]{6,5,2,1,4,3,0:T(8,128)S(1)} %pad_maximum_fusion.1), channel_id=1, source_target_pairs={{0,1},{1,0},{2,3},{3,2},{4,5},{5,4},{6,7},{7,6},{8,9},{9,8},{10,11... | collective-permute-start | bytes 4718600 | tf_op jit(solution)/shard_map/ppermute | solution.py:196
  161.2 4.8 %collective-permute-start.29 = (f32[2,2,3,1,1,32,512]{6,5,2,1,4,3,0:T(8,128)S(1)}, f32[2,2,3,1,1,32,512]{6,5,2,1,4,3,0:T(8,128)S(1)}, u32[]{:S(2)}, u32[]{:S(2)}) collective-permute-start(f32[2,2,3,1,1,32,512]{6,5,2,1,4,3,0:T(8,128)S(1)} %pad_maximum_fusion.6), channel_id=1, source_target_pairs={{0,1},{1,0},{2,3},{3,2},{4,5},{5,4},{6,7},{7,6},{8,9},{9,8},{10,11... | collective-permute-start | bytes 2359304 | tf_op jit(solution)/shard_map/ppermute | solution.py:196
  162.9 7.0 %collective-permute-start.28 = (bf16[2,3,32,512]{3,2,1,0:T(8,128)(2,1)S(1)}, bf16[2,3,32,512]{3,2,1,0:T(8,128)(2,1)S(1)}, u32[]{:S(2)}, u32[]{:S(2)}) collective-permute-start(bf16[2,3,32,512]{3,2,1,0:T(8,128)(2,1)S(1)} %get-tuple-element.66), channel_id=1, source_target_pairs={{0,4},{1,5},{4,8},{5,9},{8,12},{9,13},{12,14},{13,15},{14,10},{15,... | collective-permute-start | bytes 589832 | tf_op jit(solution)/shard_map/ppermute | solution.py:204
  164.1 6.7 %collective-permute-start.33 = (bf16[2,3,32,512]{3,2,1,0:T(8,128)(2,1)S(1)}, bf16[2,3,32,512]{3,2,1,0:T(8,128)(2,1)S(1)}, u32[]{:S(2)}, u32[]{:S(2)}) collective-permute-start(bf16[2,3,32,512]{3,2,1,0:T(8,128)(2,1)S(1)} %get-tuple-element.67), channel_id=1, source_target_pairs={{0,2},{1,3},{4,0},{5,1},{8,4},{9,5},{12,8},{13,9},{14,12},{15,13},... | collective-permute-start | bytes 589832 | tf_op jit(solution)/shard_map/ppermute | solution.py:208
  170.9 5.9 %collective-permute-start.30 = (bf16[2,3,32,512]{3,2,1,0:T(8,128)(2,1)S(1)}, bf16[2,3,32,512]{3,2,1,0:T(8,128)(2,1)S(1)}, u32[]{:S(2)}, u32[]{:S(2)}) collective-permute-start(bf16[2,3,32,512]{3,2,1,0:T(8,128)(2,1)S(1)} %get-tuple-element.61), channel_id=1, source_target_pairs={{0,4},{1,5},{4,8},{5,9},{8,12},{9,13},{12,14},{13,15},{14,10},{15,... | collective-permute-start | bytes 589832 | tf_op jit(solution)/shard_map/ppermute | solution.py:204
  172.5 5.9 %collective-permute-start.34 = (bf16[2,3,32,512]{3,2,1,0:T(8,128)(2,1)S(1)}, bf16[2,3,32,512]{3,2,1,0:T(8,128)(2,1)S(1)}, u32[]{:S(2)}, u32[]{:S(2)}) collective-permute-start(bf16[2,3,32,512]{3,2,1,0:T(8,128)(2,1)S(1)} %get-tuple-element.62), channel_id=1, source_target_pairs={{0,2},{1,3},{4,0},{5,1},{8,4},{9,5},{12,8},{13,9},{14,12},{15,13},... | collective-permute-start | bytes 589832 | tf_op jit(solution)/shard_map/ppermute | solution.py:208
  173.4 11.5 %copy-start.1 = (bf16[256,1024]{1,0:T(8,128)(2,1)S(1)}, bf16[256,1024]{1,0:T(8,128)(2,1)}, u32[]{:S(2)}) copy-start(bf16[256,1024]{1,0:T(8,128)(2,1)} %copy-done) | copy-start | bytes 1572868
  176.8 5.9 %collective-permute-start.31 = (bf16[2,3,32,512]{3,2,1,0:T(8,128)(2,1)S(1)}, bf16[2,3,32,512]{3,2,1,0:T(8,128)(2,1)S(1)}, u32[]{:S(2)}, u32[]{:S(2)}) collective-permute-start(bf16[2,3,32,512]{3,2,1,0:T(8,128)(2,1)S(1)} %fusion.9), channel_id=1, source_target_pairs={{0,4},{1,5},{4,8},{5,9},{8,12},{9,13},{12,14},{13,15},{14,10},{15,... | collective-permute-start | bytes 589832 | tf_op jit(solution)/shard_map/ppermute | solution.py:204
  182.9 5.7 %collective-permute-start.32 = (bf16[2,3,32,512]{3,2,1,0:T(8,128)(2,1)S(1)}, bf16[2,3,32,512]{3,2,1,0:T(8,128)(2,1)S(1)}, u32[]{:S(2)}, u32[]{:S(2)}) collective-permute-start(bf16[2,3,32,512]{3,2,1,0:T(8,128)(2,1)S(1)} %get-tuple-element.51), channel_id=1, source_target_pairs={{0,4},{1,5},{4,8},{5,9},{8,12},{9,13},{12,14},{13,15},{14,10},{15,... | collective-permute-start | bytes 589832 | tf_op jit(solution)/shard_map/ppermute | solution.py:204
  184.5 5.7 %collective-permute-start.35 = (bf16[2,3,32,512]{3,2,1,0:T(8,128)(2,1)S(1)}, bf16[2,3,32,512]{3,2,1,0:T(8,128)(2,1)S(1)}, u32[]{:S(2)}, u32[]{:S(2)}) collective-permute-start(bf16[2,3,32,512]{3,2,1,0:T(8,128)(2,1)S(1)} %get-tuple-element.52), channel_id=1, source_target_pairs={{0,2},{1,3},{4,0},{5,1},{8,4},{9,5},{12,8},{13,9},{14,12},{15,13},... | collective-permute-start | bytes 589832 | tf_op jit(solution)/shard_map/ppermute | solution.py:208

commit v7 on v5

--- a/solution.py
+++ b/solution.py
@@ -98,19 +98,24 @@
         e1 = (r_ref[:, head : head + 1] * d1).astype(jnp.bfloat16)
         e3 = (r_ref[:, heads + head : heads + head + 1] * d3).astype(jnp.bfloat16)
         b2 = (r_ref[:, 2 * heads + head : 2 * heads + head + 1] * (act * h3)).astype(jnp.bfloat16)
-        g_ref[head, 0] = _tn(e1, key_rows)
-        g_ref[head, 1] = _tn(e3, key_rows)
-        g_ref[head, 2] = _tn(value_rows, b2)
-
-
-def fused_block(query, key_rows, value_rows, rate_rows, wbf):
+        chips = g_ref.shape[0]
+        rows = g_ref.shape[4]
+        for which, grad in enumerate((_tn(e1, key_rows), _tn(e3, key_rows), _tn(value_rows, b2))):
+            for chip in range(chips):
+                for core in range(2):
+                    lo_row = (2 * chip + core) * rows
+                    g_ref[chip, core, head, which] = grad[lo_row : lo_row + rows]
+
+
+def fused_block(query, key_rows, value_rows, rate_rows, wbf, chips):
     tokens = query.shape[0]
     rates_t = rate_rows.reshape(-1, tokens).T
+    heads, mats, hid, dh = wbf.shape
     return pl.pallas_call(
         _block_kernel,
         out_shape=(
             jax.ShapeDtypeStruct(query.shape, jnp.bfloat16),
-            jax.ShapeDtypeStruct(wbf.shape, jnp.float32),
+            jax.ShapeDtypeStruct((chips, 2, heads, mats, hid // (2 * chips), dh), jnp.float32),
         ),
         compiler_params=pltpu.CompilerParams(vmem_limit_bytes=48 * 1024 * 1024),
     )(query, key_rows, value_rows, rates_t, wbf)
@@ -166,16 +171,14 @@
         full = jnp.moveaxis(full, (0, 1), (2, 3))
         return full.reshape(h, g, self.chips * 2 * rows, f)
 
-    def reduce(self, part):
-        h, g, r, f = part.shape
-        rows = r // (2 * self.chips)
-        q = part.reshape(h, g, self.chips, 2, rows, f)
+    def reduce(self, q):
+        _, _, h, g, rows, f = q.shape
         core = lax.axis_index("tok") % 2
 
         def chip_sum(step):
             chip = self.chip_at(step)
-            keep = lax.dynamic_slice(q, (0, 0, chip, core, 0, 0), (h, g, 1, 1, rows, f))
-            send = lax.dynamic_slice(q, (0, 0, chip, 1 - core, 0, 0), (h, g, 1, 1, rows, f))
+            keep = lax.dynamic_slice(q, (chip, core, 0, 0, 0, 0), (1, 1, h, g, rows, f))
+            send = lax.dynamic_slice(q, (chip, 1 - core, 0, 0, 0, 0), (1, 1, h, g, rows, f))
             got = lax.ppermute(send, "tok", self.swap)
             return (keep + got).reshape(h, g, rows, f)
 
@@ -207,7 +210,7 @@
         blocks = []
         for span in range(nblocks):
             gathered = ring.gather(own.astype(jnp.bfloat16))
-            normed, partial_value = fused_block(queries[span], keys[span], values[span], rates[span], gathered)
+            normed, partial_value = fused_block(queries[span], keys[span], values[span], rates[span], gathered, ring.chips)
             blocks.append(normed)
             own = renorm(own, own + ring.reduce(partial_value))
         return (jnp.stack(blocks), own)

time: 168 us -> 168 us (level)
    unnamed x22 -> x20, local copies, waits for them, and re-layouts: 7.1 us -> 2.29 us
    dynamic_slice x0 -> x2, local copies, waits for them, and re-layouts: none -> 4.8 us  [chip_sum(): lax.dynamic_slice(q, (chip, 1 - core, 0, 0, 0, 0), (1, 1, h, g, rows, f))]
where the time goes in v7:
time: 168 us
  waiting for transfers between devices  66.9 us (40%)
  starting transfers between devices  36.5 us (22%)
  between operations  25.7 us (15%)
  local copies, waits for them, and re-layouts  21.4 us (13%)
  Pallas kernels  12.6 us (8%)
  other arithmetic  4.52 us (3%)
    ppermute x8, waiting for transfers between devices, reduce(): a = lax.ppermute(a.astype(jnp.bfloat16), 'tok', self.cw).astype(jnp.float32)  30.7 us
    ppermute x8, waiting for transfers between devices, gather(): a = lax.ppermute(a, 'tok', self.cw)  25.1 us
    ppermute x8, starting transfers between devices, gather(): a = lax.ppermute(a, 'tok', self.cw)  14.9 us
    ppermute x8, starting transfers between devices, reduce(): a = lax.ppermute(a.astype(jnp.bfloat16), 'tok', self.cw).astype(jnp.float32)  13.5 us
    pallas_call x2, Pallas kernels, fused_block(): pl.pallas_call(_block_kernel, out_shape=(jax.ShapeDtypeStruct(query.shape...  12.6 us
    ppermute x6, waiting for transfers between devices, reduce(): lax.ppermute(b.astype(jnp.bfloat16), 'tok', self.ccw).astype(jnp.float32)  6.4 us
    dynamic_slice x2, local copies, waits for them, and re-layouts, chip_sum(): lax.dynamic_slice(q, (chip, 1 - core, 0, 0, 0, 0), (1, 1, h, g, rows, f))  4.8 us
    ppermute x16, starting transfers between devices, chip_sum(): got = lax.ppermute(send, 'tok', self.swap)  3.83 us
  transfers between devices with their start and end apart: 46, of which 24 were waited for; matrix products, arithmetic and copies ran while one was open for 7% of the time, Pallas kernels for 0%

profile of v7, /device:TPU:0, one launch (start us, length us, event | category | flops | bytes accessed | tf_op | source)
XLA Modules:
  0.0 167.6 jit_solution(15424610413197642488)
XLA Ops:
  1.7 3.1 %collective-permute-start = (bf16[2,3,32,512]{3,2,1,0:T(8,128)(2,1)S(1)}, bf16[2,3,32,512]{3,2,1,0:T(8,128)(2,1)S(1)}, u32[]{:S(2)}, u32[]{:S(2)}) collective-permute-start(bf16[2,3,32,512]{3,2,1,0:T(8,128)(2,1)S(1)} %get-tuple-element.17), channel_id=1, source_target_pairs={{0,4},{1,5},{4,8},{5,9},{8,12},{9,13},{12,14},{13,15},{14,10},{15,... | collective-permute-start | bytes 589832 | tf_op jit(solution)/shard_map/ppermute | solution.py:162
  26.8 2.1 %collective-permute-start.2 = (bf16[2,3,32,512]{3,2,1,0:T(8,128)(2,1)S(1)}, bf16[2,3,32,512]{3,2,1,0:T(8,128)(2,1)S(1)}, u32[]{:S(2)}, u32[]{:S(2)}) collective-permute-start(bf16[2,3,32,512]{3,2,1,0:T(8,128)(2,1)S(1)} %collective-permute-done), channel_id=1, source_target_pairs={{0,4},{1,5},{4,8},{5,9},{8,12},{9,13},{12,14},{13,15},{14,10},{15,... | collective-permute-start | bytes 589832 | tf_op jit(solution)/shard_map/ppermute | solution.py:162
  28.9 4.3 %collective-permute-done.2 = bf16[2,3,32,512]{3,2,1,0:T(8,128)(2,1)S(1)} collective-permute-done((bf16[2,3,32,512]{3,2,1,0:T(8,128)(2,1)S(1)}, bf16[2,3,32,512]{3,2,1,0:T(8,128)(2,1)S(1)}, u32[]{:S(2)}, u32[]{:S(2)}) %collective-permute-start.2) | collective-permute-done | bytes 196640 | tf_op jit(solution)/shard_map/ppermute | solution.py:162
  33.2 1.7 %collective-permute-start.4 = (bf16[2,3,32,512]{3,2,1,0:T(8,128)(2,1)S(1)}, bf16[2,3,32,512]{3,2,1,0:T(8,128)(2,1)S(1)}, u32[]{:S(2)}, u32[]{:S(2)}) collective-permute-start(bf16[2,3,32,512]{3,2,1,0:T(8,128)(2,1)S(1)} %collective-permute-done.2), channel_id=1, source_target_pairs={{0,4},{1,5},{4,8},{5,9},{8,12},{9,13},{12,14},{13,15},{14,10},{15,... | collective-permute-start | bytes 589832 | tf_op jit(solution)/shard_map/ppermute | solution.py:162
  35.3 3.6 %collective-permute-done.4 = bf16[2,3,32,512]{3,2,1,0:T(8,128)(2,1)S(1)} collective-permute-done((bf16[2,3,32,512]{3,2,1,0:T(8,128)(2,1)S(1)}, bf16[2,3,32,512]{3,2,1,0:T(8,128)(2,1)S(1)}, u32[]{:S(2)}, u32[]{:S(2)}) %collective-permute-start.4) | collective-permute-done | bytes 196640 | tf_op jit(solution)/shard_map/ppermute | solution.py:162
  38.9 1.9 %collective-permute-start.6 = (bf16[2,3,32,512]{3,2,1,0:T(8,128)(2,1)S(1)}, bf16[2,3,32,512]{3,2,1,0:T(8,128)(2,1)S(1)}, u32[]{:S(2)}, u32[]{:S(2)}) collective-permute-start(bf16[2,3,32,512]{3,2,1,0:T(8,128)(2,1)S(1)} %collective-permute-done.4), channel_id=1, source_target_pairs={{0,4},{1,5},{4,8},{5,9},{8,12},{9,13},{12,14},{13,15},{14,10},{15,... | collective-permute-start | bytes 589832 | tf_op jit(solution)/shard_map/ppermute | solution.py:162
  40.8 3.7 %collective-permute-done.6 = bf16[2,3,32,512]{3,2,1,0:T(8,128)(2,1)S(1)} collective-permute-done((bf16[2,3,32,512]{3,2,1,0:T(8,128)(2,1)S(1)}, bf16[2,3,32,512]{3,2,1,0:T(8,128)(2,1)S(1)}, u32[]{:S(2)}, u32[]{:S(2)}) %collective-permute-start.6) | collective-permute-done | bytes 196640 | tf_op jit(solution)/shard_map/ppermute | solution.py:162
  49.0 1.1 copy-done.5
  51.2 1.6 bitcast_dynamic-update-slice_fusion.1
  52.9 6.3 %shard_map.608 = (bf16[256,1024]{1,0:T(8,128)(2,1)S(1)}, f32[8,2,2,3,32,512]{5,4,3,2,1,0:T(8,128)}) custom-call(bf16[256,1024]{1,0:T(8,128)(2,1)S(1)} %get-tuple-element.50.q_ref, bf16[256,1024]{1,0:T(8,128)(2,1)S(1)} %get-tuple-element.66.k_ref, bf16[256,1024]{1,0:T(8,128)(2,1)S(1)} %get-tuple-element.46.v_ref, f32[256,6]{1,0:T(8,128)S(1)} %bitcast.182, ...), custom_call_target="tpu_custom_call" | custom-call | tf_op jit(solution)/shard_map/pallas_call | solution.py:114
  59.2 2.3 %constant_dynamic-slice_fusion.15 = (f32[1,1,2,3,32,512]{5,4,3,2,1,0:T(8,128)S(1)}, f32[1,1,2,3,32,512]{5,4,3,2,1,0:T(8,128)S(1)}, f32[1,1,2,3,32,512]{5,4,3,2,1...) fusion(f32[8,2,2,3,32,512]{5,4,3,2,1,0:T(8,128)} %get-tuple-ele, ...), kind=kLoop, calls=%fused_computation.82 | loop fusion | bytes 6291492 | tf_op jit(solution)/shard_map/dynamic_slice | solution.py:181
  64.1 1.9 %collective-permute-start.10 = (bf16[2,3,32,512]{3,2,1,0:T(8,128)(2,1)S(1)}, bf16[2,3,32,512]{3,2,1,0:T(8,128)(2,1)S(1)}, u32[]{:S(2)}, u32[]{:S(2)}) collective-permute-start(bf16[2,3,32,512]{3,2,1,0:T(8,128)(2,1)S(1)} %get-tuple-element.44), channel_id=1, source_target_pairs={{0,4},{1,5},{4,8},{5,9},{8,12},{9,13},{12,14},{13,15},{14,10},{15,... | collective-permute-start | bytes 589832 | tf_op jit(solution)/shard_map/ppermute | solution.py:190
  66.7 4.7 %collective-permute-done.10 = bf16[2,3,32,512]{3,2,1,0:T(8,128)(2,1)S(1)} collective-permute-done((bf16[2,3,32,512]{3,2,1,0:T(8,128)(2,1)S(1)}, bf16[2,3,32,512]{3,2,1,0:T(8,128)(2,1)S(1)}, u32[]{:S(2)}, u32[]{:S(2)}) %collective-permute-start.10) | collective-permute-done | bytes 196640 | tf_op jit(solution)/shard_map/ppermute | solution.py:190
  71.5 1.9 %collective-permute-start.12 = (bf16[2,3,32,512]{3,2,1,0:T(8,128)(2,1)S(1)}, bf16[2,3,32,512]{3,2,1,0:T(8,128)(2,1)S(1)}, u32[]{:S(2)}, u32[]{:S(2)}) collective-permute-start(bf16[2,3,32,512]{3,2,1,0:T(8,128)(2,1)S(1)} %fusion.11), channel_id=1, source_target_pairs={{0,4},{1,5},{4,8},{5,9},{8,12},{9,13},{12,14},{13,15},{14,10},{15,... | collective-permute-start | bytes 589832 | tf_op jit(solution)/shard_map/ppermute | solution.py:190
  73.8 4.1 %collective-permute-done.12 = bf16[2,3,32,512]{3,2,1,0:T(8,128)(2,1)S(1)} collective-permute-done((bf16[2,3,32,512]{3,2,1,0:T(8,128)(2,1)S(1)}, bf16[2,3,32,512]{3,2,1,0:T(8,128)(2,1)S(1)}, u32[]{:S(2)}, u32[]{:S(2)}) %collective-permute-start.12) | collective-permute-done | bytes 196640 | tf_op jit(solution)/shard_map/ppermute | solution.py:190
  78.1 1.8 %collective-permute-start.14 = (bf16[2,3,32,512]{3,2,1,0:T(8,128)(2,1)S(1)}, bf16[2,3,32,512]{3,2,1,0:T(8,128)(2,1)S(1)}, u32[]{:S(2)}, u32[]{:S(2)}) collective-permute-start(bf16[2,3,32,512]{3,2,1,0:T(8,128)(2,1)S(1)} %get-tuple-element.42), channel_id=1, source_target_pairs={{0,4},{1,5},{4,8},{5,9},{8,12},{9,13},{12,14},{13,15},{14,10},{15,... | collective-permute-start | bytes 589832 | tf_op jit(solution)/shard_map/ppermute | solution.py:190
  80.2 3.6 %collective-permute-done.14 = bf16[2,3,32,512]{3,2,1,0:T(8,128)(2,1)S(1)} collective-permute-done((bf16[2,3,32,512]{3,2,1,0:T(8,128)(2,1)S(1)}, bf16[2,3,32,512]{3,2,1,0:T(8,128)(2,1)S(1)}, u32[]{:S(2)}, u32[]{:S(2)}) %collective-permute-start.14) | collective-permute-done | bytes 196640 | tf_op jit(solution)/shard_map/ppermute | solution.py:190
  83.9 1.7 %collective-permute-done.20 = bf16[2,3,32,512]{3,2,1,0:T(8,128)(2,1)S(1)} collective-permute-done((bf16[2,3,32,512]{3,2,1,0:T(8,128)(2,1)S(1)}, bf16[2,3,32,512]{3,2,1,0:T(8,128)(2,1)S(1)}, u32[]{:S(2)}, u32[]{:S(2)}) %collective-permute-start.20) | collective-permute-done | bytes 196640 | tf_op jit(solution)/shard_map/ppermute | solution.py:194
  85.8 1.6 collective-permute-start.16
  87.9 3.6 %collective-permute-done.16 = bf16[2,3,32,512]{3,2,1,0:T(8,128)(2,1)S(1)} collective-permute-done((bf16[2,3,32,512]{3,2,1,0:T(8,128)(2,1)S(1)}, bf16[2,3,32,512]{3,2,1,0:T(8,128)(2,1)S(1)}, u32[]{:S(2)}, u32[]{:S(2)}) %collective-permute-start.16) | collective-permute-done | bytes 196640 | tf_op jit(solution)/shard_map/ppermute | solution.py:190
  91.5 1.6 collective-permute-done.22
  93.4 1.4 broadcast.73
  95.5 1.5 collective-permute-start.23
  97.6 5.4 %collective-permute-done.23 = bf16[2,3,32,512]{3,2,1,0:T(8,128)(2,1)S(1)} collective-permute-done((bf16[2,3,32,512]{3,2,1,0:T(8,128)(2,1)S(1)}, bf16[2,3,32,512]{3,2,1,0:T(8,128)(2,1)S(1)}, u32[]{:S(2)}, u32[]{:S(2)}) %collective-permute-start.23) | collective-permute-done | bytes 196640 | tf_op jit(solution)/shard_map/ppermute | solution.py:162
  103.0 1.5 collective-permute-start.25
  106.4 3.1 %collective-permute-done.25 = bf16[2,3,32,512]{3,2,1,0:T(8,128)(2,1)S(1)} collective-permute-done((bf16[2,3,32,512]{3,2,1,0:T(8,128)(2,1)S(1)}, bf16[2,3,32,512]{3,2,1,0:T(8,128)(2,1)S(1)}, u32[]{:S(2)}, u32[]{:S(2)}) %collective-permute-start.25) | collective-permute-done | bytes 196640 | tf_op jit(solution)/shard_map/ppermute | solution.py:162
  109.5 1.5 collective-permute-start.27
  113.0 2.3 %collective-permute-done.27 = bf16[2,3,32,512]{3,2,1,0:T(8,128)(2,1)S(1)} collective-permute-done((bf16[2,3,32,512]{3,2,1,0:T(8,128)(2,1)S(1)}, bf16[2,3,32,512]{3,2,1,0:T(8,128)(2,1)S(1)}, u32[]{:S(2)}, u32[]{:S(2)}) %collective-permute-start.27) | collective-permute-done | bytes 196640 | tf_op jit(solution)/shard_map/ppermute | solution.py:162
  115.2 1.5 collective-permute-start.29
  118.2 2.7 %collective-permute-done.29 = bf16[2,3,32,512]{3,2,1,0:T(8,128)(2,1)S(1)} collective-permute-done((bf16[2,3,32,512]{3,2,1,0:T(8,128)(2,1)S(1)}, bf16[2,3,32,512]{3,2,1,0:T(8,128)(2,1)S(1)}, u32[]{:S(2)}, u32[]{:S(2)}) %collective-permute-start.29) | collective-permute-done | bytes 196640 | tf_op jit(solution)/shard_map/ppermute | solution.py:162
  122.2 1.6 bitcast_dynamic-update-slice_fusion
  123.8 1.6 collective-permute-done.30
  125.4 1.6 bitcast_dynamic-update-slice_fusion.3
  127.0 6.3 %shard_map.609 = (bf16[256,1024]{1,0:T(8,128)(2,1)S(1)}, f32[8,2,2,3,32,512]{5,4,3,2,1,0:T(8,128)}) custom-call(bf16[256,1024]{1,0:T(8,128)(2,1)S(1)} %get-tuple-element.51.q_ref, bf16[256,1024]{1,0:T(8,128)(2,1)S(1)} %get-tuple-element.65.k_ref, bf16[256,1024]{1,0:T(8,128)(2,1)S(1)} %get-tuple-element.47.v_ref, f32[256,6]{1,0:T(8,128)S(1)} %bitcast.183, ...), custom_call_target="tpu_custom_call" | custom-call | tf_op jit(solution)/shard_map/pallas_call | solution.py:114
  133.3 2.5 %constant_dynamic-slice_fusion.2 = (f32[1,1,2,3,32,512]{5,4,3,2,1,0:T(8,128)S(1)}, f32[1,1,2,3,32,512]{5,4,3,2,1,0:T(8,128)S(1)}, f32[1,1,2,3,32,512]{5,4,3,2,1,...) fusion(f32[8,2,2,3,32,512]{5,4,3,2,1,0:T(8,128)} %get-tuple-ele, ...), kind=kLoop, calls=%fused_computation.69 | loop fusion | bytes 6291492 | tf_op jit(solution)/shard_map/dynamic_slice | solution.py:181
  136.5 1.1 collective-permute-done.32
  138.3 1.6 collective-permute-start.33
  140.9 4.4 %collective-permute-done.33 = bf16[2,3,32,512]{3,2,1,0:T(8,128)(2,1)S(1)} collective-permute-done((bf16[2,3,32,512]{3,2,1,0:T(8,128)(2,1)S(1)}, bf16[2,3,32,512]{3,2,1,0:T(8,128)(2,1)S(1)}, u32[]{:S(2)}, u32[]{:S(2)}) %collective-permute-start.33) | collective-permute-done | bytes 196640 | tf_op jit(solution)/shard_map/ppermute | solution.py:190
  145.4 1.6 collective-permute-start.35
  147.5 4.1 %collective-permute-done.35 = bf16[2,3,32,512]{3,2,1,0:T(8,128)(2,1)S(1)} collective-permute-done((bf16[2,3,32,512]{3,2,1,0:T(8,128)(2,1)S(1)}, bf16[2,3,32,512]{3,2,1,0:T(8,128)(2,1)S(1)}, u32[]{:S(2)}, u32[]{:S(2)}) %collective-permute-start.35) | collective-permute-done | bytes 196640 | tf_op jit(solution)/shard_map/ppermute | solution.py:190
  151.8 1.6 collective-permute-start.37
  153.8 3.6 %collective-permute-done.37 = bf16[2,3,32,512]{3,2,1,0:T(8,128)(2,1)S(1)} collective-permute-done((bf16[2,3,32,512]{3,2,1,0:T(8,128)(2,1)S(1)}, bf16[2,3,32,512]{3,2,1,0:T(8,128)(2,1)S(1)}, u32[]{:S(2)}, u32[]{:S(2)}) %collective-permute-start.37) | collective-permute-done | bytes 196640 | tf_op jit(solution)/shard_map/ppermute | solution.py:190
  157.5 1.5 collective-permute-done.43
  159.2 1.6 collective-permute-start.39
  161.3 1.1 pad_maximum_fusion
  162.3 2.6 %collective-permute-done.39 = bf16[2,3,32,512]{3,2,1,0:T(8,128)(2,1)S(1)} collective-permute-done((bf16[2,3,32,512]{3,2,1,0:T(8,128)(2,1)S(1)}, bf16[2,3,32,512]{3,2,1,0:T(8,128)(2,1)S(1)}, u32[]{:S(2)}, u32[]{:S(2)}) %collective-permute-start.39) | collective-permute-done | bytes 196640 | tf_op jit(solution)/shard_map/ppermute | solution.py:190
  164.9 1.6 collective-permute-done.45
  166.8 0.8 broadcast_multiply_fusion
  (115 shorter events, 22.0 us)
Async XLA Ops:
  1.7 25.1 %collective-permute-start = (bf16[2,3,32,512]{3,2,1,0:T(8,128)(2,1)S(1)}, bf16[2,3,32,512]{3,2,1,0:T(8,128)(2,1)S(1)}, u32[]{:S(2)}, u32[]{:S(2)}) collective-permute-start(bf16[2,3,32,512]{3,2,1,0:T(8,128)(2,1)S(1)} %get-tuple-element.17), channel_id=1, source_target_pairs={{0,4},{1,5},{4,8},{5,9},{8,12},{9,13},{12,14},{13,15},{14,10},{15,... | collective-permute-start | bytes 589832 | tf_op jit(solution)/shard_map/ppermute | solution.py:162
  4.8 24.0 %collective-permute-start.1 = (bf16[2,3,32,512]{3,2,1,0:T(8,128)(2,1)S(1)}, bf16[2,3,32,512]{3,2,1,0:T(8,128)(2,1)S(1)}, u32[]{:S(2)}, u32[]{:S(2)}) collective-permute-start(bf16[2,3,32,512]{3,2,1,0:T(8,128)(2,1)S(1)} %get-tuple-element.17), channel_id=1, source_target_pairs={{0,2},{1,3},{4,0},{5,1},{8,4},{9,5},{12,8},{13,9},{14,12},{15,13},... | collective-permute-start | bytes 589832 | tf_op jit(solution)/shard_map/ppermute | solution.py:165
  6.1 41.3 %copy-start.8 = (f32[2,3,2,256]{3,2,1,0:T(2,128)S(1)}, f32[2,3,2,256]{3,2,1,0:T(2,128)}, u32[]{:S(2)}) copy-start(f32[2,3,2,256]{3,2,1,0:T(2,128)} %param.68) | copy-start | bytes 36868
  10.0 38.8 %copy-start.4 = (bf16[2,256,1024]{2,1,0:T(8,128)(2,1)S(1)}, bf16[2,256,1024]{2,1,0:T(8,128)(2,1)}, u32[]{:S(2)}) copy-start(bf16[2,256,1024]{2,1,0:T(8,128)(2,1)} %param.65) | copy-start | bytes 3145732
  26.8 6.4 %collective-permute-start.2 = (bf16[2,3,32,512]{3,2,1,0:T(8,128)(2,1)S(1)}, bf16[2,3,32,512]{3,2,1,0:T(8,128)(2,1)S(1)}, u32[]{:S(2)}, u32[]{:S(2)}) collective-permute-start(bf16[2,3,32,512]{3,2,1,0:T(8,128)(2,1)S(1)} %collective-permute-done), channel_id=1, source_target_pairs={{0,4},{1,5},{4,8},{5,9},{8,12},{9,13},{12,14},{13,15},{14,10},{15,... | collective-permute-start | bytes 589832 | tf_op jit(solution)/shard_map/ppermute | solution.py:162
  28.8 6.1 %collective-permute-start.3 = (bf16[2,3,32,512]{3,2,1,0:T(8,128)(2,1)S(1)}, bf16[2,3,32,512]{3,2,1,0:T(8,128)(2,1)S(1)}, u32[]{:S(2)}, u32[]{:S(2)}) collective-permute-start(bf16[2,3,32,512]{3,2,1,0:T(8,128)(2,1)S(1)} %collective-permute-done.1), channel_id=1, source_target_pairs={{0,2},{1,3},{4,0},{5,1},{8,4},{9,5},{12,8},{13,9},{14,12},{15,13},... | collective-permute-start | bytes 589832 | tf_op jit(solution)/shard_map/ppermute | solution.py:165
  33.2 5.7 %collective-permute-start.4 = (bf16[2,3,32,512]{3,2,1,0:T(8,128)(2,1)S(1)}, bf16[2,3,32,512]{3,2,1,0:T(8,128)(2,1)S(1)}, u32[]{:S(2)}, u32[]{:S(2)}) collective-permute-start(bf16[2,3,32,512]{3,2,1,0:T(8,128)(2,1)S(1)} %collective-permute-done.2), channel_id=1, source_target_pairs={{0,4},{1,5},{4,8},{5,9},{8,12},{9,13},{12,14},{13,15},{14,10},{15,... | collective-permute-start | bytes 589832 | tf_op jit(solution)/shard_map/ppermute | solution.py:162
  34.9 5.8 %collective-permute-start.5 = (bf16[2,3,32,512]{3,2,1,0:T(8,128)(2,1)S(1)}, bf16[2,3,32,512]{3,2,1,0:T(8,128)(2,1)S(1)}, u32[]{:S(2)}, u32[]{:S(2)}) collective-permute-start(bf16[2,3,32,512]{3,2,1,0:T(8,128)(2,1)S(1)} %collective-permute-done.3), channel_id=1, source_target_pairs={{0,2},{1,3},{4,0},{5,1},{8,4},{9,5},{12,8},{13,9},{14,12},{15,13},... | collective-permute-start | bytes 589832 | tf_op jit(solution)/shard_map/ppermute | solution.py:165
  38.9 5.7 %collective-permute-start.6 = (bf16[2,3,32,512]{3,2,1,0:T(8,128)(2,1)S(1)}, bf16[2,3,32,512]{3,2,1,0:T(8,128)(2,1)S(1)}, u32[]{:S(2)}, u32[]{:S(2)}) collective-permute-start(bf16[2,3,32,512]{3,2,1,0:T(8,128)(2,1)S(1)} %collective-permute-done.4), channel_id=1, source_target_pairs={{0,4},{1,5},{4,8},{5,9},{8,12},{9,13},{12,14},{13,15},{14,10},{15,... | collective-permute-start | bytes 589832 | tf_op jit(solution)/shard_map/ppermute | solution.py:162
  44.5 6.7 %collective-permute-start.7 = (bf16[8,2,3,32,512]{4,3,0,2,1:T(8,128)(2,1)S(1)}, bf16[8,2,3,32,512]{4,3,0,2,1:T(8,128)(2,1)}, u32[]{:S(2)}, u32[]{:S(2)}) collective-permute-start(bf16[8,2,3,32,512]{4,3,0,2,1:T(8,128)(2,1)S(1)} %bitcast_dynamic-update-slice_fusion.12), channel_id=1, source_target_pairs={{0,1},{1,0},{2,3},{3,2},{4,5},{5,4},{6,7},{7,6},{8,9},{9,8},{10,11... | collective-permute-start | bytes 4718600 | tf_op jit(solution)/shard_map/ppermute | solution.py:167
  61.5 1.9 %collective-permute-start.17 = (f32[1,1,2,3,32,512]{5,4,3,2,1,0:T(8,128)S(1)}, f32[1,1,2,3,32,512]{5,4,3,2,1,0:T(8,128)S(1)}, u32[]{:S(2)}, u32[]{:S(2)}) collective-permute-start(f32[1,1,2,3,32,512]{5,4,3,2,1,0:T(8,128)S(1)} %get-tuple-element.35), channel_id=1, source_target_pairs={{0,1},{1,0},{2,3},{3,2},{4,5},{5,4},{6,7},{7,6},{8,9},{9,8},{10,11... | collective-permute-start | bytes 1179656 | tf_op jit(solution)/shard_map/ppermute | solution.py:182
  62.0 1.9 %collective-permute-start.9 = (f32[1,1,2,3,32,512]{5,4,3,2,1,0:T(8,128)S(1)}, f32[1,1,2,3,32,512]{5,4,3,2,1,0:T(8,128)S(1)}, u32[]{:S(2)}, u32[]{:S(2)}) collective-permute-start(f32[1,1,2,3,32,512]{5,4,3,2,1,0:T(8,128)S(1)} %get-tuple-element.39), channel_id=1, source_target_pairs={{0,1},{1,0},{2,3},{3,2},{4,5},{5,4},{6,7},{7,6},{8,9},{9,8},{10,11... | collective-permute-start | bytes 1179656 | tf_op jit(solution)/shard_map/ppermute | solution.py:182
  62.1 4.5 %collective-permute-start.11 = (f32[1,1,2,3,32,512]{5,4,3,2,1,0:T(8,128)S(1)}, f32[1,1,2,3,32,512]{5,4,3,2,1,0:T(8,128)S(1)}, u32[]{:S(2)}, u32[]{:S(2)}) collective-permute-start(f32[1,1,2,3,32,512]{5,4,3,2,1,0:T(8,128)S(1)} %get-tuple-element.38), channel_id=1, source_target_pairs={{0,1},{1,0},{2,3},{3,2},{4,5},{5,4},{6,7},{7,6},{8,9},{9,8},{10,11... | collective-permute-start | bytes 1179656 | tf_op jit(solution)/shard_map/ppermute | solution.py:182
  64.1 7.3 %collective-permute-start.10 = (bf16[2,3,32,512]{3,2,1,0:T(8,128)(2,1)S(1)}, bf16[2,3,32,512]{3,2,1,0:T(8,128)(2,1)S(1)}, u32[]{:S(2)}, u32[]{:S(2)}) collective-permute-start(bf16[2,3,32,512]{3,2,1,0:T(8,128)(2,1)S(1)} %get-tuple-element.44), channel_id=1, source_target_pairs={{0,4},{1,5},{4,8},{5,9},{8,12},{9,13},{12,14},{13,15},{14,10},{15,... | collective-permute-start | bytes 589832 | tf_op jit(solution)/shard_map/ppermute | solution.py:190
  66.0 7.3 %collective-permute-start.13 = (f32[1,1,2,3,32,512]{5,4,3,2,1,0:T(8,128)S(1)}, f32[1,1,2,3,32,512]{5,4,3,2,1,0:T(8,128)S(1)}, u32[]{:S(2)}, u32[]{:S(2)}) collective-permute-start(f32[1,1,2,3,32,512]{5,4,3,2,1,0:T(8,128)S(1)} %get-tuple-element.37), channel_id=1, source_target_pairs={{0,1},{1,0},{2,3},{3,2},{4,5},{5,4},{6,7},{7,6},{8,9},{9,8},{10,11... | collective-permute-start | bytes 1179656 | tf_op jit(solution)/shard_map/ppermute | solution.py:182
  66.1 7.8 %collective-permute-start.19 = (f32[1,1,2,3,32,512]{5,4,3,2,1,0:T(8,128)S(1)}, f32[1,1,2,3,32,512]{5,4,3,2,1,0:T(8,128)S(1)}, u32[]{:S(2)}, u32[]{:S(2)}) collective-permute-start(f32[1,1,2,3,32,512]{5,4,3,2,1,0:T(8,128)S(1)} %get-tuple-element.34), channel_id=1, source_target_pairs={{0,1},{1,0},{2,3},{3,2},{4,5},{5,4},{6,7},{7,6},{8,9},{9,8},{10,11... | collective-permute-start | bytes 1179656 | tf_op jit(solution)/shard_map/ppermute | solution.py:182
  66.5 7.3 %collective-permute-start.18 = (bf16[2,3,32,512]{3,2,1,0:T(8,128)(2,1)S(1)}, bf16[2,3,32,512]{3,2,1,0:T(8,128)(2,1)S(1)}, u32[]{:S(2)}, u32[]{:S(2)}) collective-permute-start(bf16[2,3,32,512]{3,2,1,0:T(8,128)(2,1)S(1)} %get-tuple-element.45), channel_id=1, source_target_pairs={{0,2},{1,3},{4,0},{5,1},{8,4},{9,5},{12,8},{13,9},{14,12},{15,13},... | collective-permute-start | bytes 589832 | tf_op jit(solution)/shard_map/ppermute | solution.py:194
  71.5 6.4 %collective-permute-start.12 = (bf16[2,3,32,512]{3,2,1,0:T(8,128)(2,1)S(1)}, bf16[2,3,32,512]{3,2,1,0:T(8,128)(2,1)S(1)}, u32[]{:S(2)}, u32[]{:S(2)}) collective-permute-start(bf16[2,3,32,512]{3,2,1,0:T(8,128)(2,1)S(1)} %fusion.11), channel_id=1, source_target_pairs={{0,4},{1,5},{4,8},{5,9},{8,12},{9,13},{12,14},{13,15},{14,10},{15,... | collective-permute-start | bytes 589832 | tf_op jit(solution)/shard_map/ppermute | solution.py:190
  73.3 6.9 %collective-permute-start.15 = (f32[1,1,2,3,32,512]{5,4,3,2,1,0:T(8,128)S(1)}, f32[1,1,2,3,32,512]{5,4,3,2,1,0:T(8,128)S(1)}, u32[]{:S(2)}, u32[]{:S(2)}) collective-permute-start(f32[1,1,2,3,32,512]{5,4,3,2,1,0:T(8,128)S(1)} %get-tuple-element.36), channel_id=1, source_target_pairs={{0,1},{1,0},{2,3},{3,2},{4,5},{5,4},{6,7},{7,6},{8,9},{9,8},{10,11... | collective-permute-start | bytes 1179656 | tf_op jit(solution)/shard_map/ppermute | solution.py:182
  73.3 6.9 %collective-permute-start.21 = (f32[1,1,2,3,32,512]{5,4,3,2,1,0:T(8,128)S(1)}, f32[1,1,2,3,32,512]{5,4,3,2,1,0:T(8,128)S(1)}, u32[]{:S(2)}, u32[]{:S(2)}) collective-permute-start(f32[1,1,2,3,32,512]{5,4,3,2,1,0:T(8,128)S(1)} %get-tuple-element.33), channel_id=1, source_target_pairs={{0,1},{1,0},{2,3},{3,2},{4,5},{5,4},{6,7},{7,6},{8,9},{9,8},{10,11... | collective-permute-start | bytes 1179656 | tf_op jit(solution)/shard_map/ppermute | solution.py:182
  78.1 5.7 %collective-permute-start.14 = (bf16[2,3,32,512]{3,2,1,0:T(8,128)(2,1)S(1)}, bf16[2,3,32,512]{3,2,1,0:T(8,128)(2,1)S(1)}, u32[]{:S(2)}, u32[]{:S(2)}) collective-permute-start(bf16[2,3,32,512]{3,2,1,0:T(8,128)(2,1)S(1)} %get-tuple-element.42), channel_id=1, source_target_pairs={{0,4},{1,5},{4,8},{5,9},{8,12},{9,13},{12,14},{13,15},{14,10},{15,... | collective-permute-start | bytes 589832 | tf_op jit(solution)/shard_map/ppermute | solution.py:190
  79.9 5.7 %collective-permute-start.20 = (bf16[2,3,32,512]{3,2,1,0:T(8,128)(2,1)S(1)}, bf16[2,3,32,512]{3,2,1,0:T(8,128)(2,1)S(1)}, u32[]{:S(2)}, u32[]{:S(2)}) collective-permute-start(bf16[2,3,32,512]{3,2,1,0:T(8,128)(2,1)S(1)} %get-tuple-element.43), channel_id=1, source_target_pairs={{0,2},{1,3},{4,0},{5,1},{8,4},{9,5},{12,8},{13,9},{14,12},{15,13},... | collective-permute-start | bytes 589832 | tf_op jit(solution)/shard_map/ppermute | solution.py:194
  80.2 7.7 %collective-permute-start.8 = (f32[1,1,2,3,32,512]{5,4,3,2,1,0:T(8,128)S(1)}, f32[1,1,2,3,32,512]{5,4,3,2,1,0:T(8,128)S(1)}, u32[]{:S(2)}, u32[]{:S(2)}) collective-permute-start(f32[1,1,2,3,32,512]{5,4,3,2,1,0:T(8,128)S(1)} %get-tuple-element.32), channel_id=1, source_target_pairs={{0,1},{1,0},{2,3},{3,2},{4,5},{5,4},{6,7},{7,6},{8,9},{9,8},{10,11... | collective-permute-start | bytes 1179656 | tf_op jit(solution)/shard_map/ppermute | solution.py:182
  85.8 5.7 %collective-permute-start.16 = (bf16[2,3,32,512]{3,2,1,0:T(8,128)(2,1)S(1)}, bf16[2,3,32,512]{3,2,1,0:T(8,128)(2,1)S(1)}, u32[]{:S(2)}, u32[]{:S(2)}) collective-permute-start(bf16[2,3,32,512]{3,2,1,0:T(8,128)(2,1)S(1)} %get-tuple-element.40), channel_id=1, source_target_pairs={{0,4},{1,5},{4,8},{5,9},{8,12},{9,13},{12,14},{13,15},{14,10},{15,... | collective-permute-start | bytes 589832 | tf_op jit(solution)/shard_map/ppermute | solution.py:190
  87.4 5.7 %collective-permute-start.22 = (bf16[2,3,32,512]{3,2,1,0:T(8,128)(2,1)S(1)}, bf16[2,3,32,512]{3,2,1,0:T(8,128)(2,1)S(1)}, u32[]{:S(2)}, u32[]{:S(2)}) collective-permute-start(bf16[2,3,32,512]{3,2,1,0:T(8,128)(2,1)S(1)} %get-tuple-element.41), channel_id=1, source_target_pairs={{0,2},{1,3},{4,0},{5,1},{8,4},{9,5},{12,8},{13,9},{14,12},{15,13},... | collective-permute-start | bytes 589832 | tf_op jit(solution)/shard_map/ppermute | solution.py:194
  95.5 7.4 %collective-permute-start.23 = (bf16[2,3,32,512]{3,2,1,0:T(8,128)(2,1)S(1)}, bf16[2,3,32,512]{3,2,1,0:T(8,128)(2,1)S(1)}, u32[]{:S(2)}, u32[]{:S(2)}) collective-permute-start(bf16[2,3,32,512]{3,2,1,0:T(8,128)(2,1)S(1)} %get-tuple-element.13), channel_id=1, source_target_pairs={{0,4},{1,5},{4,8},{5,9},{8,12},{9,13},{12,14},{13,15},{14,10},{15,... | collective-permute-start | bytes 589832 | tf_op jit(solution)/shard_map/ppermute | solution.py:162
  97.1 8.2 %collective-permute-start.24 = (bf16[2,3,32,512]{3,2,1,0:T(8,128)(2,1)S(1)}, bf16[2,3,32,512]{3,2,1,0:T(8,128)(2,1)S(1)}, u32[]{:S(2)}, u32[]{:S(2)}) collective-permute-start(bf16[2,3,32,512]{3,2,1,0:T(8,128)(2,1)S(1)} %get-tuple-element.13), channel_id=1, source_target_pairs={{0,2},{1,3},{4,0},{5,1},{8,4},{9,5},{12,8},{13,9},{14,12},{15,13},... | collective-permute-start | bytes 589832 | tf_op jit(solution)/shard_map/ppermute | solution.py:165
  103.0 6.6 %collective-permute-start.25 = (bf16[2,3,32,512]{3,2,1,0:T(8,128)(2,1)S(1)}, bf16[2,3,32,512]{3,2,1,0:T(8,128)(2,1)S(1)}, u32[]{:S(2)}, u32[]{:S(2)}) collective-permute-start(bf16[2,3,32,512]{3,2,1,0:T(8,128)(2,1)S(1)} %collective-permute-done.23), channel_id=1, source_target_pairs={{0,4},{1,5},{4,8},{5,9},{8,12},{9,13},{12,14},{13,15},{14,10},{15,... | collective-permute-start | bytes 589832 | tf_op jit(solution)/shard_map/ppermute | solution.py:162
  105.2 6.6 %collective-permute-start.26 = (bf16[2,3,32,512]{3,2,1,0:T(8,128)(2,1)S(1)}, bf16[2,3,32,512]{3,2,1,0:T(8,128)(2,1)S(1)}, u32[]{:S(2)}, u32[]{:S(2)}) collective-permute-start(bf16[2,3,32,512]{3,2,1,0:T(8,128)(2,1)S(1)} %collective-permute-done.24), channel_id=1, source_target_pairs={{0,2},{1,3},{4,0},{5,1},{8,4},{9,5},{12,8},{13,9},{14,12},{15,13},... | collective-permute-start | bytes 589832 | tf_op jit(solution)/shard_map/ppermute | solution.py:165
  109.5 5.7 %collective-permute-start.27 = (bf16[2,3,32,512]{3,2,1,0:T(8,128)(2,1)S(1)}, bf16[2,3,32,512]{3,2,1,0:T(8,128)(2,1)S(1)}, u32[]{:S(2)}, u32[]{:S(2)}) collective-permute-start(bf16[2,3,32,512]{3,2,1,0:T(8,128)(2,1)S(1)} %collective-permute-done.25), channel_id=1, source_target_pairs={{0,4},{1,5},{4,8},{5,9},{8,12},{9,13},{12,14},{13,15},{14,10},{15,... | collective-permute-start | bytes 589832 | tf_op jit(solution)/shard_map/ppermute | solution.py:162
  111.8 5.7 %collective-permute-start.28 = (bf16[2,3,32,512]{3,2,1,0:T(8,128)(2,1)S(1)}, bf16[2,3,32,512]{3,2,1,0:T(8,128)(2,1)S(1)}, u32[]{:S(2)}, u32[]{:S(2)}) collective-permute-start(bf16[2,3,32,512]{3,2,1,0:T(8,128)(2,1)S(1)} %collective-permute-done.26), channel_id=1, source_target_pairs={{0,2},{1,3},{4,0},{5,1},{8,4},{9,5},{12,8},{13,9},{14,12},{15,13},... | collective-permute-start | bytes 589832 | tf_op jit(solution)/shard_map/ppermute | solution.py:165
  115.2 5.7 %collective-permute-start.29 = (bf16[2,3,32,512]{3,2,1,0:T(8,128)(2,1)S(1)}, bf16[2,3,32,512]{3,2,1,0:T(8,128)(2,1)S(1)}, u32[]{:S(2)}, u32[]{:S(2)}) collective-permute-start(bf16[2,3,32,512]{3,2,1,0:T(8,128)(2,1)S(1)} %collective-permute-done.27), channel_id=1, source_target_pairs={{0,4},{1,5},{4,8},{5,9},{8,12},{9,13},{12,14},{13,15},{14,10},{15,... | collective-permute-start | bytes 589832 | tf_op jit(solution)/shard_map/ppermute | solution.py:162
  121.6 3.8 %collective-permute-start.30 = (bf16[8,2,3,32,512]{4,3,0,2,1:T(8,128)(2,1)}, bf16[8,2,3,32,512]{4,3,0,2,1:T(8,128)(2,1)}, u32[]{:S(2)}, u32[]{:S(2)}) collective-permute-start(bf16[8,2,3,32,512]{4,3,0,2,1:T(8,128)(2,1)} %bitcast_dynamic-update-slice_fusion.4), channel_id=1, source_target_pairs={{0,1},{1,0},{2,3},{3,2},{4,5},{5,4},{6,7},{7,6},{8,9},{9,8},{10,11... | collective-permute-start | bytes 4718600 | tf_op jit(solution)/shard_map/ppermute | solution.py:167
  135.8 1.8 %collective-permute-start.32 = (f32[1,1,2,3,32,512]{5,4,3,2,1,0:T(8,128)S(1)}, f32[1,1,2,3,32,512]{5,4,3,2,1,0:T(8,128)S(1)}, u32[]{:S(2)}, u32[]{:S(2)}) collective-permute-start(f32[1,1,2,3,32,512]{5,4,3,2,1,0:T(8,128)S(1)} %get-tuple-element.25), channel_id=1, source_target_pairs={{0,1},{1,0},{2,3},{3,2},{4,5},{5,4},{6,7},{7,6},{8,9},{9,8},{10,11... | collective-permute-start | bytes 1179656 | tf_op jit(solution)/shard_map/ppermute | solution.py:182
  136.0 2.2 %collective-permute-start.40 = (f32[1,1,2,3,32,512]{5,4,3,2,1,0:T(8,128)S(1)}, f32[1,1,2,3,32,512]{5,4,3,2,1,0:T(8,128)S(1)}, u32[]{:S(2)}, u32[]{:S(2)}) collective-permute-start(f32[1,1,2,3,32,512]{5,4,3,2,1,0:T(8,128)S(1)} %get-tuple-element.21), channel_id=1, source_target_pairs={{0,1},{1,0},{2,3},{3,2},{4,5},{5,4},{6,7},{7,6},{8,9},{9,8},{10,11... | collective-permute-start | bytes 1179656 | tf_op jit(solution)/shard_map/ppermute | solution.py:182
  136.4 4.5 %collective-permute-start.34 = (f32[1,1,2,3,32,512]{5,4,3,2,1,0:T(8,128)S(1)}, f32[1,1,2,3,32,512]{5,4,3,2,1,0:T(8,128)S(1)}, u32[]{:S(2)}, u32[]{:S(2)}) collective-permute-start(f32[1,1,2,3,32,512]{5,4,3,2,1,0:T(8,128)S(1)} %get-tuple-element.24), channel_id=1, source_target_pairs={{0,1},{1,0},{2,3},{3,2},{4,5},{5,4},{6,7},{7,6},{8,9},{9,8},{10,11... | collective-permute-start | bytes 1179656 | tf_op jit(solution)/shard_map/ppermute | solution.py:182
  138.3 7.0 %collective-permute-start.33 = (bf16[2,3,32,512]{3,2,1,0:T(8,128)(2,1)S(1)}, bf16[2,3,32,512]{3,2,1,0:T(8,128)(2,1)S(1)}, u32[]{:S(2)}, u32[]{:S(2)}) collective-permute-start(bf16[2,3,32,512]{3,2,1,0:T(8,128)(2,1)S(1)} %get-tuple-element.30), channel_id=1, source_target_pairs={{0,4},{1,5},{4,8},{5,9},{8,12},{9,13},{12,14},{13,15},{14,10},{15,... | collective-permute-start | bytes 589832 | tf_op jit(solution)/shard_map/ppermute | solution.py:190
  139.9 7.1 %collective-permute-start.36 = (f32[1,1,2,3,32,512]{5,4,3,2,1,0:T(8,128)S(1)}, f32[1,1,2,3,32,512]{5,4,3,2,1,0:T(8,128)S(1)}, u32[]{:S(2)}, u32[]{:S(2)}) collective-permute-start(f32[1,1,2,3,32,512]{5,4,3,2,1,0:T(8,128)S(1)} %get-tuple-element.23), channel_id=1, source_target_pairs={{0,1},{1,0},{2,3},{3,2},{4,5},{5,4},{6,7},{7,6},{8,9},{9,8},{10,11... | collective-permute-start | bytes 1179656 | tf_op jit(solution)/shard_map/ppermute | solution.py:182
  139.9 7.6 %collective-permute-start.42 = (f32[1,1,2,3,32,512]{5,4,3,2,1,0:T(8,128)S(1)}, f32[1,1,2,3,32,512]{5,4,3,2,1,0:T(8,128)S(1)}, u32[]{:S(2)}, u32[]{:S(2)}) collective-permute-start(f32[1,1,2,3,32,512]{5,4,3,2,1,0:T(8,128)S(1)} %get-tuple-element.20), channel_id=1, source_target_pairs={{0,1},{1,0},{2,3},{3,2},{4,5},{5,4},{6,7},{7,6},{8,9},{9,8},{10,11... | collective-permute-start | bytes 1179656 | tf_op jit(solution)/shard_map/ppermute | solution.py:182
  140.4 7.1 %collective-permute-start.41 = (bf16[2,3,32,512]{3,2,1,0:T(8,128)(2,1)S(1)}, bf16[2,3,32,512]{3,2,1,0:T(8,128)(2,1)S(1)}, u32[]{:S(2)}, u32[]{:S(2)}) collective-permute-start(bf16[2,3,32,512]{3,2,1,0:T(8,128)(2,1)S(1)} %get-tuple-element.31), channel_id=1, source_target_pairs={{0,2},{1,3},{4,0},{5,1},{8,4},{9,5},{12,8},{13,9},{14,12},{15,13},... | collective-permute-start | bytes 589832 | tf_op jit(solution)/shard_map/ppermute | solution.py:194
  145.4 6.1 %collective-permute-start.35 = (bf16[2,3,32,512]{3,2,1,0:T(8,128)(2,1)S(1)}, bf16[2,3,32,512]{3,2,1,0:T(8,128)(2,1)S(1)}, u32[]{:S(2)}, u32[]{:S(2)}) collective-permute-start(bf16[2,3,32,512]{3,2,1,0:T(8,128)(2,1)S(1)} %fusion.4), channel_id=1, source_target_pairs={{0,4},{1,5},{4,8},{5,9},{8,12},{9,13},{12,14},{13,15},{14,10},{15,... | collective-permute-start | bytes 589832 | tf_op jit(solution)/shard_map/ppermute | solution.py:190
  147.0 6.9 %collective-permute-start.38 = (f32[1,1,2,3,32,512]{5,4,3,2,1,0:T(8,128)S(1)}, f32[1,1,2,3,32,512]{5,4,3,2,1,0:T(8,128)S(1)}, u32[]{:S(2)}, u32[]{:S(2)}) collective-permute-start(f32[1,1,2,3,32,512]{5,4,3,2,1,0:T(8,128)S(1)} %get-tuple-element.22), channel_id=1, source_target_pairs={{0,1},{1,0},{2,3},{3,2},{4,5},{5,4},{6,7},{7,6},{8,9},{9,8},{10,11... | collective-permute-start | bytes 1179656 | tf_op jit(solution)/shard_map/ppermute | solution.py:182
  147.0 6.9 %collective-permute-start.44 = (f32[1,1,2,3,32,512]{5,4,3,2,1,0:T(8,128)S(1)}, f32[1,1,2,3,32,512]{5,4,3,2,1,0:T(8,128)S(1)}, u32[]{:S(2)}, u32[]{:S(2)}) collective-permute-start(f32[1,1,2,3,32,512]{5,4,3,2,1,0:T(8,128)S(1)} %get-tuple-element.19), channel_id=1, source_target_pairs={{0,1},{1,0},{2,3},{3,2},{4,5},{5,4},{6,7},{7,6},{8,9},{9,8},{10,11... | collective-permute-start | bytes 1179656 | tf_op jit(solution)/shard_map/ppermute | solution.py:182
  151.8 5.7 %collective-permute-start.37 = (bf16[2,3,32,512]{3,2,1,0:T(8,128)(2,1)S(1)}, bf16[2,3,32,512]{3,2,1,0:T(8,128)(2,1)S(1)}, u32[]{:S(2)}, u32[]{:S(2)}) collective-permute-start(bf16[2,3,32,512]{3,2,1,0:T(8,128)(2,1)S(1)} %get-tuple-element.28), channel_id=1, source_target_pairs={{0,4},{1,5},{4,8},{5,9},{8,12},{9,13},{12,14},{13,15},{14,10},{15,... | collective-permute-start | bytes 589832 | tf_op jit(solution)/shard_map/ppermute | solution.py:190
  153.3 5.7 %collective-permute-start.43 = (bf16[2,3,32,512]{3,2,1,0:T(8,128)(2,1)S(1)}, bf16[2,3,32,512]{3,2,1,0:T(8,128)(2,1)S(1)}, u32[]{:S(2)}, u32[]{:S(2)}) collective-permute-start(bf16[2,3,32,512]{3,2,1,0:T(8,128)(2,1)S(1)} %get-tuple-element.29), channel_id=1, source_target_pairs={{0,2},{1,3},{4,0},{5,1},{8,4},{9,5},{12,8},{13,9},{14,12},{15,13},... | collective-permute-start | bytes 589832 | tf_op jit(solution)/shard_map/ppermute | solution.py:194
  153.8 8.5 %collective-permute-start.31 = (f32[1,1,2,3,32,512]{5,4,3,2,1,0:T(8,128)S(1)}, f32[1,1,2,3,32,512]{5,4,3,2,1,0:T(8,128)S(1)}, u32[]{:S(2)}, u32[]{:S(2)}) collective-permute-start(f32[1,1,2,3,32,512]{5,4,3,2,1,0:T(8,128)S(1)} %get-tuple-element.18), channel_id=1, source_target_pairs={{0,1},{1,0},{2,3},{3,2},{4,5},{5,4},{6,7},{7,6},{8,9},{9,8},{10,11... | collective-permute-start | bytes 1179656 | tf_op jit(solution)/shard_map/ppermute | solution.py:182
  159.2 5.7 %collective-permute-start.39 = (bf16[2,3,32,512]{3,2,1,0:T(8,128)(2,1)S(1)}, bf16[2,3,32,512]{3,2,1,0:T(8,128)(2,1)S(1)}, u32[]{:S(2)}, u32[]{:S(2)}) collective-permute-start(bf16[2,3,32,512]{3,2,1,0:T(8,128)(2,1)S(1)} %get-tuple-element.26), channel_id=1, source_target_pairs={{0,4},{1,5},{4,8},{5,9},{8,12},{9,13},{12,14},{13,15},{14,10},{15,... | collective-permute-start | bytes 589832 | tf_op jit(solution)/shard_map/ppermute | solution.py:190
  160.8 5.7 %collective-permute-start.45 = (bf16[2,3,32,512]{3,2,1,0:T(8,128)(2,1)S(1)}, bf16[2,3,32,512]{3,2,1,0:T(8,128)(2,1)S(1)}, u32[]{:S(2)}, u32[]{:S(2)}) collective-permute-start(bf16[2,3,32,512]{3,2,1,0:T(8,128)(2,1)S(1)} %get-tuple-element.27), channel_id=1, source_target_pairs={{0,2},{1,3},{4,0},{5,1},{8,4},{9,5},{12,8},{13,9},{14,12},{15,13},... | collective-permute-start | bytes 589832 | tf_op jit(solution)/shard_map/ppermute | solution.py:194
  (8 other events, 44.7 us)

commit v8 on v7

--- a/solution.py
+++ b/solution.py
@@ -153,11 +153,18 @@
     def gather(self, own):
         h, g, rows, f = own.shape
         core = lax.axis_index("tok") % 2
+        even = self.chips % 2 == 0
         ring = jnp.zeros((self.chips, h, g, rows, f), own.dtype)
         ring = lax.dynamic_update_index_in_dim(ring, own, lax.axis_index("tok") // 2, 0)
         a = own
         b = own
+        last = self.ncw if even else 0
         for k in range(1, max(self.ncw, self.nccw) + 1):
+            if k == last:
+                a = lax.ppermute(a[..., : f // 2], "tok", self.cw)
+                b = lax.ppermute(b[..., f // 2 :], "tok", self.ccw)
+                ring = lax.dynamic_update_index_in_dim(ring, jnp.concatenate([a, b], -1), self.chip_at(k), 0)
+                continue
             if k <= self.ncw:
                 a = lax.ppermute(a, "tok", self.cw)
                 ring = lax.dynamic_update_index_in_dim(ring, a, self.chip_at(-k), 0)
@@ -183,6 +190,27 @@
             return (keep + got).reshape(h, g, rows, f)
 
         total = chip_sum(0)
+        if self.chips % 2 == 0:
+            n = self.chips // 2
+            half = f // 2
+            far = chip_sum(n)
+            a = far[..., :half]
+            b = far[..., half:]
+            for k in range(1, n + 1):
+                a = lax.ppermute(a.astype(jnp.bfloat16), "tok", self.cw).astype(jnp.float32)
+                b = lax.ppermute(b.astype(jnp.bfloat16), "tok", self.ccw).astype(jnp.float32)
+                if k < n:
+                    near_a = chip_sum(n - k)
+                    near_b = chip_sum(k - n)
+                    if k == 1:
+                        a = jnp.concatenate([a + near_a[..., :half], near_a[..., half:]], -1)
+                        b = jnp.concatenate([near_b[..., :half], b + near_b[..., half:]], -1)
+                    else:
+                        a = a + near_a
+                        b = b + near_b
+            if n == 1:
+                return total + jnp.concatenate([a, b], -1)
+            return total + a + b
         a = chip_sum(self.ncw) if self.ncw else None
         b = chip_sum(-self.nccw) if self.nccw else None
         for k in range(1, max(self.ncw, self.nccw) + 1):

time: 168 us -> 165 us (0.982)
  between operations: 25.7 us -> 23 us
  waiting for transfers between devices: 66.9 us -> 64.5 us
  starting transfers between devices: 36.5 us -> 38.5 us
    ppermute x8, waiting for transfers between devices: 30.7 us -> 15.5 us  [reduce(): a = lax.ppermute(a.astype(jnp.bfloat16), 'tok', self.cw).astype(jnp.float32)]
    ppermute x6 -> x8, waiting for transfers between devices: 6.4 us -> 17.4 us  [reduce(): lax.ppermute(b.astype(jnp.bfloat16), 'tok', self.ccw).astype(jnp.float32)]
    ppermute x8 -> x6, waiting for transfers between devices: 25.1 us -> 17.8 us  [gather(): a = lax.ppermute(a, 'tok', self.cw)]
    ppermute x0 -> x4, waiting for transfers between devices: none -> 7.02 us  [the longest x2 4.48 us: gather(): b = lax.ppermute(b[..., f // 2:], 'tok', self.ccw)]
    ppermute x0 -> x4, starting transfers between devices: none -> 4.49 us  [the longest x2 3.47 us: gather(): a = lax.ppermute(a[..., :f // 2], 'tok', self.cw)]
    ppermute x8 -> x6, starting transfers between devices: 14.9 us -> 11.6 us  [gather(): a = lax.ppermute(a, 'tok', self.cw)]
    ppermute x6 -> x8, starting transfers between devices: 2.38 us -> 3.68 us  [reduce(): lax.ppermute(b.astype(jnp.bfloat16), 'tok', self.ccw).astype(jnp.float32)]
  transfers between devices with their start and end apart: 46 -> 50, of which waited for: 24 -> 34; matrix products, arithmetic and copies ran while one was open for 7% -> 7% of each run, Pallas kernels for 0% -> 0%
where the time goes in v8:
time: 165 us
  waiting for transfers between devices  64.5 us (39%)
  starting transfers between devices  38.5 us (23%)
  between operations  23 us (14%)
  local copies, waits for them, and re-layouts  20.8 us (13%)
  Pallas kernels  12.5 us (8%)
  other arithmetic  5.43 us (3%)
    ppermute x6, waiting for transfers between devices, gather(): a = lax.ppermute(a, 'tok', self.cw)  17.8 us
    ppermute x8, waiting for transfers between devices, reduce(): lax.ppermute(b.astype(jnp.bfloat16), 'tok', self.ccw).astype(jnp.float32)  17.4 us
    ppermute x8, waiting for transfers between devices, reduce(): a = lax.ppermute(a.astype(jnp.bfloat16), 'tok', self.cw).astype(jnp.float32)  15.5 us
    ppermute x8, starting transfers between devices, reduce(): a = lax.ppermute(a.astype(jnp.bfloat16), 'tok', self.cw).astype(jnp.float32)  13.1 us
    pallas_call x2, Pallas kernels, fused_block(): pl.pallas_call(_block_kernel, out_shape=(jax.ShapeDtypeStruct(query.shape...  12.5 us
    ppermute x6, starting transfers between devices, gather(): a = lax.ppermute(a, 'tok', self.cw)  11.6 us
    dynamic_slice x2, local copies, waits for them, and re-layouts, chip_sum(): lax.dynamic_slice(q, (chip, 1 - core, 0, 0, 0, 0), (1, 1, h, g, rows, f))  4.8 us
    ppermute x2, waiting for transfers between devices, gather(): b = lax.ppermute(b[..., f // 2:], 'tok', self.ccw)  4.48 us
  transfers between devices with their start and end apart: 50, of which 34 were waited for; matrix products, arithmetic and copies ran while one was open for 7% of the time, Pallas kernels for 0%

profile of v8, /device:TPU:0, one launch (start us, length us, event | category | flops | bytes accessed | tf_op | source)
XLA Modules:
  0.0 164.7 jit_solution(17532805771160843256)
XLA Ops:
  1.7 3.1 %collective-permute-start = (bf16[2,3,32,512]{3,2,1,0:T(8,128)(2,1)S(1)}, bf16[2,3,32,512]{3,2,1,0:T(8,128)(2,1)S(1)}, u32[]{:S(2)}, u32[]{:S(2)}) collective-permute-start(bf16[2,3,32,512]{3,2,1,0:T(8,128)(2,1)S(1)} %get-tuple-element.17), channel_id=1, source_target_pairs={{0,4},{1,5},{4,8},{5,9},{8,12},{9,13},{12,14},{13,15},{14,10},{15,... | collective-permute-start | bytes 589832 | tf_op jit(solution)/shard_map/ppermute | solution.py:169
  26.0 2.1 %collective-permute-start.2 = (bf16[2,3,32,512]{3,2,1,0:T(8,128)(2,1)S(1)}, bf16[2,3,32,512]{3,2,1,0:T(8,128)(2,1)S(1)}, u32[]{:S(2)}, u32[]{:S(2)}) collective-permute-start(bf16[2,3,32,512]{3,2,1,0:T(8,128)(2,1)S(1)} %collective-permute-done), channel_id=1, source_target_pairs={{0,4},{1,5},{4,8},{5,9},{8,12},{9,13},{12,14},{13,15},{14,10},{15,... | collective-permute-start | bytes 589832 | tf_op jit(solution)/shard_map/ppermute | solution.py:169
  28.2 4.3 %collective-permute-done.2 = bf16[2,3,32,512]{3,2,1,0:T(8,128)(2,1)S(1)} collective-permute-done((bf16[2,3,32,512]{3,2,1,0:T(8,128)(2,1)S(1)}, bf16[2,3,32,512]{3,2,1,0:T(8,128)(2,1)S(1)}, u32[]{:S(2)}, u32[]{:S(2)}) %collective-permute-start.2) | collective-permute-done | bytes 196640 | tf_op jit(solution)/shard_map/ppermute | solution.py:169
  32.4 1.7 %collective-permute-start.4 = (bf16[2,3,32,512]{3,2,1,0:T(8,128)(2,1)S(1)}, bf16[2,3,32,512]{3,2,1,0:T(8,128)(2,1)S(1)}, u32[]{:S(2)}, u32[]{:S(2)}) collective-permute-start(bf16[2,3,32,512]{3,2,1,0:T(8,128)(2,1)S(1)} %collective-permute-done.2), channel_id=1, source_target_pairs={{0,4},{1,5},{4,8},{5,9},{8,12},{9,13},{12,14},{13,15},{14,10},{15,... | collective-permute-start | bytes 589832 | tf_op jit(solution)/shard_map/ppermute | solution.py:169
  34.5 3.6 %collective-permute-done.4 = bf16[2,3,32,512]{3,2,1,0:T(8,128)(2,1)S(1)} collective-permute-done((bf16[2,3,32,512]{3,2,1,0:T(8,128)(2,1)S(1)}, bf16[2,3,32,512]{3,2,1,0:T(8,128)(2,1)S(1)}, u32[]{:S(2)}, u32[]{:S(2)}) %collective-permute-start.4) | collective-permute-done | bytes 196640 | tf_op jit(solution)/shard_map/ppermute | solution.py:169
  38.1 1.9 %collective-permute-start.6 = (bf16[2,3,32,256]{3,2,1,0:T(8,128)(2,1)S(1)}, bf16[2,3,32,256]{3,2,1,0:T(8,128)(2,1)S(1)}, u32[]{:S(2)}, u32[]{:S(2)}) collective-permute-start(bf16[2,3,32,256]{3,2,1,0:T(8,128)(2,1)S(1)} %slice.104), channel_id=1, source_target_pairs={{0,4},{1,5},{4,8},{5,9},{8,12},{9,13},{12,14},{13,15},{14,10},{15,... | collective-permute-start | bytes 294920 | tf_op jit(solution)/shard_map/ppermute | solution.py:164
  40.3 2.5 %collective-permute-done.6 = bf16[2,3,32,256]{3,2,1,0:T(8,128)(2,1)S(1)} collective-permute-done((bf16[2,3,32,256]{3,2,1,0:T(8,128)(2,1)S(1)}, bf16[2,3,32,256]{3,2,1,0:T(8,128)(2,1)S(1)}, u32[]{:S(2)}, u32[]{:S(2)}) %collective-permute-start.6) | collective-permute-done | bytes 98336 | tf_op jit(solution)/shard_map/ppermute | solution.py:164
  42.8 1.9 %collective-permute-done.7 = bf16[2,3,32,256]{3,2,1,0:T(8,128)(2,1)S(1)} collective-permute-done((bf16[2,3,32,256]{3,2,1,0:T(8,128)(2,1)S(1)}, bf16[2,3,32,256]{3,2,1,0:T(8,128)(2,1)S(1)}, u32[]{:S(2)}, u32[]{:S(2)}) %collective-permute-start.7) | collective-permute-done | bytes 98336 | tf_op jit(solution)/shard_map/ppermute | solution.py:165
  47.0 1.1 copy-done.5
  49.3 1.6 bitcast_dynamic-update-slice_fusion.1
  50.9 6.3 %shard_map.608 = (bf16[256,1024]{1,0:T(8,128)(2,1)S(1)}, f32[8,2,2,3,32,512]{5,4,3,2,1,0:T(8,128)}) custom-call(bf16[256,1024]{1,0:T(8,128)(2,1)S(1)} %get-tuple-element.52.q_ref, bf16[256,1024]{1,0:T(8,128)(2,1)S(1)} %get-tuple-element.71.k_ref, bf16[256,1024]{1,0:T(8,128)(2,1)S(1)} %get-tuple-element.48.v_ref, f32[256,6]{1,0:T(8,128)S(1)} %bitcast.180, ...), custom_call_target="tpu_custom_call" | custom-call | tf_op jit(solution)/shard_map/pallas_call | solution.py:114
  57.2 2.3 %constant_dynamic-slice_fusion.15 = (f32[1,1,2,3,32,512]{5,4,3,2,1,0:T(8,128)S(1)}, f32[1,1,2,3,32,512]{5,4,3,2,1,0:T(8,128)S(1)}, f32[1,1,2,3,32,512]{5,4,3,2,1...) fusion(f32[8,2,2,3,32,512]{5,4,3,2,1,0:T(8,128)} %get-tuple-ele, ...), kind=kLoop, calls=%fused_computation.96 | loop fusion | bytes 6291492 | tf_op jit(solution)/shard_map/dynamic_slice | solution.py:188
  63.6 1.9 %collective-permute-start.11 = (bf16[2,3,32,256]{3,2,1,0:T(8,128)(2,1)S(1)}, bf16[2,3,32,256]{3,2,1,0:T(8,128)(2,1)S(1)}, u32[]{:S(2)}, u32[]{:S(2)}) collective-permute-start(bf16[2,3,32,256]{3,2,1,0:T(8,128)(2,1)S(1)} %get-tuple-element.58), channel_id=1, source_target_pairs={{0,4},{1,5},{4,8},{5,9},{8,12},{9,13},{12,14},{13,15},{14,10},{15,... | collective-permute-start | bytes 294920 | tf_op jit(solution)/shard_map/ppermute | solution.py:200
  65.5 2.4 %collective-permute-done.19 = bf16[2,3,32,256]{3,2,1,0:T(8,128)(2,1)S(1)} collective-permute-done((bf16[2,3,32,256]{3,2,1,0:T(8,128)(2,1)S(1)}, bf16[2,3,32,256]{3,2,1,0:T(8,128)(2,1)S(1)}, u32[]{:S(2)}, u32[]{:S(2)}) %collective-permute-start.19) | collective-permute-done | bytes 98336 | tf_op jit(solution)/shard_map/ppermute | solution.py:201
  68.6 1.7 %collective-permute-start.13 = (bf16[2,3,32,512]{3,2,1,0:T(8,128)(2,1)S(1)}, bf16[2,3,32,512]{3,2,1,0:T(8,128)(2,1)S(1)}, u32[]{:S(2)}, u32[]{:S(2)}) collective-permute-start(bf16[2,3,32,512]{3,2,1,0:T(8,128)(2,1)S(1)} %pad_maximum_fusion.1), channel_id=1, source_target_pairs={{0,4},{1,5},{4,8},{5,9},{8,12},{9,13},{12,14},{13,15},{14,10},{15,... | collective-permute-start | bytes 589832 | tf_op jit(solution)/shard_map/ppermute | solution.py:200
  70.9 3.5 %collective-permute-done.20 = bf16[2,3,32,512]{3,2,1,0:T(8,128)(2,1)S(1)} collective-permute-done((bf16[2,3,32,512]{3,2,1,0:T(8,128)(2,1)S(1)}, bf16[2,3,32,512]{3,2,1,0:T(8,128)(2,1)S(1)}, u32[]{:S(2)}, u32[]{:S(2)}) %collective-permute-start.20) | collective-permute-done | bytes 196640 | tf_op jit(solution)/shard_map/ppermute | solution.py:201
  75.1 1.5 collective-permute-start.15
  77.2 3.6 %collective-permute-done.15 = bf16[2,3,32,512]{3,2,1,0:T(8,128)(2,1)S(1)} collective-permute-done((bf16[2,3,32,512]{3,2,1,0:T(8,128)(2,1)S(1)}, bf16[2,3,32,512]{3,2,1,0:T(8,128)(2,1)S(1)}, u32[]{:S(2)}, u32[]{:S(2)}) %collective-permute-start.15) | collective-permute-done | bytes 196640 | tf_op jit(solution)/shard_map/ppermute | solution.py:200
  80.9 1.5 collective-permute-done.22
  82.6 1.6 collective-permute-start.17
  84.6 3.6 %collective-permute-done.17 = bf16[2,3,32,512]{3,2,1,0:T(8,128)(2,1)S(1)} collective-permute-done((bf16[2,3,32,512]{3,2,1,0:T(8,128)(2,1)S(1)}, bf16[2,3,32,512]{3,2,1,0:T(8,128)(2,1)S(1)}, u32[]{:S(2)}, u32[]{:S(2)}) %collective-permute-start.17) | collective-permute-done | bytes 196640 | tf_op jit(solution)/shard_map/ppermute | solution.py:200
  88.3 1.6 collective-permute-done.24
  90.1 1.4 broadcast.73
  92.3 1.5 collective-permute-start.25
  94.3 5.1 %collective-permute-done.25 = bf16[2,3,32,512]{3,2,1,0:T(8,128)(2,1)S(1)} collective-permute-done((bf16[2,3,32,512]{3,2,1,0:T(8,128)(2,1)S(1)}, bf16[2,3,32,512]{3,2,1,0:T(8,128)(2,1)S(1)}, u32[]{:S(2)}, u32[]{:S(2)}) %collective-permute-start.25) | collective-permute-done | bytes 196640 | tf_op jit(solution)/shard_map/ppermute | solution.py:169
  99.4 1.5 collective-permute-start.27
  102.9 2.8 %collective-permute-done.27 = bf16[2,3,32,512]{3,2,1,0:T(8,128)(2,1)S(1)} collective-permute-done((bf16[2,3,32,512]{3,2,1,0:T(8,128)(2,1)S(1)}, bf16[2,3,32,512]{3,2,1,0:T(8,128)(2,1)S(1)}, u32[]{:S(2)}, u32[]{:S(2)}) %collective-permute-start.27) | collective-permute-done | bytes 196640 | tf_op jit(solution)/shard_map/ppermute | solution.py:169
  105.7 1.5 collective-permute-start.29
  109.4 2.0 %collective-permute-done.29 = bf16[2,3,32,512]{3,2,1,0:T(8,128)(2,1)S(1)} collective-permute-done((bf16[2,3,32,512]{3,2,1,0:T(8,128)(2,1)S(1)}, bf16[2,3,32,512]{3,2,1,0:T(8,128)(2,1)S(1)}, u32[]{:S(2)}, u32[]{:S(2)}) %collective-permute-start.29) | collective-permute-done | bytes 196640 | tf_op jit(solution)/shard_map/ppermute | solution.py:169
  111.4 1.6 collective-permute-start.31
  116.1 2.6 %collective-permute-done.32 = bf16[2,3,32,256]{3,2,1,0:T(8,128)(2,1)S(1)} collective-permute-done((bf16[2,3,32,256]{3,2,1,0:T(8,128)(2,1)S(1)}, bf16[2,3,32,256]{3,2,1,0:T(8,128)(2,1)S(1)}, u32[]{:S(2)}, u32[]{:S(2)}) %collective-permute-start.32) | collective-permute-done | bytes 98336 | tf_op jit(solution)/shard_map/ppermute | solution.py:165
  119.9 1.6 bitcast_dynamic-update-slice_fusion
  121.5 1.6 collective-permute-done.33
  123.1 1.6 bitcast_dynamic-update-slice_fusion.3
  124.7 6.3 %shard_map.609 = (bf16[256,1024]{1,0:T(8,128)(2,1)S(1)}, f32[8,2,2,3,32,512]{5,4,3,2,1,0:T(8,128)}) custom-call(bf16[256,1024]{1,0:T(8,128)(2,1)S(1)} %get-tuple-element.53.q_ref, bf16[256,1024]{1,0:T(8,128)(2,1)S(1)} %get-tuple-element.70.k_ref, bf16[256,1024]{1,0:T(8,128)(2,1)S(1)} %get-tuple-element.49.v_ref, f32[256,6]{1,0:T(8,128)S(1)} %bitcast.181, ...), custom_call_target="tpu_custom_call" | custom-call | tf_op jit(solution)/shard_map/pallas_call | solution.py:114
  131.0 2.5 %constant_dynamic-slice_fusion.5 = (f32[1,1,2,3,32,512]{5,4,3,2,1,0:T(8,128)S(1)}, f32[1,1,2,3,32,512]{5,4,3,2,1,0:T(8,128)S(1)}, f32[1,1,2,3,32,512]{5,4,3,2,1,...) fusion(f32[8,2,2,3,32,512]{5,4,3,2,1,0:T(8,128)} %get-tuple-ele, ...), kind=kLoop, calls=%fused_computation.86 | loop fusion | bytes 6291492 | tf_op jit(solution)/shard_map/dynamic_slice | solution.py:188
  134.2 1.1 collective-permute-done.35
  137.8 1.6 collective-permute-start.36
  139.3 2.2 %collective-permute-done.44 = bf16[2,3,32,256]{3,2,1,0:T(8,128)(2,1)S(1)} collective-permute-done((bf16[2,3,32,256]{3,2,1,0:T(8,128)(2,1)S(1)}, bf16[2,3,32,256]{3,2,1,0:T(8,128)(2,1)S(1)}, u32[]{:S(2)}, u32[]{:S(2)}) %collective-permute-start.44) | collective-permute-done | bytes 98336 | tf_op jit(solution)/shard_map/ppermute | solution.py:201
  142.6 1.6 collective-permute-start.38
  144.7 3.1 %collective-permute-done.45 = bf16[2,3,32,512]{3,2,1,0:T(8,128)(2,1)S(1)} collective-permute-done((bf16[2,3,32,512]{3,2,1,0:T(8,128)(2,1)S(1)}, bf16[2,3,32,512]{3,2,1,0:T(8,128)(2,1)S(1)}, u32[]{:S(2)}, u32[]{:S(2)}) %collective-permute-start.45) | collective-permute-done | bytes 196640 | tf_op jit(solution)/shard_map/ppermute | solution.py:201
  148.8 1.6 collective-permute-start.40
  150.9 3.6 %collective-permute-done.40 = bf16[2,3,32,512]{3,2,1,0:T(8,128)(2,1)S(1)} collective-permute-done((bf16[2,3,32,512]{3,2,1,0:T(8,128)(2,1)S(1)}, bf16[2,3,32,512]{3,2,1,0:T(8,128)(2,1)S(1)}, u32[]{:S(2)}, u32[]{:S(2)}) %collective-permute-start.40) | collective-permute-done | bytes 196640 | tf_op jit(solution)/shard_map/ppermute | solution.py:200
  154.5 1.5 collective-permute-done.47
  156.2 1.7 %collective-permute-start.42 = (bf16[2,3,32,512]{3,2,1,0:T(8,128)(2,1)S(1)}, bf16[2,3,32,512]{3,2,1,0:T(8,128)(2,1)S(1)}, u32[]{:S(2)}, u32[]{:S(2)}) collective-permute-start(bf16[2,3,32,512]{3,2,1,0:T(8,128)(2,1)S(1)} %get-tuple-element.26), channel_id=1, source_target_pairs={{0,4},{1,5},{4,8},{5,9},{8,12},{9,13},{12,14},{13,15},{14,10},{15,... | collective-permute-start | bytes 589832 | tf_op jit(solution)/shard_map/ppermute | solution.py:200
  158.3 1.1 pad_maximum_fusion
  159.4 2.6 %collective-permute-done.42 = bf16[2,3,32,512]{3,2,1,0:T(8,128)(2,1)S(1)} collective-permute-done((bf16[2,3,32,512]{3,2,1,0:T(8,128)(2,1)S(1)}, bf16[2,3,32,512]{3,2,1,0:T(8,128)(2,1)S(1)}, u32[]{:S(2)}, u32[]{:S(2)}) %collective-permute-start.42) | collective-permute-done | bytes 196640 | tf_op jit(solution)/shard_map/ppermute | solution.py:200
  162.0 1.6 collective-permute-done.49
  (139 shorter events, 29.6 us)
Async XLA Ops:
  1.7 24.3 %collective-permute-start = (bf16[2,3,32,512]{3,2,1,0:T(8,128)(2,1)S(1)}, bf16[2,3,32,512]{3,2,1,0:T(8,128)(2,1)S(1)}, u32[]{:S(2)}, u32[]{:S(2)}) collective-permute-start(bf16[2,3,32,512]{3,2,1,0:T(8,128)(2,1)S(1)} %get-tuple-element.17), channel_id=1, source_target_pairs={{0,4},{1,5},{4,8},{5,9},{8,12},{9,13},{12,14},{13,15},{14,10},{15,... | collective-permute-start | bytes 589832 | tf_op jit(solution)/shard_map/ppermute | solution.py:169
  4.8 23.3 %collective-permute-start.1 = (bf16[2,3,32,512]{3,2,1,0:T(8,128)(2,1)S(1)}, bf16[2,3,32,512]{3,2,1,0:T(8,128)(2,1)S(1)}, u32[]{:S(2)}, u32[]{:S(2)}) collective-permute-start(bf16[2,3,32,512]{3,2,1,0:T(8,128)(2,1)S(1)} %get-tuple-element.17), channel_id=1, source_target_pairs={{0,2},{1,3},{4,0},{5,1},{8,4},{9,5},{12,8},{13,9},{14,12},{15,13},... | collective-permute-start | bytes 589832 | tf_op jit(solution)/shard_map/ppermute | solution.py:172
  26.0 6.4 %collective-permute-start.2 = (bf16[2,3,32,512]{3,2,1,0:T(8,128)(2,1)S(1)}, bf16[2,3,32,512]{3,2,1,0:T(8,128)(2,1)S(1)}, u32[]{:S(2)}, u32[]{:S(2)}) collective-permute-start(bf16[2,3,32,512]{3,2,1,0:T(8,128)(2,1)S(1)} %collective-permute-done), channel_id=1, source_target_pairs={{0,4},{1,5},{4,8},{5,9},{8,12},{9,13},{12,14},{13,15},{14,10},{15,... | collective-permute-start | bytes 589832 | tf_op jit(solution)/shard_map/ppermute | solution.py:169
  28.1 6.1 %collective-permute-start.3 = (bf16[2,3,32,512]{3,2,1,0:T(8,128)(2,1)S(1)}, bf16[2,3,32,512]{3,2,1,0:T(8,128)(2,1)S(1)}, u32[]{:S(2)}, u32[]{:S(2)}) collective-permute-start(bf16[2,3,32,512]{3,2,1,0:T(8,128)(2,1)S(1)} %collective-permute-done.1), channel_id=1, source_target_pairs={{0,2},{1,3},{4,0},{5,1},{8,4},{9,5},{12,8},{13,9},{14,12},{15,13},... | collective-permute-start | bytes 589832 | tf_op jit(solution)/shard_map/ppermute | solution.py:172
  32.4 5.7 %collective-permute-start.4 = (bf16[2,3,32,512]{3,2,1,0:T(8,128)(2,1)S(1)}, bf16[2,3,32,512]{3,2,1,0:T(8,128)(2,1)S(1)}, u32[]{:S(2)}, u32[]{:S(2)}) collective-permute-start(bf16[2,3,32,512]{3,2,1,0:T(8,128)(2,1)S(1)} %collective-permute-done.2), channel_id=1, source_target_pairs={{0,4},{1,5},{4,8},{5,9},{8,12},{9,13},{12,14},{13,15},{14,10},{15,... | collective-permute-start | bytes 589832 | tf_op jit(solution)/shard_map/ppermute | solution.py:169
  34.2 5.8 %collective-permute-start.5 = (bf16[2,3,32,512]{3,2,1,0:T(8,128)(2,1)S(1)}, bf16[2,3,32,512]{3,2,1,0:T(8,128)(2,1)S(1)}, u32[]{:S(2)}, u32[]{:S(2)}) collective-permute-start(bf16[2,3,32,512]{3,2,1,0:T(8,128)(2,1)S(1)} %collective-permute-done.3), channel_id=1, source_target_pairs={{0,2},{1,3},{4,0},{5,1},{8,4},{9,5},{12,8},{13,9},{14,12},{15,13},... | collective-permute-start | bytes 589832 | tf_op jit(solution)/shard_map/ppermute | solution.py:172
  38.1 4.7 %collective-permute-start.6 = (bf16[2,3,32,256]{3,2,1,0:T(8,128)(2,1)S(1)}, bf16[2,3,32,256]{3,2,1,0:T(8,128)(2,1)S(1)}, u32[]{:S(2)}, u32[]{:S(2)}) collective-permute-start(bf16[2,3,32,256]{3,2,1,0:T(8,128)(2,1)S(1)} %slice.104), channel_id=1, source_target_pairs={{0,4},{1,5},{4,8},{5,9},{8,12},{9,13},{12,14},{13,15},{14,10},{15,... | collective-permute-start | bytes 294920 | tf_op jit(solution)/shard_map/ppermute | solution.py:164
  40.0 4.7 %collective-permute-start.7 = (bf16[2,3,32,256]{3,2,1,0:T(8,128)(2,1)S(1)}, bf16[2,3,32,256]{3,2,1,0:T(8,128)(2,1)S(1)}, u32[]{:S(2)}, u32[]{:S(2)}) collective-permute-start(bf16[2,3,32,256]{3,2,1,0:T(8,128)(2,1)S(1)} %slice.105), channel_id=1, source_target_pairs={{0,2},{1,3},{4,0},{5,1},{8,4},{9,5},{12,8},{13,9},{14,12},{15,13},... | collective-permute-start | bytes 294920 | tf_op jit(solution)/shard_map/ppermute | solution.py:165
  44.7 4.6 %collective-permute-start.8 = (bf16[8,2,3,32,512]{4,3,0,2,1:T(8,128)(2,1)S(1)}, bf16[8,2,3,32,512]{4,3,0,2,1:T(8,128)(2,1)}, u32[]{:S(2)}, u32[]{:S(2)}) collective-permute-start(bf16[8,2,3,32,512]{4,3,0,2,1:T(8,128)(2,1)S(1)} %fusion.18), channel_id=1, source_target_pairs={{0,1},{1,0},{2,3},{3,2},{4,5},{5,4},{6,7},{7,6},{8,9},{9,8},{10,11... | collective-permute-start | bytes 4718600 | tf_op jit(solution)/shard_map/ppermute | solution.py:174
  59.5 1.9 %collective-permute-start.10 = (f32[1,1,2,3,32,512]{5,4,3,2,1,0:T(8,128)S(1)}, f32[1,1,2,3,32,512]{5,4,3,2,1,0:T(8,128)S(1)}, u32[]{:S(2)}, u32[]{:S(2)}) collective-permute-start(f32[1,1,2,3,32,512]{5,4,3,2,1,0:T(8,128)S(1)} %get-tuple-element.40), channel_id=1, source_target_pairs={{0,1},{1,0},{2,3},{3,2},{4,5},{5,4},{6,7},{7,6},{8,9},{9,8},{10,11... | collective-permute-start | bytes 1179656 | tf_op jit(solution)/shard_map/ppermute | solution.py:189
  60.1 2.4 %collective-permute-start.18 = (f32[1,1,2,3,32,512]{5,4,3,2,1,0:T(8,128)S(1)}, f32[1,1,2,3,32,512]{5,4,3,2,1,0:T(8,128)S(1)}, u32[]{:S(2)}, u32[]{:S(2)}) collective-permute-start(f32[1,1,2,3,32,512]{5,4,3,2,1,0:T(8,128)S(1)} %get-tuple-element.36), channel_id=1, source_target_pairs={{0,1},{1,0},{2,3},{3,2},{4,5},{5,4},{6,7},{7,6},{8,9},{9,8},{10,11... | collective-permute-start | bytes 1179656 | tf_op jit(solution)/shard_map/ppermute | solution.py:189
  62.8 5.1 %collective-permute-start.19 = (bf16[2,3,32,256]{3,2,1,0:T(8,128)(2,1)S(1)}, bf16[2,3,32,256]{3,2,1,0:T(8,128)(2,1)S(1)}, u32[]{:S(2)}, u32[]{:S(2)}) collective-permute-start(bf16[2,3,32,256]{3,2,1,0:T(8,128)(2,1)S(1)} %get-tuple-element.59), channel_id=1, source_target_pairs={{0,2},{1,3},{4,0},{5,1},{8,4},{9,5},{12,8},{13,9},{14,12},{15,13},... | collective-permute-start | bytes 294920 | tf_op jit(solution)/shard_map/ppermute | solution.py:201
  63.1 7.3 %collective-permute-start.14 = (f32[1,1,2,3,32,512]{5,4,3,2,1,0:T(8,128)S(1)}, f32[1,1,2,3,32,512]{5,4,3,2,1,0:T(8,128)S(1)}, u32[]{:S(2)}, u32[]{:S(2)}) collective-permute-start(f32[1,1,2,3,32,512]{5,4,3,2,1,0:T(8,128)S(1)} %get-tuple-element.38), channel_id=1, source_target_pairs={{0,1},{1,0},{2,3},{3,2},{4,5},{5,4},{6,7},{7,6},{8,9},{9,8},{10,11... | collective-permute-start | bytes 1179656 | tf_op jit(solution)/shard_map/ppermute | solution.py:189
  63.3 7.6 %collective-permute-start.21 = (f32[1,1,2,3,32,512]{5,4,3,2,1,0:T(8,128)S(1)}, f32[1,1,2,3,32,512]{5,4,3,2,1,0:T(8,128)S(1)}, u32[]{:S(2)}, u32[]{:S(2)}) collective-permute-start(f32[1,1,2,3,32,512]{5,4,3,2,1,0:T(8,128)S(1)} %get-tuple-element.35), channel_id=1, source_target_pairs={{0,1},{1,0},{2,3},{3,2},{4,5},{5,4},{6,7},{7,6},{8,9},{9,8},{10,11... | collective-permute-start | bytes 1179656 | tf_op jit(solution)/shard_map/ppermute | solution.py:189
  63.6 5.0 %collective-permute-start.11 = (bf16[2,3,32,256]{3,2,1,0:T(8,128)(2,1)S(1)}, bf16[2,3,32,256]{3,2,1,0:T(8,128)(2,1)S(1)}, u32[]{:S(2)}, u32[]{:S(2)}) collective-permute-start(bf16[2,3,32,256]{3,2,1,0:T(8,128)(2,1)S(1)} %get-tuple-element.58), channel_id=1, source_target_pairs={{0,4},{1,5},{4,8},{5,9},{8,12},{9,13},{12,14},{13,15},{14,10},{15,... | collective-permute-start | bytes 294920 | tf_op jit(solution)/shard_map/ppermute | solution.py:200
  68.0 6.4 %collective-permute-start.20 = (bf16[2,3,32,512]{3,2,1,0:T(8,128)(2,1)S(1)}, bf16[2,3,32,512]{3,2,1,0:T(8,128)(2,1)S(1)}, u32[]{:S(2)}, u32[]{:S(2)}) collective-permute-start(bf16[2,3,32,512]{3,2,1,0:T(8,128)(2,1)S(1)} %pad_maximum_fusion.2), channel_id=1, source_target_pairs={{0,2},{1,3},{4,0},{5,1},{8,4},{9,5},{12,8},{13,9},{14,12},{15,13},... | collective-permute-start | bytes 589832 | tf_op jit(solution)/shard_map/ppermute | solution.py:201
  68.6 6.3 %collective-permute-start.13 = (bf16[2,3,32,512]{3,2,1,0:T(8,128)(2,1)S(1)}, bf16[2,3,32,512]{3,2,1,0:T(8,128)(2,1)S(1)}, u32[]{:S(2)}, u32[]{:S(2)}) collective-permute-start(bf16[2,3,32,512]{3,2,1,0:T(8,128)(2,1)S(1)} %pad_maximum_fusion.1), channel_id=1, source_target_pairs={{0,4},{1,5},{4,8},{5,9},{8,12},{9,13},{12,14},{13,15},{14,10},{15,... | collective-permute-start | bytes 589832 | tf_op jit(solution)/shard_map/ppermute | solution.py:200
  70.3 6.9 %collective-permute-start.16 = (f32[1,1,2,3,32,512]{5,4,3,2,1,0:T(8,128)S(1)}, f32[1,1,2,3,32,512]{5,4,3,2,1,0:T(8,128)S(1)}, u32[]{:S(2)}, u32[]{:S(2)}) collective-permute-start(f32[1,1,2,3,32,512]{5,4,3,2,1,0:T(8,128)S(1)} %get-tuple-element.37), channel_id=1, source_target_pairs={{0,1},{1,0},{2,3},{3,2},{4,5},{5,4},{6,7},{7,6},{8,9},{9,8},{10,11... | collective-permute-start | bytes 1179656 | tf_op jit(solution)/shard_map/ppermute | solution.py:189
  70.3 6.9 %collective-permute-start.23 = (f32[1,1,2,3,32,512]{5,4,3,2,1,0:T(8,128)S(1)}, f32[1,1,2,3,32,512]{5,4,3,2,1,0:T(8,128)S(1)}, u32[]{:S(2)}, u32[]{:S(2)}) collective-permute-start(f32[1,1,2,3,32,512]{5,4,3,2,1,0:T(8,128)S(1)} %get-tuple-element.34), channel_id=1, source_target_pairs={{0,1},{1,0},{2,3},{3,2},{4,5},{5,4},{6,7},{7,6},{8,9},{9,8},{10,11... | collective-permute-start | bytes 1179656 | tf_op jit(solution)/shard_map/ppermute | solution.py:189
  75.1 5.7 %collective-permute-start.15 = (bf16[2,3,32,512]{3,2,1,0:T(8,128)(2,1)S(1)}, bf16[2,3,32,512]{3,2,1,0:T(8,128)(2,1)S(1)}, u32[]{:S(2)}, u32[]{:S(2)}) collective-permute-start(bf16[2,3,32,512]{3,2,1,0:T(8,128)(2,1)S(1)} %get-tuple-element.43), channel_id=1, source_target_pairs={{0,4},{1,5},{4,8},{5,9},{8,12},{9,13},{12,14},{13,15},{14,10},{15,... | collective-permute-start | bytes 589832 | tf_op jit(solution)/shard_map/ppermute | solution.py:200
  76.7 5.7 %collective-permute-start.22 = (bf16[2,3,32,512]{3,2,1,0:T(8,128)(2,1)S(1)}, bf16[2,3,32,512]{3,2,1,0:T(8,128)(2,1)S(1)}, u32[]{:S(2)}, u32[]{:S(2)}) collective-permute-start(bf16[2,3,32,512]{3,2,1,0:T(8,128)(2,1)S(1)} %get-tuple-element.44), channel_id=1, source_target_pairs={{0,2},{1,3},{4,0},{5,1},{8,4},{9,5},{12,8},{13,9},{14,12},{15,13},... | collective-permute-start | bytes 589832 | tf_op jit(solution)/shard_map/ppermute | solution.py:201
  77.2 7.4 %collective-permute-start.9 = (f32[1,1,2,3,32,512]{5,4,3,2,1,0:T(8,128)S(1)}, f32[1,1,2,3,32,512]{5,4,3,2,1,0:T(8,128)S(1)}, u32[]{:S(2)}, u32[]{:S(2)}) collective-permute-start(f32[1,1,2,3,32,512]{5,4,3,2,1,0:T(8,128)S(1)} %get-tuple-element.33), channel_id=1, source_target_pairs={{0,1},{1,0},{2,3},{3,2},{4,5},{5,4},{6,7},{7,6},{8,9},{9,8},{10,11... | collective-permute-start | bytes 1179656 | tf_op jit(solution)/shard_map/ppermute | solution.py:189
  82.6 5.7 %collective-permute-start.17 = (bf16[2,3,32,512]{3,2,1,0:T(8,128)(2,1)S(1)}, bf16[2,3,32,512]{3,2,1,0:T(8,128)(2,1)S(1)}, u32[]{:S(2)}, u32[]{:S(2)}) collective-permute-start(bf16[2,3,32,512]{3,2,1,0:T(8,128)(2,1)S(1)} %get-tuple-element.41), channel_id=1, source_target_pairs={{0,4},{1,5},{4,8},{5,9},{8,12},{9,13},{12,14},{13,15},{14,10},{15,... | collective-permute-start | bytes 589832 | tf_op jit(solution)/shard_map/ppermute | solution.py:200
  84.2 5.7 %collective-permute-start.24 = (bf16[2,3,32,512]{3,2,1,0:T(8,128)(2,1)S(1)}, bf16[2,3,32,512]{3,2,1,0:T(8,128)(2,1)S(1)}, u32[]{:S(2)}, u32[]{:S(2)}) collective-permute-start(bf16[2,3,32,512]{3,2,1,0:T(8,128)(2,1)S(1)} %get-tuple-element.42), channel_id=1, source_target_pairs={{0,2},{1,3},{4,0},{5,1},{8,4},{9,5},{12,8},{13,9},{14,12},{15,13},... | collective-permute-start | bytes 589832 | tf_op jit(solution)/shard_map/ppermute | solution.py:201
  92.3 7.1 %collective-permute-start.25 = (bf16[2,3,32,512]{3,2,1,0:T(8,128)(2,1)S(1)}, bf16[2,3,32,512]{3,2,1,0:T(8,128)(2,1)S(1)}, u32[]{:S(2)}, u32[]{:S(2)}) collective-permute-start(bf16[2,3,32,512]{3,2,1,0:T(8,128)(2,1)S(1)} %get-tuple-element.13), channel_id=1, source_target_pairs={{0,4},{1,5},{4,8},{5,9},{8,12},{9,13},{12,14},{13,15},{14,10},{15,... | collective-permute-start | bytes 589832 | tf_op jit(solution)/shard_map/ppermute | solution.py:169
  93.8 7.9 %collective-permute-start.26 = (bf16[2,3,32,512]{3,2,1,0:T(8,128)(2,1)S(1)}, bf16[2,3,32,512]{3,2,1,0:T(8,128)(2,1)S(1)}, u32[]{:S(2)}, u32[]{:S(2)}) collective-permute-start(bf16[2,3,32,512]{3,2,1,0:T(8,128)(2,1)S(1)} %get-tuple-element.13), channel_id=1, source_target_pairs={{0,2},{1,3},{4,0},{5,1},{8,4},{9,5},{12,8},{13,9},{14,12},{15,13},... | collective-permute-start | bytes 589832 | tf_op jit(solution)/shard_map/ppermute | solution.py:172
  99.4 6.3 %collective-permute-start.27 = (bf16[2,3,32,512]{3,2,1,0:T(8,128)(2,1)S(1)}, bf16[2,3,32,512]{3,2,1,0:T(8,128)(2,1)S(1)}, u32[]{:S(2)}, u32[]{:S(2)}) collective-permute-start(bf16[2,3,32,512]{3,2,1,0:T(8,128)(2,1)S(1)} %collective-permute-done.25), channel_id=1, source_target_pairs={{0,4},{1,5},{4,8},{5,9},{8,12},{9,13},{12,14},{13,15},{14,10},{15,... | collective-permute-start | bytes 589832 | tf_op jit(solution)/shard_map/ppermute | solution.py:169
  101.7 6.4 %collective-permute-start.28 = (bf16[2,3,32,512]{3,2,1,0:T(8,128)(2,1)S(1)}, bf16[2,3,32,512]{3,2,1,0:T(8,128)(2,1)S(1)}, u32[]{:S(2)}, u32[]{:S(2)}) collective-permute-start(bf16[2,3,32,512]{3,2,1,0:T(8,128)(2,1)S(1)} %collective-permute-done.26), channel_id=1, source_target_pairs={{0,2},{1,3},{4,0},{5,1},{8,4},{9,5},{12,8},{13,9},{14,12},{15,13},... | collective-permute-start | bytes 589832 | tf_op jit(solution)/shard_map/ppermute | solution.py:172
  105.7 5.7 %collective-permute-start.29 = (bf16[2,3,32,512]{3,2,1,0:T(8,128)(2,1)S(1)}, bf16[2,3,32,512]{3,2,1,0:T(8,128)(2,1)S(1)}, u32[]{:S(2)}, u32[]{:S(2)}) collective-permute-start(bf16[2,3,32,512]{3,2,1,0:T(8,128)(2,1)S(1)} %collective-permute-done.27), channel_id=1, source_target_pairs={{0,4},{1,5},{4,8},{5,9},{8,12},{9,13},{12,14},{13,15},{14,10},{15,... | collective-permute-start | bytes 589832 | tf_op jit(solution)/shard_map/ppermute | solution.py:169
  108.1 5.7 %collective-permute-start.30 = (bf16[2,3,32,512]{3,2,1,0:T(8,128)(2,1)S(1)}, bf16[2,3,32,512]{3,2,1,0:T(8,128)(2,1)S(1)}, u32[]{:S(2)}, u32[]{:S(2)}) collective-permute-start(bf16[2,3,32,512]{3,2,1,0:T(8,128)(2,1)S(1)} %collective-permute-done.28), channel_id=1, source_target_pairs={{0,2},{1,3},{4,0},{5,1},{8,4},{9,5},{12,8},{13,9},{14,12},{15,13},... | collective-permute-start | bytes 589832 | tf_op jit(solution)/shard_map/ppermute | solution.py:172
  111.4 4.7 %collective-permute-start.31 = (bf16[2,3,32,256]{3,2,1,0:T(8,128)(2,1)S(1)}, bf16[2,3,32,256]{3,2,1,0:T(8,128)(2,1)S(1)}, u32[]{:S(2)}, u32[]{:S(2)}) collective-permute-start(bf16[2,3,32,256]{3,2,1,0:T(8,128)(2,1)S(1)} %slice.112), channel_id=1, source_target_pairs={{0,4},{1,5},{4,8},{5,9},{8,12},{9,13},{12,14},{13,15},{14,10},{15,... | collective-permute-start | bytes 294920 | tf_op jit(solution)/shard_map/ppermute | solution.py:164
  113.8 4.8 %collective-permute-start.32 = (bf16[2,3,32,256]{3,2,1,0:T(8,128)(2,1)S(1)}, bf16[2,3,32,256]{3,2,1,0:T(8,128)(2,1)S(1)}, u32[]{:S(2)}, u32[]{:S(2)}) collective-permute-start(bf16[2,3,32,256]{3,2,1,0:T(8,128)(2,1)S(1)} %slice.113), channel_id=1, source_target_pairs={{0,2},{1,3},{4,0},{5,1},{8,4},{9,5},{12,8},{13,9},{14,12},{15,13},... | collective-permute-start | bytes 294920 | tf_op jit(solution)/shard_map/ppermute | solution.py:165
  119.4 3.8 %collective-permute-start.33 = (bf16[8,2,3,32,512]{4,3,0,2,1:T(8,128)(2,1)}, bf16[8,2,3,32,512]{4,3,0,2,1:T(8,128)(2,1)}, u32[]{:S(2)}, u32[]{:S(2)}) collective-permute-start(bf16[8,2,3,32,512]{4,3,0,2,1:T(8,128)(2,1)} %fusion.19), channel_id=1, source_target_pairs={{0,1},{1,0},{2,3},{3,2},{4,5},{5,4},{6,7},{7,6},{8,9},{9,8},{10,11... | collective-permute-start | bytes 4718600 | tf_op jit(solution)/shard_map/ppermute | solution.py:174
  133.7 2.2 %collective-permute-start.37 = (f32[1,1,2,3,32,512]{5,4,3,2,1,0:T(8,128)S(1)}, f32[1,1,2,3,32,512]{5,4,3,2,1,0:T(8,128)S(1)}, u32[]{:S(2)}, u32[]{:S(2)}) collective-permute-start(f32[1,1,2,3,32,512]{5,4,3,2,1,0:T(8,128)S(1)} %get-tuple-element.24), channel_id=1, source_target_pairs={{0,1},{1,0},{2,3},{3,2},{4,5},{5,4},{6,7},{7,6},{8,9},{9,8},{10,11... | collective-permute-start | bytes 1179656 | tf_op jit(solution)/shard_map/ppermute | solution.py:189
  134.1 2.3 %collective-permute-start.43 = (f32[1,1,2,3,32,512]{5,4,3,2,1,0:T(8,128)S(1)}, f32[1,1,2,3,32,512]{5,4,3,2,1,0:T(8,128)S(1)}, u32[]{:S(2)}, u32[]{:S(2)}) collective-permute-start(f32[1,1,2,3,32,512]{5,4,3,2,1,0:T(8,128)S(1)} %get-tuple-element.21), channel_id=1, source_target_pairs={{0,1},{1,0},{2,3},{3,2},{4,5},{5,4},{6,7},{7,6},{8,9},{9,8},{10,11... | collective-permute-start | bytes 1179656 | tf_op jit(solution)/shard_map/ppermute | solution.py:189
  136.7 4.9 %collective-permute-start.44 = (bf16[2,3,32,256]{3,2,1,0:T(8,128)(2,1)S(1)}, bf16[2,3,32,256]{3,2,1,0:T(8,128)(2,1)S(1)}, u32[]{:S(2)}, u32[]{:S(2)}) collective-permute-start(bf16[2,3,32,256]{3,2,1,0:T(8,128)(2,1)S(1)} %get-tuple-element.57), channel_id=1, source_target_pairs={{0,2},{1,3},{4,0},{5,1},{8,4},{9,5},{12,8},{13,9},{14,12},{15,13},... | collective-permute-start | bytes 294920 | tf_op jit(solution)/shard_map/ppermute | solution.py:201
  137.2 6.9 %collective-permute-start.39 = (f32[1,1,2,3,32,512]{5,4,3,2,1,0:T(8,128)S(1)}, f32[1,1,2,3,32,512]{5,4,3,2,1,0:T(8,128)S(1)}, u32[]{:S(2)}, u32[]{:S(2)}) collective-permute-start(f32[1,1,2,3,32,512]{5,4,3,2,1,0:T(8,128)S(1)} %get-tuple-element.23), channel_id=1, source_target_pairs={{0,1},{1,0},{2,3},{3,2},{4,5},{5,4},{6,7},{7,6},{8,9},{9,8},{10,11... | collective-permute-start | bytes 1179656 | tf_op jit(solution)/shard_map/ppermute | solution.py:189
  137.2 7.4 %collective-permute-start.46 = (f32[1,1,2,3,32,512]{5,4,3,2,1,0:T(8,128)S(1)}, f32[1,1,2,3,32,512]{5,4,3,2,1,0:T(8,128)S(1)}, u32[]{:S(2)}, u32[]{:S(2)}) collective-permute-start(f32[1,1,2,3,32,512]{5,4,3,2,1,0:T(8,128)S(1)} %get-tuple-element.20), channel_id=1, source_target_pairs={{0,1},{1,0},{2,3},{3,2},{4,5},{5,4},{6,7},{7,6},{8,9},{9,8},{10,11... | collective-permute-start | bytes 1179656 | tf_op jit(solution)/shard_map/ppermute | solution.py:189
  137.8 4.8 %collective-permute-start.36 = (bf16[2,3,32,256]{3,2,1,0:T(8,128)(2,1)S(1)}, bf16[2,3,32,256]{3,2,1,0:T(8,128)(2,1)S(1)}, u32[]{:S(2)}, u32[]{:S(2)}) collective-permute-start(bf16[2,3,32,256]{3,2,1,0:T(8,128)(2,1)S(1)} %get-tuple-element.56), channel_id=1, source_target_pairs={{0,4},{1,5},{4,8},{5,9},{8,12},{9,13},{12,14},{13,15},{14,10},{15,... | collective-permute-start | bytes 294920 | tf_op jit(solution)/shard_map/ppermute | solution.py:200
  141.6 6.1 %collective-permute-start.45 = (bf16[2,3,32,512]{3,2,1,0:T(8,128)(2,1)S(1)}, bf16[2,3,32,512]{3,2,1,0:T(8,128)(2,1)S(1)}, u32[]{:S(2)}, u32[]{:S(2)}) collective-permute-start(bf16[2,3,32,512]{3,2,1,0:T(8,128)(2,1)S(1)} %pad_maximum_fusion.4), channel_id=1, source_target_pairs={{0,2},{1,3},{4,0},{5,1},{8,4},{9,5},{12,8},{13,9},{14,12},{15,13},... | collective-permute-start | bytes 589832 | tf_op jit(solution)/shard_map/ppermute | solution.py:201
  142.6 6.0 %collective-permute-start.38 = (bf16[2,3,32,512]{3,2,1,0:T(8,128)(2,1)S(1)}, bf16[2,3,32,512]{3,2,1,0:T(8,128)(2,1)S(1)}, u32[]{:S(2)}, u32[]{:S(2)}) collective-permute-start(bf16[2,3,32,512]{3,2,1,0:T(8,128)(2,1)S(1)} %pad_maximum_fusion.3), channel_id=1, source_target_pairs={{0,4},{1,5},{4,8},{5,9},{8,12},{9,13},{12,14},{13,15},{14,10},{15,... | collective-permute-start | bytes 589832 | tf_op jit(solution)/shard_map/ppermute | solution.py:200
  144.1 6.7 %collective-permute-start.41 = (f32[1,1,2,3,32,512]{5,4,3,2,1,0:T(8,128)S(1)}, f32[1,1,2,3,32,512]{5,4,3,2,1,0:T(8,128)S(1)}, u32[]{:S(2)}, u32[]{:S(2)}) collective-permute-start(f32[1,1,2,3,32,512]{5,4,3,2,1,0:T(8,128)S(1)} %get-tuple-element.22), channel_id=1, source_target_pairs={{0,1},{1,0},{2,3},{3,2},{4,5},{5,4},{6,7},{7,6},{8,9},{9,8},{10,11... | collective-permute-start | bytes 1179656 | tf_op jit(solution)/shard_map/ppermute | solution.py:189
  144.1 6.7 %collective-permute-start.48 = (f32[1,1,2,3,32,512]{5,4,3,2,1,0:T(8,128)S(1)}, f32[1,1,2,3,32,512]{5,4,3,2,1,0:T(8,128)S(1)}, u32[]{:S(2)}, u32[]{:S(2)}) collective-permute-start(f32[1,1,2,3,32,512]{5,4,3,2,1,0:T(8,128)S(1)} %get-tuple-element.19), channel_id=1, source_target_pairs={{0,1},{1,0},{2,3},{3,2},{4,5},{5,4},{6,7},{7,6},{8,9},{9,8},{10,11... | collective-permute-start | bytes 1179656 | tf_op jit(solution)/shard_map/ppermute | solution.py:189
  148.8 5.7 %collective-permute-start.40 = (bf16[2,3,32,512]{3,2,1,0:T(8,128)(2,1)S(1)}, bf16[2,3,32,512]{3,2,1,0:T(8,128)(2,1)S(1)}, u32[]{:S(2)}, u32[]{:S(2)}) collective-permute-start(bf16[2,3,32,512]{3,2,1,0:T(8,128)(2,1)S(1)} %get-tuple-element.28), channel_id=1, source_target_pairs={{0,4},{1,5},{4,8},{5,9},{8,12},{9,13},{12,14},{13,15},{14,10},{15,... | collective-permute-start | bytes 589832 | tf_op jit(solution)/shard_map/ppermute | solution.py:200
  150.4 5.7 %collective-permute-start.47 = (bf16[2,3,32,512]{3,2,1,0:T(8,128)(2,1)S(1)}, bf16[2,3,32,512]{3,2,1,0:T(8,128)(2,1)S(1)}, u32[]{:S(2)}, u32[]{:S(2)}) collective-permute-start(bf16[2,3,32,512]{3,2,1,0:T(8,128)(2,1)S(1)} %get-tuple-element.29), channel_id=1, source_target_pairs={{0,2},{1,3},{4,0},{5,1},{8,4},{9,5},{12,8},{13,9},{14,12},{15,13},... | collective-permute-start | bytes 589832 | tf_op jit(solution)/shard_map/ppermute | solution.py:201
  150.9 8.5 %collective-permute-start.34 = (f32[1,1,2,3,32,512]{5,4,3,2,1,0:T(8,128)S(1)}, f32[1,1,2,3,32,512]{5,4,3,2,1,0:T(8,128)S(1)}, u32[]{:S(2)}, u32[]{:S(2)}) collective-permute-start(f32[1,1,2,3,32,512]{5,4,3,2,1,0:T(8,128)S(1)} %get-tuple-element.18), channel_id=1, source_target_pairs={{0,1},{1,0},{2,3},{3,2},{4,5},{5,4},{6,7},{7,6},{8,9},{9,8},{10,11... | collective-permute-start | bytes 1179656 | tf_op jit(solution)/shard_map/ppermute | solution.py:189
  156.2 5.7 %collective-permute-start.42 = (bf16[2,3,32,512]{3,2,1,0:T(8,128)(2,1)S(1)}, bf16[2,3,32,512]{3,2,1,0:T(8,128)(2,1)S(1)}, u32[]{:S(2)}, u32[]{:S(2)}) collective-permute-start(bf16[2,3,32,512]{3,2,1,0:T(8,128)(2,1)S(1)} %get-tuple-element.26), channel_id=1, source_target_pairs={{0,4},{1,5},{4,8},{5,9},{8,12},{9,13},{12,14},{13,15},{14,10},{15,... | collective-permute-start | bytes 589832 | tf_op jit(solution)/shard_map/ppermute | solution.py:200
  157.9 5.7 %collective-permute-start.49 = (bf16[2,3,32,512]{3,2,1,0:T(8,128)(2,1)S(1)}, bf16[2,3,32,512]{3,2,1,0:T(8,128)(2,1)S(1)}, u32[]{:S(2)}, u32[]{:S(2)}) collective-permute-start(bf16[2,3,32,512]{3,2,1,0:T(8,128)(2,1)S(1)} %get-tuple-element.27), channel_id=1, source_target_pairs={{0,2},{1,3},{4,0},{5,1},{8,4},{9,5},{12,8},{13,9},{14,12},{15,13},... | collective-permute-start | bytes 589832 | tf_op jit(solution)/shard_map/ppermute | solution.py:201
  (12 other events, 85.3 us)

commit v9 on v8

--- a/solution.py
+++ b/solution.py
@@ -71,17 +71,25 @@
     return lax.dot_general(left, right, (((0,), (0,)), ((), ())), preferred_element_type=jnp.float32)
 
 
-def _block_kernel(q_ref, k_ref, v_ref, r_ref, w_ref, o_ref, g_ref):
-    heads = w_ref.shape[0]
-    width = w_ref.shape[3]
+def _block_kernel(core_ref, q_ref, k_ref, v_ref, r_ref, mine_ref, other_ref, o_ref, g_ref, w_ref):
+    chips, heads, mats, rows, width = mine_ref.shape
+    first = core_ref[0] == 0
+    for chip in range(chips):
+        for head in range(heads):
+            for which in range(mats):
+                mine = mine_ref[chip, head, which].astype(jnp.float32)
+                other = other_ref[chip, head, which].astype(jnp.float32)
+                lo_row = 2 * chip * rows
+                w_ref[head, which, lo_row : lo_row + rows] = jnp.where(first, mine, other)
+                w_ref[head, which, lo_row + rows : lo_row + 2 * rows] = jnp.where(first, other, mine)
     for head in range(heads):
         lo = head * width
         query = q_ref[:, lo : lo + width]
         key_rows = k_ref[:, lo : lo + width]
         value_rows = v_ref[:, lo : lo + width]
-        gate = w_ref[head, 0]
-        up = w_ref[head, 1]
-        down = w_ref[head, 2]
+        gate = w_ref[head, 0].astype(jnp.bfloat16)
+        up = w_ref[head, 1].astype(jnp.bfloat16)
+        down = w_ref[head, 2].astype(jnp.bfloat16)
         a1 = _nt(query, gate)
         a3 = _nt(query, up)
         hidden_q = (a1 / (1.0 + jnp.exp(-a1)) * a3).astype(jnp.bfloat16)
@@ -107,19 +115,23 @@
                     g_ref[chip, core, head, which] = grad[lo_row : lo_row + rows]
 
 
-def fused_block(query, key_rows, value_rows, rate_rows, wbf, chips):
+def fused_block(query, key_rows, value_rows, rate_rows, mine, other):
     tokens = query.shape[0]
     rates_t = rate_rows.reshape(-1, tokens).T
-    heads, mats, hid, dh = wbf.shape
+    chips, heads, mats, rows, dh = mine.shape
+    core = (lax.axis_index("tok") % 2).astype(jnp.int32).reshape(1)
+    vmem = pl.BlockSpec(memory_space=pltpu.VMEM)
     return pl.pallas_call(
         _block_kernel,
         out_shape=(
             jax.ShapeDtypeStruct(query.shape, jnp.bfloat16),
-            jax.ShapeDtypeStruct((chips, 2, heads, mats, hid // (2 * chips), dh), jnp.float32),
+            jax.ShapeDtypeStruct((chips, 2, heads, mats, rows, dh), jnp.float32),
         ),
+        in_specs=[pl.BlockSpec(memory_space=pltpu.SMEM)] + [vmem] * 6,
+        out_specs=(vmem, vmem),
+        scratch_shapes=[pltpu.VMEM((heads, mats, chips * 2 * rows, dh), jnp.float32)],
         compiler_params=pltpu.CompilerParams(vmem_limit_bytes=48 * 1024 * 1024),
-    )(query, key_rows, value_rows, rates_t, wbf)
-
+    )(core, query, key_rows, value_rows, rates_t, mine, other)
 
 class Ring:
     def __init__(self, mesh):
@@ -171,12 +183,7 @@
             if k <= self.nccw:
                 b = lax.ppermute(b, "tok", self.ccw)
                 ring = lax.dynamic_update_index_in_dim(ring, b, self.chip_at(k), 0)
-        other = lax.ppermute(ring, "tok", self.swap)
-        full = jnp.zeros((self.chips, 2, h, g, rows, f), own.dtype)
-        full = lax.dynamic_update_slice(full, ring[:, None], (0, core, 0, 0, 0, 0))
-        full = lax.dynamic_update_slice(full, other[:, None], (0, 1 - core, 0, 0, 0, 0))
-        full = jnp.moveaxis(full, (0, 1), (2, 3))
-        return full.reshape(h, g, self.chips * 2 * rows, f)
+        return ring, lax.ppermute(ring, "tok", self.swap)
 
     def reduce(self, q):
         _, _, h, g, rows, f = q.shape
@@ -237,8 +244,8 @@
         own = fast_weights
         blocks = []
         for span in range(nblocks):
-            gathered = ring.gather(own.astype(jnp.bfloat16))
-            normed, partial_value = fused_block(queries[span], keys[span], values[span], rates[span], gathered, ring.chips)
+            mine, other = ring.gather(own.astype(jnp.bfloat16))
+            normed, partial_value = fused_block(queries[span], keys[span], values[span], rates[span], mine, other)
             blocks.append(normed)
             own = renorm(own, own + ring.reduce(partial_value))
         return (jnp.stack(blocks), own)

time: 165 us -> 167 us (1.012)
  local copies, waits for them, and re-layouts: 20.8 us -> 10.5 us
  waiting for transfers between devices: 64.5 us -> 69.9 us
  other arithmetic: 5.43 us -> 8.82 us
  Pallas kernels: 12.5 us -> 15.6 us
    dynamic_update_slice x4 -> x0, local copies, waits for them, and re-layouts: 4.99 us -> none  [the longest x2 3.22 us: gather(): lax.dynamic_update_slice(full, other[:, None], (0, 1 - core, 0, 0, 0, 0))]
    pallas_call x2, Pallas kernels: 12.5 us -> 15.6 us  [fused_block(): pl.pallas_call(_block_kernel, out_shape=(jax.ShapeDtypeStruct(query.shape...]
    ppermute x6, waiting for transfers between devices: 17.8 us -> 20.6 us  [gather(): a = lax.ppermute(a, 'tok', self.cw)]
    convert_element_type x4, other arithmetic: 0.85 us -> 3.07 us  [reduce(): a = lax.ppermute(a.astype(jnp.bfloat16), 'tok', self.cw).astype(jnp.float32)]
    ppermute x2, waiting for transfers between devices: 2.54 us -> 4.75 us  [gather(): a = lax.ppermute(a[..., :f // 2], 'tok', self.cw)]
    dynamic_update_slice x6, local copies, waits for them, and re-layouts: 2.22 us -> 0.1 us  [gather(): ring = lax.dynamic_update_index_in_dim(ring, a, self.chip_at(-k), 0)]
    dynamic_update_slice x6, local copies, waits for them, and re-layouts: 2.19 us -> 0.12 us  [gather(): ring = lax.dynamic_update_index_in_dim(ring, b, self.chip_at(k), 0)]
    another operation x4 -> x2, local copies, waits for them, and re-layouts: 2.3 us -> 0.35 us
  transfers between devices with their start and end apart: 50 -> 50, of which waited for: 34 -> 32; matrix products, arithmetic and copies ran while one was open for 7% -> 4% of each run, Pallas kernels for 0% -> 0%
where the time goes in v9:
time: 167 us; the launch traced here: 166 us
  waiting for transfers between devices  69.9 us (42%)
  starting transfers between devices  38.6 us (23%)
  between operations  22.9 us (14%)
  Pallas kernels  15.6 us (9%)
  local copies, waits for them, and re-layouts  10.5 us (6%)
  other arithmetic  8.82 us (5%)
    ppermute x6, waiting for transfers between devices, gather(): a = lax.ppermute(a, 'tok', self.cw)  20.6 us
    ppermute x8, waiting for transfers between devices, reduce(): lax.ppermute(b.astype(jnp.bfloat16), 'tok', self.ccw).astype(jnp.float32)  17.4 us
    pallas_call x2, Pallas kernels, fused_block(): pl.pallas_call(_block_kernel, out_shape=(jax.ShapeDtypeStruct(query.shape...  15.6 us
    ppermute x8, waiting for transfers between devices, reduce(): a = lax.ppermute(a.astype(jnp.bfloat16), 'tok', self.cw).astype(jnp.float32)  15.3 us
    ppermute x8, starting transfers between devices, reduce(): a = lax.ppermute(a.astype(jnp.bfloat16), 'tok', self.cw).astype(jnp.float32)  13.4 us
    ppermute x6, starting transfers between devices, gather(): a = lax.ppermute(a, 'tok', self.cw)  11.8 us
    dynamic_slice x2, local copies, waits for them, and re-layouts, chip_sum(): lax.dynamic_slice(q, (chip, 1 - core, 0, 0, 0, 0), (1, 1, h, g, rows, f))  5.58 us
    ppermute x2, waiting for transfers between devices, gather(): a = lax.ppermute(a[..., :f // 2], 'tok', self.cw)  4.75 us
  transfers between devices with their start and end apart: 50, of which 32 were waited for; matrix products, arithmetic and copies ran while one was open for 4% of the time, Pallas kernels for 0%

profile of v9, /device:TPU:0, one launch (start us, length us, event | category | flops | bytes accessed | tf_op | source)
XLA Modules:
  0.0 166.1 jit_solution(5593321790214188518)
XLA Ops:
  1.7 3.1 %collective-permute-start = (bf16[2,3,32,512]{3,2,1,0:T(8,128)(2,1)S(1)}, bf16[2,3,32,512]{3,2,1,0:T(8,128)(2,1)S(1)}, u32[]{:S(2)}, u32[]{:S(2)}) collective-permute-start(bf16[2,3,32,512]{3,2,1,0:T(8,128)(2,1)S(1)} %get-tuple-element.17), channel_id=1, source_target_pairs={{0,4},{1,5},{4,8},{5,9},{8,12},{9,13},{12,14},{13,15},{14,10},{15,... | collective-permute-start | bytes 589832 | tf_op jit(solution)/shard_map/ppermute | solution.py:181
  25.9 2.1 %collective-permute-start.2 = (bf16[2,3,32,512]{3,2,1,0:T(8,128)(2,1)S(1)}, bf16[2,3,32,512]{3,2,1,0:T(8,128)(2,1)S(1)}, u32[]{:S(2)}, u32[]{:S(2)}) collective-permute-start(bf16[2,3,32,512]{3,2,1,0:T(8,128)(2,1)S(1)} %collective-permute-done), channel_id=1, source_target_pairs={{0,4},{1,5},{4,8},{5,9},{8,12},{9,13},{12,14},{13,15},{14,10},{15,... | collective-permute-start | bytes 589832 | tf_op jit(solution)/shard_map/ppermute | solution.py:181
  28.0 4.3 %collective-permute-done.2 = bf16[2,3,32,512]{3,2,1,0:T(8,128)(2,1)S(1)} collective-permute-done((bf16[2,3,32,512]{3,2,1,0:T(8,128)(2,1)S(1)}, bf16[2,3,32,512]{3,2,1,0:T(8,128)(2,1)S(1)}, u32[]{:S(2)}, u32[]{:S(2)}) %collective-permute-start.2) | collective-permute-done | bytes 196640 | tf_op jit(solution)/shard_map/ppermute | solution.py:181
  32.3 1.7 %collective-permute-start.4 = (bf16[2,3,32,512]{3,2,1,0:T(8,128)(2,1)S(1)}, bf16[2,3,32,512]{3,2,1,0:T(8,128)(2,1)S(1)}, u32[]{:S(2)}, u32[]{:S(2)}) collective-permute-start(bf16[2,3,32,512]{3,2,1,0:T(8,128)(2,1)S(1)} %collective-permute-done.2), channel_id=1, source_target_pairs={{0,4},{1,5},{4,8},{5,9},{8,12},{9,13},{12,14},{13,15},{14,10},{15,... | collective-permute-start | bytes 589832 | tf_op jit(solution)/shard_map/ppermute | solution.py:181
  34.4 3.6 %collective-permute-done.4 = bf16[2,3,32,512]{3,2,1,0:T(8,128)(2,1)S(1)} collective-permute-done((bf16[2,3,32,512]{3,2,1,0:T(8,128)(2,1)S(1)}, bf16[2,3,32,512]{3,2,1,0:T(8,128)(2,1)S(1)}, u32[]{:S(2)}, u32[]{:S(2)}) %collective-permute-start.4) | collective-permute-done | bytes 196640 | tf_op jit(solution)/shard_map/ppermute | solution.py:181
  38.0 1.9 %collective-permute-start.6 = (bf16[2,3,32,256]{3,2,1,0:T(8,128)(2,1)S(1)}, bf16[2,3,32,256]{3,2,1,0:T(8,128)(2,1)S(1)}, u32[]{:S(2)}, u32[]{:S(2)}) collective-permute-start(bf16[2,3,32,256]{3,2,1,0:T(8,128)(2,1)S(1)} %slice.104), channel_id=1, source_target_pairs={{0,4},{1,5},{4,8},{5,9},{8,12},{9,13},{12,14},{13,15},{14,10},{15,... | collective-permute-start | bytes 294920 | tf_op jit(solution)/shard_map/ppermute | solution.py:176
  40.2 2.5 %collective-permute-done.6 = bf16[2,3,32,256]{3,2,1,0:T(8,128)(2,1)S(1)} collective-permute-done((bf16[2,3,32,256]{3,2,1,0:T(8,128)(2,1)S(1)}, bf16[2,3,32,256]{3,2,1,0:T(8,128)(2,1)S(1)}, u32[]{:S(2)}, u32[]{:S(2)}) %collective-permute-start.6) | collective-permute-done | bytes 98336 | tf_op jit(solution)/shard_map/ppermute | solution.py:176
  42.6 1.9 %collective-permute-done.7 = bf16[2,3,32,256]{3,2,1,0:T(8,128)(2,1)S(1)} collective-permute-done((bf16[2,3,32,256]{3,2,1,0:T(8,128)(2,1)S(1)}, bf16[2,3,32,256]{3,2,1,0:T(8,128)(2,1)S(1)}, u32[]{:S(2)}, u32[]{:S(2)}) %collective-permute-start.7) | collective-permute-done | bytes 98336 | tf_op jit(solution)/shard_map/ppermute | solution.py:177
  46.9 1.1 copy-done.8
  48.6 7.8 %shard_map.608 = (bf16[256,1024]{1,0:T(8,128)(2,1)S(1)}, f32[8,2,2,3,32,512]{5,4,3,2,1,0:T(8,128)}) custom-call(s32[1]{0:T(128)} %bitcast.core_ref, bf16[256,1024]{1,0:T(8,128)(2,1)S(1)} %get-tuple-element.52.q_ref, bf16[256,1024]{1,0:T(8,128)(2,1)S(1)} %get-tuple-element.71.k_ref, bf16[256,1024]{1,0:T(8,128)(2,1)S(1)} %get-tuple-element.48.v_ref, ...), custom_call_target="tpu_custom_call" | custom-call | tf_op jit(solution)/shard_map/pallas_call | solution.py:124
  56.3 3.3 %constant_dynamic-slice_fusion.15 = (f32[1,1,2,3,32,512]{5,4,3,2,1,0:T(8,128)S(1)}, f32[1,1,2,3,32,512]{5,4,3,2,1,0:T(8,128)S(1)}, f32[1,1,2,3,32,512]{5,4,3,2,1...) fusion(f32[8,2,2,3,32,512]{5,4,3,2,1,0:T(8,128)} %get-tuple-ele, ...), kind=kLoop, calls=%fused_computation.92 | loop fusion | bytes 6291492 | tf_op jit(solution)/shard_map/dynamic_slice | solution.py:195
  60.7 1.2 collective-permute-done.10
  63.0 1.8 %add_bitcast_fusion.3 = (f32[2,3,32,512]{3,2,1,0:T(8,128)S(1)}, f32[2,3,32,512]{3,2,1,0:T(8,128)S(1)}, bf16[2,3,32,512]{3,2,1,0:T(8,128)(2,1)S(1)}) fusion(f32[1,1,2,3,32,512]{5,4,3,2,1,0:T(8,128)} %collective-permute-done.12, f32[8,2,2,3,32,512]{5,4,3,2,1,0:T(8,128)} %get-tuple-element.7, s32[]{:T(128)S(6)} %select_n.455, s32[]{:T(128)S(6)} %select_n.462, ...), kind=kLoop, calls=%fused_computation.37 | loop fusion | flops 393216 | bytes 3342352 | tf_op jit(solution)/shard_map/reshape | solution.py:197
  65.6 1.9 %collective-permute-start.11 = (bf16[2,3,32,256]{3,2,1,0:T(8,128)(2,1)S(1)}, bf16[2,3,32,256]{3,2,1,0:T(8,128)(2,1)S(1)}, u32[]{:S(2)}, u32[]{:S(2)}) collective-permute-start(bf16[2,3,32,256]{3,2,1,0:T(8,128)(2,1)S(1)} %get-tuple-element.58), channel_id=1, source_target_pairs={{0,4},{1,5},{4,8},{5,9},{8,12},{9,13},{12,14},{13,15},{14,10},{15,... | collective-permute-start | bytes 294920 | tf_op jit(solution)/shard_map/ppermute | solution.py:207
  67.5 2.4 %collective-permute-done.19 = bf16[2,3,32,256]{3,2,1,0:T(8,128)(2,1)S(1)} collective-permute-done((bf16[2,3,32,256]{3,2,1,0:T(8,128)(2,1)S(1)}, bf16[2,3,32,256]{3,2,1,0:T(8,128)(2,1)S(1)}, u32[]{:S(2)}, u32[]{:S(2)}) %collective-permute-start.19) | collective-permute-done | bytes 98336 | tf_op jit(solution)/shard_map/ppermute | solution.py:208
  70.6 1.7 %collective-permute-start.13 = (bf16[2,3,32,512]{3,2,1,0:T(8,128)(2,1)S(1)}, bf16[2,3,32,512]{3,2,1,0:T(8,128)(2,1)S(1)}, u32[]{:S(2)}, u32[]{:S(2)}) collective-permute-start(bf16[2,3,32,512]{3,2,1,0:T(8,128)(2,1)S(1)} %pad_maximum_fusion.1), channel_id=1, source_target_pairs={{0,4},{1,5},{4,8},{5,9},{8,12},{9,13},{12,14},{13,15},{14,10},{15,... | collective-permute-start | bytes 589832 | tf_op jit(solution)/shard_map/ppermute | solution.py:207
  72.9 3.5 %collective-permute-done.20 = bf16[2,3,32,512]{3,2,1,0:T(8,128)(2,1)S(1)} collective-permute-done((bf16[2,3,32,512]{3,2,1,0:T(8,128)(2,1)S(1)}, bf16[2,3,32,512]{3,2,1,0:T(8,128)(2,1)S(1)}, u32[]{:S(2)}, u32[]{:S(2)}) %collective-permute-start.20) | collective-permute-done | bytes 196640 | tf_op jit(solution)/shard_map/ppermute | solution.py:208
  76.9 1.3 fusion.9
  78.2 1.5 collective-permute-start.15
  80.3 3.6 %collective-permute-done.15 = bf16[2,3,32,512]{3,2,1,0:T(8,128)(2,1)S(1)} collective-permute-done((bf16[2,3,32,512]{3,2,1,0:T(8,128)(2,1)S(1)}, bf16[2,3,32,512]{3,2,1,0:T(8,128)(2,1)S(1)}, u32[]{:S(2)}, u32[]{:S(2)}) %collective-permute-start.15) | collective-permute-done | bytes 196640 | tf_op jit(solution)/shard_map/ppermute | solution.py:207
  84.0 1.5 collective-permute-done.22
  85.4 1.3 fusion.8
  86.8 1.6 collective-permute-start.17
  88.9 3.6 %collective-permute-done.17 = bf16[2,3,32,512]{3,2,1,0:T(8,128)(2,1)S(1)} collective-permute-done((bf16[2,3,32,512]{3,2,1,0:T(8,128)(2,1)S(1)}, bf16[2,3,32,512]{3,2,1,0:T(8,128)(2,1)S(1)}, u32[]{:S(2)}, u32[]{:S(2)}) %collective-permute-start.17) | collective-permute-done | bytes 196640 | tf_op jit(solution)/shard_map/ppermute | solution.py:207
  92.5 1.6 collective-permute-done.24
  94.1 1.2 multiply_reduce_fusion.2
  95.6 1.7 collective-permute-start.25
  97.7 5.1 %collective-permute-done.25 = bf16[2,3,32,512]{3,2,1,0:T(8,128)(2,1)S(1)} collective-permute-done((bf16[2,3,32,512]{3,2,1,0:T(8,128)(2,1)S(1)}, bf16[2,3,32,512]{3,2,1,0:T(8,128)(2,1)S(1)}, u32[]{:S(2)}, u32[]{:S(2)}) %collective-permute-start.25) | collective-permute-done | bytes 196640 | tf_op jit(solution)/shard_map/ppermute | solution.py:181
  102.8 1.6 collective-permute-start.27
  104.9 4.1 %collective-permute-done.27 = bf16[2,3,32,512]{3,2,1,0:T(8,128)(2,1)S(1)} collective-permute-done((bf16[2,3,32,512]{3,2,1,0:T(8,128)(2,1)S(1)}, bf16[2,3,32,512]{3,2,1,0:T(8,128)(2,1)S(1)}, u32[]{:S(2)}, u32[]{:S(2)}) %collective-permute-start.27) | collective-permute-done | bytes 196640 | tf_op jit(solution)/shard_map/ppermute | solution.py:181
  109.0 1.6 collective-permute-start.29
  111.2 3.5 %collective-permute-done.29 = bf16[2,3,32,512]{3,2,1,0:T(8,128)(2,1)S(1)} collective-permute-done((bf16[2,3,32,512]{3,2,1,0:T(8,128)(2,1)S(1)}, bf16[2,3,32,512]{3,2,1,0:T(8,128)(2,1)S(1)}, u32[]{:S(2)}, u32[]{:S(2)}) %collective-permute-start.29) | collective-permute-done | bytes 196640 | tf_op jit(solution)/shard_map/ppermute | solution.py:181
  114.7 1.7 %collective-permute-start.31 = (bf16[2,3,32,256]{3,2,1,0:T(8,128)(2,1)S(1)}, bf16[2,3,32,256]{3,2,1,0:T(8,128)(2,1)S(1)}, u32[]{:S(2)}, u32[]{:S(2)}) collective-permute-start(bf16[2,3,32,256]{3,2,1,0:T(8,128)(2,1)S(1)} %slice.112), channel_id=1, source_target_pairs={{0,4},{1,5},{4,8},{5,9},{8,12},{9,13},{12,14},{13,15},{14,10},{15,... | collective-permute-start | bytes 294920 | tf_op jit(solution)/shard_map/ppermute | solution.py:176
  117.1 2.3 %collective-permute-done.31 = bf16[2,3,32,256]{3,2,1,0:T(8,128)(2,1)S(1)} collective-permute-done((bf16[2,3,32,256]{3,2,1,0:T(8,128)(2,1)S(1)}, bf16[2,3,32,256]{3,2,1,0:T(8,128)(2,1)S(1)}, u32[]{:S(2)}, u32[]{:S(2)}) %collective-permute-start.31) | collective-permute-done | bytes 98336 | tf_op jit(solution)/shard_map/ppermute | solution.py:176
  119.4 1.9 %collective-permute-done.32 = bf16[2,3,32,256]{3,2,1,0:T(8,128)(2,1)S(1)} collective-permute-done((bf16[2,3,32,256]{3,2,1,0:T(8,128)(2,1)S(1)}, bf16[2,3,32,256]{3,2,1,0:T(8,128)(2,1)S(1)}, u32[]{:S(2)}, u32[]{:S(2)}) %collective-permute-start.32) | collective-permute-done | bytes 98336 | tf_op jit(solution)/shard_map/ppermute | solution.py:177
  121.5 3.4 %collective-permute-done.33.other_ref = bf16[8,2,3,32,512]{4,3,2,1,0:T(8,128)(2,1)} collective-permute-done((bf16[8,2,3,32,512]{4,3,2,1,0:T(8,128)(2,1)S(1)}, bf16[8,2,3,32,512]{4,3,2,1,0:T(8,128)(2,1)}, u32[]{:S(2)}, u32[]{:S(2)}) %collective-permute-start.33) | collective-permute-done | bytes 1572896 | tf_op jit(solution)/shard_map/ppermute | solution.py:186
  124.9 7.8 %shard_map.609 = (bf16[256,1024]{1,0:T(8,128)(2,1)S(1)}, f32[8,2,2,3,32,512]{5,4,3,2,1,0:T(8,128)}) custom-call(s32[1]{0:T(128)} %bitcast.core_ref, bf16[256,1024]{1,0:T(8,128)(2,1)S(1)} %get-tuple-element.53.q_ref, bf16[256,1024]{1,0:T(8,128)(2,1)S(1)} %get-tuple-element.70.k_ref, bf16[256,1024]{1,0:T(8,128)(2,1)S(1)} %get-tuple-element.49.v_ref, ...), custom_call_target="tpu_custom_call" | custom-call | tf_op jit(solution)/shard_map/pallas_call | solution.py:124
  132.7 2.3 %constant_dynamic-slice_fusion = (f32[1,1,2,3,32,512]{5,4,3,2,1,0:T(8,128)S(1)}, f32[1,1,2,3,32,512]{5,4,3,2,1,0:T(8,128)S(1)}, f32[1,1,2,3,32,512]{5,4,3,2,1,0:...) fusion(f32[8,2,2,3,32,512]{5,4,3,2,1,0:T(8,128)} %get-tuple-ele, ...), kind=kLoop, calls=%fused_computation.77 | loop fusion | bytes 6291492 | tf_op jit(solution)/shard_map/dynamic_slice | solution.py:195
  139.1 1.7 %collective-permute-start.36 = (bf16[2,3,32,256]{3,2,1,0:T(8,128)(2,1)S(1)}, bf16[2,3,32,256]{3,2,1,0:T(8,128)(2,1)S(1)}, u32[]{:S(2)}, u32[]{:S(2)}) collective-permute-start(bf16[2,3,32,256]{3,2,1,0:T(8,128)(2,1)S(1)} %get-tuple-element.56), channel_id=1, source_target_pairs={{0,4},{1,5},{4,8},{5,9},{8,12},{9,13},{12,14},{13,15},{14,10},{15,... | collective-permute-start | bytes 294920 | tf_op jit(solution)/shard_map/ppermute | solution.py:207
  140.9 2.2 %collective-permute-done.44 = bf16[2,3,32,256]{3,2,1,0:T(8,128)(2,1)S(1)} collective-permute-done((bf16[2,3,32,256]{3,2,1,0:T(8,128)(2,1)S(1)}, bf16[2,3,32,256]{3,2,1,0:T(8,128)(2,1)S(1)}, u32[]{:S(2)}, u32[]{:S(2)}) %collective-permute-start.44) | collective-permute-done | bytes 98336 | tf_op jit(solution)/shard_map/ppermute | solution.py:208
  144.0 1.7 %collective-permute-start.38 = (bf16[2,3,32,512]{3,2,1,0:T(8,128)(2,1)S(1)}, bf16[2,3,32,512]{3,2,1,0:T(8,128)(2,1)S(1)}, u32[]{:S(2)}, u32[]{:S(2)}) collective-permute-start(bf16[2,3,32,512]{3,2,1,0:T(8,128)(2,1)S(1)} %pad_maximum_fusion.3), channel_id=1, source_target_pairs={{0,4},{1,5},{4,8},{5,9},{8,12},{9,13},{12,14},{13,15},{14,10},{15,... | collective-permute-start | bytes 589832 | tf_op jit(solution)/shard_map/ppermute | solution.py:207
  146.2 3.1 %collective-permute-done.45 = bf16[2,3,32,512]{3,2,1,0:T(8,128)(2,1)S(1)} collective-permute-done((bf16[2,3,32,512]{3,2,1,0:T(8,128)(2,1)S(1)}, bf16[2,3,32,512]{3,2,1,0:T(8,128)(2,1)S(1)}, u32[]{:S(2)}, u32[]{:S(2)}) %collective-permute-start.45) | collective-permute-done | bytes 196640 | tf_op jit(solution)/shard_map/ppermute | solution.py:208
  150.2 1.7 %collective-permute-start.40 = (bf16[2,3,32,512]{3,2,1,0:T(8,128)(2,1)S(1)}, bf16[2,3,32,512]{3,2,1,0:T(8,128)(2,1)S(1)}, u32[]{:S(2)}, u32[]{:S(2)}) collective-permute-start(bf16[2,3,32,512]{3,2,1,0:T(8,128)(2,1)S(1)} %get-tuple-element.28), channel_id=1, source_target_pairs={{0,4},{1,5},{4,8},{5,9},{8,12},{9,13},{12,14},{13,15},{14,10},{15,... | collective-permute-start | bytes 589832 | tf_op jit(solution)/shard_map/ppermute | solution.py:207
  152.3 3.6 %collective-permute-done.40 = bf16[2,3,32,512]{3,2,1,0:T(8,128)(2,1)S(1)} collective-permute-done((bf16[2,3,32,512]{3,2,1,0:T(8,128)(2,1)S(1)}, bf16[2,3,32,512]{3,2,1,0:T(8,128)(2,1)S(1)}, u32[]{:S(2)}, u32[]{:S(2)}) %collective-permute-start.40) | collective-permute-done | bytes 196640 | tf_op jit(solution)/shard_map/ppermute | solution.py:207
  155.9 1.6 collective-permute-done.47
  157.8 1.6 collective-permute-start.42
  160.9 2.6 %collective-permute-done.42 = bf16[2,3,32,512]{3,2,1,0:T(8,128)(2,1)S(1)} collective-permute-done((bf16[2,3,32,512]{3,2,1,0:T(8,128)(2,1)S(1)}, bf16[2,3,32,512]{3,2,1,0:T(8,128)(2,1)S(1)}, u32[]{:S(2)}, u32[]{:S(2)}) %collective-permute-start.42) | collective-permute-done | bytes 196640 | tf_op jit(solution)/shard_map/ppermute | solution.py:207
  163.5 1.5 collective-permute-done.49
  (139 shorter events, 22.0 us)
Async XLA Ops:
  1.7 24.2 %collective-permute-start = (bf16[2,3,32,512]{3,2,1,0:T(8,128)(2,1)S(1)}, bf16[2,3,32,512]{3,2,1,0:T(8,128)(2,1)S(1)}, u32[]{:S(2)}, u32[]{:S(2)}) collective-permute-start(bf16[2,3,32,512]{3,2,1,0:T(8,128)(2,1)S(1)} %get-tuple-element.17), channel_id=1, source_target_pairs={{0,4},{1,5},{4,8},{5,9},{8,12},{9,13},{12,14},{13,15},{14,10},{15,... | collective-permute-start | bytes 589832 | tf_op jit(solution)/shard_map/ppermute | solution.py:181
  4.8 23.1 %collective-permute-start.1 = (bf16[2,3,32,512]{3,2,1,0:T(8,128)(2,1)S(1)}, bf16[2,3,32,512]{3,2,1,0:T(8,128)(2,1)S(1)}, u32[]{:S(2)}, u32[]{:S(2)}) collective-permute-start(bf16[2,3,32,512]{3,2,1,0:T(8,128)(2,1)S(1)} %get-tuple-element.17), channel_id=1, source_target_pairs={{0,2},{1,3},{4,0},{5,1},{8,4},{9,5},{12,8},{13,9},{14,12},{15,13},... | collective-permute-start | bytes 589832 | tf_op jit(solution)/shard_map/ppermute | solution.py:184
  25.9 6.4 %collective-permute-start.2 = (bf16[2,3,32,512]{3,2,1,0:T(8,128)(2,1)S(1)}, bf16[2,3,32,512]{3,2,1,0:T(8,128)(2,1)S(1)}, u32[]{:S(2)}, u32[]{:S(2)}) collective-permute-start(bf16[2,3,32,512]{3,2,1,0:T(8,128)(2,1)S(1)} %collective-permute-done), channel_id=1, source_target_pairs={{0,4},{1,5},{4,8},{5,9},{8,12},{9,13},{12,14},{13,15},{14,10},{15,... | collective-permute-start | bytes 589832 | tf_op jit(solution)/shard_map/ppermute | solution.py:181
  27.9 6.1 %collective-permute-start.3 = (bf16[2,3,32,512]{3,2,1,0:T(8,128)(2,1)S(1)}, bf16[2,3,32,512]{3,2,1,0:T(8,128)(2,1)S(1)}, u32[]{:S(2)}, u32[]{:S(2)}) collective-permute-start(bf16[2,3,32,512]{3,2,1,0:T(8,128)(2,1)S(1)} %collective-permute-done.1), channel_id=1, source_target_pairs={{0,2},{1,3},{4,0},{5,1},{8,4},{9,5},{12,8},{13,9},{14,12},{15,13},... | collective-permute-start | bytes 589832 | tf_op jit(solution)/shard_map/ppermute | solution.py:184
  32.3 5.7 %collective-permute-start.4 = (bf16[2,3,32,512]{3,2,1,0:T(8,128)(2,1)S(1)}, bf16[2,3,32,512]{3,2,1,0:T(8,128)(2,1)S(1)}, u32[]{:S(2)}, u32[]{:S(2)}) collective-permute-start(bf16[2,3,32,512]{3,2,1,0:T(8,128)(2,1)S(1)} %collective-permute-done.2), channel_id=1, source_target_pairs={{0,4},{1,5},{4,8},{5,9},{8,12},{9,13},{12,14},{13,15},{14,10},{15,... | collective-permute-start | bytes 589832 | tf_op jit(solution)/shard_map/ppermute | solution.py:181
  34.0 5.8 %collective-permute-start.5 = (bf16[2,3,32,512]{3,2,1,0:T(8,128)(2,1)S(1)}, bf16[2,3,32,512]{3,2,1,0:T(8,128)(2,1)S(1)}, u32[]{:S(2)}, u32[]{:S(2)}) collective-permute-start(bf16[2,3,32,512]{3,2,1,0:T(8,128)(2,1)S(1)} %collective-permute-done.3), channel_id=1, source_target_pairs={{0,2},{1,3},{4,0},{5,1},{8,4},{9,5},{12,8},{13,9},{14,12},{15,13},... | collective-permute-start | bytes 589832 | tf_op jit(solution)/shard_map/ppermute | solution.py:184
  38.0 4.7 %collective-permute-start.6 = (bf16[2,3,32,256]{3,2,1,0:T(8,128)(2,1)S(1)}, bf16[2,3,32,256]{3,2,1,0:T(8,128)(2,1)S(1)}, u32[]{:S(2)}, u32[]{:S(2)}) collective-permute-start(bf16[2,3,32,256]{3,2,1,0:T(8,128)(2,1)S(1)} %slice.104), channel_id=1, source_target_pairs={{0,4},{1,5},{4,8},{5,9},{8,12},{9,13},{12,14},{13,15},{14,10},{15,... | collective-permute-start | bytes 294920 | tf_op jit(solution)/shard_map/ppermute | solution.py:176
  39.8 4.7 %collective-permute-start.7 = (bf16[2,3,32,256]{3,2,1,0:T(8,128)(2,1)S(1)}, bf16[2,3,32,256]{3,2,1,0:T(8,128)(2,1)S(1)}, u32[]{:S(2)}, u32[]{:S(2)}) collective-permute-start(bf16[2,3,32,256]{3,2,1,0:T(8,128)(2,1)S(1)} %slice.105), channel_id=1, source_target_pairs={{0,2},{1,3},{4,0},{5,1},{8,4},{9,5},{12,8},{13,9},{14,12},{15,13},... | collective-permute-start | bytes 294920 | tf_op jit(solution)/shard_map/ppermute | solution.py:177
  44.5 4.0 %collective-permute-start.8 = (bf16[8,2,3,32,512]{4,3,2,1,0:T(8,128)(2,1)S(1)}, bf16[8,2,3,32,512]{4,3,2,1,0:T(8,128)(2,1)}, u32[]{:S(2)}, u32[]{:S(2)}) collective-permute-start(bf16[8,2,3,32,512]{4,3,2,1,0:T(8,128)(2,1)S(1)} %fusion.18.mine_ref), channel_id=1, source_target_pairs={{0,1},{1,0},{2,3},{3,2},{4,5},{5,4},{6,7},{7,6},{8,9},{9,8},{10,11... | collective-permute-start | bytes 4718600 | tf_op jit(solution)/shard_map/ppermute | solution.py:186
  59.6 2.2 %collective-permute-start.10 = (f32[1,1,2,3,32,512]{5,4,3,2,1,0:T(8,128)}, f32[1,1,2,3,32,512]{5,4,3,2,1,0:T(8,128)}, u32[]{:S(2)}, u32[]{:S(2)}) collective-permute-start(f32[1,1,2,3,32,512]{5,4,3,2,1,0:T(8,128)} %get-tuple-element.40), channel_id=1, source_target_pairs={{0,1},{1,0},{2,3},{3,2},{4,5},{5,4},{6,7},{7,6},{8,9},{9,8},{10,11... | collective-permute-start | bytes 1179656 | tf_op jit(solution)/shard_map/ppermute | solution.py:196
  60.2 2.3 %collective-permute-start.12 = (f32[1,1,2,3,32,512]{5,4,3,2,1,0:T(8,128)}, f32[1,1,2,3,32,512]{5,4,3,2,1,0:T(8,128)}, u32[]{:S(2)}, u32[]{:S(2)}) collective-permute-start(f32[1,1,2,3,32,512]{5,4,3,2,1,0:T(8,128)} %get-tuple-element.39), channel_id=1, source_target_pairs={{0,1},{1,0},{2,3},{3,2},{4,5},{5,4},{6,7},{7,6},{8,9},{9,8},{10,11... | collective-permute-start | bytes 1179656 | tf_op jit(solution)/shard_map/ppermute | solution.py:196
  60.2 2.7 %collective-permute-start.18 = (f32[1,1,2,3,32,512]{5,4,3,2,1,0:T(8,128)}, f32[1,1,2,3,32,512]{5,4,3,2,1,0:T(8,128)}, u32[]{:S(2)}, u32[]{:S(2)}) collective-permute-start(f32[1,1,2,3,32,512]{5,4,3,2,1,0:T(8,128)} %get-tuple-element.36), channel_id=1, source_target_pairs={{0,1},{1,0},{2,3},{3,2},{4,5},{5,4},{6,7},{7,6},{8,9},{9,8},{10,11... | collective-permute-start | bytes 1179656 | tf_op jit(solution)/shard_map/ppermute | solution.py:196
  64.8 5.1 %collective-permute-start.19 = (bf16[2,3,32,256]{3,2,1,0:T(8,128)(2,1)S(1)}, bf16[2,3,32,256]{3,2,1,0:T(8,128)(2,1)S(1)}, u32[]{:S(2)}, u32[]{:S(2)}) collective-permute-start(bf16[2,3,32,256]{3,2,1,0:T(8,128)(2,1)S(1)} %get-tuple-element.59), channel_id=1, source_target_pairs={{0,2},{1,3},{4,0},{5,1},{8,4},{9,5},{12,8},{13,9},{14,12},{15,13},... | collective-permute-start | bytes 294920 | tf_op jit(solution)/shard_map/ppermute | solution.py:208
  65.1 7.3 %collective-permute-start.14 = (f32[1,1,2,3,32,512]{5,4,3,2,1,0:T(8,128)S(1)}, f32[1,1,2,3,32,512]{5,4,3,2,1,0:T(8,128)S(1)}, u32[]{:S(2)}, u32[]{:S(2)}) collective-permute-start(f32[1,1,2,3,32,512]{5,4,3,2,1,0:T(8,128)S(1)} %get-tuple-element.38), channel_id=1, source_target_pairs={{0,1},{1,0},{2,3},{3,2},{4,5},{5,4},{6,7},{7,6},{8,9},{9,8},{10,11... | collective-permute-start | bytes 1179656 | tf_op jit(solution)/shard_map/ppermute | solution.py:196
  65.3 7.6 %collective-permute-start.21 = (f32[1,1,2,3,32,512]{5,4,3,2,1,0:T(8,128)S(1)}, f32[1,1,2,3,32,512]{5,4,3,2,1,0:T(8,128)S(1)}, u32[]{:S(2)}, u32[]{:S(2)}) collective-permute-start(f32[1,1,2,3,32,512]{5,4,3,2,1,0:T(8,128)S(1)} %get-tuple-element.35), channel_id=1, source_target_pairs={{0,1},{1,0},{2,3},{3,2},{4,5},{5,4},{6,7},{7,6},{8,9},{9,8},{10,11... | collective-permute-start | bytes 1179656 | tf_op jit(solution)/shard_map/ppermute | solution.py:196
  65.6 5.0 %collective-permute-start.11 = (bf16[2,3,32,256]{3,2,1,0:T(8,128)(2,1)S(1)}, bf16[2,3,32,256]{3,2,1,0:T(8,128)(2,1)S(1)}, u32[]{:S(2)}, u32[]{:S(2)}) collective-permute-start(bf16[2,3,32,256]{3,2,1,0:T(8,128)(2,1)S(1)} %get-tuple-element.58), channel_id=1, source_target_pairs={{0,4},{1,5},{4,8},{5,9},{8,12},{9,13},{12,14},{13,15},{14,10},{15,... | collective-permute-start | bytes 294920 | tf_op jit(solution)/shard_map/ppermute | solution.py:207
  70.0 6.4 %collective-permute-start.20 = (bf16[2,3,32,512]{3,2,1,0:T(8,128)(2,1)S(1)}, bf16[2,3,32,512]{3,2,1,0:T(8,128)(2,1)S(1)}, u32[]{:S(2)}, u32[]{:S(2)}) collective-permute-start(bf16[2,3,32,512]{3,2,1,0:T(8,128)(2,1)S(1)} %pad_maximum_fusion.2), channel_id=1, source_target_pairs={{0,2},{1,3},{4,0},{5,1},{8,4},{9,5},{12,8},{13,9},{14,12},{15,13},... | collective-permute-start | bytes 589832 | tf_op jit(solution)/shard_map/ppermute | solution.py:208
  70.6 6.3 %collective-permute-start.13 = (bf16[2,3,32,512]{3,2,1,0:T(8,128)(2,1)S(1)}, bf16[2,3,32,512]{3,2,1,0:T(8,128)(2,1)S(1)}, u32[]{:S(2)}, u32[]{:S(2)}) collective-permute-start(bf16[2,3,32,512]{3,2,1,0:T(8,128)(2,1)S(1)} %pad_maximum_fusion.1), channel_id=1, source_target_pairs={{0,4},{1,5},{4,8},{5,9},{8,12},{9,13},{12,14},{13,15},{14,10},{15,... | collective-permute-start | bytes 589832 | tf_op jit(solution)/shard_map/ppermute | solution.py:207
  72.3 8.0 %collective-permute-start.16 = (f32[1,1,2,3,32,512]{5,4,3,2,1,0:T(8,128)S(1)}, f32[1,1,2,3,32,512]{5,4,3,2,1,0:T(8,128)S(1)}, u32[]{:S(2)}, u32[]{:S(2)}) collective-permute-start(f32[1,1,2,3,32,512]{5,4,3,2,1,0:T(8,128)S(1)} %get-tuple-element.37), channel_id=1, source_target_pairs={{0,1},{1,0},{2,3},{3,2},{4,5},{5,4},{6,7},{7,6},{8,9},{9,8},{10,11... | collective-permute-start | bytes 1179656 | tf_op jit(solution)/shard_map/ppermute | solution.py:196
  72.3 8.0 %collective-permute-start.23 = (f32[1,1,2,3,32,512]{5,4,3,2,1,0:T(8,128)S(1)}, f32[1,1,2,3,32,512]{5,4,3,2,1,0:T(8,128)S(1)}, u32[]{:S(2)}, u32[]{:S(2)}) collective-permute-start(f32[1,1,2,3,32,512]{5,4,3,2,1,0:T(8,128)S(1)} %get-tuple-element.34), channel_id=1, source_target_pairs={{0,1},{1,0},{2,3},{3,2},{4,5},{5,4},{6,7},{7,6},{8,9},{9,8},{10,11... | collective-permute-start | bytes 1179656 | tf_op jit(solution)/shard_map/ppermute | solution.py:196
  78.2 5.7 %collective-permute-start.15 = (bf16[2,3,32,512]{3,2,1,0:T(8,128)(2,1)S(1)}, bf16[2,3,32,512]{3,2,1,0:T(8,128)(2,1)S(1)}, u32[]{:S(2)}, u32[]{:S(2)}) collective-permute-start(bf16[2,3,32,512]{3,2,1,0:T(8,128)(2,1)S(1)} %get-tuple-element.43), channel_id=1, source_target_pairs={{0,4},{1,5},{4,8},{5,9},{8,12},{9,13},{12,14},{13,15},{14,10},{15,... | collective-permute-start | bytes 589832 | tf_op jit(solution)/shard_map/ppermute | solution.py:207
  79.8 5.7 %collective-permute-start.22 = (bf16[2,3,32,512]{3,2,1,0:T(8,128)(2,1)S(1)}, bf16[2,3,32,512]{3,2,1,0:T(8,128)(2,1)S(1)}, u32[]{:S(2)}, u32[]{:S(2)}) collective-permute-start(bf16[2,3,32,512]{3,2,1,0:T(8,128)(2,1)S(1)} %get-tuple-element.44), channel_id=1, source_target_pairs={{0,2},{1,3},{4,0},{5,1},{8,4},{9,5},{12,8},{13,9},{14,12},{15,13},... | collective-permute-start | bytes 589832 | tf_op jit(solution)/shard_map/ppermute | solution.py:208
  80.3 8.5 %collective-permute-start.9 = (f32[1,1,2,3,32,512]{5,4,3,2,1,0:T(8,128)S(1)}, f32[1,1,2,3,32,512]{5,4,3,2,1,0:T(8,128)S(1)}, u32[]{:S(2)}, u32[]{:S(2)}) collective-permute-start(f32[1,1,2,3,32,512]{5,4,3,2,1,0:T(8,128)S(1)} %get-tuple-element.33), channel_id=1, source_target_pairs={{0,1},{1,0},{2,3},{3,2},{4,5},{5,4},{6,7},{7,6},{8,9},{9,8},{10,11... | collective-permute-start | bytes 1179656 | tf_op jit(solution)/shard_map/ppermute | solution.py:196
  86.8 5.7 %collective-permute-start.17 = (bf16[2,3,32,512]{3,2,1,0:T(8,128)(2,1)S(1)}, bf16[2,3,32,512]{3,2,1,0:T(8,128)(2,1)S(1)}, u32[]{:S(2)}, u32[]{:S(2)}) collective-permute-start(bf16[2,3,32,512]{3,2,1,0:T(8,128)(2,1)S(1)} %get-tuple-element.41), channel_id=1, source_target_pairs={{0,4},{1,5},{4,8},{5,9},{8,12},{9,13},{12,14},{13,15},{14,10},{15,... | collective-permute-start | bytes 589832 | tf_op jit(solution)/shard_map/ppermute | solution.py:207
  88.4 5.7 %collective-permute-start.24 = (bf16[2,3,32,512]{3,2,1,0:T(8,128)(2,1)S(1)}, bf16[2,3,32,512]{3,2,1,0:T(8,128)(2,1)S(1)}, u32[]{:S(2)}, u32[]{:S(2)}) collective-permute-start(bf16[2,3,32,512]{3,2,1,0:T(8,128)(2,1)S(1)} %get-tuple-element.42), channel_id=1, source_target_pairs={{0,2},{1,3},{4,0},{5,1},{8,4},{9,5},{12,8},{13,9},{14,12},{15,13},... | collective-permute-start | bytes 589832 | tf_op jit(solution)/shard_map/ppermute | solution.py:208
  95.6 7.2 %collective-permute-start.25 = (bf16[2,3,32,512]{3,2,1,0:T(8,128)(2,1)S(1)}, bf16[2,3,32,512]{3,2,1,0:T(8,128)(2,1)S(1)}, u32[]{:S(2)}, u32[]{:S(2)}) collective-permute-start(bf16[2,3,32,512]{3,2,1,0:T(8,128)(2,1)S(1)} %get-tuple-element.13), channel_id=1, source_target_pairs={{0,4},{1,5},{4,8},{5,9},{8,12},{9,13},{12,14},{13,15},{14,10},{15,... | collective-permute-start | bytes 589832 | tf_op jit(solution)/shard_map/ppermute | solution.py:181
  97.2 7.2 %collective-permute-start.26 = (bf16[2,3,32,512]{3,2,1,0:T(8,128)(2,1)S(1)}, bf16[2,3,32,512]{3,2,1,0:T(8,128)(2,1)S(1)}, u32[]{:S(2)}, u32[]{:S(2)}) collective-permute-start(bf16[2,3,32,512]{3,2,1,0:T(8,128)(2,1)S(1)} %get-tuple-element.13), channel_id=1, source_target_pairs={{0,2},{1,3},{4,0},{5,1},{8,4},{9,5},{12,8},{13,9},{14,12},{15,13},... | collective-permute-start | bytes 589832 | tf_op jit(solution)/shard_map/ppermute | solution.py:184
  102.8 6.3 %collective-permute-start.27 = (bf16[2,3,32,512]{3,2,1,0:T(8,128)(2,1)S(1)}, bf16[2,3,32,512]{3,2,1,0:T(8,128)(2,1)S(1)}, u32[]{:S(2)}, u32[]{:S(2)}) collective-permute-start(bf16[2,3,32,512]{3,2,1,0:T(8,128)(2,1)S(1)} %collective-permute-done.25), channel_id=1, source_target_pairs={{0,4},{1,5},{4,8},{5,9},{8,12},{9,13},{12,14},{13,15},{14,10},{15,... | collective-permute-start | bytes 589832 | tf_op jit(solution)/shard_map/ppermute | solution.py:181
  104.4 6.3 %collective-permute-start.28 = (bf16[2,3,32,512]{3,2,1,0:T(8,128)(2,1)S(1)}, bf16[2,3,32,512]{3,2,1,0:T(8,128)(2,1)S(1)}, u32[]{:S(2)}, u32[]{:S(2)}) collective-permute-start(bf16[2,3,32,512]{3,2,1,0:T(8,128)(2,1)S(1)} %collective-permute-done.26), channel_id=1, source_target_pairs={{0,2},{1,3},{4,0},{5,1},{8,4},{9,5},{12,8},{13,9},{14,12},{15,13},... | collective-permute-start | bytes 589832 | tf_op jit(solution)/shard_map/ppermute | solution.py:184
  109.0 5.7 %collective-permute-start.29 = (bf16[2,3,32,512]{3,2,1,0:T(8,128)(2,1)S(1)}, bf16[2,3,32,512]{3,2,1,0:T(8,128)(2,1)S(1)}, u32[]{:S(2)}, u32[]{:S(2)}) collective-permute-start(bf16[2,3,32,512]{3,2,1,0:T(8,128)(2,1)S(1)} %collective-permute-done.27), channel_id=1, source_target_pairs={{0,4},{1,5},{4,8},{5,9},{8,12},{9,13},{12,14},{13,15},{14,10},{15,... | collective-permute-start | bytes 589832 | tf_op jit(solution)/shard_map/ppermute | solution.py:181
  110.7 5.7 %collective-permute-start.30 = (bf16[2,3,32,512]{3,2,1,0:T(8,128)(2,1)S(1)}, bf16[2,3,32,512]{3,2,1,0:T(8,128)(2,1)S(1)}, u32[]{:S(2)}, u32[]{:S(2)}) collective-permute-start(bf16[2,3,32,512]{3,2,1,0:T(8,128)(2,1)S(1)} %collective-permute-done.28), channel_id=1, source_target_pairs={{0,2},{1,3},{4,0},{5,1},{8,4},{9,5},{12,8},{13,9},{14,12},{15,13},... | collective-permute-start | bytes 589832 | tf_op jit(solution)/shard_map/ppermute | solution.py:184
  114.7 4.7 %collective-permute-start.31 = (bf16[2,3,32,256]{3,2,1,0:T(8,128)(2,1)S(1)}, bf16[2,3,32,256]{3,2,1,0:T(8,128)(2,1)S(1)}, u32[]{:S(2)}, u32[]{:S(2)}) collective-permute-start(bf16[2,3,32,256]{3,2,1,0:T(8,128)(2,1)S(1)} %slice.112), channel_id=1, source_target_pairs={{0,4},{1,5},{4,8},{5,9},{8,12},{9,13},{12,14},{13,15},{14,10},{15,... | collective-permute-start | bytes 294920 | tf_op jit(solution)/shard_map/ppermute | solution.py:176
  116.4 4.8 %collective-permute-start.32 = (bf16[2,3,32,256]{3,2,1,0:T(8,128)(2,1)S(1)}, bf16[2,3,32,256]{3,2,1,0:T(8,128)(2,1)S(1)}, u32[]{:S(2)}, u32[]{:S(2)}) collective-permute-start(bf16[2,3,32,256]{3,2,1,0:T(8,128)(2,1)S(1)} %slice.113), channel_id=1, source_target_pairs={{0,2},{1,3},{4,0},{5,1},{8,4},{9,5},{12,8},{13,9},{14,12},{15,13},... | collective-permute-start | bytes 294920 | tf_op jit(solution)/shard_map/ppermute | solution.py:177
  121.3 3.6 %collective-permute-start.33 = (bf16[8,2,3,32,512]{4,3,2,1,0:T(8,128)(2,1)S(1)}, bf16[8,2,3,32,512]{4,3,2,1,0:T(8,128)(2,1)}, u32[]{:S(2)}, u32[]{:S(2)}) collective-permute-start(bf16[8,2,3,32,512]{4,3,2,1,0:T(8,128)(2,1)S(1)} %fusion.19.mine_ref), channel_id=1, source_target_pairs={{0,1},{1,0},{2,3},{3,2},{4,5},{5,4},{6,7},{7,6},{8,9},{9,8},{10,11... | collective-permute-start | bytes 4718600 | tf_op jit(solution)/shard_map/ppermute | solution.py:186
  135.6 2.3 %collective-permute-start.43 = (f32[1,1,2,3,32,512]{5,4,3,2,1,0:T(8,128)S(1)}, f32[1,1,2,3,32,512]{5,4,3,2,1,0:T(8,128)S(1)}, u32[]{:S(2)}, u32[]{:S(2)}) collective-permute-start(f32[1,1,2,3,32,512]{5,4,3,2,1,0:T(8,128)S(1)} %get-tuple-element.21), channel_id=1, source_target_pairs={{0,1},{1,0},{2,3},{3,2},{4,5},{5,4},{6,7},{7,6},{8,9},{9,8},{10,11... | collective-permute-start | bytes 1179656 | tf_op jit(solution)/shard_map/ppermute | solution.py:196
  138.2 4.9 %collective-permute-start.44 = (bf16[2,3,32,256]{3,2,1,0:T(8,128)(2,1)S(1)}, bf16[2,3,32,256]{3,2,1,0:T(8,128)(2,1)S(1)}, u32[]{:S(2)}, u32[]{:S(2)}) collective-permute-start(bf16[2,3,32,256]{3,2,1,0:T(8,128)(2,1)S(1)} %get-tuple-element.57), channel_id=1, source_target_pairs={{0,2},{1,3},{4,0},{5,1},{8,4},{9,5},{12,8},{13,9},{14,12},{15,13},... | collective-permute-start | bytes 294920 | tf_op jit(solution)/shard_map/ppermute | solution.py:208
  138.6 7.0 %collective-permute-start.39 = (f32[1,1,2,3,32,512]{5,4,3,2,1,0:T(8,128)S(1)}, f32[1,1,2,3,32,512]{5,4,3,2,1,0:T(8,128)S(1)}, u32[]{:S(2)}, u32[]{:S(2)}) collective-permute-start(f32[1,1,2,3,32,512]{5,4,3,2,1,0:T(8,128)S(1)} %get-tuple-element.23), channel_id=1, source_target_pairs={{0,1},{1,0},{2,3},{3,2},{4,5},{5,4},{6,7},{7,6},{8,9},{9,8},{10,11... | collective-permute-start | bytes 1179656 | tf_op jit(solution)/shard_map/ppermute | solution.py:196
  138.6 7.5 %collective-permute-start.46 = (f32[1,1,2,3,32,512]{5,4,3,2,1,0:T(8,128)S(1)}, f32[1,1,2,3,32,512]{5,4,3,2,1,0:T(8,128)S(1)}, u32[]{:S(2)}, u32[]{:S(2)}) collective-permute-start(f32[1,1,2,3,32,512]{5,4,3,2,1,0:T(8,128)S(1)} %get-tuple-element.20), channel_id=1, source_target_pairs={{0,1},{1,0},{2,3},{3,2},{4,5},{5,4},{6,7},{7,6},{8,9},{9,8},{10,11... | collective-permute-start | bytes 1179656 | tf_op jit(solution)/shard_map/ppermute | solution.py:196
  139.1 4.8 %collective-permute-start.36 = (bf16[2,3,32,256]{3,2,1,0:T(8,128)(2,1)S(1)}, bf16[2,3,32,256]{3,2,1,0:T(8,128)(2,1)S(1)}, u32[]{:S(2)}, u32[]{:S(2)}) collective-permute-start(bf16[2,3,32,256]{3,2,1,0:T(8,128)(2,1)S(1)} %get-tuple-element.56), channel_id=1, source_target_pairs={{0,4},{1,5},{4,8},{5,9},{8,12},{9,13},{12,14},{13,15},{14,10},{15,... | collective-permute-start | bytes 294920 | tf_op jit(solution)/shard_map/ppermute | solution.py:207
  143.1 6.1 %collective-permute-start.45 = (bf16[2,3,32,512]{3,2,1,0:T(8,128)(2,1)S(1)}, bf16[2,3,32,512]{3,2,1,0:T(8,128)(2,1)S(1)}, u32[]{:S(2)}, u32[]{:S(2)}) collective-permute-start(bf16[2,3,32,512]{3,2,1,0:T(8,128)(2,1)S(1)} %pad_maximum_fusion.4), channel_id=1, source_target_pairs={{0,2},{1,3},{4,0},{5,1},{8,4},{9,5},{12,8},{13,9},{14,12},{15,13},... | collective-permute-start | bytes 589832 | tf_op jit(solution)/shard_map/ppermute | solution.py:208
  144.0 6.0 %collective-permute-start.38 = (bf16[2,3,32,512]{3,2,1,0:T(8,128)(2,1)S(1)}, bf16[2,3,32,512]{3,2,1,0:T(8,128)(2,1)S(1)}, u32[]{:S(2)}, u32[]{:S(2)}) collective-permute-start(bf16[2,3,32,512]{3,2,1,0:T(8,128)(2,1)S(1)} %pad_maximum_fusion.3), channel_id=1, source_target_pairs={{0,4},{1,5},{4,8},{5,9},{8,12},{9,13},{12,14},{13,15},{14,10},{15,... | collective-permute-start | bytes 589832 | tf_op jit(solution)/shard_map/ppermute | solution.py:207
  145.6 6.6 %collective-permute-start.41 = (f32[1,1,2,3,32,512]{5,4,3,2,1,0:T(8,128)S(1)}, f32[1,1,2,3,32,512]{5,4,3,2,1,0:T(8,128)S(1)}, u32[]{:S(2)}, u32[]{:S(2)}) collective-permute-start(f32[1,1,2,3,32,512]{5,4,3,2,1,0:T(8,128)S(1)} %get-tuple-element.22), channel_id=1, source_target_pairs={{0,1},{1,0},{2,3},{3,2},{4,5},{5,4},{6,7},{7,6},{8,9},{9,8},{10,11... | collective-permute-start | bytes 1179656 | tf_op jit(solution)/shard_map/ppermute | solution.py:196
  145.7 6.6 %collective-permute-start.48 = (f32[1,1,2,3,32,512]{5,4,3,2,1,0:T(8,128)S(1)}, f32[1,1,2,3,32,512]{5,4,3,2,1,0:T(8,128)S(1)}, u32[]{:S(2)}, u32[]{:S(2)}) collective-permute-start(f32[1,1,2,3,32,512]{5,4,3,2,1,0:T(8,128)S(1)} %get-tuple-element.19), channel_id=1, source_target_pairs={{0,1},{1,0},{2,3},{3,2},{4,5},{5,4},{6,7},{7,6},{8,9},{9,8},{10,11... | collective-permute-start | bytes 1179656 | tf_op jit(solution)/shard_map/ppermute | solution.py:196
  150.2 5.7 %collective-permute-start.40 = (bf16[2,3,32,512]{3,2,1,0:T(8,128)(2,1)S(1)}, bf16[2,3,32,512]{3,2,1,0:T(8,128)(2,1)S(1)}, u32[]{:S(2)}, u32[]{:S(2)}) collective-permute-start(bf16[2,3,32,512]{3,2,1,0:T(8,128)(2,1)S(1)} %get-tuple-element.28), channel_id=1, source_target_pairs={{0,4},{1,5},{4,8},{5,9},{8,12},{9,13},{12,14},{13,15},{14,10},{15,... | collective-permute-start | bytes 589832 | tf_op jit(solution)/shard_map/ppermute | solution.py:207
  151.9 5.7 %collective-permute-start.47 = (bf16[2,3,32,512]{3,2,1,0:T(8,128)(2,1)S(1)}, bf16[2,3,32,512]{3,2,1,0:T(8,128)(2,1)S(1)}, u32[]{:S(2)}, u32[]{:S(2)}) collective-permute-start(bf16[2,3,32,512]{3,2,1,0:T(8,128)(2,1)S(1)} %get-tuple-element.29), channel_id=1, source_target_pairs={{0,2},{1,3},{4,0},{5,1},{8,4},{9,5},{12,8},{13,9},{14,12},{15,13},... | collective-permute-start | bytes 589832 | tf_op jit(solution)/shard_map/ppermute | solution.py:208
  152.3 8.7 %collective-permute-start.34 = (f32[1,1,2,3,32,512]{5,4,3,2,1,0:T(8,128)S(1)}, f32[1,1,2,3,32,512]{5,4,3,2,1,0:T(8,128)S(1)}, u32[]{:S(2)}, u32[]{:S(2)}) collective-permute-start(f32[1,1,2,3,32,512]{5,4,3,2,1,0:T(8,128)S(1)} %get-tuple-element.18), channel_id=1, source_target_pairs={{0,1},{1,0},{2,3},{3,2},{4,5},{5,4},{6,7},{7,6},{8,9},{9,8},{10,11... | collective-permute-start | bytes 1179656 | tf_op jit(solution)/shard_map/ppermute | solution.py:196
  157.8 5.7 %collective-permute-start.42 = (bf16[2,3,32,512]{3,2,1,0:T(8,128)(2,1)S(1)}, bf16[2,3,32,512]{3,2,1,0:T(8,128)(2,1)S(1)}, u32[]{:S(2)}, u32[]{:S(2)}) collective-permute-start(bf16[2,3,32,512]{3,2,1,0:T(8,128)(2,1)S(1)} %get-tuple-element.26), channel_id=1, source_target_pairs={{0,4},{1,5},{4,8},{5,9},{8,12},{9,13},{12,14},{13,15},{14,10},{15,... | collective-permute-start | bytes 589832 | tf_op jit(solution)/shard_map/ppermute | solution.py:207
  159.3 5.7 %collective-permute-start.49 = (bf16[2,3,32,512]{3,2,1,0:T(8,128)(2,1)S(1)}, bf16[2,3,32,512]{3,2,1,0:T(8,128)(2,1)S(1)}, u32[]{:S(2)}, u32[]{:S(2)}) collective-permute-start(bf16[2,3,32,512]{3,2,1,0:T(8,128)(2,1)S(1)} %get-tuple-element.27), channel_id=1, source_target_pairs={{0,2},{1,3},{4,0},{5,1},{8,4},{9,5},{12,8},{13,9},{14,12},{15,13},... | collective-permute-start | bytes 589832 | tf_op jit(solution)/shard_map/ppermute | solution.py:208
  (15 other events, 110.9 us)

commit v10 on v8

--- a/solution.py
+++ b/solution.py
@@ -71,7 +71,7 @@
     return lax.dot_general(left, right, (((0,), (0,)), ((), ())), preferred_element_type=jnp.float32)
 
 
-def _block_kernel(q_ref, k_ref, v_ref, r_ref, w_ref, o_ref, g_ref):
+def _block_kernel(core_ref, offs_ref, q_ref, k_ref, v_ref, r_ref, w_ref, o_ref, g_ref):
     heads = w_ref.shape[0]
     width = w_ref.shape[3]
     for head in range(heads):
@@ -98,28 +98,35 @@
         e1 = (r_ref[:, head : head + 1] * d1).astype(jnp.bfloat16)
         e3 = (r_ref[:, heads + head : heads + head + 1] * d3).astype(jnp.bfloat16)
         b2 = (r_ref[:, 2 * heads + head : 2 * heads + head + 1] * (act * h3)).astype(jnp.bfloat16)
-        chips = g_ref.shape[0]
+        chips = g_ref.shape[1]
         rows = g_ref.shape[4]
+        own = core_ref[0]
         for which, grad in enumerate((_tn(e1, key_rows), _tn(e3, key_rows), _tn(value_rows, b2))):
             for chip in range(chips):
                 for core in range(2):
                     lo_row = (2 * chip + core) * rows
-                    g_ref[chip, core, head, which] = grad[lo_row : lo_row + rows]
-
-
-def fused_block(query, key_rows, value_rows, rate_rows, wbf, chips):
+                    slot = core + own - 2 * core * own
+                    g_ref[slot, offs_ref[chip], head, which] = grad[lo_row : lo_row + rows]
+
+
+def fused_block(query, key_rows, value_rows, rate_rows, wbf, offs):
     tokens = query.shape[0]
     rates_t = rate_rows.reshape(-1, tokens).T
     heads, mats, hid, dh = wbf.shape
+    chips = offs.shape[0]
+    core = (lax.axis_index("tok") % 2).astype(jnp.int32).reshape(1)
+    vmem = pl.BlockSpec(memory_space=pltpu.VMEM)
+    smem = pl.BlockSpec(memory_space=pltpu.SMEM)
     return pl.pallas_call(
         _block_kernel,
         out_shape=(
             jax.ShapeDtypeStruct(query.shape, jnp.bfloat16),
-            jax.ShapeDtypeStruct((chips, 2, heads, mats, hid // (2 * chips), dh), jnp.float32),
+            jax.ShapeDtypeStruct((2, chips, heads, mats, hid // (2 * chips), dh), jnp.float32),
         ),
+        in_specs=[smem, smem] + [vmem] * 5,
+        out_specs=(vmem, vmem),
         compiler_params=pltpu.CompilerParams(vmem_limit_bytes=48 * 1024 * 1024),
-    )(query, key_rows, value_rows, rates_t, wbf)
-
+    )(core, offs, query, key_rows, value_rows, rates_t, wbf)
 
 class Ring:
     def __init__(self, mesh):
@@ -178,16 +185,16 @@
         full = jnp.moveaxis(full, (0, 1), (2, 3))
         return full.reshape(h, g, self.chips * 2 * rows, f)
 
+    def offsets(self):
+        table = [[(self.place[c] - self.place[t // 2]) % self.chips for c in range(self.chips)] for t in range(2 * self.chips)]
+        return jnp.array(table, jnp.int32)[lax.axis_index("tok")]
+
     def reduce(self, q):
         _, _, h, g, rows, f = q.shape
-        core = lax.axis_index("tok") % 2
 
         def chip_sum(step):
-            chip = self.chip_at(step)
-            keep = lax.dynamic_slice(q, (chip, core, 0, 0, 0, 0), (1, 1, h, g, rows, f))
-            send = lax.dynamic_slice(q, (chip, 1 - core, 0, 0, 0, 0), (1, 1, h, g, rows, f))
-            got = lax.ppermute(send, "tok", self.swap)
-            return (keep + got).reshape(h, g, rows, f)
+            j = step % self.chips
+            return q[0, j] + lax.ppermute(q[1, j], "tok", self.swap)
 
         total = chip_sum(0)
         if self.chips % 2 == 0:
@@ -234,11 +241,12 @@
 
     def on_device(queries, keys, values, rates, fast_weights):
         nblocks = queries.shape[0]
+        offs = ring.offsets()
         own = fast_weights
         blocks = []
         for span in range(nblocks):
             gathered = ring.gather(own.astype(jnp.bfloat16))
-            normed, partial_value = fused_block(queries[span], keys[span], values[span], rates[span], gathered, ring.chips)
+            normed, partial_value = fused_block(queries[span], keys[span], values[span], rates[span], gathered, offs)
             blocks.append(normed)
             own = renorm(own, own + ring.reduce(partial_value))
         return (jnp.stack(blocks), own)

time: 165 us -> 166 us (level)
  local copies, waits for them, and re-layouts: 20.8 us -> 27.2 us
  waiting for transfers between devices: 64.5 us -> 60.6 us
  between operations: 23 us -> 19.3 us
    squeeze x0 -> x3, local copies, waits for them, and re-layouts: none -> 5.43 us  [the longest x2 4.74 us: chip_sum(): return q[0, j] + lax.ppermute(q[1, j], 'tok', self.swap)]
    dynamic_slice x2 -> x0, local copies, waits for them, and re-layouts: 4.8 us -> none  [chip_sum(): lax.dynamic_slice(q, (chip, 1 - core, 0, 0, 0, 0), (1, 1, h, g, rows, f))]
    ppermute x6, waiting for transfers between devices: 17.8 us -> 15.3 us  [gather(): a = lax.ppermute(a, 'tok', self.cw)]
    unnamed x20 -> x14, local copies, waits for them, and re-layouts: 2.28 us -> 0.03 us
    dynamic_update_slice x6, local copies, waits for them, and re-layouts: 2.19 us -> 4.17 us  [gather(): ring = lax.dynamic_update_index_in_dim(ring, b, self.chip_at(k), 0)]
    dynamic_update_slice x6, local copies, waits for them, and re-layouts: 2.22 us -> 4.11 us  [gather(): ring = lax.dynamic_update_index_in_dim(ring, a, self.chip_at(-k), 0)]
  transfers between devices with their start and end apart: 50 -> 50, of which waited for: 34 -> 34; matrix products, arithmetic and copies ran while one was open for 7% -> 11% of each run, Pallas kernels for 0% -> 0%
where the time goes in v10:
time: 166 us
  waiting for transfers between devices  60.6 us (37%)
  starting transfers between devices  38.3 us (23%)
  local copies, waits for them, and re-layouts  27.2 us (16%)
  between operations  19.3 us (12%)
  Pallas kernels  13.7 us (8%)
  other arithmetic  6.78 us (4%)
    ppermute x8, waiting for transfers between devices, reduce(): lax.ppermute(b.astype(jnp.bfloat16), 'tok', self.ccw).astype(jnp.float32)  17.5 us
    ppermute x8, waiting for transfers between devices, reduce(): a = lax.ppermute(a.astype(jnp.bfloat16), 'tok', self.cw).astype(jnp.float32)  15.4 us
    ppermute x6, waiting for transfers between devices, gather(): a = lax.ppermute(a, 'tok', self.cw)  15.3 us
    pallas_call x2, Pallas kernels, fused_block(): pl.pallas_call(_block_kernel, out_shape=(jax.ShapeDtypeStruct(query.shape...  13.7 us
    ppermute x8, starting transfers between devices, reduce(): a = lax.ppermute(a.astype(jnp.bfloat16), 'tok', self.cw).astype(jnp.float32)  13.1 us
    ppermute x6, starting transfers between devices, gather(): a = lax.ppermute(a, 'tok', self.cw)  11.6 us
    squeeze x2, local copies, waits for them, and re-layouts, chip_sum(): return q[0, j] + lax.ppermute(q[1, j], 'tok', self.swap)  4.74 us
    ppermute x2, waiting for transfers between devices, gather(): b = lax.ppermute(b[..., f // 2:], 'tok', self.ccw)  4.45 us
  transfers between devices with their start and end apart: 50, of which 34 were waited for; matrix products, arithmetic and copies ran while one was open for 11% of the time, Pallas kernels for 0%

profile of v10, /device:TPU:0, one launch (start us, length us, event | category | flops | bytes accessed | tf_op | source)
XLA Modules:
  0.0 165.9 jit_solution(16916034587278802017)
XLA Ops:
  0.7 1.4 broadcast.57.clone
  2.8 3.1 %collective-permute-start = (bf16[2,3,32,512]{3,2,1,0:T(8,128)(2,1)S(1)}, bf16[2,3,32,512]{3,2,1,0:T(8,128)(2,1)S(1)}, u32[]{:S(2)}, u32[]{:S(2)}) collective-permute-start(bf16[2,3,32,512]{3,2,1,0:T(8,128)(2,1)S(1)} %get-tuple-element.17), channel_id=1, source_target_pairs={{0,4},{1,5},{4,8},{5,9},{8,12},{9,13},{12,14},{13,15},{14,10},{15,... | collective-permute-start | bytes 589832 | tf_op jit(solution)/shard_map/ppermute | solution.py:176
  25.4 2.1 %collective-permute-start.2 = (bf16[2,3,32,512]{3,2,1,0:T(8,128)(2,1)S(1)}, bf16[2,3,32,512]{3,2,1,0:T(8,128)(2,1)S(1)}, u32[]{:S(2)}, u32[]{:S(2)}) collective-permute-start(bf16[2,3,32,512]{3,2,1,0:T(8,128)(2,1)S(1)} %collective-permute-done), channel_id=1, source_target_pairs={{0,4},{1,5},{4,8},{5,9},{8,12},{9,13},{12,14},{13,15},{14,10},{15,... | collective-permute-start | bytes 589832 | tf_op jit(solution)/shard_map/ppermute | solution.py:176
  28.9 3.0 %collective-permute-done.2 = bf16[2,3,32,512]{3,2,1,0:T(8,128)(2,1)S(1)} collective-permute-done((bf16[2,3,32,512]{3,2,1,0:T(8,128)(2,1)S(1)}, bf16[2,3,32,512]{3,2,1,0:T(8,128)(2,1)S(1)}, u32[]{:S(2)}, u32[]{:S(2)}) %collective-permute-start.2) | collective-permute-done | bytes 196640 | tf_op jit(solution)/shard_map/ppermute | solution.py:176
  31.8 1.7 %collective-permute-start.4 = (bf16[2,3,32,512]{3,2,1,0:T(8,128)(2,1)S(1)}, bf16[2,3,32,512]{3,2,1,0:T(8,128)(2,1)S(1)}, u32[]{:S(2)}, u32[]{:S(2)}) collective-permute-start(bf16[2,3,32,512]{3,2,1,0:T(8,128)(2,1)S(1)} %collective-permute-done.2), channel_id=1, source_target_pairs={{0,4},{1,5},{4,8},{5,9},{8,12},{9,13},{12,14},{13,15},{14,10},{15,... | collective-permute-start | bytes 589832 | tf_op jit(solution)/shard_map/ppermute | solution.py:176
  35.2 2.3 %collective-permute-done.4 = bf16[2,3,32,512]{3,2,1,0:T(8,128)(2,1)S(1)} collective-permute-done((bf16[2,3,32,512]{3,2,1,0:T(8,128)(2,1)S(1)}, bf16[2,3,32,512]{3,2,1,0:T(8,128)(2,1)S(1)}, u32[]{:S(2)}, u32[]{:S(2)}) %collective-permute-start.4) | collective-permute-done | bytes 196640 | tf_op jit(solution)/shard_map/ppermute | solution.py:176
  37.5 1.9 %collective-permute-start.6 = (bf16[2,3,32,256]{3,2,1,0:T(8,128)(2,1)S(1)}, bf16[2,3,32,256]{3,2,1,0:T(8,128)(2,1)S(1)}, u32[]{:S(2)}, u32[]{:S(2)}) collective-permute-start(bf16[2,3,32,256]{3,2,1,0:T(8,128)(2,1)S(1)} %slice.232), channel_id=1, source_target_pairs={{0,4},{1,5},{4,8},{5,9},{8,12},{9,13},{12,14},{13,15},{14,10},{15,... | collective-permute-start | bytes 294920 | tf_op jit(solution)/shard_map/ppermute | solution.py:171
  41.1 1.1 collective-permute-done.6
  42.2 1.9 %collective-permute-done.7 = bf16[2,3,32,256]{3,2,1,0:T(8,128)(2,1)S(1)} collective-permute-done((bf16[2,3,32,256]{3,2,1,0:T(8,128)(2,1)S(1)}, bf16[2,3,32,256]{3,2,1,0:T(8,128)(2,1)S(1)}, u32[]{:S(2)}, u32[]{:S(2)}) %collective-permute-start.7) | collective-permute-done | bytes 98336 | tf_op jit(solution)/shard_map/ppermute | solution.py:172
  45.7 1.7 %slice_bitcast_fusion.3 = (bf16[256,1024]{1,0:T(8,128)(2,1)S(1)}, bf16[256,1024]{1,0:T(8,128)(2,1)S(1)}, bf16[256,1024]{1,0:T(8,128)(2,1)S(1)}, bf16[256,1024]{1,0:T(8,128)(2,1)S(1)}) fusion(bf16[2,256,1024]{2,1,0:T(8,128)(2,1)} %param.36, bf16[2,256,1024]{2,1,0:T(8,128)(2,1)} %param.35), kind=kLoop, calls=%fused_computation.8 | loop fusion | bytes 4194304 | tf_op jit(solution)/shard_map/squeeze | solution.py:249
  47.8 1.6 bitcast_dynamic-update-slice_fusion.2
  49.5 1.6 bitcast_dynamic-update-slice_fusion.1
  51.1 6.8 %shard_map.329 = (bf16[256,1024]{1,0:T(8,128)(2,1)S(1)}, f32[2,8,2,3,32,512]{5,4,3,2,1,0:T(8,128)}) custom-call(s32[1]{0:T(128)} %bitcast.core_ref, s32[8]{0:T(128)S(1)} %fusion.30.offs_ref, bf16[256,1024]{1,0:T(8,128)(2,1)S(1)} %get-tuple-element.52.q_ref, bf16[256,1024]{1,0:T(8,128)(2,1)S(1)} %get-tuple-element.70.k_ref, ...), custom_call_target="tpu_custom_call" | custom-call | tf_op jit(solution)/shard_map/pallas_call | solution.py:120
  57.9 2.3 %slice_bitcast_fusion.21 = (f32[2,3,32,512]{3,2,1,0:T(8,128)S(1)}, f32[2,3,32,512]{3,2,1,0:T(8,128)S(1)}, f32[2,3,32,512]{3,2,1,0:T(8,128)S(1)}, f32[2,3,32,512]...) fusion(f32[2,8,2,3,32,512]{5,4,3,2,1,0:T(8,128)} %get-tuple-ele, ...), kind=kLoop, calls=%fused_computation.70 | loop fusion | bytes 6291456 | tf_op jit(solution)/shard_map/squeeze | solution.py:197
  64.4 1.8 %collective-permute-start.11 = (bf16[2,3,32,256]{3,2,1,0:T(8,128)(2,1)S(1)}, bf16[2,3,32,256]{3,2,1,0:T(8,128)(2,1)S(1)}, u32[]{:S(2)}, u32[]{:S(2)}) collective-permute-start(bf16[2,3,32,256]{3,2,1,0:T(8,128)(2,1)S(1)} %get-tuple-element.58), channel_id=1, source_target_pairs={{0,4},{1,5},{4,8},{5,9},{8,12},{9,13},{12,14},{13,15},{14,10},{15,... | collective-permute-start | bytes 294920 | tf_op jit(solution)/shard_map/ppermute | solution.py:207
  66.2 2.4 %collective-permute-done.19 = bf16[2,3,32,256]{3,2,1,0:T(8,128)(2,1)S(1)} collective-permute-done((bf16[2,3,32,256]{3,2,1,0:T(8,128)(2,1)S(1)}, bf16[2,3,32,256]{3,2,1,0:T(8,128)(2,1)S(1)}, u32[]{:S(2)}, u32[]{:S(2)}) %collective-permute-start.19) | collective-permute-done | bytes 98336 | tf_op jit(solution)/shard_map/ppermute | solution.py:208
  69.4 1.7 %collective-permute-start.13 = (bf16[2,3,32,512]{3,2,1,0:T(8,128)(2,1)S(1)}, bf16[2,3,32,512]{3,2,1,0:T(8,128)(2,1)S(1)}, u32[]{:S(2)}, u32[]{:S(2)}) collective-permute-start(bf16[2,3,32,512]{3,2,1,0:T(8,128)(2,1)S(1)} %pad_maximum_fusion.1), channel_id=1, source_target_pairs={{0,4},{1,5},{4,8},{5,9},{8,12},{9,13},{12,14},{13,15},{14,10},{15,... | collective-permute-start | bytes 589832 | tf_op jit(solution)/shard_map/ppermute | solution.py:207
  71.6 3.5 %collective-permute-done.20 = bf16[2,3,32,512]{3,2,1,0:T(8,128)(2,1)S(1)} collective-permute-done((bf16[2,3,32,512]{3,2,1,0:T(8,128)(2,1)S(1)}, bf16[2,3,32,512]{3,2,1,0:T(8,128)(2,1)S(1)}, u32[]{:S(2)}, u32[]{:S(2)}) %collective-permute-start.20) | collective-permute-done | bytes 196640 | tf_op jit(solution)/shard_map/ppermute | solution.py:208
  75.9 1.6 collective-permute-start.15
  78.0 3.6 %collective-permute-done.15 = bf16[2,3,32,512]{3,2,1,0:T(8,128)(2,1)S(1)} collective-permute-done((bf16[2,3,32,512]{3,2,1,0:T(8,128)(2,1)S(1)}, bf16[2,3,32,512]{3,2,1,0:T(8,128)(2,1)S(1)}, u32[]{:S(2)}, u32[]{:S(2)}) %collective-permute-start.15) | collective-permute-done | bytes 196640 | tf_op jit(solution)/shard_map/ppermute | solution.py:207
  81.6 1.5 collective-permute-done.22
  83.3 1.6 collective-permute-start.17
  85.4 3.6 %collective-permute-done.17 = bf16[2,3,32,512]{3,2,1,0:T(8,128)(2,1)S(1)} collective-permute-done((bf16[2,3,32,512]{3,2,1,0:T(8,128)(2,1)S(1)}, bf16[2,3,32,512]{3,2,1,0:T(8,128)(2,1)S(1)}, u32[]{:S(2)}, u32[]{:S(2)}) %collective-permute-start.17) | collective-permute-done | bytes 196640 | tf_op jit(solution)/shard_map/ppermute | solution.py:207
  89.0 1.6 collective-permute-done.24
  90.9 1.4 broadcast.57
  93.0 1.6 collective-permute-start.25
  95.1 5.1 %collective-permute-done.25 = bf16[2,3,32,512]{3,2,1,0:T(8,128)(2,1)S(1)} collective-permute-done((bf16[2,3,32,512]{3,2,1,0:T(8,128)(2,1)S(1)}, bf16[2,3,32,512]{3,2,1,0:T(8,128)(2,1)S(1)}, u32[]{:S(2)}, u32[]{:S(2)}) %collective-permute-start.25) | collective-permute-done | bytes 196640 | tf_op jit(solution)/shard_map/ppermute | solution.py:176
  100.2 1.6 collective-permute-start.27
  103.6 2.9 %collective-permute-done.27 = bf16[2,3,32,512]{3,2,1,0:T(8,128)(2,1)S(1)} collective-permute-done((bf16[2,3,32,512]{3,2,1,0:T(8,128)(2,1)S(1)}, bf16[2,3,32,512]{3,2,1,0:T(8,128)(2,1)S(1)}, u32[]{:S(2)}, u32[]{:S(2)}) %collective-permute-start.27) | collective-permute-done | bytes 196640 | tf_op jit(solution)/shard_map/ppermute | solution.py:176
  106.5 1.6 collective-permute-start.29
  110.0 2.1 %collective-permute-done.29 = bf16[2,3,32,512]{3,2,1,0:T(8,128)(2,1)S(1)} collective-permute-done((bf16[2,3,32,512]{3,2,1,0:T(8,128)(2,1)S(1)}, bf16[2,3,32,512]{3,2,1,0:T(8,128)(2,1)S(1)}, u32[]{:S(2)}, u32[]{:S(2)}) %collective-permute-start.29) | collective-permute-done | bytes 196640 | tf_op jit(solution)/shard_map/ppermute | solution.py:176
  112.2 1.6 collective-permute-start.31
  116.8 2.6 %collective-permute-done.32 = bf16[2,3,32,256]{3,2,1,0:T(8,128)(2,1)S(1)} collective-permute-done((bf16[2,3,32,256]{3,2,1,0:T(8,128)(2,1)S(1)}, bf16[2,3,32,256]{3,2,1,0:T(8,128)(2,1)S(1)}, u32[]{:S(2)}, u32[]{:S(2)}) %collective-permute-start.32) | collective-permute-done | bytes 98336 | tf_op jit(solution)/shard_map/ppermute | solution.py:172
  120.6 1.6 bitcast_dynamic-update-slice_fusion
  122.2 1.6 collective-permute-done.33
  123.8 1.6 bitcast_dynamic-update-slice_fusion.3
  125.4 6.9 %shard_map.330 = (bf16[256,1024]{1,0:T(8,128)(2,1)S(1)}, f32[2,8,2,3,32,512]{5,4,3,2,1,0:T(8,128)}) custom-call(s32[1]{0:T(128)} %bitcast.core_ref, s32[8]{0:T(128)S(1)} %fusion.30.offs_ref, bf16[256,1024]{1,0:T(8,128)(2,1)S(1)} %get-tuple-element.53.q_ref, bf16[256,1024]{1,0:T(8,128)(2,1)S(1)} %get-tuple-element.69.k_ref, ...), custom_call_target="tpu_custom_call" | custom-call | tf_op jit(solution)/shard_map/pallas_call | solution.py:120
  132.3 2.4 %slice_bitcast_fusion.13 = (f32[2,3,32,512]{3,2,1,0:T(8,128)S(1)}, f32[2,3,32,512]{3,2,1,0:T(8,128)S(1)}, f32[2,3,32,512]{3,2,1,0:T(8,128)S(1)}, f32[2,3,32,512]...) fusion(f32[2,8,2,3,32,512]{5,4,3,2,1,0:T(8,128)} %get-tuple-ele, ...), kind=kLoop, calls=%fused_computation.60 | loop fusion | bytes 6291456 | tf_op jit(solution)/shard_map/squeeze | solution.py:197
  139.0 1.6 collective-permute-start.36
  140.6 2.2 %collective-permute-done.44 = bf16[2,3,32,256]{3,2,1,0:T(8,128)(2,1)S(1)} collective-permute-done((bf16[2,3,32,256]{3,2,1,0:T(8,128)(2,1)S(1)}, bf16[2,3,32,256]{3,2,1,0:T(8,128)(2,1)S(1)}, u32[]{:S(2)}, u32[]{:S(2)}) %collective-permute-start.44) | collective-permute-done | bytes 98336 | tf_op jit(solution)/shard_map/ppermute | solution.py:208
  143.8 1.6 collective-permute-start.38
  145.9 3.1 %collective-permute-done.45 = bf16[2,3,32,512]{3,2,1,0:T(8,128)(2,1)S(1)} collective-permute-done((bf16[2,3,32,512]{3,2,1,0:T(8,128)(2,1)S(1)}, bf16[2,3,32,512]{3,2,1,0:T(8,128)(2,1)S(1)}, u32[]{:S(2)}, u32[]{:S(2)}) %collective-permute-start.45) | collective-permute-done | bytes 196640 | tf_op jit(solution)/shard_map/ppermute | solution.py:208
  150.0 1.6 collective-permute-start.40
  152.1 3.6 %collective-permute-done.40 = bf16[2,3,32,512]{3,2,1,0:T(8,128)(2,1)S(1)} collective-permute-done((bf16[2,3,32,512]{3,2,1,0:T(8,128)(2,1)S(1)}, bf16[2,3,32,512]{3,2,1,0:T(8,128)(2,1)S(1)}, u32[]{:S(2)}, u32[]{:S(2)}) %collective-permute-start.40) | collective-permute-done | bytes 196640 | tf_op jit(solution)/shard_map/ppermute | solution.py:207
  155.8 1.5 collective-permute-done.47
  157.5 1.6 collective-permute-start.42
  160.7 2.6 %collective-permute-done.42 = bf16[2,3,32,512]{3,2,1,0:T(8,128)(2,1)S(1)} collective-permute-done((bf16[2,3,32,512]{3,2,1,0:T(8,128)(2,1)S(1)}, bf16[2,3,32,512]{3,2,1,0:T(8,128)(2,1)S(1)}, u32[]{:S(2)}, u32[]{:S(2)}) %collective-permute-start.42) | collective-permute-done | bytes 196640 | tf_op jit(solution)/shard_map/ppermute | solution.py:207
  163.2 1.5 collective-permute-done.49
  (134 shorter events, 35.5 us)
Async XLA Ops:
  2.8 22.6 %collective-permute-start = (bf16[2,3,32,512]{3,2,1,0:T(8,128)(2,1)S(1)}, bf16[2,3,32,512]{3,2,1,0:T(8,128)(2,1)S(1)}, u32[]{:S(2)}, u32[]{:S(2)}) collective-permute-start(bf16[2,3,32,512]{3,2,1,0:T(8,128)(2,1)S(1)} %get-tuple-element.17), channel_id=1, source_target_pairs={{0,4},{1,5},{4,8},{5,9},{8,12},{9,13},{12,14},{13,15},{14,10},{15,... | collective-permute-start | bytes 589832 | tf_op jit(solution)/shard_map/ppermute | solution.py:176
  5.8 21.7 %collective-permute-start.1 = (bf16[2,3,32,512]{3,2,1,0:T(8,128)(2,1)S(1)}, bf16[2,3,32,512]{3,2,1,0:T(8,128)(2,1)S(1)}, u32[]{:S(2)}, u32[]{:S(2)}) collective-permute-start(bf16[2,3,32,512]{3,2,1,0:T(8,128)(2,1)S(1)} %get-tuple-element.17), channel_id=1, source_target_pairs={{0,2},{1,3},{4,0},{5,1},{8,4},{9,5},{12,8},{13,9},{14,12},{15,13},... | collective-permute-start | bytes 589832 | tf_op jit(solution)/shard_map/ppermute | solution.py:179
  25.4 6.4 %collective-permute-start.2 = (bf16[2,3,32,512]{3,2,1,0:T(8,128)(2,1)S(1)}, bf16[2,3,32,512]{3,2,1,0:T(8,128)(2,1)S(1)}, u32[]{:S(2)}, u32[]{:S(2)}) collective-permute-start(bf16[2,3,32,512]{3,2,1,0:T(8,128)(2,1)S(1)} %collective-permute-done), channel_id=1, source_target_pairs={{0,4},{1,5},{4,8},{5,9},{8,12},{9,13},{12,14},{13,15},{14,10},{15,... | collective-permute-start | bytes 589832 | tf_op jit(solution)/shard_map/ppermute | solution.py:176
  27.5 6.1 %collective-permute-start.3 = (bf16[2,3,32,512]{3,2,1,0:T(8,128)(2,1)S(1)}, bf16[2,3,32,512]{3,2,1,0:T(8,128)(2,1)S(1)}, u32[]{:S(2)}, u32[]{:S(2)}) collective-permute-start(bf16[2,3,32,512]{3,2,1,0:T(8,128)(2,1)S(1)} %collective-permute-done.1), channel_id=1, source_target_pairs={{0,2},{1,3},{4,0},{5,1},{8,4},{9,5},{12,8},{13,9},{14,12},{15,13},... | collective-permute-start | bytes 589832 | tf_op jit(solution)/shard_map/ppermute | solution.py:179
  31.8 5.7 %collective-permute-start.4 = (bf16[2,3,32,512]{3,2,1,0:T(8,128)(2,1)S(1)}, bf16[2,3,32,512]{3,2,1,0:T(8,128)(2,1)S(1)}, u32[]{:S(2)}, u32[]{:S(2)}) collective-permute-start(bf16[2,3,32,512]{3,2,1,0:T(8,128)(2,1)S(1)} %collective-permute-done.2), channel_id=1, source_target_pairs={{0,4},{1,5},{4,8},{5,9},{8,12},{9,13},{12,14},{13,15},{14,10},{15,... | collective-permute-start | bytes 589832 | tf_op jit(solution)/shard_map/ppermute | solution.py:176
  33.6 5.8 %collective-permute-start.5 = (bf16[2,3,32,512]{3,2,1,0:T(8,128)(2,1)S(1)}, bf16[2,3,32,512]{3,2,1,0:T(8,128)(2,1)S(1)}, u32[]{:S(2)}, u32[]{:S(2)}) collective-permute-start(bf16[2,3,32,512]{3,2,1,0:T(8,128)(2,1)S(1)} %collective-permute-done.3), channel_id=1, source_target_pairs={{0,2},{1,3},{4,0},{5,1},{8,4},{9,5},{12,8},{13,9},{14,12},{15,13},... | collective-permute-start | bytes 589832 | tf_op jit(solution)/shard_map/ppermute | solution.py:179
  37.5 4.7 %collective-permute-start.6 = (bf16[2,3,32,256]{3,2,1,0:T(8,128)(2,1)S(1)}, bf16[2,3,32,256]{3,2,1,0:T(8,128)(2,1)S(1)}, u32[]{:S(2)}, u32[]{:S(2)}) collective-permute-start(bf16[2,3,32,256]{3,2,1,0:T(8,128)(2,1)S(1)} %slice.232), channel_id=1, source_target_pairs={{0,4},{1,5},{4,8},{5,9},{8,12},{9,13},{12,14},{13,15},{14,10},{15,... | collective-permute-start | bytes 294920 | tf_op jit(solution)/shard_map/ppermute | solution.py:171
  39.4 4.7 %collective-permute-start.7 = (bf16[2,3,32,256]{3,2,1,0:T(8,128)(2,1)S(1)}, bf16[2,3,32,256]{3,2,1,0:T(8,128)(2,1)S(1)}, u32[]{:S(2)}, u32[]{:S(2)}) collective-permute-start(bf16[2,3,32,256]{3,2,1,0:T(8,128)(2,1)S(1)} %slice.233), channel_id=1, source_target_pairs={{0,2},{1,3},{4,0},{5,1},{8,4},{9,5},{12,8},{13,9},{14,12},{15,13},... | collective-permute-start | bytes 294920 | tf_op jit(solution)/shard_map/ppermute | solution.py:172
  44.7 4.7 %collective-permute-start.8 = (bf16[8,2,3,32,512]{4,3,0,2,1:T(8,128)(2,1)}, bf16[8,2,3,32,512]{4,3,0,2,1:T(8,128)(2,1)}, u32[]{:S(2)}, u32[]{:S(2)}) collective-permute-start(bf16[8,2,3,32,512]{4,3,0,2,1:T(8,128)(2,1)} %fusion.28), channel_id=1, source_target_pairs={{0,1},{1,0},{2,3},{3,2},{4,5},{5,4},{6,7},{7,6},{8,9},{9,8},{10,11... | collective-permute-start | bytes 4718600 | tf_op jit(solution)/shard_map/ppermute | solution.py:181
  60.2 1.9 %collective-permute-start.10 = (f32[2,3,32,512]{3,2,1,0:T(8,128)S(1)}, f32[2,3,32,512]{3,2,1,0:T(8,128)S(1)}, u32[]{:S(2)}, u32[]{:S(2)}) collective-permute-start(f32[2,3,32,512]{3,2,1,0:T(8,128)S(1)} %get-tuple-element.40), channel_id=1, source_target_pairs={{0,1},{1,0},{2,3},{3,2},{4,5},{5,4},{6,7},{7,6},{8,9},{9,8},{10,11... | collective-permute-start | bytes 1179656 | tf_op jit(solution)/shard_map/ppermute | solution.py:197
  60.9 2.4 %collective-permute-start.18 = (f32[2,3,32,512]{3,2,1,0:T(8,128)S(1)}, f32[2,3,32,512]{3,2,1,0:T(8,128)S(1)}, u32[]{:S(2)}, u32[]{:S(2)}) collective-permute-start(f32[2,3,32,512]{3,2,1,0:T(8,128)S(1)} %get-tuple-element.36), channel_id=1, source_target_pairs={{0,1},{1,0},{2,3},{3,2},{4,5},{5,4},{6,7},{7,6},{8,9},{9,8},{10,11... | collective-permute-start | bytes 1179656 | tf_op jit(solution)/shard_map/ppermute | solution.py:197
  63.6 5.1 %collective-permute-start.19 = (bf16[2,3,32,256]{3,2,1,0:T(8,128)(2,1)S(1)}, bf16[2,3,32,256]{3,2,1,0:T(8,128)(2,1)S(1)}, u32[]{:S(2)}, u32[]{:S(2)}) collective-permute-start(bf16[2,3,32,256]{3,2,1,0:T(8,128)(2,1)S(1)} %get-tuple-element.59), channel_id=1, source_target_pairs={{0,2},{1,3},{4,0},{5,1},{8,4},{9,5},{12,8},{13,9},{14,12},{15,13},... | collective-permute-start | bytes 294920 | tf_op jit(solution)/shard_map/ppermute | solution.py:208
  63.8 7.3 %collective-permute-start.14 = (f32[2,3,32,512]{3,2,1,0:T(8,128)S(1)}, f32[2,3,32,512]{3,2,1,0:T(8,128)S(1)}, u32[]{:S(2)}, u32[]{:S(2)}) collective-permute-start(f32[2,3,32,512]{3,2,1,0:T(8,128)S(1)} %get-tuple-element.38), channel_id=1, source_target_pairs={{0,1},{1,0},{2,3},{3,2},{4,5},{5,4},{6,7},{7,6},{8,9},{9,8},{10,11... | collective-permute-start | bytes 1179656 | tf_op jit(solution)/shard_map/ppermute | solution.py:197
  64.1 7.6 %collective-permute-start.21 = (f32[2,3,32,512]{3,2,1,0:T(8,128)S(1)}, f32[2,3,32,512]{3,2,1,0:T(8,128)S(1)}, u32[]{:S(2)}, u32[]{:S(2)}) collective-permute-start(f32[2,3,32,512]{3,2,1,0:T(8,128)S(1)} %get-tuple-element.35), channel_id=1, source_target_pairs={{0,1},{1,0},{2,3},{3,2},{4,5},{5,4},{6,7},{7,6},{8,9},{9,8},{10,11... | collective-permute-start | bytes 1179656 | tf_op jit(solution)/shard_map/ppermute | solution.py:197
  64.4 5.0 %collective-permute-start.11 = (bf16[2,3,32,256]{3,2,1,0:T(8,128)(2,1)S(1)}, bf16[2,3,32,256]{3,2,1,0:T(8,128)(2,1)S(1)}, u32[]{:S(2)}, u32[]{:S(2)}) collective-permute-start(bf16[2,3,32,256]{3,2,1,0:T(8,128)(2,1)S(1)} %get-tuple-element.58), channel_id=1, source_target_pairs={{0,4},{1,5},{4,8},{5,9},{8,12},{9,13},{12,14},{13,15},{14,10},{15,... | collective-permute-start | bytes 294920 | tf_op jit(solution)/shard_map/ppermute | solution.py:207
  68.7 6.4 %collective-permute-start.20 = (bf16[2,3,32,512]{3,2,1,0:T(8,128)(2,1)S(1)}, bf16[2,3,32,512]{3,2,1,0:T(8,128)(2,1)S(1)}, u32[]{:S(2)}, u32[]{:S(2)}) collective-permute-start(bf16[2,3,32,512]{3,2,1,0:T(8,128)(2,1)S(1)} %pad_maximum_fusion.2), channel_id=1, source_target_pairs={{0,2},{1,3},{4,0},{5,1},{8,4},{9,5},{12,8},{13,9},{14,12},{15,13},... | collective-permute-start | bytes 589832 | tf_op jit(solution)/shard_map/ppermute | solution.py:208
  69.4 6.2 %collective-permute-start.13 = (bf16[2,3,32,512]{3,2,1,0:T(8,128)(2,1)S(1)}, bf16[2,3,32,512]{3,2,1,0:T(8,128)(2,1)S(1)}, u32[]{:S(2)}, u32[]{:S(2)}) collective-permute-start(bf16[2,3,32,512]{3,2,1,0:T(8,128)(2,1)S(1)} %pad_maximum_fusion.1), channel_id=1, source_target_pairs={{0,4},{1,5},{4,8},{5,9},{8,12},{9,13},{12,14},{13,15},{14,10},{15,... | collective-permute-start | bytes 589832 | tf_op jit(solution)/shard_map/ppermute | solution.py:207
  71.1 6.9 %collective-permute-start.16 = (f32[2,3,32,512]{3,2,1,0:T(8,128)S(1)}, f32[2,3,32,512]{3,2,1,0:T(8,128)S(1)}, u32[]{:S(2)}, u32[]{:S(2)}) collective-permute-start(f32[2,3,32,512]{3,2,1,0:T(8,128)S(1)} %get-tuple-element.37), channel_id=1, source_target_pairs={{0,1},{1,0},{2,3},{3,2},{4,5},{5,4},{6,7},{7,6},{8,9},{9,8},{10,11... | collective-permute-start | bytes 1179656 | tf_op jit(solution)/shard_map/ppermute | solution.py:197
  71.1 6.9 %collective-permute-start.23 = (f32[2,3,32,512]{3,2,1,0:T(8,128)S(1)}, f32[2,3,32,512]{3,2,1,0:T(8,128)S(1)}, u32[]{:S(2)}, u32[]{:S(2)}) collective-permute-start(f32[2,3,32,512]{3,2,1,0:T(8,128)S(1)} %get-tuple-element.34), channel_id=1, source_target_pairs={{0,1},{1,0},{2,3},{3,2},{4,5},{5,4},{6,7},{7,6},{8,9},{9,8},{10,11... | collective-permute-start | bytes 1179656 | tf_op jit(solution)/shard_map/ppermute | solution.py:197
  75.9 5.7 %collective-permute-start.15 = (bf16[2,3,32,512]{3,2,1,0:T(8,128)(2,1)S(1)}, bf16[2,3,32,512]{3,2,1,0:T(8,128)(2,1)S(1)}, u32[]{:S(2)}, u32[]{:S(2)}) collective-permute-start(bf16[2,3,32,512]{3,2,1,0:T(8,128)(2,1)S(1)} %get-tuple-element.43), channel_id=1, source_target_pairs={{0,4},{1,5},{4,8},{5,9},{8,12},{9,13},{12,14},{13,15},{14,10},{15,... | collective-permute-start | bytes 589832 | tf_op jit(solution)/shard_map/ppermute | solution.py:207
  77.4 5.7 %collective-permute-start.22 = (bf16[2,3,32,512]{3,2,1,0:T(8,128)(2,1)S(1)}, bf16[2,3,32,512]{3,2,1,0:T(8,128)(2,1)S(1)}, u32[]{:S(2)}, u32[]{:S(2)}) collective-permute-start(bf16[2,3,32,512]{3,2,1,0:T(8,128)(2,1)S(1)} %get-tuple-element.44), channel_id=1, source_target_pairs={{0,2},{1,3},{4,0},{5,1},{8,4},{9,5},{12,8},{13,9},{14,12},{15,13},... | collective-permute-start | bytes 589832 | tf_op jit(solution)/shard_map/ppermute | solution.py:208
  78.0 7.4 %collective-permute-start.9 = (f32[2,3,32,512]{3,2,1,0:T(8,128)S(1)}, f32[2,3,32,512]{3,2,1,0:T(8,128)S(1)}, u32[]{:S(2)}, u32[]{:S(2)}) collective-permute-start(f32[2,3,32,512]{3,2,1,0:T(8,128)S(1)} %get-tuple-element.33), channel_id=1, source_target_pairs={{0,1},{1,0},{2,3},{3,2},{4,5},{5,4},{6,7},{7,6},{8,9},{9,8},{10,11... | collective-permute-start | bytes 1179656 | tf_op jit(solution)/shard_map/ppermute | solution.py:197
  83.3 5.7 %collective-permute-start.17 = (bf16[2,3,32,512]{3,2,1,0:T(8,128)(2,1)S(1)}, bf16[2,3,32,512]{3,2,1,0:T(8,128)(2,1)S(1)}, u32[]{:S(2)}, u32[]{:S(2)}) collective-permute-start(bf16[2,3,32,512]{3,2,1,0:T(8,128)(2,1)S(1)} %get-tuple-element.41), channel_id=1, source_target_pairs={{0,4},{1,5},{4,8},{5,9},{8,12},{9,13},{12,14},{13,15},{14,10},{15,... | collective-permute-start | bytes 589832 | tf_op jit(solution)/shard_map/ppermute | solution.py:207
  85.0 5.7 %collective-permute-start.24 = (bf16[2,3,32,512]{3,2,1,0:T(8,128)(2,1)S(1)}, bf16[2,3,32,512]{3,2,1,0:T(8,128)(2,1)S(1)}, u32[]{:S(2)}, u32[]{:S(2)}) collective-permute-start(bf16[2,3,32,512]{3,2,1,0:T(8,128)(2,1)S(1)} %get-tuple-element.42), channel_id=1, source_target_pairs={{0,2},{1,3},{4,0},{5,1},{8,4},{9,5},{12,8},{13,9},{14,12},{15,13},... | collective-permute-start | bytes 589832 | tf_op jit(solution)/shard_map/ppermute | solution.py:208
  93.0 7.1 %collective-permute-start.25 = (bf16[2,3,32,512]{3,2,1,0:T(8,128)(2,1)S(1)}, bf16[2,3,32,512]{3,2,1,0:T(8,128)(2,1)S(1)}, u32[]{:S(2)}, u32[]{:S(2)}) collective-permute-start(bf16[2,3,32,512]{3,2,1,0:T(8,128)(2,1)S(1)} %get-tuple-element.13), channel_id=1, source_target_pairs={{0,4},{1,5},{4,8},{5,9},{8,12},{9,13},{12,14},{13,15},{14,10},{15,... | collective-permute-start | bytes 589832 | tf_op jit(solution)/shard_map/ppermute | solution.py:176
  94.6 7.8 %collective-permute-start.26 = (bf16[2,3,32,512]{3,2,1,0:T(8,128)(2,1)S(1)}, bf16[2,3,32,512]{3,2,1,0:T(8,128)(2,1)S(1)}, u32[]{:S(2)}, u32[]{:S(2)}) collective-permute-start(bf16[2,3,32,512]{3,2,1,0:T(8,128)(2,1)S(1)} %get-tuple-element.13), channel_id=1, source_target_pairs={{0,2},{1,3},{4,0},{5,1},{8,4},{9,5},{12,8},{13,9},{14,12},{15,13},... | collective-permute-start | bytes 589832 | tf_op jit(solution)/shard_map/ppermute | solution.py:179
  100.2 6.3 %collective-permute-start.27 = (bf16[2,3,32,512]{3,2,1,0:T(8,128)(2,1)S(1)}, bf16[2,3,32,512]{3,2,1,0:T(8,128)(2,1)S(1)}, u32[]{:S(2)}, u32[]{:S(2)}) collective-permute-start(bf16[2,3,32,512]{3,2,1,0:T(8,128)(2,1)S(1)} %collective-permute-done.25), channel_id=1, source_target_pairs={{0,4},{1,5},{4,8},{5,9},{8,12},{9,13},{12,14},{13,15},{14,10},{15,... | collective-permute-start | bytes 589832 | tf_op jit(solution)/shard_map/ppermute | solution.py:176
  102.4 6.4 %collective-permute-start.28 = (bf16[2,3,32,512]{3,2,1,0:T(8,128)(2,1)S(1)}, bf16[2,3,32,512]{3,2,1,0:T(8,128)(2,1)S(1)}, u32[]{:S(2)}, u32[]{:S(2)}) collective-permute-start(bf16[2,3,32,512]{3,2,1,0:T(8,128)(2,1)S(1)} %collective-permute-done.26), channel_id=1, source_target_pairs={{0,2},{1,3},{4,0},{5,1},{8,4},{9,5},{12,8},{13,9},{14,12},{15,13},... | collective-permute-start | bytes 589832 | tf_op jit(solution)/shard_map/ppermute | solution.py:179
  106.5 5.7 %collective-permute-start.29 = (bf16[2,3,32,512]{3,2,1,0:T(8,128)(2,1)S(1)}, bf16[2,3,32,512]{3,2,1,0:T(8,128)(2,1)S(1)}, u32[]{:S(2)}, u32[]{:S(2)}) collective-permute-start(bf16[2,3,32,512]{3,2,1,0:T(8,128)(2,1)S(1)} %collective-permute-done.27), channel_id=1, source_target_pairs={{0,4},{1,5},{4,8},{5,9},{8,12},{9,13},{12,14},{13,15},{14,10},{15,... | collective-permute-start | bytes 589832 | tf_op jit(solution)/shard_map/ppermute | solution.py:176
  108.9 5.7 %collective-permute-start.30 = (bf16[2,3,32,512]{3,2,1,0:T(8,128)(2,1)S(1)}, bf16[2,3,32,512]{3,2,1,0:T(8,128)(2,1)S(1)}, u32[]{:S(2)}, u32[]{:S(2)}) collective-permute-start(bf16[2,3,32,512]{3,2,1,0:T(8,128)(2,1)S(1)} %collective-permute-done.28), channel_id=1, source_target_pairs={{0,2},{1,3},{4,0},{5,1},{8,4},{9,5},{12,8},{13,9},{14,12},{15,13},... | collective-permute-start | bytes 589832 | tf_op jit(solution)/shard_map/ppermute | solution.py:179
  112.2 4.7 %collective-permute-start.31 = (bf16[2,3,32,256]{3,2,1,0:T(8,128)(2,1)S(1)}, bf16[2,3,32,256]{3,2,1,0:T(8,128)(2,1)S(1)}, u32[]{:S(2)}, u32[]{:S(2)}) collective-permute-start(bf16[2,3,32,256]{3,2,1,0:T(8,128)(2,1)S(1)} %slice.240), channel_id=1, source_target_pairs={{0,4},{1,5},{4,8},{5,9},{8,12},{9,13},{12,14},{13,15},{14,10},{15,... | collective-permute-start | bytes 294920 | tf_op jit(solution)/shard_map/ppermute | solution.py:171
  114.5 4.8 %collective-permute-start.32 = (bf16[2,3,32,256]{3,2,1,0:T(8,128)(2,1)S(1)}, bf16[2,3,32,256]{3,2,1,0:T(8,128)(2,1)S(1)}, u32[]{:S(2)}, u32[]{:S(2)}) collective-permute-start(bf16[2,3,32,256]{3,2,1,0:T(8,128)(2,1)S(1)} %slice.241), channel_id=1, source_target_pairs={{0,2},{1,3},{4,0},{5,1},{8,4},{9,5},{12,8},{13,9},{14,12},{15,13},... | collective-permute-start | bytes 294920 | tf_op jit(solution)/shard_map/ppermute | solution.py:172
  120.1 3.8 %collective-permute-start.33 = (bf16[8,2,3,32,512]{4,3,0,2,1:T(8,128)(2,1)}, bf16[8,2,3,32,512]{4,3,0,2,1:T(8,128)(2,1)}, u32[]{:S(2)}, u32[]{:S(2)}) collective-permute-start(bf16[8,2,3,32,512]{4,3,0,2,1:T(8,128)(2,1)} %fusion.29), channel_id=1, source_target_pairs={{0,1},{1,0},{2,3},{3,2},{4,5},{5,4},{6,7},{7,6},{8,9},{9,8},{10,11... | collective-permute-start | bytes 4718600 | tf_op jit(solution)/shard_map/ppermute | solution.py:181
  135.0 2.1 %collective-permute-start.37 = (f32[2,3,32,512]{3,2,1,0:T(8,128)S(1)}, f32[2,3,32,512]{3,2,1,0:T(8,128)S(1)}, u32[]{:S(2)}, u32[]{:S(2)}) collective-permute-start(f32[2,3,32,512]{3,2,1,0:T(8,128)S(1)} %get-tuple-element.24), channel_id=1, source_target_pairs={{0,1},{1,0},{2,3},{3,2},{4,5},{5,4},{6,7},{7,6},{8,9},{9,8},{10,11... | collective-permute-start | bytes 1179656 | tf_op jit(solution)/shard_map/ppermute | solution.py:197
  135.3 2.3 %collective-permute-start.43 = (f32[2,3,32,512]{3,2,1,0:T(8,128)S(1)}, f32[2,3,32,512]{3,2,1,0:T(8,128)S(1)}, u32[]{:S(2)}, u32[]{:S(2)}) collective-permute-start(f32[2,3,32,512]{3,2,1,0:T(8,128)S(1)} %get-tuple-element.21), channel_id=1, source_target_pairs={{0,1},{1,0},{2,3},{3,2},{4,5},{5,4},{6,7},{7,6},{8,9},{9,8},{10,11... | collective-permute-start | bytes 1179656 | tf_op jit(solution)/shard_map/ppermute | solution.py:197
  138.0 4.9 %collective-permute-start.44 = (bf16[2,3,32,256]{3,2,1,0:T(8,128)(2,1)S(1)}, bf16[2,3,32,256]{3,2,1,0:T(8,128)(2,1)S(1)}, u32[]{:S(2)}, u32[]{:S(2)}) collective-permute-start(bf16[2,3,32,256]{3,2,1,0:T(8,128)(2,1)S(1)} %get-tuple-element.57), channel_id=1, source_target_pairs={{0,2},{1,3},{4,0},{5,1},{8,4},{9,5},{12,8},{13,9},{14,12},{15,13},... | collective-permute-start | bytes 294920 | tf_op jit(solution)/shard_map/ppermute | solution.py:208
  138.5 6.9 %collective-permute-start.39 = (f32[2,3,32,512]{3,2,1,0:T(8,128)S(1)}, f32[2,3,32,512]{3,2,1,0:T(8,128)S(1)}, u32[]{:S(2)}, u32[]{:S(2)}) collective-permute-start(f32[2,3,32,512]{3,2,1,0:T(8,128)S(1)} %get-tuple-element.23), channel_id=1, source_target_pairs={{0,1},{1,0},{2,3},{3,2},{4,5},{5,4},{6,7},{7,6},{8,9},{9,8},{10,11... | collective-permute-start | bytes 1179656 | tf_op jit(solution)/shard_map/ppermute | solution.py:197
  138.5 7.4 %collective-permute-start.46 = (f32[2,3,32,512]{3,2,1,0:T(8,128)S(1)}, f32[2,3,32,512]{3,2,1,0:T(8,128)S(1)}, u32[]{:S(2)}, u32[]{:S(2)}) collective-permute-start(f32[2,3,32,512]{3,2,1,0:T(8,128)S(1)} %get-tuple-element.20), channel_id=1, source_target_pairs={{0,1},{1,0},{2,3},{3,2},{4,5},{5,4},{6,7},{7,6},{8,9},{9,8},{10,11... | collective-permute-start | bytes 1179656 | tf_op jit(solution)/shard_map/ppermute | solution.py:197
  139.0 4.8 %collective-permute-start.36 = (bf16[2,3,32,256]{3,2,1,0:T(8,128)(2,1)S(1)}, bf16[2,3,32,256]{3,2,1,0:T(8,128)(2,1)S(1)}, u32[]{:S(2)}, u32[]{:S(2)}) collective-permute-start(bf16[2,3,32,256]{3,2,1,0:T(8,128)(2,1)S(1)} %get-tuple-element.56), channel_id=1, source_target_pairs={{0,4},{1,5},{4,8},{5,9},{8,12},{9,13},{12,14},{13,15},{14,10},{15,... | collective-permute-start | bytes 294920 | tf_op jit(solution)/shard_map/ppermute | solution.py:207
  142.9 6.2 %collective-permute-start.45 = (bf16[2,3,32,512]{3,2,1,0:T(8,128)(2,1)S(1)}, bf16[2,3,32,512]{3,2,1,0:T(8,128)(2,1)S(1)}, u32[]{:S(2)}, u32[]{:S(2)}) collective-permute-start(bf16[2,3,32,512]{3,2,1,0:T(8,128)(2,1)S(1)} %pad_maximum_fusion.4), channel_id=1, source_target_pairs={{0,2},{1,3},{4,0},{5,1},{8,4},{9,5},{12,8},{13,9},{14,12},{15,13},... | collective-permute-start | bytes 589832 | tf_op jit(solution)/shard_map/ppermute | solution.py:208
  143.8 6.0 %collective-permute-start.38 = (bf16[2,3,32,512]{3,2,1,0:T(8,128)(2,1)S(1)}, bf16[2,3,32,512]{3,2,1,0:T(8,128)(2,1)S(1)}, u32[]{:S(2)}, u32[]{:S(2)}) collective-permute-start(bf16[2,3,32,512]{3,2,1,0:T(8,128)(2,1)S(1)} %pad_maximum_fusion.3), channel_id=1, source_target_pairs={{0,4},{1,5},{4,8},{5,9},{8,12},{9,13},{12,14},{13,15},{14,10},{15,... | collective-permute-start | bytes 589832 | tf_op jit(solution)/shard_map/ppermute | solution.py:207
  145.4 6.7 %collective-permute-start.41 = (f32[2,3,32,512]{3,2,1,0:T(8,128)S(1)}, f32[2,3,32,512]{3,2,1,0:T(8,128)S(1)}, u32[]{:S(2)}, u32[]{:S(2)}) collective-permute-start(f32[2,3,32,512]{3,2,1,0:T(8,128)S(1)} %get-tuple-element.22), channel_id=1, source_target_pairs={{0,1},{1,0},{2,3},{3,2},{4,5},{5,4},{6,7},{7,6},{8,9},{9,8},{10,11... | collective-permute-start | bytes 1179656 | tf_op jit(solution)/shard_map/ppermute | solution.py:197
  145.4 6.7 %collective-permute-start.48 = (f32[2,3,32,512]{3,2,1,0:T(8,128)S(1)}, f32[2,3,32,512]{3,2,1,0:T(8,128)S(1)}, u32[]{:S(2)}, u32[]{:S(2)}) collective-permute-start(f32[2,3,32,512]{3,2,1,0:T(8,128)S(1)} %get-tuple-element.19), channel_id=1, source_target_pairs={{0,1},{1,0},{2,3},{3,2},{4,5},{5,4},{6,7},{7,6},{8,9},{9,8},{10,11... | collective-permute-start | bytes 1179656 | tf_op jit(solution)/shard_map/ppermute | solution.py:197
  150.0 5.7 %collective-permute-start.40 = (bf16[2,3,32,512]{3,2,1,0:T(8,128)(2,1)S(1)}, bf16[2,3,32,512]{3,2,1,0:T(8,128)(2,1)S(1)}, u32[]{:S(2)}, u32[]{:S(2)}) collective-permute-start(bf16[2,3,32,512]{3,2,1,0:T(8,128)(2,1)S(1)} %get-tuple-element.28), channel_id=1, source_target_pairs={{0,4},{1,5},{4,8},{5,9},{8,12},{9,13},{12,14},{13,15},{14,10},{15,... | collective-permute-start | bytes 589832 | tf_op jit(solution)/shard_map/ppermute | solution.py:207
  151.6 5.7 %collective-permute-start.47 = (bf16[2,3,32,512]{3,2,1,0:T(8,128)(2,1)S(1)}, bf16[2,3,32,512]{3,2,1,0:T(8,128)(2,1)S(1)}, u32[]{:S(2)}, u32[]{:S(2)}) collective-permute-start(bf16[2,3,32,512]{3,2,1,0:T(8,128)(2,1)S(1)} %get-tuple-element.29), channel_id=1, source_target_pairs={{0,2},{1,3},{4,0},{5,1},{8,4},{9,5},{12,8},{13,9},{14,12},{15,13},... | collective-permute-start | bytes 589832 | tf_op jit(solution)/shard_map/ppermute | solution.py:208
  152.1 8.5 %collective-permute-start.34 = (f32[2,3,32,512]{3,2,1,0:T(8,128)S(1)}, f32[2,3,32,512]{3,2,1,0:T(8,128)S(1)}, u32[]{:S(2)}, u32[]{:S(2)}) collective-permute-start(f32[2,3,32,512]{3,2,1,0:T(8,128)S(1)} %get-tuple-element.18), channel_id=1, source_target_pairs={{0,1},{1,0},{2,3},{3,2},{4,5},{5,4},{6,7},{7,6},{8,9},{9,8},{10,11... | collective-permute-start | bytes 1179656 | tf_op jit(solution)/shard_map/ppermute | solution.py:197
  157.5 5.7 %collective-permute-start.42 = (bf16[2,3,32,512]{3,2,1,0:T(8,128)(2,1)S(1)}, bf16[2,3,32,512]{3,2,1,0:T(8,128)(2,1)S(1)}, u32[]{:S(2)}, u32[]{:S(2)}) collective-permute-start(bf16[2,3,32,512]{3,2,1,0:T(8,128)(2,1)S(1)} %get-tuple-element.26), channel_id=1, source_target_pairs={{0,4},{1,5},{4,8},{5,9},{8,12},{9,13},{12,14},{13,15},{14,10},{15,... | collective-permute-start | bytes 589832 | tf_op jit(solution)/shard_map/ppermute | solution.py:207
  159.1 5.7 %collective-permute-start.49 = (bf16[2,3,32,512]{3,2,1,0:T(8,128)(2,1)S(1)}, bf16[2,3,32,512]{3,2,1,0:T(8,128)(2,1)S(1)}, u32[]{:S(2)}, u32[]{:S(2)}) collective-permute-start(bf16[2,3,32,512]{3,2,1,0:T(8,128)(2,1)S(1)} %get-tuple-element.27), channel_id=1, source_target_pairs={{0,2},{1,3},{4,0},{5,1},{8,4},{9,5},{12,8},{13,9},{14,12},{15,13},... | collective-permute-start | bytes 589832 | tf_op jit(solution)/shard_map/ppermute | solution.py:208
  (9 other events, 66.2 us)
